TPU v7x, 32 devices: a whole 2x2x4 slice. The times are simulated.
32 devices in a mesh: ens: 2 (over y), step: 8 (over z, x), rows: 2 (over core).
Axes of the slice: x: 2, y: 2, z: 4, core: 2. Of those that a mesh axis runs over, the one named last changes fastest.
Arguments:
- iterates: float32 [8, 8, 32, 512], P('step', 'ens', 'rows'), parts along dimension 1, may hold values from -6 to 6
- window_start: float32 [8, 32, 512], P('ens', 'rows'), parts along dimension 0, may hold values from -6 to 6
- coarse: bfloat16 [24, 32, 512], P('ens', 'rows'), parts along dimension 0, may hold values from -6 to 6
- step_levels: int32 [8, 2], P('step'), may hold values from 0 to 16, as said below
- level_embed: bfloat16 [17, 128], replicated, may hold values from -3 to 3
- lift_weight: bfloat16 [16, 128], replicated, may hold values from -1.5 to 1.5
- conv_first: bfloat16 [3, 3, 128, 128], replicated, may hold values from -0.1875 to 0.1875
- conv_second: bfloat16 [3, 3, 128, 128], replicated, may hold values from -0.1875 to 0.1875
- project_weight: bfloat16 [128, 384], replicated, may hold values from -0.5 to 0.5
- mix_weight: bfloat16 [128, 128], replicated, may hold values from -6 to 6
- output_weight: bfloat16 [128, 4], replicated, may hold values from -0.5 to 0.5
Outputs:
- trajectory: float32 [8, 8, 32, 512], P('step', 'ens', 'rows'), parts along dimension 1
- denoised: float32 [8, 8, 32, 512], P('step', 'ens', 'rows'), parts along dimension 1
There are 2 independent parts, one for each index of `ens`. A program takes and returns all parts, laid end to end along the dimension named above; an argument that names none is the same for every part. Nothing has to cross between parts.
Inputs may be any that keep to these rules, and one draw needn't show every extreme that they name: `step_levels`: row k gives the plan levels at which step k starts and ends: each step ends 1 or 3 levels after it starts (half of the steps each), each step starts where the one before it ends, the first starts at level 0 and the last ends at level 16.
All inputs are finite; a program needn't handle non-finite values.
Results may differ from a plain program's by a relative error of at most 0.0028.
Values may be sent and summed in bfloat16 or wider, within the bound.
No kernel may reach another device: no remote copies, remote signals or barrier semaphores. Data moves between devices by JAX's collectives and lax.ppermute only.
A program may use at most 64 MiB of HBM per device.

v0:
```python
import jax
import jax.numpy as jnp
from jax import lax
from jax.sharding import PartitionSpec as P

HEAD_DIM = 64


SIGMA_TOP = 8.0
SIGMA_END = 0.002


def from_behind(x, axis, by):
    devices = lax.axis_size(axis)
    pairs = [(i, i + by) for i in range(devices) if 0 <= i + by < devices]
    return lax.ppermute(x, axis, pairs)


def with_halo(x, sides, width):
    for axis, dim in sides:
        devices, length = (lax.axis_size(axis), x.shape[dim])
        up = [(i, (i + 1) % devices) for i in range(devices - 1)]
        down = [(j, i) for i, j in up]
        last = lax.slice_in_dim(x, length - width, length, axis=dim)
        leading = lax.slice_in_dim(x, 0, width, axis=dim)
        before = lax.ppermute(last, axis, up)
        after = lax.ppermute(leading, axis, down)
        x = jnp.concatenate([before, x, after], axis=dim)
    return x


def noise_level(levels, level_count):
    fraction = levels.astype(jnp.float32) / jnp.float32(level_count - 1)
    return SIGMA_TOP * jnp.exp(fraction * jnp.log(jnp.float32(SIGMA_END / SIGMA_TOP)))


def normalize(values):
    return values * lax.rsqrt(jnp.mean(values * values, axis=-1, keepdims=True) + 1e-06)


def silu_norm(values):
    return jax.nn.silu(normalize(values)).astype(jnp.bfloat16)


def feature_map(values):
    return jnp.where(values > 0, values + 1.0, jnp.exp(jnp.minimum(values, 0.0)))


def conv_band(padded, weight):
    band_rows = padded.shape[0] - 2
    band_width = padded.shape[1]
    col_padded = jnp.pad(padded, ((0, 0), (1, 1), (0, 0)))
    stacked = jnp.concatenate(
        [
            col_padded[:, 0:band_width],
            col_padded[:, 1 : band_width + 1],
            col_padded[:, 2 : band_width + 2],
        ],
        axis=-1,
    )
    folded = weight.reshape(3, 3 * weight.shape[2], weight.shape[3])
    result = jnp.zeros((band_rows, band_width, weight.shape[3]), jnp.float32)
    for row_shift in range(3):
        result = result + jnp.einsum(
            "rwk,kf->rwf",
            stacked[row_shift : row_shift + band_rows],
            folded[row_shift],
            preferred_element_type=jnp.float32,
        )
    return result


def local(
    iterates,
    window_start,
    coarse,
    step_levels,
    level_embed,
    lift_weight,
    conv_first,
    conv_second,
    project_weight,
    mix_weight,
    output_weight,
):
    level_count = 2 * lax.axis_size("step") + 1
    previous = from_behind(iterates, "step", 1)
    current = jnp.where(lax.axis_index("step") == 0, window_start, previous[0])
    levels = step_levels[0]
    sigmas = noise_level(levels, level_count)
    sigma_low = sigmas[0]
    sigma_high = sigmas[1]
    spread = sigma_low * sigma_low + 0.25
    scale_in = lax.rsqrt(spread)
    scale_skip = 0.25 / spread
    scale_out = 0.5 * sigma_low * lax.rsqrt(spread)
    inputs = jnp.concatenate([(scale_in * current).astype(jnp.bfloat16), coarse], axis=0)
    picker = (jnp.arange(level_count) == levels[0]).astype(jnp.bfloat16)[None]
    embed_row = jnp.dot(picker, level_embed, preferred_element_type=jnp.float32)[0]
    lifted = (
        jnp.einsum("crw,cf->rwf", inputs, lift_weight, preferred_element_type=jnp.float32)
        + embed_row
    ).astype(jnp.bfloat16)
    band_rows = lifted.shape[0]
    band_width = lifted.shape[1]
    feat_dim = lifted.shape[2]
    act_first = silu_norm(lifted.astype(jnp.float32))
    padded = with_halo(act_first, (("rows", 0),), 1)
    middle = conv_band(padded, conv_first)
    act_next = silu_norm(middle)
    padded_next = with_halo(act_next, (("rows", 0),), 1)
    hidden = lifted.astype(jnp.float32) + conv_band(padded_next, conv_second)
    head_count = feat_dim // HEAD_DIM
    pooled = (
        hidden.reshape(band_rows // 4, 4, band_width // 4, 4, feat_dim)
        .mean(axis=(1, 3))
        .reshape(-1, feat_dim)
    )
    tokens = normalize(pooled).astype(jnp.bfloat16)
    projected = jnp.dot(tokens, project_weight, preferred_element_type=jnp.float32)
    queries = feature_map(projected[:, :feat_dim]).reshape(-1, head_count, HEAD_DIM)
    key_feats = feature_map(projected[:, feat_dim : 2 * feat_dim]).astype(jnp.bfloat16)
    value_rows = projected[:, 2 * feat_dim :].astype(jnp.bfloat16)
    key_piece = lax.all_gather(key_feats, "rows", axis=0, tiled=True)
    value_piece = lax.all_gather(value_rows, "rows", axis=0, tiled=True)
    piece_rows = key_piece.shape[0]
    key_heads = key_piece.reshape(piece_rows, head_count, HEAD_DIM)
    value_heads = value_piece.reshape(piece_rows, head_count, HEAD_DIM)
    summary_part = jnp.einsum(
        "thd,the->hde", key_heads, value_heads, preferred_element_type=jnp.float32
    )
    totals_part = jnp.sum(key_heads.astype(jnp.float32), axis=0)
    numerator = jnp.einsum("thd,hde->the", queries, summary_part, precision=lax.Precision.HIGHEST)
    denominator = jnp.einsum("thd,hd->th", queries, totals_part, precision=lax.Precision.HIGHEST)
    context = (numerator / denominator[:, :, None]).reshape(-1, feat_dim).astype(jnp.bfloat16)
    mixed = jnp.dot(context, mix_weight, preferred_element_type=jnp.float32)
    mixed = jnp.broadcast_to(
        mixed.reshape(band_rows // 4, 1, band_width // 4, 1, feat_dim),
        (band_rows // 4, 4, band_width // 4, 4, feat_dim),
    ).reshape(band_rows, band_width, feat_dim)
    act_out = silu_norm(hidden + mixed)
    out_field = jnp.einsum(
        "rwf,fc->crw", act_out, output_weight, preferred_element_type=jnp.float32
    )
    denoised = scale_skip * current + scale_out * out_field
    drift_step = (sigma_high - sigma_low) * (current - denoised) / sigma_low
    flattened = drift_step.reshape(1, -1)
    columns = lax.all_to_all(flattened, "step", split_axis=1, concat_axis=0, tiled=True)
    running = jnp.cumsum(columns, axis=0)
    summed = lax.all_to_all(running, "step", split_axis=0, concat_axis=1, tiled=True).reshape(
        drift_step.shape
    )
    trajectory = window_start + summed
    return (trajectory[None], denoised[None])


def solution(mesh):
    return jax.shard_map(
        local,
        mesh=mesh,
        in_specs=(
            P("step", "ens", "rows", None),
            P("ens", "rows", None),
            P("ens", "rows", None),
            P("step", None),
            P(),
            P(),
            P(),
            P(),
            P(),
            P(),
            P(),
        ),
        out_specs=(P("step", "ens", "rows", None), P("step", "ens", "rows", None)),
        check_vma=False,
    )
```

profile of v0, /device:TPU:0, one launch (start us, length us, event | category | flops | bytes accessed | tf_op | source)
XLA Modules:
  0.0 91.7 jit_solution(10086689503256885799)
XLA Ops:
  0.6 1.0 %copy.32 = f32[1,4,16,512]{3,1,2,0:T(4,128)S(1)} copy(f32[1,4,16,512]{3,2,1,0:T(8,128)} %param.11) | data formatting | bytes 262144 | tf_op args[0]
  1.7 4.8 %collective-permute-start = (f32[1,4,16,512]{3,1,2,0:T(4,128)S(1)}, f32[1,4,16,512]{3,1,2,0:T(4,128)S(1)}, u32[]{:S(2)}, u32[]{:S(2)}) collective-permute-start(f32[1,4,16,512]{3,1,2,0:T(4,128)S(1)} %copy.32), channel_id=1, source_target_pairs={{0,2},{2,4},{4,6},{6,8},{8,10},{10,12},{12,14},{1,3},{3,5},{5,7},{... | collective-permute-start | bytes 393224 | tf_op jit(solution)/shard_map/ppermute | solution.py:16
  6.5 0.7 exponential_multiply_fusion
  7.2 0.6 fusion.42
  9.2 1.0 %copy.34 = bf16[12,16,512]{2,0,1:T(8,128)(2,1)S(1)} copy(bf16[12,16,512]{2,1,0:T(8,128)(2,1)} %param.13) | data formatting | bytes 393216 | tf_op args[2]
  12.2 1.5 %convolution_bitcast_fusion.1 = f32[128]{0:T(128)S(1)} fusion(bf16[17,128]{1,0:T(8,128)(2,1)} %param.15, s32[]{:T(128)} %bitcast.110), kind=kOutput, calls=%fused_computation.34 | convolution fusion | flops 4369 | bytes 4868 | tf_op jit(solution)/shard_map/dot_general | solution.py:99
  13.6 1.0 %multiply_convert_fusion.7 = (bf16[4,16,512]{2,0,1:T(4,128)(2,1)S(1)}, f32[4,16,512]{2,0,1:T(4,128)S(1)}) fusion(f32[]{:T(128)S(6)} %rsqrt.37, f32[1,4,16,512]{3,1,2,0:T(4,128)S(1)} %collective-permute-done, f32[4,16,512]{2,1,0:T(8,128)} %param.12, pred[]{:T(512)S(6)} %eq.11), kind=kLoop, calls=%fused_computation.52 | loop fusion | flops 98304 | bytes 458757 | tf_op jit(solution)/shard_map/convert_element_type | solution.py:97
  14.7 2.6 %fusion.7 = (f32[16,512]{1,0:T(8,128)S(1)}, bf16[16,512,128]{2,1,0:T(8,128)(2,1)S(1)}) fusion(f32[128]{0:T(128)S(1)} %convolution_bitcast_fusion.1, bf16[16,128]{1,0:T(8,128)(2,1)} %param.16, bf16[12,16,512]{2,0,1:T(8,128)(2,1)S(1)} %copy.34, bf16[4,16,512]{2,0,1:T(4,128)(2,1)S(1)} %get-tuple-element.12), kind=kOutput, calls=%fused_computation.14 | convolution fusion | flops 39313408 | bytes 2396672 | tf_op jit(solution)/shard_map/crw,cf->rwf/dot_general | solution.py:101
  17.3 1.5 %fusion.6 = bf16[16,512,128]{2,1,0:T(8,128)(2,1)S(1)} fusion(bf16[16,512,128]{2,1,0:T(8,128)(2,1)S(1)} %get-tuple-element.35, f32[16,512]{1,0:T(8,128)S(1)} %add_rsqrt_fusion.2), kind=kLoop, calls=%fused_computation.13 | loop fusion | flops 7340032 | bytes 4227072 | tf_op jit(solution)/shard_map/convert_element_type | solution.py:42
  18.8 1.5 %collective-permute-start.1 = (bf16[1,512,128]{2,1,0:T(8,128)(2,1)S(1)}, bf16[1,512,128]{2,1,0:T(8,128)(2,1)S(1)}, u32[]{:S(2)}, u32[]{:S(2)}) collective-permute-start(bf16[1,512,128]{2,1,0:T(8,128)(2,1)S(1)} %get-tuple-element.20), channel_id=1, source_target_pairs={{0,1},{2,3},{4,5},{6,7},{8,9},{10,11},{12,13},{14,15},{16,17},{18,... | collective-permute-start | bytes 393224 | tf_op jit(solution)/shard_map/ppermute | solution.py:26
  20.3 1.3 %collective-permute-start.2 = (bf16[1,512,128]{2,1,0:T(8,128)(2,1)S(1)}, bf16[1,512,128]{2,1,0:T(8,128)(2,1)S(1)}, u32[]{:S(2)}, u32[]{:S(2)}) collective-permute-start(bf16[1,512,128]{2,1,0:T(8,128)(2,1)S(1)} %get-tuple-element.21), channel_id=1, source_target_pairs={{1,0},{3,2},{5,4},{7,6},{9,8},{11,10},{13,12},{15,14},{17,16},{19,... | collective-permute-start | bytes 393224 | tf_op jit(solution)/shard_map/ppermute | solution.py:27
  21.7 1.9 %collective-permute-done.2 = bf16[1,512,128]{2,1,0:T(8,128)(2,1)S(1)} collective-permute-done((bf16[1,512,128]{2,1,0:T(8,128)(2,1)S(1)}, bf16[1,512,128]{2,1,0:T(8,128)(2,1)S(1)}, u32[]{:S(2)}, u32[]{:S(2)}) %collective-permute-start.2) | collective-permute-done | bytes 131104 | tf_op jit(solution)/shard_map/ppermute | solution.py:27
  23.6 1.4 %fusion.12 = bf16[18,514,128]{2,1,0:T(8,128)(2,1)S(1)} fusion(bf16[1,512,128]{2,1,0:T(8,128)(2,1)S(1)} %collective-permute-done.2, bf16[16,512,128]{2,1,0:T(8,128)(2,1)S(1)} %fusion.6, bf16[1,512,128]{2,1,0:T(8,128)(2,1)S(1)} %collective-permute-done.1), kind=kLoop, calls=%fused_computation.27 | loop fusion | flops 14211072 | bytes 4727808 | tf_op jit(solution)/shard_map/concatenate | solution.py:28
  25.0 1.4 %fusion.37 = (bf16[18,512,128]{2,1,0:T(8,128)(2,1)S(1)}, bf16[18,512,128]{2,1,0:T(8,128)(2,1)S(1)}) fusion(bf16[18,514,128]{2,1,0:T(8,128)(2,1)S(1)} %fusion.12), kind=kLoop, calls=%fused_computation.71 | loop fusion | bytes 9437184 | tf_op jit(solution)/shard_map/slice | solution.py:55
  26.5 1.1 %pad_maximum_fusion = bf16[18,512,384]{2,1,0:T(8,128)(2,1)S(1)} fusion(bf16[18,512,128]{2,1,0:T(8,128)(2,1)S(1)} %get-tuple-element.17, bf16[1,512,128]{2,1,0:T(8,128)(2,1)S(1)} %collective-permute-done.2, bf16[16,512,128]{2,1,0:T(8,128)(2,1)S(1)} %fusion.6, bf16[1,512,128]{2,1,0:T(8,128)(2,1)S(1)} %collective-permute-done.1, ...), kind=kLoop, calls=%fused_computation.2 | loop fusion | flops 35389440 | bytes 14155776 | tf_op jit(solution)/shard_map/concatenate | solution.py:53
  27.6 1.8 %fusion.46 = f32[16,512,128]{2,1,0:T(8,128)S(1)} fusion(bf16[18,512,384]{2,1,0:T(8,128)(2,1)S(1)} %pad_maximum_fusion, bf16[384,128,1]{1,0,2:T(8,128)(2,1)S(1)} %bitcast.106), kind=kOutput, calls=%fused_computation.80 | convolution fusion | flops 805306368 | bytes 11370496 | tf_op jit(solution)/shard_map/rwk,kf->rwf/dot_general | solution.py:64
  29.4 1.8 %fusion.47 = f32[16,512,128]{2,1,0:T(8,128)S(1)} fusion(bf16[18,512,384]{2,1,0:T(8,128)(2,1)S(1)} %pad_maximum_fusion, bf16[384,128,1]{1,0,2:T(8,128)(2,1)S(1)} %bitcast.104), kind=kOutput, calls=%fused_computation.81 | convolution fusion | flops 805306368 | bytes 11370496 | tf_op jit(solution)/shard_map/rwk,kf->rwf/dot_general | solution.py:64
  31.2 2.1 %multiply_reduce_fusion.1 = (f32[16,512]{1,0:T(8,128)S(1)}, f32[16,512,128]{2,1,0:T(8,128)S(1)}) fusion(bf16[18,512,384]{2,1,0:T(8,128)(2,1)S(1)} %pad_maximum_fusion, bf16[384,128,1]{1,0,2:T(8,128)(2,1)S(1)} %bitcast.102, f32[16,512,128]{2,1,0:T(8,128)S(1)} %fusion.46, f32[16,512,128]{2,1,0:T(8,128)S(1)} %fusion.47), kind=kOutput, calls=%fused_computation.18 | convolution fusion | flops 809492480 | bytes 19791872 | tf_op jit(solution)/shard_map/rwk,kf->rwf/dot_general | solution.py:64
  33.3 1.4 %multiply_convert_fusion.1 = bf16[16,512,128]{2,1,0:T(8,128)(2,1)S(1)} fusion(f32[16,512,128]{2,1,0:T(8,128)S(1)} %get-tuple-element.37, f32[16,512]{1,0:T(8,128)S(1)} %add_rsqrt_fusion.1), kind=kLoop, calls=%fused_computation.17 | loop fusion | flops 6291456 | bytes 6324224 | tf_op jit(solution)/shard_map/convert_element_type | solution.py:42
  34.8 2.1 %collective-permute-start.3 = (bf16[1,512,128]{2,1,0:T(8,128)(2,1)S(1)}, bf16[1,512,128]{2,1,0:T(8,128)(2,1)S(1)}, u32[]{:S(2)}, u32[]{:S(2)}) collective-permute-start(bf16[1,512,128]{2,1,0:T(8,128)(2,1)S(1)} %get-tuple-element.18), channel_id=1, source_target_pairs={{0,1},{2,3},{4,5},{6,7},{8,9},{10,11},{12,13},{14,15},{16,17},{18,... | collective-permute-start | bytes 393224 | tf_op jit(solution)/shard_map/ppermute | solution.py:26
  36.9 1.5 %collective-permute-start.4 = (bf16[1,512,128]{2,1,0:T(8,128)(2,1)S(1)}, bf16[1,512,128]{2,1,0:T(8,128)(2,1)S(1)}, u32[]{:S(2)}, u32[]{:S(2)}) collective-permute-start(bf16[1,512,128]{2,1,0:T(8,128)(2,1)S(1)} %get-tuple-element.19), channel_id=1, source_target_pairs={{1,0},{3,2},{5,4},{7,6},{9,8},{11,10},{13,12},{15,14},{17,16},{19,... | collective-permute-start | bytes 393224 | tf_op jit(solution)/shard_map/ppermute | solution.py:27
  38.4 1.7 %collective-permute-done.4 = bf16[1,512,128]{2,1,0:T(8,128)(2,1)S(1)} collective-permute-done((bf16[1,512,128]{2,1,0:T(8,128)(2,1)S(1)}, bf16[1,512,128]{2,1,0:T(8,128)(2,1)S(1)}, u32[]{:S(2)}, u32[]{:S(2)}) %collective-permute-start.4) | collective-permute-done | bytes 131104 | tf_op jit(solution)/shard_map/ppermute | solution.py:27
  40.1 1.4 %select_maximum_fusion = bf16[18,514,128]{2,1,0:T(8,128)(2,1)S(1)} fusion(bf16[1,512,128]{2,1,0:T(8,128)(2,1)S(1)} %collective-permute-done.4, bf16[16,512,128]{2,1,0:T(8,128)(2,1)S(1)} %multiply_convert_fusion.1, bf16[1,512,128]{2,1,0:T(8,128)(2,1)S(1)} %collective-permute-done.3), kind=kLoop, calls=%fused_computation.21 | loop fusion | flops 14211072 | bytes 4727808 | tf_op jit(solution)/shard_map/concatenate | solution.py:28
  41.5 1.5 %fusion.36 = (bf16[18,512,128]{2,1,0:T(8,128)(2,1)S(1)}, bf16[18,512,128]{2,1,0:T(8,128)(2,1)S(1)}) fusion(bf16[18,514,128]{2,1,0:T(8,128)(2,1)S(1)} %select_maximum_fusion), kind=kLoop, calls=%fused_computation.70 | loop fusion | bytes 9437184 | tf_op jit(solution)/shard_map/slice | solution.py:55
  43.0 1.1 %pad_maximum_fusion.1 = bf16[18,512,384]{2,1,0:T(8,128)(2,1)S(1)} fusion(bf16[18,512,128]{2,1,0:T(8,128)(2,1)S(1)} %get-tuple-element.15, bf16[1,512,128]{2,1,0:T(8,128)(2,1)S(1)} %collective-permute-done.4, bf16[16,512,128]{2,1,0:T(8,128)(2,1)S(1)} %multiply_convert_fusion.1, bf16[1,512,128]{2,1,0:T(8,128)(2,1)S(1)} %collective-permute-done.3, ...), kind=kLoop, calls=%fused_computation.3 | loop fusion | flops 35389440 | bytes 14155776 | tf_op jit(solution)/shard_map/concatenate | solution.py:53
  44.2 1.8 %fusion.48 = f32[16,512,128]{2,1,0:T(8,128)S(1)} fusion(bf16[18,512,384]{2,1,0:T(8,128)(2,1)S(1)} %pad_maximum_fusion.1, bf16[384,128,1]{1,0,2:T(8,128)(2,1)S(1)} %bitcast.107), kind=kOutput, calls=%fused_computation.82 | convolution fusion | flops 805306368 | bytes 11370496 | tf_op jit(solution)/shard_map/rwk,kf->rwf/dot_general | solution.py:64
  46.0 1.8 %fusion.49 = f32[16,512,128]{2,1,0:T(8,128)S(1)} fusion(bf16[18,512,384]{2,1,0:T(8,128)(2,1)S(1)} %pad_maximum_fusion.1, bf16[384,128,1]{1,0,2:T(8,128)(2,1)S(1)} %bitcast.105), kind=kOutput, calls=%fused_computation.83 | convolution fusion | flops 805306368 | bytes 11370496 | tf_op jit(solution)/shard_map/rwk,kf->rwf/dot_general | solution.py:64
  47.8 3.9 %convert_add_fusion = f32[16,512,128]{2,1,0:T(8,128)} fusion(bf16[16,512,128]{2,1,0:T(8,128)(2,1)S(1)} %get-tuple-element.35, f32[16,512,128]{2,1,0:T(8,128)S(1)} %fusion.48, f32[16,512,128]{2,1,0:T(8,128)S(1)} %fusion.49, bf16[18,512,384]{2,1,0:T(8,128)(2,1)S(1)} %pad_maximum_fusion.1, bf16[384,128,1]{1,0,2:T(8,128)(2,1)S(1)} %bitcast.103), kind=kOutput, calls=%fused_computation.4 | convolution fusion | flops 809500672 | bytes 21856256 | tf_op jit(solution)/shard_map/rwk,kf->rwf/dot_general | solution.py:64
  51.7 3.2 %reduce_sum.60 = f32[4,128,128]{2,1,0:T(8,128)S(1)} reduce(f32[4,4,128,4,128]{4,3,2,1,0:T(4,128)} %bitcast.96, f32[]{:T(128)} %constant.40.clone.1), dimensions={1,3}, to_apply=%region_2.3 | reduce | flops 983040 | bytes 4456452 | tf_op jit(solution)/shard_map/reduce_sum | solution.py:116
  55.2 0.3 fusion.43
  55.7 2.0 %all_gather.6 = bf16[1024,128]{0,1:T(8,128)(2,1)S(1)} all-gather(bf16[512,128]{0,1:T(8,128)(2,1)S(1)} %get-tuple-element.23), channel_id=1, replica_groups=mesh['ens'=2,'step'=8,'rows'=2] {'rows'}, dimensions={0}, use_global_device_ids=true | all-gather | bytes 393216 | tf_op jit(solution)/shard_map/all_gather | solution.py:124
  57.8 0.2 fusion.45
  58.1 2.2 %all_gather.7 = bf16[1024,128]{0,1:T(8,128)(2,1)S(1)} all-gather(bf16[512,128]{0,1:T(8,128)(2,1)S(1)} %slice.130), channel_id=1, replica_groups=mesh['ens'=2,'step'=8,'rows'=2] {'rows'}, dimensions={0}, use_global_device_ids=true | all-gather | bytes 393216 | tf_op jit(solution)/shard_map/all_gather | solution.py:125
  60.3 0.2 fusion.44
  60.6 0.4 fusion.15
  61.0 0.2 fusion.24
  61.2 0.8 broadcast_in_dim.6
  62.0 1.1 %copy-done.1 = f32[16,512,128]{2,1,0:T(8,128)S(1)} copy-done((f32[16,512,128]{2,1,0:T(8,128)S(1)}, f32[16,512,128]{2,1,0:T(8,128)}, u32[]{:S(2)}) %copy-start.1) | copy-done | bytes 4194328
  63.2 1.2 %multiply_reduce_fusion = (f32[16,512]{1,0:T(8,128)S(1)}, f32[16,512,128]{2,1,0:T(8,128)S(1)}) fusion(f32[16,512,128]{2,1,0:T(8,128)S(1)} %copy-done.1, f32[16,512,128]{2,1,0:T(8,128)S(1)} %bitcast.97), kind=kLoop, calls=%fused_computation.16 | loop fusion | flops 3137536 | bytes 12615680 | tf_op jit(solution)/shard_map/reduce_sum | solution.py:38
  64.4 1.9 %fusion.17 = f32[4,16,512]{2,0,1:T(4,128)S(1)} fusion(f32[16,512,128]{2,1,0:T(8,128)S(1)} %get-tuple-element.11, f32[16,512]{1,0:T(8,128)S(1)} %add_rsqrt_fusion, f32[]{:T(128)S(6)} %mul.111, bf16[128,4]{0,1:T(4,128)(2,1)S(1)} %copy-done.6), kind=kOutput, calls=%fused_computation.33 | convolution fusion | flops 14712832 | bytes 4359172 | tf_op jit(solution)/shard_map/rwf,fc->crw/dot_general | solution.py:142
  66.3 0.7 fusion.26
  67.2 12.0 %all_to_all.24 = f32[1,8,4096]{2,0,1:T(1,128)S(1)} all-to-all(f32[1,8,4096]{2,0,1:T(1,128)S(1)} %all_to_all.21), channel_id=1, replica_groups=mesh['ens'=2,'step'=8,'rows'=2] {'step'}, dimensions={1} | all-to-all | bytes 262144 | tf_op jit(solution)/shard_map/all_to_all | solution.py:148
  79.2 0.7 fusion.22
  80.0 3.4 %all-to-all-start.1 = ((f32[8,1,4096]{2,1,0:T(1,128)}), f32[8,1,4096]{2,1,0:T(1,128)S(1)}, u32[]{:S(2)}, u32[]{:S(2)}) async-start(f32[8,1,4096]{2,1,0:T(1,128)} %fusion.22), calls=%async_computation.1 | async-start | bytes 262144 | tf_op jit(solution)/shard_map/all_to_all | solution.py:150
  83.4 0.7 copy.39
  84.0 6.6 %all-to-all-done.1 = f32[8,1,4096]{2,1,0:T(1,128)S(1)} async-done(((f32[8,1,4096]{2,1,0:T(1,128)}), f32[8,1,4096]{2,1,0:T(1,128)S(1)}, u32[]{:S(2)}, u32[]{:S(2)}) %all-to-all-start.1) | async-done | bytes 131104 | tf_op jit(solution)/shard_map/all_to_all | solution.py:150
  90.6 0.3 reduce.2
  91.0 0.7 add_bitcast_fusion
  (35 shorter events, 1.1 us)
Async XLA Ops:
  0.6 54.6 %copy-start = (bf16[128,384]{1,0:T(8,128)(2,1)S(1)}, bf16[128,384]{1,0:T(8,128)(2,1)}, u32[]{:S(2)}) copy-start(bf16[128,384]{1,0:T(8,128)(2,1)} %param.19) | copy-start | bytes 294916
  1.7 12.0 %collective-permute-start = (f32[1,4,16,512]{3,1,2,0:T(4,128)S(1)}, f32[1,4,16,512]{3,1,2,0:T(4,128)S(1)}, u32[]{:S(2)}, u32[]{:S(2)}) collective-permute-start(f32[1,4,16,512]{3,1,2,0:T(4,128)S(1)} %copy.32), channel_id=1, source_target_pairs={{0,2},{2,4},{4,6},{6,8},{8,10},{10,12},{12,14},{1,3},{3,5},{5,7},{... | collective-permute-start | bytes 393224 | tf_op jit(solution)/shard_map/ppermute | solution.py:16
  14.7 7.0 %copy-start.3 = (bf16[3,3,128,128]{3,2,1,0:T(8,128)(2,1)S(1)}, bf16[3,3,128,128]{3,2,1,0:T(8,128)(2,1)}, u32[]{:S(2)}) copy-start(bf16[3,3,128,128]{3,2,1,0:T(8,128)(2,1)} %param.17) | copy-start | bytes 884740
  18.8 2.8 %collective-permute-start.1 = (bf16[1,512,128]{2,1,0:T(8,128)(2,1)S(1)}, bf16[1,512,128]{2,1,0:T(8,128)(2,1)S(1)}, u32[]{:S(2)}, u32[]{:S(2)}) collective-permute-start(bf16[1,512,128]{2,1,0:T(8,128)(2,1)S(1)} %get-tuple-element.20), channel_id=1, source_target_pairs={{0,1},{2,3},{4,5},{6,7},{8,9},{10,11},{12,13},{14,15},{16,17},{18,... | collective-permute-start | bytes 393224 | tf_op jit(solution)/shard_map/ppermute | solution.py:26
  20.3 3.2 %collective-permute-start.2 = (bf16[1,512,128]{2,1,0:T(8,128)(2,1)S(1)}, bf16[1,512,128]{2,1,0:T(8,128)(2,1)S(1)}, u32[]{:S(2)}, u32[]{:S(2)}) collective-permute-start(bf16[1,512,128]{2,1,0:T(8,128)(2,1)S(1)} %get-tuple-element.21), channel_id=1, source_target_pairs={{1,0},{3,2},{5,4},{7,6},{9,8},{11,10},{13,12},{15,14},{17,16},{19,... | collective-permute-start | bytes 393224 | tf_op jit(solution)/shard_map/ppermute | solution.py:27
  33.3 5.1 %copy-start.4 = (bf16[3,3,128,128]{3,2,1,0:T(8,128)(2,1)S(1)}, bf16[3,3,128,128]{3,2,1,0:T(8,128)(2,1)}, u32[]{:S(2)}) copy-start(bf16[3,3,128,128]{3,2,1,0:T(8,128)(2,1)} %param.18) | copy-start | bytes 884740
  34.8 3.6 %collective-permute-start.3 = (bf16[1,512,128]{2,1,0:T(8,128)(2,1)S(1)}, bf16[1,512,128]{2,1,0:T(8,128)(2,1)S(1)}, u32[]{:S(2)}, u32[]{:S(2)}) collective-permute-start(bf16[1,512,128]{2,1,0:T(8,128)(2,1)S(1)} %get-tuple-element.18), channel_id=1, source_target_pairs={{0,1},{2,3},{4,5},{6,7},{8,9},{10,11},{12,13},{14,15},{16,17},{18,... | collective-permute-start | bytes 393224 | tf_op jit(solution)/shard_map/ppermute | solution.py:26
  36.9 3.2 %collective-permute-start.4 = (bf16[1,512,128]{2,1,0:T(8,128)(2,1)S(1)}, bf16[1,512,128]{2,1,0:T(8,128)(2,1)S(1)}, u32[]{:S(2)}, u32[]{:S(2)}) collective-permute-start(bf16[1,512,128]{2,1,0:T(8,128)(2,1)S(1)} %get-tuple-element.19), channel_id=1, source_target_pairs={{1,0},{3,2},{5,4},{7,6},{9,8},{11,10},{13,12},{15,14},{17,16},{19,... | collective-permute-start | bytes 393224 | tf_op jit(solution)/shard_map/ppermute | solution.py:27
  51.7 9.3 %copy-start.5 = (bf16[128,128]{1,0:T(8,128)(2,1)S(1)}, bf16[128,128]{1,0:T(8,128)(2,1)}, u32[]{:S(2)}) copy-start(bf16[128,128]{1,0:T(8,128)(2,1)} %param.20) | copy-start | bytes 98308
  61.0 2.2 %copy-start.1 = (f32[16,512,128]{2,1,0:T(8,128)S(1)}, f32[16,512,128]{2,1,0:T(8,128)}, u32[]{:S(2)}) copy-start(f32[16,512,128]{2,1,0:T(8,128)} %convert_add_fusion) | copy-start | bytes 12582916
  63.2 1.2 %copy-start.6 = (bf16[128,4]{0,1:T(4,128)(2,1)S(1)}, bf16[128,4]{0,1:T(4,128)(2,1)}, u32[]{:S(2)}) copy-start(bf16[128,4]{0,1:T(4,128)(2,1)} %param.21) | copy-start | bytes 3076
  64.4 26.6 %copy-start.2 = (f32[4,16,512]{2,1,0:T(8,128)S(1)}, f32[4,16,512]{2,1,0:T(8,128)}, u32[]{:S(2)}) copy-start(f32[4,16,512]{2,1,0:T(8,128)} %param.12) | copy-start | bytes 393220
  80.0 10.7 %all-to-all-start.1 = ((f32[8,1,4096]{2,1,0:T(1,128)}), f32[8,1,4096]{2,1,0:T(1,128)S(1)}, u32[]{:S(2)}, u32[]{:S(2)}) async-start(f32[8,1,4096]{2,1,0:T(1,128)} %fusion.22), calls=%async_computation.1 | async-start | bytes 262144 | tf_op jit(solution)/shard_map/all_to_all | solution.py:150
where the time goes:
time: 92.3 us; the launch traced here: 91.7 us
  matrix products  20.5 us (22%)
  other arithmetic  17.1 us (19%)
  blocking collectives  16.2 us (18%)
  starting transfers between devices  14.5 us (16%)
  waiting for transfers between devices  10.2 us (11%)
  local copies, waits for them, and re-layouts  8.69 us (9%)
  between operations  4.39 us (5%)
    dot_general x6, matrix products, conv_band(): jnp.einsum('rwk,kf->rwf', stacked[row_shift:row_shift + band_rows], folde...  13.1 us
    all_to_all x1, blocking collectives, local(): lax.all_to_all(flattened, 'step', split_axis=1, concat_axis=0, tiled=True)  12 us
    all_to_all x1, waiting for transfers between devices, local(): lax.all_to_all(running, 'step', split_axis=0, concat_axis=1, tiled=True)  6.58 us
    ppermute x1, starting transfers between devices, from_behind(): return lax.ppermute(x, axis, pairs)  4.85 us
    unnamed x17, local copies, waits for them, and re-layouts  3.94 us
    ppermute x2, waiting for transfers between devices, with_halo(): after = lax.ppermute(leading, axis, down)  3.6 us
    ppermute x2, starting transfers between devices, with_halo(): before = lax.ppermute(last, axis, up)  3.53 us
    all_to_all x1, starting transfers between devices, local(): lax.all_to_all(running, 'step', split_axis=0, concat_axis=1, tiled=True)  3.37 us
  transfers between devices with their start and end apart: 6, of which 3 were waited for; matrix products, arithmetic and copies ran while one was open for 5% of the time, Pallas kernels for 0%

commit v1 on v0

--- a/solution.py
+++ b/solution.py
@@ -19,13 +19,38 @@
 def with_halo(x, sides, width):
     for axis, dim in sides:
         devices, length = (lax.axis_size(axis), x.shape[dim])
-        up = [(i, (i + 1) % devices) for i in range(devices - 1)]
-        down = [(j, i) for i, j in up]
         last = lax.slice_in_dim(x, length - width, length, axis=dim)
         leading = lax.slice_in_dim(x, 0, width, axis=dim)
-        before = lax.ppermute(last, axis, up)
-        after = lax.ppermute(leading, axis, down)
+        if devices == 2:
+            me = lax.axis_index(axis)
+            outgoing = jnp.where(me == 0, last, leading)
+            incoming = lax.ppermute(outgoing, axis, [(0, 1), (1, 0)])
+            zero = jnp.zeros_like(incoming)
+            before = jnp.where(me == 0, zero, incoming)
+            after = jnp.where(me == 0, incoming, zero)
+        else:
+            up = [(i, i + 1) for i in range(devices - 1)]
+            down = [(j, i) for i, j in up]
+            before = lax.ppermute(last, axis, up)
+            after = lax.ppermute(leading, axis, down)
         x = jnp.concatenate([before, x, after], axis=dim)
+    return x
+
+
+def band_sum(x, axis):
+    devices = lax.axis_size(axis)
+    if devices == 2:
+        return x + lax.ppermute(x, axis, [(0, 1), (1, 0)])
+    return lax.psum(x, axis)
+
+
+def prefix_sum(x, axis):
+    devices = lax.axis_size(axis)
+    shift = 1
+    while shift < devices:
+        pairs = [(i, i + shift) for i in range(devices - shift)]
+        x = x + lax.ppermute(x, axis, pairs)
+        shift *= 2
     return x
 
 
@@ -121,15 +146,15 @@
     queries = feature_map(projected[:, :feat_dim]).reshape(-1, head_count, HEAD_DIM)
     key_feats = feature_map(projected[:, feat_dim : 2 * feat_dim]).astype(jnp.bfloat16)
     value_rows = projected[:, 2 * feat_dim :].astype(jnp.bfloat16)
-    key_piece = lax.all_gather(key_feats, "rows", axis=0, tiled=True)
-    value_piece = lax.all_gather(value_rows, "rows", axis=0, tiled=True)
-    piece_rows = key_piece.shape[0]
-    key_heads = key_piece.reshape(piece_rows, head_count, HEAD_DIM)
-    value_heads = value_piece.reshape(piece_rows, head_count, HEAD_DIM)
-    summary_part = jnp.einsum(
+    key_heads = key_feats.reshape(-1, head_count, HEAD_DIM)
+    value_heads = value_rows.reshape(-1, head_count, HEAD_DIM)
+    summary_own = jnp.einsum(
         "thd,the->hde", key_heads, value_heads, preferred_element_type=jnp.float32
     )
-    totals_part = jnp.sum(key_heads.astype(jnp.float32), axis=0)
+    totals_own = jnp.sum(key_heads.astype(jnp.float32), axis=0)
+    stats = band_sum(jnp.concatenate([summary_own, totals_own[:, None, :]], axis=1), "rows")
+    summary_part = stats[:, :HEAD_DIM]
+    totals_part = stats[:, HEAD_DIM]
     numerator = jnp.einsum("thd,hde->the", queries, summary_part, precision=lax.Precision.HIGHEST)
     denominator = jnp.einsum("thd,hd->th", queries, totals_part, precision=lax.Precision.HIGHEST)
     context = (numerator / denominator[:, :, None]).reshape(-1, feat_dim).astype(jnp.bfloat16)
@@ -144,12 +169,7 @@
     )
     denoised = scale_skip * current + scale_out * out_field
     drift_step = (sigma_high - sigma_low) * (current - denoised) / sigma_low
-    flattened = drift_step.reshape(1, -1)
-    columns = lax.all_to_all(flattened, "step", split_axis=1, concat_axis=0, tiled=True)
-    running = jnp.cumsum(columns, axis=0)
-    summed = lax.all_to_all(running, "step", split_axis=0, concat_axis=1, tiled=True).reshape(
-        drift_step.shape
-    )
+    summed = prefix_sum(drift_step, "step")
     trajectory = window_start + summed
     return (trajectory[None], denoised[None])
 

time: 92.3 us -> 81.3 us (0.88)
  blocking collectives: 16.2 us -> 0 us
  starting transfers between devices: 14.5 us -> 19.5 us
    all_to_all x1 -> x0, blocking collectives: 12 us -> none  [local(): lax.all_to_all(flattened, 'step', split_axis=1, concat_axis=0, tiled=True)]
    ppermute x4 -> x6, starting transfers between devices: 6.29 us -> 14.7 us  [the longest x3 14.2 us: prefix_sum(): x = x + lax.ppermute(x, axis, pairs)]
    all_to_all x1 -> x0, waiting for transfers between devices: 6.58 us -> none  [local(): lax.all_to_all(running, 'step', split_axis=0, concat_axis=1, tiled=True)]
    ppermute x4 -> x6, waiting for transfers between devices: 3.61 us -> 10 us  [the longest x3 7.56 us: prefix_sum(): x = x + lax.ppermute(x, axis, pairs)]
    all_gather x2 -> x0, blocking collectives: 4.21 us -> none  [the longest x1 2.21 us: local(): value_piece = lax.all_gather(value_rows, 'rows', axis=0, tiled=True)]
    all_to_all x1 -> x0, starting transfers between devices: 3.37 us -> none  [local(): lax.all_to_all(running, 'step', split_axis=0, concat_axis=1, tiled=True)]
    unnamed x17 -> x18, local copies, waits for them, and re-layouts: 3.94 us -> 4.64 us
  transfers between devices with their start and end apart: 6 -> 7, of which waited for: 3 -> 5; matrix products, arithmetic and copies ran while one was open for 5% -> 6% of each run, Pallas kernels for 0% -> 0%
where the time goes in v1:
time: 81.3 us; the launch traced here: 80 us
  matrix products  20.5 us (25%)
  starting transfers between devices  19.5 us (24%)
  other arithmetic  16.3 us (20%)
  waiting for transfers between devices  10 us (12%)
  local copies, waits for them, and re-layouts  9.4 us (12%)
  between operations  4.36 us (5%)
    ppermute x3, starting transfers between devices, prefix_sum(): x = x + lax.ppermute(x, axis, pairs)  14.2 us
    dot_general x6, matrix products, conv_band(): jnp.einsum('rwk,kf->rwf', stacked[row_shift:row_shift + band_rows], folde...  13.2 us
    ppermute x3, waiting for transfers between devices, prefix_sum(): x = x + lax.ppermute(x, axis, pairs)  7.56 us
    ppermute x1, starting transfers between devices, from_behind(): return lax.ppermute(x, axis, pairs)  4.85 us
    unnamed x18, local copies, waits for them, and re-layouts  4.64 us
    reduce_sum x1, other arithmetic, local(): pooled = hidden.reshape(band_rows // 4, 4, band_width // 4, 4, feat_dim)....  3.22 us
    convert_element_type x2, other arithmetic, silu_norm(): return jax.nn.silu(normalize(values)).astype(jnp.bfloat16)  3.11 us
    concatenate x2, other arithmetic, with_halo(): x = jnp.concatenate([before, x, after], axis=dim)  2.92 us
  transfers between devices with their start and end apart: 7, of which 5 were waited for; matrix products, arithmetic and copies ran while one was open for 6% of the time, Pallas kernels for 0%

profile of v1, /device:TPU:0, one launch (start us, length us, event | category | flops | bytes accessed | tf_op | source)
XLA Modules:
  0.0 80.0 jit_solution(7615758347937239277)
XLA Ops:
  0.6 1.0 %copy.29 = f32[1,4,16,512]{3,1,2,0:T(4,128)S(1)} copy(f32[1,4,16,512]{3,2,1,0:T(8,128)} %param.11) | data formatting | bytes 262144 | tf_op args[0]
  1.7 4.8 %collective-permute-start = (f32[1,4,16,512]{3,1,2,0:T(4,128)S(1)}, f32[1,4,16,512]{3,1,2,0:T(4,128)S(1)}, u32[]{:S(2)}, u32[]{:S(2)}) collective-permute-start(f32[1,4,16,512]{3,1,2,0:T(4,128)S(1)} %copy.29), channel_id=1, source_target_pairs={{0,2},{2,4},{4,6},{6,8},{8,10},{10,12},{12,14},{1,3},{3,5},{5,7},{... | collective-permute-start | bytes 393224 | tf_op jit(solution)/shard_map/ppermute | solution.py:16
  6.5 0.7 exponential_multiply_fusion
  7.2 0.6 fusion.39
  7.8 1.0 %copy.31 = bf16[12,16,512]{2,0,1:T(8,128)(2,1)S(1)} copy(bf16[12,16,512]{2,1,0:T(8,128)(2,1)} %param.13) | data formatting | bytes 393216 | tf_op args[2]
  10.2 1.5 %convolution_bitcast_fusion.1 = f32[128]{0:T(128)S(1)} fusion(bf16[17,128]{1,0:T(8,128)(2,1)} %param.15, s32[]{:T(128)} %bitcast.108), kind=kOutput, calls=%fused_computation.34 | convolution fusion | flops 4369 | bytes 4868 | tf_op jit(solution)/shard_map/dot_general | solution.py:124
  11.6 1.0 %multiply_convert_fusion.7 = (bf16[4,16,512]{2,0,1:T(4,128)(2,1)S(1)}, f32[4,16,512]{2,0,1:T(4,128)S(1)}) fusion(f32[]{:T(128)S(6)} %rsqrt.37, f32[1,4,16,512]{3,1,2,0:T(4,128)S(1)} %collective-permute-done, f32[4,16,512]{2,1,0:T(8,128)} %param.12, pred[]{:T(512)S(6)} %eq.19), kind=kLoop, calls=%fused_computation.52 | loop fusion | flops 98304 | bytes 458757 | tf_op jit(solution)/shard_map/convert_element_type | solution.py:122
  12.7 2.6 %fusion.7 = (f32[16,512]{1,0:T(8,128)S(1)}, bf16[16,512,128]{2,1,0:T(8,128)(2,1)S(1)}) fusion(f32[128]{0:T(128)S(1)} %convolution_bitcast_fusion.1, bf16[16,128]{1,0:T(8,128)(2,1)} %param.16, bf16[12,16,512]{2,0,1:T(8,128)(2,1)S(1)} %copy.31, bf16[4,16,512]{2,0,1:T(4,128)(2,1)S(1)} %get-tuple-element.12), kind=kOutput, calls=%fused_computation.14 | convolution fusion | flops 39313408 | bytes 2396672 | tf_op jit(solution)/shard_map/crw,cf->rwf/dot_general | solution.py:126
  15.3 1.7 %fusion.6 = bf16[16,512,128]{2,1,0:T(8,128)(2,1)S(1)} fusion(bf16[16,512,128]{2,1,0:T(8,128)(2,1)S(1)} %get-tuple-element.34, f32[16,512]{1,0:T(8,128)S(1)} %add_rsqrt_fusion.2), kind=kLoop, calls=%fused_computation.13 | loop fusion | flops 7340032 | bytes 4227072 | tf_op jit(solution)/shard_map/convert_element_type | solution.py:67
  17.2 1.3 %collective-permute-done.1 = bf16[1,512,128]{2,1,0:T(8,128)(2,1)S(1)} collective-permute-done((bf16[1,512,128]{2,1,0:T(8,128)(2,1)S(1)}, bf16[1,512,128]{2,1,0:T(8,128)(2,1)S(1)}, u32[]{:S(2)}, u32[]{:S(2)}) %collective-permute-start.1) | collective-permute-done | bytes 131104 | tf_op jit(solution)/shard_map/ppermute | solution.py:27
  18.5 1.5 %fusion.12 = bf16[18,514,128]{2,1,0:T(8,128)(2,1)S(1)} fusion(bf16[1,512,128]{2,1,0:T(8,128)(2,1)S(1)} %get-tuple-element.30, bf16[16,512,128]{2,1,0:T(8,128)(2,1)S(1)} %fusion.6, bf16[1,512,128]{2,1,0:T(8,128)(2,1)S(1)} %get-tuple-element.29), kind=kLoop, calls=%fused_computation.27 | loop fusion | flops 14211072 | bytes 4727808 | tf_op jit(solution)/shard_map/concatenate | solution.py:36
  19.9 1.4 %fusion.36 = (bf16[18,512,128]{2,1,0:T(8,128)(2,1)S(1)}, bf16[18,512,128]{2,1,0:T(8,128)(2,1)S(1)}) fusion(bf16[18,514,128]{2,1,0:T(8,128)(2,1)S(1)} %fusion.12), kind=kLoop, calls=%fused_computation.78 | loop fusion | bytes 9437184 | tf_op jit(solution)/shard_map/slice | solution.py:80
  21.4 1.1 %pad_maximum_fusion = bf16[18,512,384]{2,1,0:T(8,128)(2,1)S(1)} fusion(bf16[18,512,128]{2,1,0:T(8,128)(2,1)S(1)} %get-tuple-element.17, bf16[1,512,128]{2,1,0:T(8,128)(2,1)S(1)} %get-tuple-element.30, bf16[16,512,128]{2,1,0:T(8,128)(2,1)S(1)} %fusion.6, bf16[1,512,128]{2,1,0:T(8,128)(2,1)S(1)} %get-tuple-element.29, ...), kind=kLoop, calls=%fused_computation.2 | loop fusion | flops 35389440 | bytes 14155776 | tf_op jit(solution)/shard_map/concatenate | solution.py:78
  22.5 1.8 %fusion.43 = f32[16,512,128]{2,1,0:T(8,128)S(1)} fusion(bf16[18,512,384]{2,1,0:T(8,128)(2,1)S(1)} %pad_maximum_fusion, bf16[384,128,1]{1,0,2:T(8,128)(2,1)S(1)} %bitcast.105), kind=kOutput, calls=%fused_computation.85 | convolution fusion | flops 805306368 | bytes 11370496 | tf_op jit(solution)/shard_map/rwk,kf->rwf/dot_general | solution.py:89
  24.4 1.8 %fusion.44 = f32[16,512,128]{2,1,0:T(8,128)S(1)} fusion(bf16[18,512,384]{2,1,0:T(8,128)(2,1)S(1)} %pad_maximum_fusion, bf16[384,128,1]{1,0,2:T(8,128)(2,1)S(1)} %bitcast.103), kind=kOutput, calls=%fused_computation.86 | convolution fusion | flops 805306368 | bytes 11370496 | tf_op jit(solution)/shard_map/rwk,kf->rwf/dot_general | solution.py:89
  26.2 2.1 %multiply_reduce_fusion.1 = (f32[16,512]{1,0:T(8,128)S(1)}, f32[16,512,128]{2,1,0:T(8,128)S(1)}) fusion(bf16[18,512,384]{2,1,0:T(8,128)(2,1)S(1)} %pad_maximum_fusion, bf16[384,128,1]{1,0,2:T(8,128)(2,1)S(1)} %bitcast.100, f32[16,512,128]{2,1,0:T(8,128)S(1)} %fusion.43, f32[16,512,128]{2,1,0:T(8,128)S(1)} %fusion.44), kind=kOutput, calls=%fused_computation.18 | convolution fusion | flops 809492480 | bytes 19791872 | tf_op jit(solution)/shard_map/rwk,kf->rwf/dot_general | solution.py:89
  28.3 1.4 %multiply_convert_fusion.1 = bf16[16,512,128]{2,1,0:T(8,128)(2,1)S(1)} fusion(f32[16,512,128]{2,1,0:T(8,128)S(1)} %get-tuple-element.36, f32[16,512]{1,0:T(8,128)S(1)} %add_rsqrt_fusion.1), kind=kLoop, calls=%fused_computation.17 | loop fusion | flops 6291456 | bytes 6324224 | tf_op jit(solution)/shard_map/convert_element_type | solution.py:67
  29.8 0.2 collective-permute-start.2
  30.0 1.2 %collective-permute-done.2 = bf16[1,512,128]{2,1,0:T(8,128)(2,1)S(1)} collective-permute-done((bf16[1,512,128]{2,1,0:T(8,128)(2,1)S(1)}, bf16[1,512,128]{2,1,0:T(8,128)(2,1)S(1)}, u32[]{:S(2)}, u32[]{:S(2)}) %collective-permute-start.2) | collective-permute-done | bytes 131104 | tf_op jit(solution)/shard_map/ppermute | solution.py:27
  31.2 1.5 %select_maximum_fusion = bf16[18,514,128]{2,1,0:T(8,128)(2,1)S(1)} fusion(bf16[1,512,128]{2,1,0:T(8,128)(2,1)S(1)} %get-tuple-element.28, bf16[16,512,128]{2,1,0:T(8,128)(2,1)S(1)} %multiply_convert_fusion.1, bf16[1,512,128]{2,1,0:T(8,128)(2,1)S(1)} %get-tuple-element.27), kind=kLoop, calls=%fused_computation.21 | loop fusion | flops 14211072 | bytes 4727808 | tf_op jit(solution)/shard_map/concatenate | solution.py:36
  32.7 1.5 %fusion.35 = (bf16[18,512,128]{2,1,0:T(8,128)(2,1)S(1)}, bf16[18,512,128]{2,1,0:T(8,128)(2,1)S(1)}) fusion(bf16[18,514,128]{2,1,0:T(8,128)(2,1)S(1)} %select_maximum_fusion), kind=kLoop, calls=%fused_computation.77 | loop fusion | bytes 9437184 | tf_op jit(solution)/shard_map/slice | solution.py:80
  34.1 1.4 %pad_maximum_fusion.1 = bf16[18,512,384]{2,1,0:T(8,128)(2,1)S(1)} fusion(bf16[18,512,128]{2,1,0:T(8,128)(2,1)S(1)} %get-tuple-element.15, bf16[1,512,128]{2,1,0:T(8,128)(2,1)S(1)} %get-tuple-element.28, bf16[16,512,128]{2,1,0:T(8,128)(2,1)S(1)} %multiply_convert_fusion.1, bf16[1,512,128]{2,1,0:T(8,128)(2,1)S(1)} %get-tuple-element.27, ...), kind=kLoop, calls=%fused_computation.3 | loop fusion | flops 35389440 | bytes 14155776 | tf_op jit(solution)/shard_map/concatenate | solution.py:78
  35.5 1.8 %fusion.45 = f32[16,512,128]{2,1,0:T(8,128)S(1)} fusion(bf16[18,512,384]{2,1,0:T(8,128)(2,1)S(1)} %pad_maximum_fusion.1, bf16[384,128,1]{1,0,2:T(8,128)(2,1)S(1)} %bitcast.104), kind=kOutput, calls=%fused_computation.87 | convolution fusion | flops 805306368 | bytes 11370496 | tf_op jit(solution)/shard_map/rwk,kf->rwf/dot_general | solution.py:89
  37.3 1.8 %fusion.46 = f32[16,512,128]{2,1,0:T(8,128)S(1)} fusion(bf16[18,512,384]{2,1,0:T(8,128)(2,1)S(1)} %pad_maximum_fusion.1, bf16[384,128,1]{1,0,2:T(8,128)(2,1)S(1)} %bitcast.102), kind=kOutput, calls=%fused_computation.88 | convolution fusion | flops 805306368 | bytes 11370496 | tf_op jit(solution)/shard_map/rwk,kf->rwf/dot_general | solution.py:89
  39.1 3.9 %convert_add_fusion = f32[16,512,128]{2,1,0:T(8,128)} fusion(bf16[16,512,128]{2,1,0:T(8,128)(2,1)S(1)} %get-tuple-element.34, f32[16,512,128]{2,1,0:T(8,128)S(1)} %fusion.45, f32[16,512,128]{2,1,0:T(8,128)S(1)} %fusion.46, bf16[18,512,384]{2,1,0:T(8,128)(2,1)S(1)} %pad_maximum_fusion.1, bf16[384,128,1]{1,0,2:T(8,128)(2,1)S(1)} %bitcast.101), kind=kOutput, calls=%fused_computation.4 | convolution fusion | flops 809500672 | bytes 21856256 | tf_op jit(solution)/shard_map/rwk,kf->rwf/dot_general | solution.py:89
  43.0 3.2 %reduce_sum.58 = f32[4,128,128]{2,1,0:T(8,128)S(1)} reduce(f32[4,4,128,4,128]{4,3,2,1,0:T(4,128)} %bitcast.94, f32[]{:T(128)} %constant.41.clone.1), dimensions={1,3}, to_apply=%region_2.3 | reduce | flops 983040 | bytes 4456452 | tf_op jit(solution)/shard_map/reduce_sum | solution.py:141
  46.5 0.3 fusion.40
  46.8 0.2 convert_reduce_fusion
  47.1 0.2 broadcast_in_dim.24
  47.3 0.2 fusion.41
  47.5 0.2 collective-permute-start.3
  49.8 0.2 slice_reduce_fusion
  50.0 0.2 fusion.42
  50.3 0.4 fusion.15
  50.7 0.2 fusion.22
  50.9 0.8 %broadcast_in_dim.9 = f32[4,4,128,4,128]{4,3,2,1,0:T(4,128)S(1)} broadcast(f32[4,128,128]{2,1,0:T(8,128)S(1)} %fusion.22), dimensions={0,2,4} | broadcast | bytes 4456448 | tf_op jit(solution)/shard_map/broadcast_in_dim | solution.py:162
  51.7 1.1 %copy-done.1 = f32[16,512,128]{2,1,0:T(8,128)S(1)} copy-done((f32[16,512,128]{2,1,0:T(8,128)S(1)}, f32[16,512,128]{2,1,0:T(8,128)}, u32[]{:S(2)}) %copy-start.1) | copy-done | bytes 4194328
  52.9 1.2 %multiply_reduce_fusion = (f32[16,512]{1,0:T(8,128)S(1)}, f32[16,512,128]{2,1,0:T(8,128)S(1)}) fusion(f32[16,512,128]{2,1,0:T(8,128)S(1)} %copy-done.1, f32[16,512,128]{2,1,0:T(8,128)S(1)} %bitcast.95), kind=kLoop, calls=%fused_computation.16 | loop fusion | flops 3137536 | bytes 12615680 | tf_op jit(solution)/shard_map/reduce_sum | solution.py:63
  54.1 1.9 %fusion.17 = f32[4,16,512]{2,0,1:T(4,128)S(1)} fusion(f32[16,512,128]{2,1,0:T(8,128)S(1)} %get-tuple-element.9, f32[16,512]{1,0:T(8,128)S(1)} %add_rsqrt_fusion, f32[]{:T(128)S(6)} %mul.111, bf16[128,4]{0,1:T(4,128)(2,1)S(1)} %copy-done.6), kind=kOutput, calls=%fused_computation.33 | convolution fusion | flops 14712832 | bytes 4359172 | tf_op jit(solution)/shard_map/rwf,fc->crw/dot_general | solution.py:167
  56.0 0.7 fusion.24
  56.7 3.4 %collective-permute-start.4 = (f32[4,16,512]{2,0,1:T(4,128)S(1)}, f32[4,16,512]{2,0,1:T(4,128)S(1)}, u32[]{:S(2)}, u32[]{:S(2)}) collective-permute-start(f32[4,16,512]{2,0,1:T(4,128)S(1)} %get-tuple-element.26), channel_id=1, source_target_pairs={{0,2},{2,4},{4,6},{6,8},{8,10},{10,12},{12,14},{1,3},{3,5},{5,7},{... | collective-permute-start | bytes 393224 | tf_op jit(solution)/shard_map/ppermute | solution.py:52
  60.1 3.3 %collective-permute-done.4 = f32[4,16,512]{2,0,1:T(4,128)S(1)} collective-permute-done((f32[4,16,512]{2,0,1:T(4,128)S(1)}, f32[4,16,512]{2,0,1:T(4,128)S(1)}, u32[]{:S(2)}, u32[]{:S(2)}) %collective-permute-start.4) | collective-permute-done | bytes 131104 | tf_op jit(solution)/shard_map/ppermute | solution.py:52
  63.4 5.3 %collective-permute-start.5 = (f32[4,16,512]{2,0,1:T(4,128)S(1)}, f32[4,16,512]{2,0,1:T(4,128)S(1)}, u32[]{:S(2)}, u32[]{:S(2)}) collective-permute-start(f32[4,16,512]{2,0,1:T(4,128)S(1)} %add.124), channel_id=1, source_target_pairs={{0,4},{2,6},{4,8},{6,10},{8,12},{10,14},{1,5},{3,7},{5,9},{7,11},{... | collective-permute-start | bytes 393224 | tf_op jit(solution)/shard_map/ppermute | solution.py:52
  68.8 2.5 %collective-permute-done.5 = f32[4,16,512]{2,0,1:T(4,128)S(1)} collective-permute-done((f32[4,16,512]{2,0,1:T(4,128)S(1)}, f32[4,16,512]{2,0,1:T(4,128)S(1)}, u32[]{:S(2)}, u32[]{:S(2)}) %collective-permute-start.5) | collective-permute-done | bytes 131104 | tf_op jit(solution)/shard_map/ppermute | solution.py:52
  71.3 5.4 %collective-permute-start.6 = (f32[4,16,512]{2,0,1:T(4,128)S(1)}, f32[4,16,512]{2,0,1:T(4,128)S(1)}, u32[]{:S(2)}, u32[]{:S(2)}) collective-permute-start(f32[4,16,512]{2,0,1:T(4,128)S(1)} %add.125), channel_id=1, source_target_pairs={{0,8},{2,10},{4,12},{6,14},{1,9},{3,11},{5,13},{7,15},{16,24},{18,... | collective-permute-start | bytes 393224 | tf_op jit(solution)/shard_map/ppermute | solution.py:52
  76.7 0.7 copy.36
  77.4 1.8 %collective-permute-done.6 = f32[4,16,512]{2,0,1:T(4,128)S(1)} collective-permute-done((f32[4,16,512]{2,0,1:T(4,128)S(1)}, f32[4,16,512]{2,0,1:T(4,128)S(1)}, u32[]{:S(2)}, u32[]{:S(2)}) %collective-permute-start.6) | collective-permute-done | bytes 131104 | tf_op jit(solution)/shard_map/ppermute | solution.py:52
  79.4 0.7 copy.35
  (36 shorter events, 1.0 us)
Async XLA Ops:
  0.6 45.9 %copy-start = (bf16[128,384]{1,0:T(8,128)(2,1)S(1)}, bf16[128,384]{1,0:T(8,128)(2,1)}, u32[]{:S(2)}) copy-start(bf16[128,384]{1,0:T(8,128)(2,1)} %param.19) | copy-start | bytes 294916
  1.7 10.0 %collective-permute-start = (f32[1,4,16,512]{3,1,2,0:T(4,128)S(1)}, f32[1,4,16,512]{3,1,2,0:T(4,128)S(1)}, u32[]{:S(2)}, u32[]{:S(2)}) collective-permute-start(f32[1,4,16,512]{3,1,2,0:T(4,128)S(1)} %copy.29), channel_id=1, source_target_pairs={{0,2},{2,4},{4,6},{6,8},{8,10},{10,12},{12,14},{1,3},{3,5},{5,7},{... | collective-permute-start | bytes 393224 | tf_op jit(solution)/shard_map/ppermute | solution.py:16
  12.7 4.4 %copy-start.3 = (bf16[3,3,128,128]{3,2,1,0:T(8,128)(2,1)S(1)}, bf16[3,3,128,128]{3,2,1,0:T(8,128)(2,1)}, u32[]{:S(2)}) copy-start(bf16[3,3,128,128]{3,2,1,0:T(8,128)(2,1)} %param.17) | copy-start | bytes 884740
  17.0 1.4 %collective-permute-start.1 = (bf16[1,512,128]{2,1,0:T(8,128)(2,1)S(1)}, bf16[1,512,128]{2,1,0:T(8,128)(2,1)S(1)}, u32[]{:S(2)}, u32[]{:S(2)}) collective-permute-start(bf16[1,512,128]{2,1,0:T(8,128)(2,1)S(1)} %slice_select_fusion.1), channel_id=1, source_target_pairs={{0,1},{1,0},{2,3},{3,2},{4,5},{5,4},{6,7},{7,6},{8,9},{9,8},{10,11... | collective-permute-start | bytes 393224 | tf_op jit(solution)/shard_map/ppermute | solution.py:27
  28.2 1.7 %copy-start.4 = (bf16[3,3,128,128]{3,2,1,0:T(8,128)(2,1)S(1)}, bf16[3,3,128,128]{3,2,1,0:T(8,128)(2,1)}, u32[]{:S(2)}) copy-start(bf16[3,3,128,128]{3,2,1,0:T(8,128)(2,1)} %param.18) | copy-start | bytes 884740
  29.8 1.4 %collective-permute-start.2 = (bf16[1,512,128]{2,1,0:T(8,128)(2,1)S(1)}, bf16[1,512,128]{2,1,0:T(8,128)(2,1)S(1)}, u32[]{:S(2)}, u32[]{:S(2)}) collective-permute-start(bf16[1,512,128]{2,1,0:T(8,128)(2,1)S(1)} %slice_select_fusion), channel_id=1, source_target_pairs={{0,1},{1,0},{2,3},{3,2},{4,5},{5,4},{6,7},{7,6},{8,9},{9,8},{10,11... | collective-permute-start | bytes 393224 | tf_op jit(solution)/shard_map/ppermute | solution.py:27
  43.0 7.7 %copy-start.5 = (bf16[128,128]{1,0:T(8,128)(2,1)S(1)}, bf16[128,128]{1,0:T(8,128)(2,1)}, u32[]{:S(2)}) copy-start(bf16[128,128]{1,0:T(8,128)(2,1)} %param.20) | copy-start | bytes 98308
  47.5 2.2 %collective-permute-start.3 = (f32[2,65,64]{1,2,0:T(8,128)S(1)}, f32[2,65,64]{1,2,0:T(8,128)S(1)}, u32[]{:S(2)}, u32[]{:S(2)}) collective-permute-start(f32[2,65,64]{1,2,0:T(8,128)S(1)} %pad_maximum_fusion.2), channel_id=1, source_target_pairs={{0,1},{1,0},{2,3},{3,2},{4,5},{5,4},{6,7},{7,6},{8,9},{9,8},{10,11... | collective-permute-start | bytes 99848 | tf_op jit(solution)/shard_map/ppermute | solution.py:43
  50.7 2.2 %copy-start.1 = (f32[16,512,128]{2,1,0:T(8,128)S(1)}, f32[16,512,128]{2,1,0:T(8,128)}, u32[]{:S(2)}) copy-start(f32[16,512,128]{2,1,0:T(8,128)} %convert_add_fusion) | copy-start | bytes 12582916
  52.9 1.2 %copy-start.6 = (bf16[128,4]{0,1:T(4,128)(2,1)S(1)}, bf16[128,4]{0,1:T(4,128)(2,1)}, u32[]{:S(2)}) copy-start(bf16[128,4]{0,1:T(4,128)(2,1)} %param.21) | copy-start | bytes 3076
  54.1 25.2 %copy-start.2 = (f32[4,16,512]{2,1,0:T(8,128)S(1)}, f32[4,16,512]{2,1,0:T(8,128)}, u32[]{:S(2)}) copy-start(f32[4,16,512]{2,1,0:T(8,128)} %param.12) | copy-start | bytes 393220
  56.7 6.7 %collective-permute-start.4 = (f32[4,16,512]{2,0,1:T(4,128)S(1)}, f32[4,16,512]{2,0,1:T(4,128)S(1)}, u32[]{:S(2)}, u32[]{:S(2)}) collective-permute-start(f32[4,16,512]{2,0,1:T(4,128)S(1)} %get-tuple-element.26), channel_id=1, source_target_pairs={{0,2},{2,4},{4,6},{6,8},{8,10},{10,12},{12,14},{1,3},{3,5},{5,7},{... | collective-permute-start | bytes 393224 | tf_op jit(solution)/shard_map/ppermute | solution.py:52
  63.4 7.8 %collective-permute-start.5 = (f32[4,16,512]{2,0,1:T(4,128)S(1)}, f32[4,16,512]{2,0,1:T(4,128)S(1)}, u32[]{:S(2)}, u32[]{:S(2)}) collective-permute-start(f32[4,16,512]{2,0,1:T(4,128)S(1)} %add.124), channel_id=1, source_target_pairs={{0,4},{2,6},{4,8},{6,10},{8,12},{10,14},{1,5},{3,7},{5,9},{7,11},{... | collective-permute-start | bytes 393224 | tf_op jit(solution)/shard_map/ppermute | solution.py:52
  71.3 7.9 %collective-permute-start.6 = (f32[4,16,512]{2,0,1:T(4,128)S(1)}, f32[4,16,512]{2,0,1:T(4,128)S(1)}, u32[]{:S(2)}, u32[]{:S(2)}) collective-permute-start(f32[4,16,512]{2,0,1:T(4,128)S(1)} %add.125), channel_id=1, source_target_pairs={{0,8},{2,10},{4,12},{6,14},{1,9},{3,11},{5,13},{7,15},{16,24},{18,... | collective-permute-start | bytes 393224 | tf_op jit(solution)/shard_map/ppermute | solution.py:52

commit v2 on v1

--- a/solution.py
+++ b/solution.py
@@ -52,6 +52,13 @@
         x = x + lax.ppermute(x, axis, pairs)
         shift *= 2
     return x
+
+
+def gathered_prefix(x, axis):
+    every = lax.all_gather(x, axis, axis=0)
+    keep = jnp.arange(every.shape[0]) <= lax.axis_index(axis)
+    keep = keep.reshape((-1,) + (1,) * x.ndim)
+    return jnp.sum(jnp.where(keep, every, 0.0), axis=0)
 
 
 def noise_level(levels, level_count):
@@ -169,7 +176,7 @@
     )
     denoised = scale_skip * current + scale_out * out_field
     drift_step = (sigma_high - sigma_low) * (current - denoised) / sigma_low
-    summed = prefix_sum(drift_step, "step")
+    summed = gathered_prefix(drift_step, "step")
     trajectory = window_start + summed
     return (trajectory[None], denoised[None])
 

time: 81.3 us -> 115 us (1.41)
  waiting for transfers between devices: 10 us -> 42.4 us
  starting transfers between devices: 19.5 us -> 5.38 us
  between operations: 4.36 us -> 17.8 us
  other arithmetic: 16.3 us -> 18.3 us
    all_gather x0 -> x1, waiting for transfers between devices: none -> 39.9 us  [gathered_prefix(): every = lax.all_gather(x, axis, axis=0)]
    ppermute x3 -> x0, starting transfers between devices: 14.2 us -> none  [prefix_sum(): x = x + lax.ppermute(x, axis, pairs)]
    ppermute x3 -> x0, waiting for transfers between devices: 7.56 us -> none  [prefix_sum(): x = x + lax.ppermute(x, axis, pairs)]
    reduce_sum x0 -> x1, other arithmetic: none -> 2.09 us  [gathered_prefix(): return jnp.sum(jnp.where(keep, every, 0.0), axis=0)]
  transfers between devices with their start and end apart: 7 -> 5, of which waited for: 5 -> 3; matrix products, arithmetic and copies ran while one was open for 6% -> 4% of each run, Pallas kernels for 0% -> 0%
where the time goes in v2:
time: 115 us; the launch traced here: 114 us
  waiting for transfers between devices  42.4 us (37%)
  matrix products  20.5 us (18%)
  other arithmetic  18.3 us (16%)
  between operations  17.8 us (15%)
  local copies, waits for them, and re-layouts  10.1 us (9%)
  starting transfers between devices  5.38 us (5%)
    all_gather x1, waiting for transfers between devices, gathered_prefix(): every = lax.all_gather(x, axis, axis=0)  39.9 us
    dot_general x6, matrix products, conv_band(): jnp.einsum('rwk,kf->rwf', stacked[row_shift:row_shift + band_rows], folde...  13.2 us
    ppermute x1, starting transfers between devices, from_behind(): return lax.ppermute(x, axis, pairs)  4.85 us
    unnamed x18, local copies, waits for them, and re-layouts  4.6 us
    reduce_sum x1, other arithmetic, local(): pooled = hidden.reshape(band_rows // 4, 4, band_width // 4, 4, feat_dim)....  3.22 us
    convert_element_type x2, other arithmetic, silu_norm(): return jax.nn.silu(normalize(values)).astype(jnp.bfloat16)  3.11 us
    concatenate x2, other arithmetic, with_halo(): x = jnp.concatenate([before, x, after], axis=dim)  2.92 us
    slice x2, local copies, waits for them, and re-layouts, conv_band(): col_padded[:, 0:band_width]  2.9 us
  transfers between devices with their start and end apart: 5, of which 3 were waited for; matrix products, arithmetic and copies ran while one was open for 4% of the time, Pallas kernels for 0%

profile of v2, /device:TPU:0, one launch (start us, length us, event | category | flops | bytes accessed | tf_op | source)
XLA Modules:
  0.0 114.4 jit_solution(11399255053419545133)
XLA Ops:
  7.2 1.0 copy.35
  8.2 4.8 %collective-permute-start = (f32[1,4,16,512]{3,1,2,0:T(4,128)S(1)}, f32[1,4,16,512]{3,1,2,0:T(4,128)S(1)}, u32[]{:S(2)}, u32[]{:S(2)}) collective-permute-start(f32[1,4,16,512]{3,1,2,0:T(4,128)S(1)} %copy.35), channel_id=1, source_target_pairs={{0,2},{2,4},{4,6},{6,8},{8,10},{10,12},{12,14},{1,3},{3,5},{5,7},{... | collective-permute-start | bytes 393224 | tf_op jit(solution)/shard_map/ppermute | solution.py:16
  13.1 0.7 exponential_multiply_fusion
  13.7 0.6 fusion.40
  14.3 1.0 copy.37
  16.7 1.5 %convolution_bitcast_fusion.1 = f32[128]{0:T(128)S(1)} fusion(bf16[17,128]{1,0:T(8,128)(2,1)} %param.15, s32[]{:T(128)} %bitcast.110), kind=kOutput, calls=%fused_computation.34 | convolution fusion | flops 4369 | bytes 4868 | tf_op jit(solution)/shard_map/dot_general | solution.py:131
  18.2 1.0 multiply_convert_fusion.7
  19.2 2.6 %fusion.7 = (f32[16,512]{1,0:T(8,128)S(1)}, bf16[16,512,128]{2,1,0:T(8,128)(2,1)S(1)}) fusion(f32[128]{0:T(128)S(1)} %convolution_bitcast_fusion.1, bf16[16,128]{1,0:T(8,128)(2,1)} %param.16, bf16[12,16,512]{2,0,1:T(8,128)(2,1)S(1)} %copy.37, bf16[4,16,512]{2,0,1:T(4,128)(2,1)S(1)} %get-tuple-element.14), kind=kOutput, calls=%fused_computation.14 | convolution fusion | flops 39313408 | bytes 2396672 | tf_op jit(solution)/shard_map/crw,cf->rwf/dot_general | solution.py:133
  21.9 1.7 %fusion.6 = bf16[16,512,128]{2,1,0:T(8,128)(2,1)S(1)} fusion(bf16[16,512,128]{2,1,0:T(8,128)(2,1)S(1)} %get-tuple-element.36, f32[16,512]{1,0:T(8,128)S(1)} %add_rsqrt_fusion.2), kind=kLoop, calls=%fused_computation.13 | loop fusion | flops 7340032 | bytes 4227072 | tf_op jit(solution)/shard_map/convert_element_type | solution.py:74
  23.7 1.3 %collective-permute-done.1 = bf16[1,512,128]{2,1,0:T(8,128)(2,1)S(1)} collective-permute-done((bf16[1,512,128]{2,1,0:T(8,128)(2,1)S(1)}, bf16[1,512,128]{2,1,0:T(8,128)(2,1)S(1)}, u32[]{:S(2)}, u32[]{:S(2)}) %collective-permute-start.1) | collective-permute-done | bytes 131104 | tf_op jit(solution)/shard_map/ppermute | solution.py:27
  25.0 1.5 %fusion.12 = bf16[18,514,128]{2,1,0:T(8,128)(2,1)S(1)} fusion(bf16[1,512,128]{2,1,0:T(8,128)(2,1)S(1)} %get-tuple-element.32, bf16[16,512,128]{2,1,0:T(8,128)(2,1)S(1)} %fusion.6, bf16[1,512,128]{2,1,0:T(8,128)(2,1)S(1)} %get-tuple-element.31), kind=kLoop, calls=%fused_computation.27 | loop fusion | flops 14211072 | bytes 4727808 | tf_op jit(solution)/shard_map/concatenate | solution.py:36
  26.5 1.4 %fusion.37 = (bf16[18,512,128]{2,1,0:T(8,128)(2,1)S(1)}, bf16[18,512,128]{2,1,0:T(8,128)(2,1)S(1)}) fusion(bf16[18,514,128]{2,1,0:T(8,128)(2,1)S(1)} %fusion.12), kind=kLoop, calls=%fused_computation.81 | loop fusion | bytes 9437184 | tf_op jit(solution)/shard_map/slice | solution.py:87
  27.9 1.1 pad_maximum_fusion
  29.1 1.8 %fusion.44 = f32[16,512,128]{2,1,0:T(8,128)S(1)} fusion(bf16[18,512,384]{2,1,0:T(8,128)(2,1)S(1)} %pad_maximum_fusion, bf16[384,128,1]{1,0,2:T(8,128)(2,1)S(1)} %bitcast.107), kind=kOutput, calls=%fused_computation.88 | convolution fusion | flops 805306368 | bytes 11370496 | tf_op jit(solution)/shard_map/rwk,kf->rwf/dot_general | solution.py:96
  30.9 1.8 %fusion.45 = f32[16,512,128]{2,1,0:T(8,128)S(1)} fusion(bf16[18,512,384]{2,1,0:T(8,128)(2,1)S(1)} %pad_maximum_fusion, bf16[384,128,1]{1,0,2:T(8,128)(2,1)S(1)} %bitcast.105), kind=kOutput, calls=%fused_computation.89 | convolution fusion | flops 805306368 | bytes 11370496 | tf_op jit(solution)/shard_map/rwk,kf->rwf/dot_general | solution.py:96
  32.7 2.1 %multiply_reduce_fusion.1 = (f32[16,512]{1,0:T(8,128)S(1)}, f32[16,512,128]{2,1,0:T(8,128)S(1)}) fusion(bf16[18,512,384]{2,1,0:T(8,128)(2,1)S(1)} %pad_maximum_fusion, bf16[384,128,1]{1,0,2:T(8,128)(2,1)S(1)} %bitcast.102, f32[16,512,128]{2,1,0:T(8,128)S(1)} %fusion.44, f32[16,512,128]{2,1,0:T(8,128)S(1)} %fusion.45), kind=kOutput, calls=%fused_computation.18 | convolution fusion | flops 809492480 | bytes 19791872 | tf_op jit(solution)/shard_map/rwk,kf->rwf/dot_general | solution.py:96
  34.8 1.4 %multiply_convert_fusion.1 = bf16[16,512,128]{2,1,0:T(8,128)(2,1)S(1)} fusion(f32[16,512,128]{2,1,0:T(8,128)S(1)} %get-tuple-element.38, f32[16,512]{1,0:T(8,128)S(1)} %add_rsqrt_fusion.1), kind=kLoop, calls=%fused_computation.17 | loop fusion | flops 6291456 | bytes 6324224 | tf_op jit(solution)/shard_map/convert_element_type | solution.py:74
  36.3 0.2 collective-permute-start.2
  36.5 1.2 %collective-permute-done.2 = bf16[1,512,128]{2,1,0:T(8,128)(2,1)S(1)} collective-permute-done((bf16[1,512,128]{2,1,0:T(8,128)(2,1)S(1)}, bf16[1,512,128]{2,1,0:T(8,128)(2,1)S(1)}, u32[]{:S(2)}, u32[]{:S(2)}) %collective-permute-start.2) | collective-permute-done | bytes 131104 | tf_op jit(solution)/shard_map/ppermute | solution.py:27
  37.7 1.5 %select_maximum_fusion = bf16[18,514,128]{2,1,0:T(8,128)(2,1)S(1)} fusion(bf16[1,512,128]{2,1,0:T(8,128)(2,1)S(1)} %get-tuple-element.30, bf16[16,512,128]{2,1,0:T(8,128)(2,1)S(1)} %multiply_convert_fusion.1, bf16[1,512,128]{2,1,0:T(8,128)(2,1)S(1)} %get-tuple-element.29), kind=kLoop, calls=%fused_computation.21 | loop fusion | flops 14211072 | bytes 4727808 | tf_op jit(solution)/shard_map/concatenate | solution.py:36
  39.2 1.5 %fusion.36 = (bf16[18,512,128]{2,1,0:T(8,128)(2,1)S(1)}, bf16[18,512,128]{2,1,0:T(8,128)(2,1)S(1)}) fusion(bf16[18,514,128]{2,1,0:T(8,128)(2,1)S(1)} %select_maximum_fusion), kind=kLoop, calls=%fused_computation.80 | loop fusion | bytes 9437184 | tf_op jit(solution)/shard_map/slice | solution.py:87
  40.7 1.4 %pad_maximum_fusion.1 = bf16[18,512,384]{2,1,0:T(8,128)(2,1)S(1)} fusion(bf16[18,512,128]{2,1,0:T(8,128)(2,1)S(1)} %get-tuple-element.17, bf16[1,512,128]{2,1,0:T(8,128)(2,1)S(1)} %get-tuple-element.30, bf16[16,512,128]{2,1,0:T(8,128)(2,1)S(1)} %multiply_convert_fusion.1, bf16[1,512,128]{2,1,0:T(8,128)(2,1)S(1)} %get-tuple-element.29, ...), kind=kLoop, calls=%fused_computation.3 | loop fusion | flops 35389440 | bytes 14155776 | tf_op jit(solution)/shard_map/concatenate | solution.py:85
  42.0 1.8 %fusion.46 = f32[16,512,128]{2,1,0:T(8,128)S(1)} fusion(bf16[18,512,384]{2,1,0:T(8,128)(2,1)S(1)} %pad_maximum_fusion.1, bf16[384,128,1]{1,0,2:T(8,128)(2,1)S(1)} %bitcast.106), kind=kOutput, calls=%fused_computation.90 | convolution fusion | flops 805306368 | bytes 11370496 | tf_op jit(solution)/shard_map/rwk,kf->rwf/dot_general | solution.py:96
  43.8 1.8 %fusion.47 = f32[16,512,128]{2,1,0:T(8,128)S(1)} fusion(bf16[18,512,384]{2,1,0:T(8,128)(2,1)S(1)} %pad_maximum_fusion.1, bf16[384,128,1]{1,0,2:T(8,128)(2,1)S(1)} %bitcast.104), kind=kOutput, calls=%fused_computation.91 | convolution fusion | flops 805306368 | bytes 11370496 | tf_op jit(solution)/shard_map/rwk,kf->rwf/dot_general | solution.py:96
  45.7 3.9 %convert_add_fusion = f32[16,512,128]{2,1,0:T(8,128)} fusion(bf16[16,512,128]{2,1,0:T(8,128)(2,1)S(1)} %get-tuple-element.36, f32[16,512,128]{2,1,0:T(8,128)S(1)} %fusion.46, f32[16,512,128]{2,1,0:T(8,128)S(1)} %fusion.47, bf16[18,512,384]{2,1,0:T(8,128)(2,1)S(1)} %pad_maximum_fusion.1, bf16[384,128,1]{1,0,2:T(8,128)(2,1)S(1)} %bitcast.103), kind=kOutput, calls=%fused_computation.4 | convolution fusion | flops 809500672 | bytes 21856256 | tf_op jit(solution)/shard_map/rwk,kf->rwf/dot_general | solution.py:96
  49.6 3.2 %reduce_sum.67 = f32[4,128,128]{2,1,0:T(8,128)S(1)} reduce(f32[4,4,128,4,128]{4,3,2,1,0:T(4,128)} %bitcast.95, f32[]{:T(128)} %constant.41.clone.1), dimensions={1,3}, to_apply=%region_2.3 | reduce | flops 983040 | bytes 4456452 | tf_op jit(solution)/shard_map/reduce_sum | solution.py:148
  52.8 0.1 multiply_reduce_fusion.2
  52.9 0.1 fusion.22
  53.1 0.3 fusion.41
  53.4 0.2 convert_reduce_fusion
  53.6 0.2 broadcast_in_dim.38
  53.8 0.2 fusion.42
  54.1 0.2 collective-permute-start.3
  56.4 0.2 slice_reduce_fusion
  56.6 0.2 fusion.43
  56.8 0.4 fusion.15
  57.3 0.2 fusion.23
  57.5 0.8 broadcast_in_dim.34
  58.3 1.1 copy-done.1
  59.4 1.2 %multiply_reduce_fusion = (f32[16,512]{1,0:T(8,128)S(1)}, f32[16,512,128]{2,1,0:T(8,128)S(1)}) fusion(f32[16,512,128]{2,1,0:T(8,128)S(1)} %copy-done.1, f32[16,512,128]{2,1,0:T(8,128)S(1)} %bitcast.96), kind=kLoop, calls=%fused_computation.16 | loop fusion | flops 3137536 | bytes 12615680 | tf_op jit(solution)/shard_map/reduce_sum | solution.py:70
  60.6 1.9 %fusion.17 = f32[4,16,512]{2,0,1:T(4,128)S(1)} fusion(f32[16,512,128]{2,1,0:T(8,128)S(1)} %get-tuple-element.11, f32[16,512]{1,0:T(8,128)S(1)} %add_rsqrt_fusion, f32[]{:T(128)S(6)} %mul.111, bf16[128,4]{0,1:T(4,128)(2,1)S(1)} %copy-done.6), kind=kOutput, calls=%fused_computation.33 | convolution fusion | flops 14712832 | bytes 4359172 | tf_op jit(solution)/shard_map/rwf,fc->crw/dot_general | solution.py:174
  62.5 0.7 fusion.25
  63.2 0.7 copy.40
  64.0 0.7 copy.44
  64.7 39.9 %all-gather.3.cloned.1.call-done = f32[32,16,512]{2,1,0:T(8,128)} async-done(((f32[4,16,512]{2,1,0:T(8,128)}), f32[32,16,512]{2,1,0:T(8,128)}) %all-gather.3.cloned.1.call-update) | async-done | bytes 1048592 | tf_op jit(solution)/shard_map/all_gather | solution.py:58
  104.6 2.1 %fusion.18 = f32[4,16,512]{2,0,1:T(4,128)S(1)} fusion(f32[8,4,16,512]{3,2,1,0:T(8,128)} %bitcast.99, pred[8]{0:T(512)(128)(4,1)S(1)} %iota_compare_fusion.2), kind=kLoop, calls=%fused_computation.36 | loop fusion | flops 491520 | bytes 1179656 | tf_op jit(solution)/shard_map/reduce_sum | solution.py:61
  106.7 0.1 add_bitcast_fusion
  106.8 0.7 copy.43
  (34 shorter events, 0.6 us)
Async XLA Ops:
  7.2 45.9 %copy-start = (bf16[128,384]{1,0:T(8,128)(2,1)S(1)}, bf16[128,384]{1,0:T(8,128)(2,1)}, u32[]{:S(2)}) copy-start(bf16[128,384]{1,0:T(8,128)(2,1)} %param.19) | copy-start | bytes 294916
  7.2 97.4 %all-gather.3.cloned.1.call-start = ((), (), s32[]{:S(2)}) async-start(), calls=%async_computation | async-start | bytes 1179648 | tf_op jit(solution)/shard_map/all_gather | solution.py:58
  8.2 10.0 %collective-permute-start = (f32[1,4,16,512]{3,1,2,0:T(4,128)S(1)}, f32[1,4,16,512]{3,1,2,0:T(4,128)S(1)}, u32[]{:S(2)}, u32[]{:S(2)}) collective-permute-start(f32[1,4,16,512]{3,1,2,0:T(4,128)S(1)} %copy.35), channel_id=1, source_target_pairs={{0,2},{2,4},{4,6},{6,8},{8,10},{10,12},{12,14},{1,3},{3,5},{5,7},{... | collective-permute-start | bytes 393224 | tf_op jit(solution)/shard_map/ppermute | solution.py:16
  19.2 4.4 %copy-start.3 = (bf16[3,3,128,128]{3,2,1,0:T(8,128)(2,1)S(1)}, bf16[3,3,128,128]{3,2,1,0:T(8,128)(2,1)}, u32[]{:S(2)}) copy-start(bf16[3,3,128,128]{3,2,1,0:T(8,128)(2,1)} %param.17) | copy-start | bytes 884740
  23.6 1.4 %collective-permute-start.1 = (bf16[1,512,128]{2,1,0:T(8,128)(2,1)S(1)}, bf16[1,512,128]{2,1,0:T(8,128)(2,1)S(1)}, u32[]{:S(2)}, u32[]{:S(2)}) collective-permute-start(bf16[1,512,128]{2,1,0:T(8,128)(2,1)S(1)} %slice_select_fusion.1), channel_id=1, source_target_pairs={{0,1},{1,0},{2,3},{3,2},{4,5},{5,4},{6,7},{7,6},{8,9},{9,8},{10,11... | collective-permute-start | bytes 393224 | tf_op jit(solution)/shard_map/ppermute | solution.py:27
  34.8 1.7 %copy-start.4 = (bf16[3,3,128,128]{3,2,1,0:T(8,128)(2,1)S(1)}, bf16[3,3,128,128]{3,2,1,0:T(8,128)(2,1)}, u32[]{:S(2)}) copy-start(bf16[3,3,128,128]{3,2,1,0:T(8,128)(2,1)} %param.18) | copy-start | bytes 884740
  36.3 1.4 %collective-permute-start.2 = (bf16[1,512,128]{2,1,0:T(8,128)(2,1)S(1)}, bf16[1,512,128]{2,1,0:T(8,128)(2,1)S(1)}, u32[]{:S(2)}, u32[]{:S(2)}) collective-permute-start(bf16[1,512,128]{2,1,0:T(8,128)(2,1)S(1)} %slice_select_fusion), channel_id=1, source_target_pairs={{0,1},{1,0},{2,3},{3,2},{4,5},{5,4},{6,7},{7,6},{8,9},{9,8},{10,11... | collective-permute-start | bytes 393224 | tf_op jit(solution)/shard_map/ppermute | solution.py:27
  49.5 7.7 %copy-start.5 = (bf16[128,128]{1,0:T(8,128)(2,1)S(1)}, bf16[128,128]{1,0:T(8,128)(2,1)}, u32[]{:S(2)}) copy-start(bf16[128,128]{1,0:T(8,128)(2,1)} %param.20) | copy-start | bytes 98308
  54.1 2.2 %collective-permute-start.3 = (f32[2,65,64]{1,2,0:T(8,128)S(1)}, f32[2,65,64]{1,2,0:T(8,128)S(1)}, u32[]{:S(2)}, u32[]{:S(2)}) collective-permute-start(f32[2,65,64]{1,2,0:T(8,128)S(1)} %pad_maximum_fusion.2), channel_id=1, source_target_pairs={{0,1},{1,0},{2,3},{3,2},{4,5},{5,4},{6,7},{7,6},{8,9},{9,8},{10,11... | collective-permute-start | bytes 99848 | tf_op jit(solution)/shard_map/ppermute | solution.py:43
  57.2 2.2 %copy-start.1 = (f32[16,512,128]{2,1,0:T(8,128)S(1)}, f32[16,512,128]{2,1,0:T(8,128)}, u32[]{:S(2)}) copy-start(f32[16,512,128]{2,1,0:T(8,128)} %convert_add_fusion) | copy-start | bytes 12582916
  59.4 1.2 %copy-start.6 = (bf16[128,4]{0,1:T(4,128)(2,1)S(1)}, bf16[128,4]{0,1:T(4,128)(2,1)}, u32[]{:S(2)}) copy-start(bf16[128,4]{0,1:T(4,128)(2,1)} %param.21) | copy-start | bytes 3076
  60.6 46.1 %copy-start.2 = (f32[4,16,512]{2,1,0:T(8,128)S(1)}, f32[4,16,512]{2,1,0:T(8,128)}, u32[]{:S(2)}) copy-start(f32[4,16,512]{2,1,0:T(8,128)} %param.12) | copy-start | bytes 393220
Sparse Core Ops, SparseCore 0:
  64.1 40.4 all-gather.2

commit v3 on v1

v3 whole, which is shorter than its diff:
```python
import jax
import jax.numpy as jnp
from jax import lax
from jax.experimental import pallas as pl
from jax.experimental.pallas import tpu as pltpu
from jax.sharding import PartitionSpec as P

HEAD_DIM = 64
HALO = 2
CHUNK_ROWS = 2

SIGMA_TOP = 8.0
SIGMA_END = 0.002


def from_behind(x, axis, by):
    devices = lax.axis_size(axis)
    pairs = [(i, i + by) for i in range(devices) if 0 <= i + by < devices]
    return lax.ppermute(x, axis, pairs)


def with_halo(x, axis, dim, width):
    devices, length = (lax.axis_size(axis), x.shape[dim])
    last = lax.slice_in_dim(x, length - width, length, axis=dim)
    leading = lax.slice_in_dim(x, 0, width, axis=dim)
    if devices == 2:
        me = lax.axis_index(axis)
        outgoing = jnp.where(me == 0, last, leading)
        incoming = lax.ppermute(outgoing, axis, [(0, 1), (1, 0)])
        zero = jnp.zeros_like(incoming)
        before = jnp.where(me == 0, zero, incoming)
        after = jnp.where(me == 0, incoming, zero)
    else:
        up = [(i, i + 1) for i in range(devices - 1)]
        down = [(j, i) for i, j in up]
        before = lax.ppermute(last, axis, up)
        after = lax.ppermute(leading, axis, down)
    return jnp.concatenate([before, x, after], axis=dim)


def band_sum(x, axis):
    devices = lax.axis_size(axis)
    if devices == 2:
        return x + lax.ppermute(x, axis, [(0, 1), (1, 0)])
    return lax.psum(x, axis)


def prefix_sum(x, axis):
    devices = lax.axis_size(axis)
    shift = 1
    while shift < devices:
        pairs = [(i, i + shift) for i in range(devices - shift)]
        x = x + lax.ppermute(x, axis, pairs)
        shift *= 2
    return x


def noise_level(levels, level_count):
    fraction = levels.astype(jnp.float32) / jnp.float32(level_count - 1)
    return SIGMA_TOP * jnp.exp(fraction * jnp.log(jnp.float32(SIGMA_END / SIGMA_TOP)))


def normalize_features(values):
    mean_square = jnp.sum(values * values, axis=0, keepdims=True) * (1.0 / values.shape[0])
    return values * lax.rsqrt(mean_square + 1e-06)


def silu(values):
    return values / (1.0 + jnp.exp(-values))


def feature_map(values):
    return jnp.where(values > 0, values + 1.0, jnp.exp(jnp.minimum(values, 0.0)))


def conv_chunk(source, weight, first_row, rows, width, column):
    span = rows * width
    stacked = jnp.concatenate(
        [source[:, (first_row + i) * width : (first_row + i) * width + span] for i in range(3)],
        axis=0,
    )
    taps = jnp.dot(weight, stacked, preferred_element_type=jnp.float32)
    feat = taps.shape[0] // 3
    left = pltpu.roll(taps[0:feat], 1, 1)
    right = pltpu.roll(taps[2 * feat : 3 * feat], span - 1, 1)
    result = taps[feat : 2 * feat]
    result = result + jnp.where(column != 0, left, 0.0)
    result = result + jnp.where(column != width - 1, right, 0.0)
    return result


def trunk_kernel(
    band_ref, inputs_ref, lift_ref, embed_ref, first_ref, second_ref, pool_ref,
    hidden_ref, pooled_ref, act_first, lifted_keep, act_next, *, width, band_rows, bands,
):
    band = band_ref[0]
    top_outside = band == 0
    bottom_outside = band == bands - 1
    span = CHUNK_ROWS * width
    column = lax.broadcasted_iota(jnp.int32, (1, span), 1) % width
    upper_row = lax.broadcasted_iota(jnp.int32, (1, span), 1) < width
    lift_w = lift_ref[...]
    embed = embed_ref[...]
    in_rows = band_rows + 2 * HALO
    for q in range(in_rows // CHUNK_ROWS):
        start = q * span
        lifted = jnp.dot(lift_w, inputs_ref[:, start : start + span], preferred_element_type=jnp.float32)
        lifted = (lifted + embed).astype(jnp.bfloat16)
        row0 = q * CHUNK_ROWS
        if HALO <= row0 < HALO + band_rows:
            keep = (row0 - HALO) * width
            lifted_keep[:, keep : keep + span] = lifted
        act = silu(normalize_features(lifted.astype(jnp.float32)))
        if row0 < HALO:
            act = jnp.where(top_outside, 0.0, act)
        if row0 >= HALO + band_rows:
            act = jnp.where(bottom_outside, 0.0, act)
        act_first[:, start : start + span] = act.astype(jnp.bfloat16)
    first_w = first_ref[...]
    mid_rows = band_rows + 2
    for q in range(mid_rows // CHUNK_ROWS):
        start = q * span
        middle = conv_chunk(act_first, first_w, q * CHUNK_ROWS, CHUNK_ROWS, width, column)
        act = silu(normalize_features(middle))
        if q == 0:
            act = jnp.where(jnp.logical_and(top_outside, upper_row), 0.0, act)
        if q == mid_rows // CHUNK_ROWS - 1:
            act = jnp.where(jnp.logical_and(bottom_outside, jnp.logical_not(upper_row)), 0.0, act)
        act_next[:, start : start + span] = act.astype(jnp.bfloat16)
    second_w = second_ref[...]
    for q in range(band_rows // CHUNK_ROWS):
        start = q * span
        conv = conv_chunk(act_next, second_w, q * CHUNK_ROWS, CHUNK_ROWS, width, column)
        hidden_ref[:, start : start + span] = lifted_keep[:, start : start + span].astype(jnp.float32) + conv
    pool_w = pool_ref[...]
    tokens_per_row = width // 4
    for a in range(band_rows // 4):
        row_sum = hidden_ref[:, (4 * a) * width : (4 * a + 1) * width]
        for u in range(1, 4):
            row_sum = row_sum + hidden_ref[:, (4 * a + u) * width : (4 * a + u + 1) * width]
        pooled_ref[:, a * tokens_per_row : (a + 1) * tokens_per_row] = jnp.dot(
            row_sum, pool_w, precision=lax.Precision.HIGHEST, preferred_element_type=jnp.float32
        )


def head_kernel(hidden_ref, mixed_ref, expand_ref, out_w_ref, field_ref, *, width, band_rows):
    expand = expand_ref[...]
    out_w = out_w_ref[...]
    tokens_per_row = width // 4
    for a in range(band_rows // 4):
        spread = jnp.dot(
            mixed_ref[:, a * tokens_per_row : (a + 1) * tokens_per_row],
            expand,
            precision=lax.Precision.HIGHEST,
            preferred_element_type=jnp.float32,
        )
        for u in range(4):
            start = (4 * a + u) * width
            combined = hidden_ref[:, start : start + width] + spread
            act = silu(normalize_features(combined)).astype(jnp.bfloat16)
            field = jnp.dot(out_w, act, preferred_element_type=jnp.float32)
            field_ref[:, start : start + width] = field[0:8]


def vmem():
    return pl.BlockSpec(memory_space=pltpu.VMEM)


def local(
    iterates,
    window_start,
    coarse,
    step_levels,
    level_embed,
    lift_weight,
    conv_first,
    conv_second,
    project_weight,
    mix_weight,
    output_weight,
):
    level_count = 2 * lax.axis_size("step") + 1
    bands = lax.axis_size("rows")
    previous = from_behind(iterates, "step", 1)
    current = jnp.where(lax.axis_index("step") == 0, window_start, previous[0])
    levels = step_levels[0]
    sigmas = noise_level(levels, level_count)
    sigma_low = sigmas[0]
    sigma_high = sigmas[1]
    spread = sigma_low * sigma_low + 0.25
    scale_in = lax.rsqrt(spread)
    scale_skip = 0.25 / spread
    scale_out = 0.5 * sigma_low * lax.rsqrt(spread)

    channels, band_rows, width = current.shape
    feat = lift_weight.shape[1]
    coarse_halo = with_halo(coarse, "rows", 1, HALO)
    current_halo = with_halo(current, "rows", 1, HALO)
    inputs = jnp.concatenate([(scale_in * current_halo).astype(jnp.bfloat16), coarse_halo], axis=0)
    inputs = inputs.reshape(inputs.shape[0], -1)
    picker = (jnp.arange(level_count) == levels[0]).astype(jnp.bfloat16)[None]
    embed_row = jnp.dot(picker, level_embed, preferred_element_type=jnp.float32)[0]

    def stack_taps(weight):
        return weight.transpose(1, 3, 0, 2).reshape(3 * feat, 3 * feat)

    tokens_per_row = width // 4
    pool_matrix = jnp.where(
        jnp.arange(width)[:, None] // 4 == jnp.arange(tokens_per_row)[None, :], 1.0 / 16.0, 0.0
    ).astype(jnp.float32)
    expand_matrix = jnp.where(
        jnp.arange(tokens_per_row)[:, None] == jnp.arange(width)[None, :] // 4, 1.0, 0.0
    ).astype(jnp.float32)
    band_index = lax.axis_index("rows").astype(jnp.int32).reshape(1)

    pixels = band_rows * width
    tokens = (band_rows // 4) * tokens_per_row
    trunk = pl.pallas_call(
        lambda *refs: trunk_kernel(*refs, width=width, band_rows=band_rows, bands=bands),
        out_shape=(
            jax.ShapeDtypeStruct((feat, pixels), jnp.float32),
            jax.ShapeDtypeStruct((feat, tokens), jnp.float32),
        ),
        in_specs=[pl.BlockSpec(memory_space=pltpu.SMEM)] + [vmem()] * 6,
        out_specs=(vmem(), vmem()),
        scratch_shapes=[
            pltpu.VMEM((feat, (band_rows + 2 * HALO) * width), jnp.bfloat16),
            pltpu.VMEM((feat, pixels), jnp.bfloat16),
            pltpu.VMEM((feat, (band_rows + 2) * width), jnp.bfloat16),
        ],
    )
    hidden, pooled = trunk(
        band_index,
        inputs,
        lift_weight.T,
        embed_row.reshape(feat, 1),
        stack_taps(conv_first),
        stack_taps(conv_second),
        pool_matrix,
    )

    head_count = feat // HEAD_DIM
    token_feats = normalize_features(pooled).astype(jnp.bfloat16)
    projected = jnp.dot(project_weight.T, token_feats, preferred_element_type=jnp.float32)
    queries = feature_map(projected[:feat]).reshape(head_count, HEAD_DIM, tokens)
    key_feats = feature_map(projected[feat : 2 * feat]).astype(jnp.bfloat16).reshape(head_count, HEAD_DIM, tokens)
    value_rows = projected[2 * feat :].astype(jnp.bfloat16).reshape(head_count, HEAD_DIM, tokens)
    summary_own = jnp.einsum("hdt,het->hde", key_feats, value_rows, preferred_element_type=jnp.float32)
    totals_own = jnp.sum(key_feats.astype(jnp.float32), axis=2)
    stats = band_sum(jnp.concatenate([summary_own, totals_own[:, None, :]], axis=1), "rows")
    summary = stats[:, :HEAD_DIM]
    totals = stats[:, HEAD_DIM]
    numerator = jnp.einsum("hdt,hde->het", queries, summary, precision=lax.Precision.HIGHEST)
    denominator = jnp.einsum("hdt,hd->ht", queries, totals, precision=lax.Precision.HIGHEST)
    context = (numerator / denominator[:, None, :]).reshape(feat, tokens).astype(jnp.bfloat16)
    mixed = jnp.dot(mix_weight.T, context, preferred_element_type=jnp.float32)

    out_w = jnp.zeros((16, feat), jnp.bfloat16).at[:channels].set(output_weight.T)
    head = pl.pallas_call(
        lambda *refs: head_kernel(*refs, width=width, band_rows=band_rows),
        out_shape=jax.ShapeDtypeStruct((8, pixels), jnp.float32),
        in_specs=[vmem()] * 4,
        out_specs=vmem(),
    )
    field = head(hidden, mixed, expand_matrix, out_w)
    out_field = field[:channels].reshape(channels, band_rows, width)

    denoised = scale_skip * current + scale_out * out_field
    drift_step = (sigma_high - sigma_low) * (current - denoised) / sigma_low
    summed = prefix_sum(drift_step, "step")
    trajectory = window_start + summed
    return (trajectory[None], denoised[None])


def solution(mesh):
    return jax.shard_map(
        local,
        mesh=mesh,
        in_specs=(
            P("step", "ens", "rows", None),
            P("ens", "rows", None),
            P("ens", "rows", None),
            P("step", None),
            P(),
            P(),
            P(),
            P(),
            P(),
            P(),
            P(),
        ),
        out_specs=(P("step", "ens", "rows", None), P("step", "ens", "rows", None)),
        check_vma=False,
    )
```

time: 81.3 us -> 74.2 us (0.913)
  the two profiles are of different devices: /device:TPU:0 before, /device:TPU:28 now
where the time goes in v3:
time: 74.2 us; the launch traced here: 73.6 us
  waiting for transfers between devices  20.9 us (28%)
  Pallas kernels  18.4 us (25%)
  other arithmetic  9.77 us (13%)
  starting transfers between devices  8.75 us (12%)
  local copies, waits for them, and re-layouts  6.48 us (9%)
  matrix products  5.16 us (7%)
  between operations  4.06 us (5%)
    ppermute x3, waiting for transfers between devices, prefix_sum(): x = x + lax.ppermute(x, axis, pairs)  20.9 us
    pallas_call x1, Pallas kernels, local(): trunk(band_index, inputs, lift_weight.T, embed_row.reshape(feat, 1), stac...  12.4 us
    pallas_call x1, Pallas kernels, local(): field = head(hidden, mixed, expand_matrix, out_w)  6.08 us
    ppermute x3, starting transfers between devices, prefix_sum(): x = x + lax.ppermute(x, axis, pairs)  4.49 us
    ppermute x1, starting transfers between devices, from_behind(): return lax.ppermute(x, axis, pairs)  3.53 us
    transpose x2, local copies, waits for them, and re-layouts, stack_taps(): return weight.transpose(1, 3, 0, 2).reshape(3 * feat, 3 * feat)  2.41 us
    dot_general x1, matrix products, local(): jnp.dot(picker, level_embed, preferred_element_type=jnp.float32)[0]  2.18 us
    broadcast_in_dim x2, other arithmetic, local(): return (trajectory[None], denoised[None])  2.02 us
  transfers between devices with their start and end apart: 7, of which 3 were waited for; matrix products, arithmetic and copies ran while one was open for 17% of the time, Pallas kernels for 0%

profile of v3, /device:TPU:28, one launch (start us, length us, event | category | flops | bytes accessed | tf_op | source)
XLA Modules:
  0.0 73.6 jit_solution(11910385681246215531)
XLA Ops:
  0.6 0.0 copy-start
  0.6 3.5 %collective-permute-start = (f32[1,4,16,512]{3,2,1,0:T(8,128)}, f32[1,4,16,512]{3,2,1,0:T(8,128)S(1)}, u32[]{:S(2)}, u32[]{:S(2)}) collective-permute-start(f32[1,4,16,512]{3,2,1,0:T(8,128)} %param.13), channel_id=1, source_target_pairs={{0,2},{2,4},{4,6},{6,8},{8,10},{10,12},{12,14},{1,3},{3,5},{5,7},{... | collective-permute-start | bytes 393224 | tf_op jit(solution)/shard_map/ppermute | solution.py:19
  4.2 1.0 %broadcast_select_fusion.2 = bf16[12,2,512]{2,1,0:T(2,128)(2,1)S(1)} fusion(pred[]{:T(512)S(6)} %eq.46, bf16[12,16,512]{2,1,0:T(8,128)(2,1)} %param.15), kind=kLoop, calls=%fused_computation.34 | loop fusion | flops 12288 | bytes 73729 | tf_op jit(solution)/shard_map/jit(_where)/select_n | solution.py:28
  5.2 0.1 collective-permute-start.2
  5.3 0.7 exponential_multiply_fusion
  5.9 1.2 %copy.20 = bf16[3,128,3,128]{3,2,1,0:T(4,128)(2,1)S(1)} copy(bf16[3,128,3,128]{1,3,0,2:T(8,128)(2,1)} %bitcast.76) | data formatting | bytes 589824 | tf_op jit(solution)/shard_map/transpose | solution.py:205
  7.1 1.2 %copy.21 = bf16[3,128,3,128]{3,2,1,0:T(4,128)(2,1)S(1)} copy(bf16[3,128,3,128]{1,3,0,2:T(8,128)(2,1)} %bitcast.77) | data formatting | bytes 589824 | tf_op jit(solution)/shard_map/transpose | solution.py:205
  8.4 0.8 %fusion.1.refs_6_ = f32[512,128]{1,0:T(8,128)} fusion(s32[512]{0:T(512)S(1)} %add_select_fusion), kind=kLoop, calls=%fused_computation.17 | loop fusion | flops 131072 | bytes 264192 | tf_op jit(solution)/shard_map/jit(_where)/select_n | solution.py:208
  9.2 0.9 %copy_bitcast_fusion = (bf16[384,384]{1,0:T(8,128)(2,1)}, bf16[384,384]{1,0:T(8,128)(2,1)}) fusion(bf16[48,8,3,128]{3,2,1,0:T(4,128)(2,1)S(1)} %bitcast.68, bf16[48,8,3,128]{3,2,1,0:T(4,128)(2,1)S(1)} %bitcast.67), kind=kLoop, calls=%fused_computation.6 | loop fusion | bytes 1179648 | tf_op jit(solution)/shard_map/reshape | solution.py:205
  10.1 2.2 %convolution_bitcast_fusion.2.refs_3_ = f32[128,1]{1,0:T(8,128)} fusion(bf16[17,128]{1,0:T(8,128)(2,1)} %param.17, s32[]{:T(128)} %bitcast.83), kind=kOutput, calls=%fused_computation.4 | convolution fusion | flops 4369 | bytes 4868 | tf_op jit(solution)/shard_map/dot_general | solution.py:202
  12.3 0.6 fusion.15
  14.1 1.4 %copy.19 = bf16[16,128]{0,1:T(8,128)(2,1)} copy(bf16[16,128]{1,0:T(8,128)(2,1)} %param.18) | data formatting | bytes 8192 | tf_op args[5]
  15.6 0.0 collective-permute-done.2
  15.6 0.0 copy-start.3
  15.6 0.0 collective-permute-done
  15.7 0.6 collective-permute-start.1
  16.2 1.0 %pad_maximum_fusion.1 = bf16[12,20,512]{2,1,0:T(8,128)(2,1)S(1)} fusion(bf16[12,2,512]{2,1,0:T(2,128)(2,1)S(1)} %get-tuple-element.24, bf16[12,16,512]{2,1,0:T(8,128)(2,1)} %param.15, bf16[12,2,512]{2,1,0:T(2,128)(2,1)S(1)} %get-tuple-element.23), kind=kLoop, calls=%fused_computation.8 | loop fusion | flops 737280 | bytes 491520 | tf_op jit(solution)/shard_map/concatenate | solution.py:38
  17.3 0.0 copy-start.2
  17.3 0.1 copy.29
  17.4 0.0 collective-permute-done.1
  17.6 0.8 %pad_maximum_fusion.refs_1_ = bf16[16,10240]{1,0:T(8,128)(2,1)} fusion(bf16[12,10240]{1,0:T(8,128)(2,1)S(1)} %bitcast.69, bf16[4,10240]{1,0:T(4,128)(2,1)S(1)} %bitcast.75), kind=kLoop, calls=%fused_computation.5 | loop fusion | flops 655360 | bytes 655360 | tf_op jit(solution)/shard_map/concatenate | solution.py:199
  18.4 12.4 %shard_map.122 = (f32[128,8192]{1,0:T(8,128)}, f32[128,512]{1,0:T(8,128)}) custom-call(s32[1]{0:T(128)} %bitcast.3.refs_0_, bf16[16,10240]{1,0:T(8,128)(2,1)} %pad_maximum_fusion.refs_1_, bf16[128,16]{1,0:T(8,128)(2,1)} %bitcast.78, f32[128,1]{1,0:T(8,128)} %convolution_bitcast_fusion.2.refs_3_, bf16[384,384]{1,0:T(8,128)(2,1)} %get-tuple-element.30.refs_4_, ...), custom_call_target="tpu_custom_call" | custom-call | tf_op jit(solution)/shard_map/pallas_call | solution.py:232
  30.8 1.0 %multiply_reduce_fusion = f32[512]{0:T(512)S(1)} fusion(f32[128,512]{1,0:T(8,128)} %get-tuple-element.17), kind=kLoop, calls=%fused_computation.15 | loop fusion | flops 130560 | bytes 264192 | tf_op jit(solution)/shard_map/reduce_sum | solution.py:64
  31.8 1.3 %convolution_bitcast_fusion = f32[384,512]{1,0:T(8,128)S(1)} fusion(bf16[128,384]{1,0:T(8,128)(2,1)S(1)} %copy-done, f32[128,512]{1,0:T(8,128)} %get-tuple-element.17, f32[512]{0:T(512)S(1)} %add_rsqrt_fusion), kind=kOutput, calls=%fused_computation | convolution fusion | flops 50462720 | bytes 1148928 | tf_op jit(solution)/shard_map/dot_general | solution.py:244
  33.0 0.2 convert_reduce_fusion
  33.3 0.2 broadcast_in_dim.42
  33.5 0.2 fusion.16
  33.6 0.1 pad_maximum_fusion.2
  33.7 0.1 collective-permute-start.3
  33.8 0.7 fusion.2.refs_2_
  34.6 0.6 scatter.4.refs_3_
  37.0 0.0 collective-permute-done.3
  37.1 0.2 fusion.27
  37.3 0.0 copy-start.1
  37.3 0.2 slice_reduce_fusion
  37.4 0.3 fusion.17
  37.7 0.4 fusion
  38.1 0.9 %convolution_bitcast_fusion.1.refs_1_ = f32[128,512]{1,0:T(8,128)} fusion(bf16[128,512]{1,0:T(8,128)(2,1)S(1)} %bitcast.79, bf16[128,128]{1,0:T(8,128)(2,1)S(1)} %copy-done.2), kind=kOutput, calls=%fused_computation.2 | convolution fusion | flops 16777216 | bytes 425984 | tf_op jit(solution)/shard_map/dot_general | solution.py:256
  39.0 6.1 %shard_map.123 = f32[8,8192]{1,0:T(8,128)} custom-call(f32[128,8192]{1,0:T(8,128)} %get-tuple-element.16.refs_0_, f32[128,512]{1,0:T(8,128)} %convolution_bitcast_fusion.1.refs_1_, f32[128,512]{1,0:T(8,128)} %fusion.2.refs_2_, bf16[16,128]{1,0:T(8,128)(2,1)} %scatter.4.refs_3_), custom_call_target="tpu_custom_call" | custom-call | tf_op jit(solution)/shard_map/pallas_call | solution.py:265
  45.1 1.0 %slice_multiply_fusion = f32[4,8192]{1,0:T(4,128)S(1)} fusion(f32[8,8192]{1,0:T(8,128)} %shard_map.123, f32[]{:T(128)S(6)} %mul.74), kind=kLoop, calls=%fused_computation.22 | loop fusion | flops 32768 | bytes 262148 | tf_op jit(solution)/shard_map/mul | solution.py:268
  46.1 1.3 %fusion.5 = (f32[1,4,16,512]{3,2,1,0:T(8,128)}, f32[4,16,512]{2,1,0:T(8,128)S(1)}) fusion(f32[1,4,16,512]{3,1,2,0:T(4,128)S(1)} %bitcast.72, f32[4,16,512]{2,1,0:T(8,128)S(1)} %bitcast_select_fusion, f32[]{:T(128)S(6)} %div.32, f32[]{:T(128)} %bitcast.1, f32[]{:T(128)S(6)} %sub.18), kind=kLoop, calls=%fused_computation.27 | loop fusion | flops 163840 | bytes 524300 | tf_op jit(solution)/shard_map/broadcast_in_dim | solution.py:272
  47.4 1.9 %collective-permute-start.4 = (f32[4,16,512]{2,1,0:T(8,128)S(1)}, f32[4,16,512]{2,1,0:T(8,128)S(1)}, u32[]{:S(2)}, u32[]{:S(2)}) collective-permute-start(f32[4,16,512]{2,1,0:T(8,128)S(1)} %get-tuple-element.22), channel_id=1, source_target_pairs={{0,2},{2,4},{4,6},{6,8},{8,10},{10,12},{12,14},{1,3},{3,5},{5,7},{... | collective-permute-start | bytes 393224 | tf_op jit(solution)/shard_map/ppermute | solution.py:53
  49.3 6.7 %collective-permute-done.4 = f32[4,16,512]{2,1,0:T(8,128)S(1)} collective-permute-done((f32[4,16,512]{2,1,0:T(8,128)S(1)}, f32[4,16,512]{2,1,0:T(8,128)S(1)}, u32[]{:S(2)}, u32[]{:S(2)}) %collective-permute-start.4) | collective-permute-done | bytes 131104 | tf_op jit(solution)/shard_map/ppermute | solution.py:53
  56.1 1.3 %collective-permute-start.5 = (f32[4,16,512]{2,1,0:T(8,128)S(1)}, f32[4,16,512]{2,1,0:T(8,128)S(1)}, u32[]{:S(2)}, u32[]{:S(2)}) collective-permute-start(f32[4,16,512]{2,1,0:T(8,128)S(1)} %add.61), channel_id=1, source_target_pairs={{0,4},{2,6},{4,8},{6,10},{8,12},{10,14},{1,5},{3,7},{5,9},{7,11},{... | collective-permute-start | bytes 393224 | tf_op jit(solution)/shard_map/ppermute | solution.py:53
  57.4 5.7 %collective-permute-done.5 = f32[4,16,512]{2,1,0:T(8,128)S(1)} collective-permute-done((f32[4,16,512]{2,1,0:T(8,128)S(1)}, f32[4,16,512]{2,1,0:T(8,128)S(1)}, u32[]{:S(2)}, u32[]{:S(2)}) %collective-permute-start.5) | collective-permute-done | bytes 131104 | tf_op jit(solution)/shard_map/ppermute | solution.py:53
  63.1 1.3 %collective-permute-start.6 = (f32[4,16,512]{2,1,0:T(8,128)S(1)}, f32[4,16,512]{2,1,0:T(8,128)S(1)}, u32[]{:S(2)}, u32[]{:S(2)}) collective-permute-start(f32[4,16,512]{2,1,0:T(8,128)S(1)} %add.62), channel_id=1, source_target_pairs={{0,8},{2,10},{4,12},{6,14},{1,9},{3,11},{5,13},{7,15},{16,24},{18,... | collective-permute-start | bytes 393224 | tf_op jit(solution)/shard_map/ppermute | solution.py:53
  64.4 8.5 %collective-permute-done.6 = f32[4,16,512]{2,1,0:T(8,128)S(1)} collective-permute-done((f32[4,16,512]{2,1,0:T(8,128)S(1)}, f32[4,16,512]{2,1,0:T(8,128)S(1)}, u32[]{:S(2)}, u32[]{:S(2)}) %collective-permute-start.6) | collective-permute-done | bytes 131104 | tf_op jit(solution)/shard_map/ppermute | solution.py:53
  72.9 0.7 add_bitcast_fusion
  (17 shorter events, 0.3 us)
Async XLA Ops:
  0.6 31.1 %copy-start = (bf16[128,384]{1,0:T(8,128)(2,1)S(1)}, bf16[128,384]{1,0:T(8,128)(2,1)}, u32[]{:S(2)}) copy-start(bf16[128,384]{1,0:T(8,128)(2,1)} %param.21) | copy-start | bytes 294916
  0.6 15.0 %collective-permute-start = (f32[1,4,16,512]{3,2,1,0:T(8,128)}, f32[1,4,16,512]{3,2,1,0:T(8,128)S(1)}, u32[]{:S(2)}, u32[]{:S(2)}) collective-permute-start(f32[1,4,16,512]{3,2,1,0:T(8,128)} %param.13), channel_id=1, source_target_pairs={{0,2},{2,4},{4,6},{6,8},{8,10},{10,12},{12,14},{1,3},{3,5},{5,7},{... | collective-permute-start | bytes 393224 | tf_op jit(solution)/shard_map/ppermute | solution.py:19
  5.2 10.4 %collective-permute-start.2 = (bf16[12,2,512]{2,1,0:T(2,128)(2,1)S(1)}, bf16[12,2,512]{2,1,0:T(2,128)(2,1)S(1)}, u32[]{:S(2)}, u32[]{:S(2)}) collective-permute-start(bf16[12,2,512]{2,1,0:T(2,128)(2,1)S(1)} %broadcast_select_fusion.2), channel_id=1, source_target_pairs={{0,1},{1,0},{2,3},{3,2},{4,5},{5,4},{6,7},{7,6},{8,9},{9,8},{10,11... | collective-permute-start | bytes 73736 | tf_op jit(solution)/shard_map/ppermute | solution.py:29
  15.6 19.0 %copy-start.3 = (bf16[128,4]{0,1:T(4,128)(2,1)S(1)}, bf16[128,4]{0,1:T(4,128)(2,1)}, u32[]{:S(2)}) copy-start(bf16[128,4]{0,1:T(4,128)(2,1)} %param.23) | copy-start | bytes 3076
  15.7 1.8 %collective-permute-start.1 = (f32[4,2,512]{2,1,0:T(2,128)S(1)}, f32[4,2,512]{2,1,0:T(2,128)S(1)}, u32[]{:S(2)}, u32[]{:S(2)}) collective-permute-start(f32[4,2,512]{2,1,0:T(2,128)S(1)} %slice_select_fusion), channel_id=1, source_target_pairs={{0,1},{1,0},{2,3},{3,2},{4,5},{5,4},{6,7},{7,6},{8,9},{9,8},{10,11... | collective-permute-start | bytes 49160 | tf_op jit(solution)/shard_map/ppermute | solution.py:29
  17.3 20.8 %copy-start.2 = (bf16[128,128]{1,0:T(8,128)(2,1)S(1)}, bf16[128,128]{1,0:T(8,128)(2,1)}, u32[]{:S(2)}) copy-start(bf16[128,128]{1,0:T(8,128)(2,1)} %param.22) | copy-start | bytes 98308
  33.7 3.3 %collective-permute-start.3 = (f32[2,65,64]{1,2,0:T(8,128)S(1)}, f32[2,65,64]{1,2,0:T(8,128)S(1)}, u32[]{:S(2)}, u32[]{:S(2)}) collective-permute-start(f32[2,65,64]{1,2,0:T(8,128)S(1)} %pad_maximum_fusion.2), channel_id=1, source_target_pairs={{0,1},{1,0},{2,3},{3,2},{4,5},{5,4},{6,7},{7,6},{8,9},{9,8},{10,11... | collective-permute-start | bytes 99848 | tf_op jit(solution)/shard_map/ppermute | solution.py:44
  37.3 35.6 %copy-start.1 = (f32[4,16,512]{2,1,0:T(8,128)S(1)}, f32[4,16,512]{2,1,0:T(8,128)}, u32[]{:S(2)}) copy-start(f32[4,16,512]{2,1,0:T(8,128)} %param.14) | copy-start | bytes 393220
  47.4 8.7 %collective-permute-start.4 = (f32[4,16,512]{2,1,0:T(8,128)S(1)}, f32[4,16,512]{2,1,0:T(8,128)S(1)}, u32[]{:S(2)}, u32[]{:S(2)}) collective-permute-start(f32[4,16,512]{2,1,0:T(8,128)S(1)} %get-tuple-element.22), channel_id=1, source_target_pairs={{0,2},{2,4},{4,6},{6,8},{8,10},{10,12},{12,14},{1,3},{3,5},{5,7},{... | collective-permute-start | bytes 393224 | tf_op jit(solution)/shard_map/ppermute | solution.py:53
  56.1 7.0 %collective-permute-start.5 = (f32[4,16,512]{2,1,0:T(8,128)S(1)}, f32[4,16,512]{2,1,0:T(8,128)S(1)}, u32[]{:S(2)}, u32[]{:S(2)}) collective-permute-start(f32[4,16,512]{2,1,0:T(8,128)S(1)} %add.61), channel_id=1, source_target_pairs={{0,4},{2,6},{4,8},{6,10},{8,12},{10,14},{1,5},{3,7},{5,9},{7,11},{... | collective-permute-start | bytes 393224 | tf_op jit(solution)/shard_map/ppermute | solution.py:53
  63.1 9.8 %collective-permute-start.6 = (f32[4,16,512]{2,1,0:T(8,128)S(1)}, f32[4,16,512]{2,1,0:T(8,128)S(1)}, u32[]{:S(2)}, u32[]{:S(2)}) collective-permute-start(f32[4,16,512]{2,1,0:T(8,128)S(1)} %add.62), channel_id=1, source_target_pairs={{0,8},{2,10},{4,12},{6,14},{1,9},{3,11},{5,13},{7,15},{16,24},{18,... | collective-permute-start | bytes 393224 | tf_op jit(solution)/shard_map/ppermute | solution.py:53

commit v4 on v3

--- a/solution.py
+++ b/solution.py
@@ -89,9 +89,23 @@
     return result
 
 
+def transposed(block):
+    return block.astype(jnp.float32).T
+
+
+def stack_taps(weight_ref):
+    return jnp.concatenate(
+        [
+            jnp.concatenate([transposed(weight_ref[i, j]) for i in range(3)], axis=1)
+            for j in range(3)
+        ],
+        axis=0,
+    ).astype(jnp.bfloat16)
+
+
 def trunk_kernel(
-    band_ref, inputs_ref, lift_ref, embed_ref, first_ref, second_ref, pool_ref,
-    hidden_ref, pooled_ref, act_first, lifted_keep, act_next, *, width, band_rows, bands,
+    band_ref, inputs_ref, lift_ref, embed_ref, first_ref, second_ref, project_ref,
+    hidden_ref, query_ref, stats_ref, act_first, lifted_keep, act_next, *, width, band_rows, bands,
 ):
     band = band_ref[0]
     top_outside = band == 0
@@ -116,7 +130,7 @@
         if row0 >= HALO + band_rows:
             act = jnp.where(bottom_outside, 0.0, act)
         act_first[:, start : start + span] = act.astype(jnp.bfloat16)
-    first_w = first_ref[...]
+    first_w = stack_taps(first_ref)
     mid_rows = band_rows + 2
     for q in range(mid_rows // CHUNK_ROWS):
         start = q * span
@@ -127,43 +141,120 @@
         if q == mid_rows // CHUNK_ROWS - 1:
             act = jnp.where(jnp.logical_and(bottom_outside, jnp.logical_not(upper_row)), 0.0, act)
         act_next[:, start : start + span] = act.astype(jnp.bfloat16)
-    second_w = second_ref[...]
+    second_w = stack_taps(second_ref)
     for q in range(band_rows // CHUNK_ROWS):
         start = q * span
         conv = conv_chunk(act_next, second_w, q * CHUNK_ROWS, CHUNK_ROWS, width, column)
         hidden_ref[:, start : start + span] = lifted_keep[:, start : start + span].astype(jnp.float32) + conv
-    pool_w = pool_ref[...]
     tokens_per_row = width // 4
+    pool_w = jnp.where(
+        lax.broadcasted_iota(jnp.int32, (width, tokens_per_row), 0) // 4
+        == lax.broadcasted_iota(jnp.int32, (width, tokens_per_row), 1),
+        1.0 / 16.0,
+        0.0,
+    ).astype(jnp.float32)
+    pooled = []
     for a in range(band_rows // 4):
         row_sum = hidden_ref[:, (4 * a) * width : (4 * a + 1) * width]
         for u in range(1, 4):
             row_sum = row_sum + hidden_ref[:, (4 * a + u) * width : (4 * a + u + 1) * width]
-        pooled_ref[:, a * tokens_per_row : (a + 1) * tokens_per_row] = jnp.dot(
-            row_sum, pool_w, precision=lax.Precision.HIGHEST, preferred_element_type=jnp.float32
+        pooled.append(
+            jnp.dot(row_sum, pool_w, precision=lax.Precision.HIGHEST, preferred_element_type=jnp.float32)
         )
-
-
-def head_kernel(hidden_ref, mixed_ref, expand_ref, out_w_ref, field_ref, *, width, band_rows):
-    expand = expand_ref[...]
+    pooled = jnp.concatenate(pooled, axis=1)
+    feat = pooled.shape[0]
+    tokens = normalize_features(pooled).astype(jnp.bfloat16)
+    project_t = jnp.concatenate(
+        [transposed(project_ref[:, g * feat : (g + 1) * feat]) for g in range(3)], axis=0
+    ).astype(jnp.bfloat16)
+    projected = jnp.dot(project_t, tokens, preferred_element_type=jnp.float32)
+    query_ref[...] = feature_map(projected[:feat])
+    key_feats = feature_map(projected[feat : 2 * feat]).astype(jnp.bfloat16)
+    value_rows = projected[2 * feat :].astype(jnp.bfloat16)
+    ones = jnp.ones((HEAD_DIM, key_feats.shape[1]), jnp.bfloat16)
+    contract_tokens = (((1,), (1,)), ((), ()))
+    for h in range(feat // HEAD_DIM):
+        keys_h = key_feats[h * HEAD_DIM : (h + 1) * HEAD_DIM]
+        values_h = value_rows[h * HEAD_DIM : (h + 1) * HEAD_DIM]
+        summary_t = lax.dot_general(values_h, keys_h, contract_tokens, preferred_element_type=jnp.float32)
+        totals = lax.dot_general(ones, keys_h, contract_tokens, preferred_element_type=jnp.float32)
+        stats_ref[h * HEAD_DIM : (h + 1) * HEAD_DIM, :] = jnp.concatenate([summary_t, totals], axis=1)
+
+
+def head_kernel(
+    scalar_ref, hidden_ref, query_ref, stats_ref, mix_ref, out_w_ref, current_ref,
+    denoised_ref, drift_ref, *, width, band_rows,
+):
+    scale_skip = scalar_ref[0]
+    scale_out = scalar_ref[1]
+    sigma_gap = scalar_ref[2]
+    sigma_low = scalar_ref[3]
+    feat = query_ref.shape[0]
+    contexts = []
+    for h in range(feat // HEAD_DIM):
+        rows = slice(h * HEAD_DIM, (h + 1) * HEAD_DIM)
+        queries_h = query_ref[rows, :]
+        numerator = jnp.dot(
+            stats_ref[rows, 0:HEAD_DIM], queries_h,
+            precision=lax.Precision.HIGHEST, preferred_element_type=jnp.float32,
+        )
+        denominator = jnp.dot(
+            stats_ref[rows, HEAD_DIM : 2 * HEAD_DIM], queries_h,
+            precision=lax.Precision.HIGHEST, preferred_element_type=jnp.float32,
+        )
+        contexts.append(numerator / denominator)
+    context = jnp.concatenate(contexts, axis=0).astype(jnp.bfloat16)
+    mix_t = transposed(mix_ref[...]).astype(jnp.bfloat16)
+    mixed = jnp.dot(mix_t, context, preferred_element_type=jnp.float32)
+    tokens_per_row = width // 4
+    expand = jnp.where(
+        lax.broadcasted_iota(jnp.int32, (tokens_per_row, width), 0)
+        == lax.broadcasted_iota(jnp.int32, (tokens_per_row, width), 1) // 4,
+        1.0,
+        0.0,
+    ).astype(jnp.float32)
     out_w = out_w_ref[...]
-    tokens_per_row = width // 4
+    channels = current_ref.shape[0]
     for a in range(band_rows // 4):
         spread = jnp.dot(
-            mixed_ref[:, a * tokens_per_row : (a + 1) * tokens_per_row],
+            mixed[:, a * tokens_per_row : (a + 1) * tokens_per_row],
             expand,
             precision=lax.Precision.HIGHEST,
             preferred_element_type=jnp.float32,
         )
         for u in range(4):
-            start = (4 * a + u) * width
+            r = 4 * a + u
+            start = r * width
             combined = hidden_ref[:, start : start + width] + spread
             act = silu(normalize_features(combined)).astype(jnp.bfloat16)
-            field = jnp.dot(out_w, act, preferred_element_type=jnp.float32)
-            field_ref[:, start : start + width] = field[0:8]
+            field = jnp.dot(out_w, act, preferred_element_type=jnp.float32)[0:channels]
+            state = current_ref[:, r, :]
+            denoised = scale_skip * state + scale_out * field
+            denoised_ref[:, r, :] = denoised
+            drift_ref[:, r, :] = sigma_gap * (state - denoised) / sigma_low
 
 
 def vmem():
     return pl.BlockSpec(memory_space=pltpu.VMEM)
+
+
+def smem():
+    return pl.BlockSpec(memory_space=pltpu.SMEM)
+
+
+def edge_rows(x, axis, dim, width):
+    length = x.shape[dim]
+    last = lax.slice_in_dim(x, length - width, length, axis=dim)
+    leading = lax.slice_in_dim(x, 0, width, axis=dim)
+    return jnp.where(lax.axis_index(axis) == 0, last, leading)
+
+
+def place_halo(x, incoming, axis, dim):
+    me = lax.axis_index(axis)
+    zero = jnp.zeros_like(incoming)
+    before = jnp.where(me == 0, zero, incoming)
+    after = jnp.where(me == 0, incoming, zero)
+    return jnp.concatenate([before, x, after], axis=dim)
 
 
 def local(
@@ -181,8 +272,21 @@
 ):
     level_count = 2 * lax.axis_size("step") + 1
     bands = lax.axis_size("rows")
+    steps = lax.axis_size("step")
+    first_step = lax.axis_index("step") == 0
     previous = from_behind(iterates, "step", 1)
-    current = jnp.where(lax.axis_index("step") == 0, window_start, previous[0])
+    if bands == 2:
+        pairs = [(j * 2 + b, (j + 1) * 2 + (1 - b)) for j in range(steps - 1) for b in range(2)]
+        iterate_halo = lax.ppermute(edge_rows(iterates[0], "rows", 1, HALO), ("step", "rows"), pairs)
+        start_halo = lax.ppermute(edge_rows(window_start, "rows", 1, HALO), "rows", [(0, 1), (1, 0)])
+        coarse_halo = lax.ppermute(edge_rows(coarse, "rows", 1, HALO), "rows", [(0, 1), (1, 0)])
+    current = jnp.where(first_step, window_start, previous[0])
+    if bands == 2:
+        current_halo = place_halo(current, jnp.where(first_step, start_halo, iterate_halo), "rows", 1)
+        coarse_halo = place_halo(coarse, coarse_halo, "rows", 1)
+    else:
+        current_halo = with_halo(current, "rows", 1, HALO)
+        coarse_halo = with_halo(coarse, "rows", 1, HALO)
     levels = step_levels[0]
     sigmas = noise_level(levels, level_count)
     sigma_low = sigmas[0]
@@ -194,79 +298,52 @@
 
     channels, band_rows, width = current.shape
     feat = lift_weight.shape[1]
-    coarse_halo = with_halo(coarse, "rows", 1, HALO)
-    current_halo = with_halo(current, "rows", 1, HALO)
     inputs = jnp.concatenate([(scale_in * current_halo).astype(jnp.bfloat16), coarse_halo], axis=0)
     inputs = inputs.reshape(inputs.shape[0], -1)
     picker = (jnp.arange(level_count) == levels[0]).astype(jnp.bfloat16)[None]
     embed_row = jnp.dot(picker, level_embed, preferred_element_type=jnp.float32)[0]
-
-    def stack_taps(weight):
-        return weight.transpose(1, 3, 0, 2).reshape(3 * feat, 3 * feat)
-
-    tokens_per_row = width // 4
-    pool_matrix = jnp.where(
-        jnp.arange(width)[:, None] // 4 == jnp.arange(tokens_per_row)[None, :], 1.0 / 16.0, 0.0
-    ).astype(jnp.float32)
-    expand_matrix = jnp.where(
-        jnp.arange(tokens_per_row)[:, None] == jnp.arange(width)[None, :] // 4, 1.0, 0.0
-    ).astype(jnp.float32)
     band_index = lax.axis_index("rows").astype(jnp.int32).reshape(1)
 
     pixels = band_rows * width
-    tokens = (band_rows // 4) * tokens_per_row
+    tokens = (band_rows // 4) * (width // 4)
     trunk = pl.pallas_call(
         lambda *refs: trunk_kernel(*refs, width=width, band_rows=band_rows, bands=bands),
         out_shape=(
             jax.ShapeDtypeStruct((feat, pixels), jnp.float32),
             jax.ShapeDtypeStruct((feat, tokens), jnp.float32),
+            jax.ShapeDtypeStruct((feat, 2 * HEAD_DIM), jnp.float32),
         ),
-        in_specs=[pl.BlockSpec(memory_space=pltpu.SMEM)] + [vmem()] * 6,
-        out_specs=(vmem(), vmem()),
+        in_specs=[smem()] + [vmem()] * 6,
+        out_specs=(vmem(), vmem(), vmem()),
         scratch_shapes=[
             pltpu.VMEM((feat, (band_rows + 2 * HALO) * width), jnp.bfloat16),
             pltpu.VMEM((feat, pixels), jnp.bfloat16),
             pltpu.VMEM((feat, (band_rows + 2) * width), jnp.bfloat16),
         ],
     )
-    hidden, pooled = trunk(
+    hidden, queries, stats_own = trunk(
         band_index,
         inputs,
         lift_weight.T,
         embed_row.reshape(feat, 1),
-        stack_taps(conv_first),
-        stack_taps(conv_second),
-        pool_matrix,
-    )
-
-    head_count = feat // HEAD_DIM
-    token_feats = normalize_features(pooled).astype(jnp.bfloat16)
-    projected = jnp.dot(project_weight.T, token_feats, preferred_element_type=jnp.float32)
-    queries = feature_map(projected[:feat]).reshape(head_count, HEAD_DIM, tokens)
-    key_feats = feature_map(projected[feat : 2 * feat]).astype(jnp.bfloat16).reshape(head_count, HEAD_DIM, tokens)
-    value_rows = projected[2 * feat :].astype(jnp.bfloat16).reshape(head_count, HEAD_DIM, tokens)
-    summary_own = jnp.einsum("hdt,het->hde", key_feats, value_rows, preferred_element_type=jnp.float32)
-    totals_own = jnp.sum(key_feats.astype(jnp.float32), axis=2)
-    stats = band_sum(jnp.concatenate([summary_own, totals_own[:, None, :]], axis=1), "rows")
-    summary = stats[:, :HEAD_DIM]
-    totals = stats[:, HEAD_DIM]
-    numerator = jnp.einsum("hdt,hde->het", queries, summary, precision=lax.Precision.HIGHEST)
-    denominator = jnp.einsum("hdt,hd->ht", queries, totals, precision=lax.Precision.HIGHEST)
-    context = (numerator / denominator[:, None, :]).reshape(feat, tokens).astype(jnp.bfloat16)
-    mixed = jnp.dot(mix_weight.T, context, preferred_element_type=jnp.float32)
-
-    out_w = jnp.zeros((16, feat), jnp.bfloat16).at[:channels].set(output_weight.T)
+        conv_first,
+        conv_second,
+        project_weight,
+    )
+    stats = band_sum(stats_own, "rows")
+
+    out_w = jnp.pad(output_weight.T, ((0, 16 - channels), (0, 0)))
+    scalars = jnp.stack([scale_skip, scale_out, sigma_high - sigma_low, sigma_low]).astype(jnp.float32)
     head = pl.pallas_call(
         lambda *refs: head_kernel(*refs, width=width, band_rows=band_rows),
-        out_shape=jax.ShapeDtypeStruct((8, pixels), jnp.float32),
-        in_specs=[vmem()] * 4,
-        out_specs=vmem(),
-    )
-    field = head(hidden, mixed, expand_matrix, out_w)
-    out_field = field[:channels].reshape(channels, band_rows, width)
-
-    denoised = scale_skip * current + scale_out * out_field
-    drift_step = (sigma_high - sigma_low) * (current - denoised) / sigma_low
+        out_shape=(
+            jax.ShapeDtypeStruct(current.shape, jnp.float32),
+            jax.ShapeDtypeStruct(current.shape, jnp.float32),
+        ),
+        in_specs=[smem()] + [vmem()] * 6,
+        out_specs=(vmem(), vmem()),
+    )
+    denoised, drift_step = head(scalars, hidden, queries, stats, mix_weight, out_w, current)
     summed = prefix_sum(drift_step, "step")
     trajectory = window_start + summed
     return (trajectory[None], denoised[None])

time: 74.2 us -> 70.3 us (0.947)
  the two profiles are of different devices: /device:TPU:28 before, /device:TPU:0 now
where the time goes in v4:
time: 70.3 us; the launch traced here: 69.7 us
  starting transfers between devices  22.1 us (31%)
  Pallas kernels  19.4 us (28%)
  other arithmetic  10.7 us (15%)
  waiting for transfers between devices  8.46 us (12%)
  between operations  3.95 us (6%)
  local copies, waits for them, and re-layouts  3.44 us (5%)
  matrix products  1.49 us (2%)
    ppermute x3, starting transfers between devices, prefix_sum(): x = x + lax.ppermute(x, axis, pairs)  13.1 us
    pallas_call x1, Pallas kernels, local(): trunk(band_index, inputs, lift_weight.T, embed_row.reshape(feat, 1), conv...  12.5 us
    ppermute x3, waiting for transfers between devices, prefix_sum(): x = x + lax.ppermute(x, axis, pairs)  8.45 us
    pallas_call x1, Pallas kernels, local(): head(scalars, hidden, queries, stats, mix_weight, out_w, current)  6.94 us
    ppermute x1, starting transfers between devices, from_behind(): return lax.ppermute(x, axis, pairs)  4.84 us
    ppermute x1, starting transfers between devices, local(): lax.ppermute(edge_rows(iterates[0], 'rows', 1, HALO), ('step', 'rows'), p...  2.8 us
    select_n x3, other arithmetic, edge_rows(): return jnp.where(lax.axis_index(axis) == 0, last, leading)  2.77 us
    unnamed x10, local copies, waits for them, and re-layouts  1.59 us
  transfers between devices with their start and end apart: 8, of which 3 were waited for; matrix products, arithmetic and copies ran while one was open for 14% of the time, Pallas kernels for 0%

profile of v4, /device:TPU:0, one launch (start us, length us, event | category | flops | bytes accessed | tf_op | source)
XLA Modules:
  0.0 69.7 jit_solution(17653624615154178584)
XLA Ops:
  0.6 0.0 copy-start
  0.7 1.0 %broadcast_select_fusion.2 = bf16[12,2,512]{2,1,0:T(2,128)(2,1)S(1)} fusion(pred[]{:T(512)S(6)} %eq.20, bf16[12,16,512]{2,1,0:T(8,128)(2,1)} %param.13), kind=kLoop, calls=%fused_computation.10 | loop fusion | flops 12288 | bytes 73729 | tf_op jit(solution)/shard_map/jit(_where)/select_n | solution.py:249
  1.6 0.5 collective-permute-start.3
  2.2 0.9 %slice_select_fusion.1 = f32[4,2,512]{2,1,0:T(2,128)S(1)} fusion(f32[4,16,512]{2,1,0:T(8,128)} %param.12, pred[]{:T(512)S(6)} %eq.20), kind=kLoop, calls=%fused_computation.12 | loop fusion | flops 4096 | bytes 49153 | tf_op jit(solution)/shard_map/jit(_where)/select_n | solution.py:249
  3.0 0.1 collective-permute-start
  3.2 4.8 %collective-permute-start.2 = (f32[1,4,16,512]{3,2,1,0:T(8,128)}, f32[1,4,16,512]{3,2,1,0:T(8,128)S(1)}, u32[]{:S(2)}, u32[]{:S(2)}) collective-permute-start(f32[1,4,16,512]{3,2,1,0:T(8,128)} %param.11), channel_id=1, source_target_pairs={{0,2},{2,4},{4,6},{6,8},{8,10},{10,12},{12,14},{1,3},{3,5},{5,7},{... | collective-permute-start | bytes 393224 | tf_op jit(solution)/shard_map/ppermute | solution.py:19
  8.0 0.9 %slice_select_fusion = f32[4,2,512]{2,1,0:T(2,128)S(1)} fusion(f32[4,16,512]{2,1,0:T(8,128)} %bitcast.34, pred[]{:T(512)S(6)} %eq.20), kind=kLoop, calls=%fused_computation.11 | loop fusion | flops 4096 | bytes 49153 | tf_op jit(solution)/shard_map/jit(_where)/select_n | solution.py:249
  8.9 2.8 %collective-permute-start.1 = (f32[4,2,512]{2,1,0:T(2,128)S(1)}, f32[4,2,512]{2,1,0:T(2,128)S(1)}, u32[]{:S(2)}, u32[]{:S(2)}) collective-permute-start(f32[4,2,512]{2,1,0:T(2,128)S(1)} %slice_select_fusion), channel_id=1, source_target_pairs={{0,3},{1,2},{2,5},{3,4},{4,7},{5,6},{6,9},{7,8},{8,11},{9,10},{10,... | collective-permute-start | bytes 49160 | tf_op jit(solution)/shard_map/ppermute | solution.py:280
  11.7 0.7 exponential_multiply_fusion
  12.4 0.0 copy-done
  12.4 1.5 %convolution_bitcast_fusion.refs_3_ = f32[128,1]{1,0:T(8,128)} fusion(bf16[17,128]{1,0:T(8,128)(2,1)S(1)} %copy-done, s32[]{:T(128)} %bitcast.36), kind=kOutput, calls=%fused_computation | convolution fusion | flops 4369 | bytes 4868 | tf_op jit(solution)/shard_map/dot_general | solution.py:304
  13.9 0.6 fusion.6
  17.6 1.4 %copy.15 = bf16[16,128]{0,1:T(8,128)(2,1)} copy(bf16[16,128]{1,0:T(8,128)(2,1)} %param.16) | data formatting | bytes 8192 | tf_op args[5]
  19.0 1.3 %pad.4.refs_5_ = bf16[16,128]{1,0:T(8,128)(2,1)} pad(bf16[4,128]{1,0:T(4,128)(2,1)} %bitcast.35, bf16[]{:T(256)} %constant.28.clone.1), padding=0_12x0_0 | pad | bytes 5122 | tf_op jit(solution)/shard_map/jit(_pad)/pad | solution.py:335
  20.3 0.0 collective-permute-done
  20.3 0.0 collective-permute-done.1
  20.3 0.0 collective-permute-done.3
  20.4 1.1 %pad_maximum_fusion.1 = bf16[12,20,512]{2,1,0:T(8,128)(2,1)S(1)} fusion(bf16[12,2,512]{2,1,0:T(2,128)(2,1)S(1)} %get-tuple-element.15, bf16[12,16,512]{2,1,0:T(8,128)(2,1)} %param.13, bf16[12,2,512]{2,1,0:T(2,128)(2,1)S(1)} %get-tuple-element.14), kind=kLoop, calls=%fused_computation.2 | loop fusion | flops 737280 | bytes 491520 | tf_op jit(solution)/shard_map/concatenate | solution.py:257
  21.5 0.1 copy.18
  21.6 0.0 copy-start.2
  21.6 0.0 collective-permute-done.2
  21.6 1.0 %bitcast_select_fusion.refs_6_ = f32[4,16,512]{2,1,0:T(8,128)S(1)} fusion(f32[4,16,512]{2,1,0:T(8,128)} %param.12, f32[1,4,16,512]{3,2,1,0:T(8,128)S(1)} %collective-permute-done.2, pred[]{:T(512)S(6)} %eq.21), kind=kLoop, calls=%fused_computation.5 | loop fusion | flops 32768 | bytes 393217 | tf_op jit(solution)/shard_map/jit(_where)/select_n | solution.py:283
  22.6 0.0 copy-start.1
  22.7 0.9 %pad_maximum_fusion.refs_1_ = bf16[16,10240]{1,0:T(8,128)(2,1)} fusion(bf16[12,10240]{1,0:T(8,128)(2,1)S(1)} %bitcast.31, bf16[4,10240]{1,0:T(4,128)(2,1)S(1)} %bitcast.32), kind=kLoop, calls=%fused_computation.1 | loop fusion | flops 655360 | bytes 655360 | tf_op jit(solution)/shard_map/concatenate | solution.py:301
  23.6 12.5 %shard_map.122 = (f32[128,8192]{1,0:T(8,128)}, f32[128,512]{1,0:T(8,128)}, f32[128,128]{1,0:T(8,128)}) custom-call(s32[1]{0:T(128)} %bitcast.5.refs_0_, bf16[16,10240]{1,0:T(8,128)(2,1)} %pad_maximum_fusion.refs_1_, bf16[128,16]{1,0:T(8,128)(2,1)} %bitcast.33, f32[128,1]{1,0:T(8,128)} %convolution_bitcast_fusion.refs_3_, bf16[3,3,128,128]{3,2,1,0:T(8,128)(2,1)} %refs_4_.2, ...), custom_call_target="tpu_custom_call" | custom-call | tf_op jit(solution)/shard_map/pallas_call | solution.py:324
  36.1 0.8 %collective-permute-start.4 = (f32[128,128]{1,0:T(8,128)}, f32[128,128]{1,0:T(8,128)S(1)}, u32[]{:S(2)}, u32[]{:S(2)}) collective-permute-start(f32[128,128]{1,0:T(8,128)} %get-tuple-element.9), channel_id=1, source_target_pairs={{0,1},{1,0},{2,3},{3,2},{4,5},{5,4},{6,7},{7,6},{8,9},{9,8},{10,11... | collective-permute-start | bytes 196616 | tf_op jit(solution)/shard_map/ppermute | solution.py:44
  36.8 1.2 %pad_maximum_fusion.2.refs_0_ = f32[4]{0:T(128)} fusion(f32[1]{0:T(128)} %bitcast, f32[1]{0:T(128)S(6)} %sub.4, f32[1]{0:T(128)} %bitcast.3, f32[1]{0:T(128)S(6)} %div.5), kind=kLoop, calls=%fused_computation.18 | loop fusion | flops 12 | bytes 32 | tf_op jit(solution)/shard_map/stack | solution.py:336
  38.0 0.0 collective-permute-done.4
  38.0 1.5 %add.22.refs_3_ = f32[128,128]{1,0:T(8,128)} add(f32[128,128]{1,0:T(8,128)} %get-tuple-element.9, f32[128,128]{1,0:T(8,128)S(1)} %collective-permute-done.4) | non-fusion elementwise | flops 16384 | bytes 196608 | tf_op jit(solution)/shard_map/add | solution.py:44
  39.5 0.0 copy-done.1
  39.5 6.9 %shard_map.123 = (f32[4,16,512]{2,1,0:T(8,128)}, f32[4,16,512]{2,1,0:T(8,128)}) custom-call(f32[4]{0:T(128)} %pad_maximum_fusion.2.refs_0_, f32[128,8192]{1,0:T(8,128)} %get-tuple-element.7.refs_1_, f32[128,512]{1,0:T(8,128)} %get-tuple-element.8.refs_2_, f32[128,128]{1,0:T(8,128)} %add.22.refs_3_, bf16[128,128]{1,0:T(8,128)(2,1)} %refs_4_.3, ...), custom_call_target="tpu_custom_call" | custom-call | tf_op jit(solution)/shard_map/pallas_call | solution.py:346
  46.5 2.5 %collective-permute-start.5 = (f32[4,16,512]{2,1,0:T(8,128)}, f32[4,16,512]{2,1,0:T(8,128)S(1)}, u32[]{:S(2)}, u32[]{:S(2)}) collective-permute-start(f32[4,16,512]{2,1,0:T(8,128)} %get-tuple-element.10), channel_id=1, source_target_pairs={{0,2},{2,4},{4,6},{6,8},{8,10},{10,12},{12,14},{1,3},{3,5},{5,7},{... | collective-permute-start | bytes 393224 | tf_op jit(solution)/shard_map/ppermute | solution.py:53
  48.9 3.5 %collective-permute-done.5 = f32[4,16,512]{2,1,0:T(8,128)S(1)} collective-permute-done((f32[4,16,512]{2,1,0:T(8,128)}, f32[4,16,512]{2,1,0:T(8,128)S(1)}, u32[]{:S(2)}, u32[]{:S(2)}) %collective-permute-start.5) | collective-permute-done | bytes 131104 | tf_op jit(solution)/shard_map/ppermute | solution.py:53
  52.4 0.9 %add.23 = f32[4,16,512]{2,1,0:T(8,128)S(1)} add(f32[4,16,512]{2,1,0:T(8,128)} %get-tuple-element.10, f32[4,16,512]{2,1,0:T(8,128)S(1)} %collective-permute-done.5) | non-fusion elementwise | flops 32768 | bytes 393216 | tf_op jit(solution)/shard_map/add | solution.py:53
  53.3 5.3 %collective-permute-start.6 = (f32[4,16,512]{2,1,0:T(8,128)S(1)}, f32[4,16,512]{2,1,0:T(8,128)S(1)}, u32[]{:S(2)}, u32[]{:S(2)}) collective-permute-start(f32[4,16,512]{2,1,0:T(8,128)S(1)} %add.23), channel_id=1, source_target_pairs={{0,4},{2,6},{4,8},{6,10},{8,12},{10,14},{1,5},{3,7},{5,9},{7,11},{... | collective-permute-start | bytes 393224 | tf_op jit(solution)/shard_map/ppermute | solution.py:53
  58.6 2.5 %collective-permute-done.6 = f32[4,16,512]{2,1,0:T(8,128)S(1)} collective-permute-done((f32[4,16,512]{2,1,0:T(8,128)S(1)}, f32[4,16,512]{2,1,0:T(8,128)S(1)}, u32[]{:S(2)}, u32[]{:S(2)}) %collective-permute-start.6) | collective-permute-done | bytes 131104 | tf_op jit(solution)/shard_map/ppermute | solution.py:53
  61.1 5.4 %collective-permute-start.7 = (f32[4,16,512]{2,1,0:T(8,128)S(1)}, f32[4,16,512]{2,1,0:T(8,128)S(1)}, u32[]{:S(2)}, u32[]{:S(2)}) collective-permute-start(f32[4,16,512]{2,1,0:T(8,128)S(1)} %add.24), channel_id=1, source_target_pairs={{0,8},{2,10},{4,12},{6,14},{1,9},{3,11},{5,13},{7,15},{16,24},{18,... | collective-permute-start | bytes 393224 | tf_op jit(solution)/shard_map/ppermute | solution.py:53
  66.5 2.5 %collective-permute-done.7 = f32[4,16,512]{2,1,0:T(8,128)S(1)} collective-permute-done((f32[4,16,512]{2,1,0:T(8,128)S(1)}, f32[4,16,512]{2,1,0:T(8,128)S(1)}, u32[]{:S(2)}, u32[]{:S(2)}) %collective-permute-start.7) | collective-permute-done | bytes 131104 | tf_op jit(solution)/shard_map/ppermute | solution.py:53
  69.0 0.0 copy-done.2
  69.0 0.7 add_bitcast_fusion
  (6 shorter events, 0.2 us)
Async XLA Ops:
  0.6 11.8 %copy-start = (bf16[17,128]{1,0:T(8,128)(2,1)S(1)}, bf16[17,128]{1,0:T(8,128)(2,1)}, u32[]{:S(2)}) copy-start(bf16[17,128]{1,0:T(8,128)(2,1)} %param.15) | copy-start | bytes 13060
  1.6 18.7 %collective-permute-start.3 = (bf16[12,2,512]{2,1,0:T(2,128)(2,1)S(1)}, bf16[12,2,512]{2,1,0:T(2,128)(2,1)S(1)}, u32[]{:S(2)}, u32[]{:S(2)}) collective-permute-start(bf16[12,2,512]{2,1,0:T(2,128)(2,1)S(1)} %broadcast_select_fusion.2), channel_id=1, source_target_pairs={{0,1},{1,0},{2,3},{3,2},{4,5},{5,4},{6,7},{7,6},{8,9},{9,8},{10,11... | collective-permute-start | bytes 73736 | tf_op jit(solution)/shard_map/ppermute | solution.py:282
  3.0 17.3 %collective-permute-start = (f32[4,2,512]{2,1,0:T(2,128)S(1)}, f32[4,2,512]{2,1,0:T(2,128)S(1)}, u32[]{:S(2)}, u32[]{:S(2)}) collective-permute-start(f32[4,2,512]{2,1,0:T(2,128)S(1)} %slice_select_fusion.1), channel_id=1, source_target_pairs={{0,1},{1,0},{2,3},{3,2},{4,5},{5,4},{6,7},{7,6},{8,9},{9,8},{10,11... | collective-permute-start | bytes 49160 | tf_op jit(solution)/shard_map/ppermute | solution.py:281
  3.2 18.4 %collective-permute-start.2 = (f32[1,4,16,512]{3,2,1,0:T(8,128)}, f32[1,4,16,512]{3,2,1,0:T(8,128)S(1)}, u32[]{:S(2)}, u32[]{:S(2)}) collective-permute-start(f32[1,4,16,512]{3,2,1,0:T(8,128)} %param.11), channel_id=1, source_target_pairs={{0,2},{2,4},{4,6},{6,8},{8,10},{10,12},{12,14},{1,3},{3,5},{5,7},{... | collective-permute-start | bytes 393224 | tf_op jit(solution)/shard_map/ppermute | solution.py:19
  8.9 11.4 %collective-permute-start.1 = (f32[4,2,512]{2,1,0:T(2,128)S(1)}, f32[4,2,512]{2,1,0:T(2,128)S(1)}, u32[]{:S(2)}, u32[]{:S(2)}) collective-permute-start(f32[4,2,512]{2,1,0:T(2,128)S(1)} %slice_select_fusion), channel_id=1, source_target_pairs={{0,3},{1,2},{2,5},{3,4},{4,7},{5,6},{6,9},{7,8},{8,11},{9,10},{10,... | collective-permute-start | bytes 49160 | tf_op jit(solution)/shard_map/ppermute | solution.py:280
  21.6 47.4 %copy-start.2 = (f32[4,16,512]{2,1,0:T(8,128)S(1)}, f32[4,16,512]{2,1,0:T(8,128)}, u32[]{:S(2)}) copy-start(f32[4,16,512]{2,1,0:T(8,128)} %param.12) | copy-start | bytes 393220
  22.6 16.9 %copy-start.1 = (f32[4,16,512]{2,1,0:T(8,128)}, f32[4,16,512]{2,1,0:T(8,128)S(1)}, u32[]{:S(2)}) copy-start(f32[4,16,512]{2,1,0:T(8,128)S(1)} %bitcast_select_fusion.refs_6_) | copy-start | bytes 393220
  36.1 2.0 %collective-permute-start.4 = (f32[128,128]{1,0:T(8,128)}, f32[128,128]{1,0:T(8,128)S(1)}, u32[]{:S(2)}, u32[]{:S(2)}) collective-permute-start(f32[128,128]{1,0:T(8,128)} %get-tuple-element.9), channel_id=1, source_target_pairs={{0,1},{1,0},{2,3},{3,2},{4,5},{5,4},{6,7},{7,6},{8,9},{9,8},{10,11... | collective-permute-start | bytes 196616 | tf_op jit(solution)/shard_map/ppermute | solution.py:44
  46.5 5.9 %collective-permute-start.5 = (f32[4,16,512]{2,1,0:T(8,128)}, f32[4,16,512]{2,1,0:T(8,128)S(1)}, u32[]{:S(2)}, u32[]{:S(2)}) collective-permute-start(f32[4,16,512]{2,1,0:T(8,128)} %get-tuple-element.10), channel_id=1, source_target_pairs={{0,2},{2,4},{4,6},{6,8},{8,10},{10,12},{12,14},{1,3},{3,5},{5,7},{... | collective-permute-start | bytes 393224 | tf_op jit(solution)/shard_map/ppermute | solution.py:53
  53.3 7.8 %collective-permute-start.6 = (f32[4,16,512]{2,1,0:T(8,128)S(1)}, f32[4,16,512]{2,1,0:T(8,128)S(1)}, u32[]{:S(2)}, u32[]{:S(2)}) collective-permute-start(f32[4,16,512]{2,1,0:T(8,128)S(1)} %add.23), channel_id=1, source_target_pairs={{0,4},{2,6},{4,8},{6,10},{8,12},{10,14},{1,5},{3,7},{5,9},{7,11},{... | collective-permute-start | bytes 393224 | tf_op jit(solution)/shard_map/ppermute | solution.py:53
  61.1 7.9 %collective-permute-start.7 = (f32[4,16,512]{2,1,0:T(8,128)S(1)}, f32[4,16,512]{2,1,0:T(8,128)S(1)}, u32[]{:S(2)}, u32[]{:S(2)}) collective-permute-start(f32[4,16,512]{2,1,0:T(8,128)S(1)} %add.24), channel_id=1, source_target_pairs={{0,8},{2,10},{4,12},{6,14},{1,9},{3,11},{5,13},{7,15},{16,24},{18,... | collective-permute-start | bytes 393224 | tf_op jit(solution)/shard_map/ppermute | solution.py:53

commit v5 on v4

--- a/solution.py
+++ b/solution.py
@@ -1,4 +1,5 @@
 import jax
+import numpy as np
 import jax.numpy as jnp
 from jax import lax
 from jax.experimental import pallas as pl
@@ -11,6 +12,7 @@
 
 SIGMA_TOP = 8.0
 SIGMA_END = 0.002
+LOG_RATIO = float(np.log(np.float32(SIGMA_END / SIGMA_TOP)))
 
 
 def from_behind(x, axis, by):
@@ -103,22 +105,61 @@
     ).astype(jnp.bfloat16)
 
 
+def step_scalars(levels_ref, level_count, shape):
+    def sigma(k):
+        level = jnp.full(shape, levels_ref[0, k].astype(jnp.float32))
+        fraction = level / jnp.float32(level_count - 1)
+        return SIGMA_TOP * jnp.exp(fraction * LOG_RATIO)
+
+    sigma_low = sigma(0)
+    sigma_high = sigma(1)
+    spread = sigma_low * sigma_low + 0.25
+    return sigma_low, sigma_high, spread
+
+
 def trunk_kernel(
-    band_ref, inputs_ref, lift_ref, embed_ref, first_ref, second_ref, project_ref,
-    hidden_ref, query_ref, stats_ref, act_first, lifted_keep, act_next, *, width, band_rows, bands,
+    levels_ref, previous_ref, start_ref, start_other_ref, iterate_halo_ref, coarse_ref,
+    coarse_other_ref, lift_ref, embed_ref, first_ref, second_ref, project_ref,
+    hidden_ref, query_ref, stats_ref, inputs, act_first, lifted_keep, act_next,
+    *, width, band_rows, bands, level_count,
 ):
-    band = band_ref[0]
+    band = lax.axis_index("rows")
+    first_step = lax.axis_index("step") == 0
     top_outside = band == 0
     bottom_outside = band == bands - 1
+    channels = start_ref.shape[0]
+    sigma_low, _, spread = step_scalars(levels_ref, level_count, (1, width))
+    scale_in = lax.rsqrt(spread)
+    for u in range(band_rows + 2 * HALO):
+        v = u - HALO
+        if 0 <= v < band_rows:
+            state = jnp.where(first_step, start_ref[:, v, :], previous_ref[0, :, v, :])
+            cond = coarse_ref[:, v, :]
+        elif v < 0:
+            state = jnp.where(first_step, start_other_ref[:, band_rows + v, :], iterate_halo_ref[:, v + HALO, :])
+            cond = coarse_other_ref[:, band_rows + v, :]
+        else:
+            state = jnp.where(first_step, start_other_ref[:, v - band_rows, :], iterate_halo_ref[:, v - band_rows, :])
+            cond = coarse_other_ref[:, v - band_rows, :]
+        scaled = (scale_in * state).astype(jnp.bfloat16).astype(jnp.float32)
+        inputs[0:channels, u * width : (u + 1) * width] = scaled
+        inputs[channels:, u * width : (u + 1) * width] = cond.astype(jnp.float32)
+    level = levels_ref[0, 0]
+    table = embed_ref[...].astype(jnp.float32)
+    picked = jnp.where(lax.broadcasted_iota(jnp.int32, table.shape, 0) == level, table, 0.0)
+    embed_row = jnp.sum(picked, axis=0, keepdims=True)
+    feat = table.shape[1]
+    embed = jnp.broadcast_to(embed_row, (feat, feat)).T[:, 0:1]
+    lift_w = transposed(lift_ref[...]).astype(jnp.bfloat16)
+
     span = CHUNK_ROWS * width
     column = lax.broadcasted_iota(jnp.int32, (1, span), 1) % width
     upper_row = lax.broadcasted_iota(jnp.int32, (1, span), 1) < width
-    lift_w = lift_ref[...]
-    embed = embed_ref[...]
     in_rows = band_rows + 2 * HALO
     for q in range(in_rows // CHUNK_ROWS):
         start = q * span
-        lifted = jnp.dot(lift_w, inputs_ref[:, start : start + span], preferred_element_type=jnp.float32)
+        chunk = inputs[:, start : start + span].astype(jnp.bfloat16)
+        lifted = jnp.dot(lift_w, chunk, preferred_element_type=jnp.float32)
         lifted = (lifted + embed).astype(jnp.bfloat16)
         row0 = q * CHUNK_ROWS
         if HALO <= row0 < HALO + band_rows:
@@ -162,7 +203,6 @@
             jnp.dot(row_sum, pool_w, precision=lax.Precision.HIGHEST, preferred_element_type=jnp.float32)
         )
     pooled = jnp.concatenate(pooled, axis=1)
-    feat = pooled.shape[0]
     tokens = normalize_features(pooled).astype(jnp.bfloat16)
     project_t = jnp.concatenate(
         [transposed(project_ref[:, g * feat : (g + 1) * feat]) for g in range(3)], axis=0
@@ -182,24 +222,26 @@
 
 
 def head_kernel(
-    scalar_ref, hidden_ref, query_ref, stats_ref, mix_ref, out_w_ref, current_ref,
-    denoised_ref, drift_ref, *, width, band_rows,
+    levels_ref, hidden_ref, query_ref, stats_own_ref, stats_other_ref, mix_ref, out_w_ref,
+    previous_ref, start_ref, denoised_ref, seed_ref, *, width, band_rows, level_count,
 ):
-    scale_skip = scalar_ref[0]
-    scale_out = scalar_ref[1]
-    sigma_gap = scalar_ref[2]
-    sigma_low = scalar_ref[3]
+    first_step = lax.axis_index("step") == 0
+    sigma_low, sigma_high, spread = step_scalars(levels_ref, level_count, (1, width))
+    scale_skip = 0.25 / spread
+    scale_out = 0.5 * sigma_low * lax.rsqrt(spread)
+    sigma_gap = sigma_high - sigma_low
     feat = query_ref.shape[0]
     contexts = []
     for h in range(feat // HEAD_DIM):
         rows = slice(h * HEAD_DIM, (h + 1) * HEAD_DIM)
         queries_h = query_ref[rows, :]
+        stats_h = stats_own_ref[rows, :] + stats_other_ref[rows, :]
         numerator = jnp.dot(
-            stats_ref[rows, 0:HEAD_DIM], queries_h,
+            stats_h[:, 0:HEAD_DIM], queries_h,
             precision=lax.Precision.HIGHEST, preferred_element_type=jnp.float32,
         )
         denominator = jnp.dot(
-            stats_ref[rows, HEAD_DIM : 2 * HEAD_DIM], queries_h,
+            stats_h[:, HEAD_DIM : 2 * HEAD_DIM], queries_h,
             precision=lax.Precision.HIGHEST, preferred_element_type=jnp.float32,
         )
         contexts.append(numerator / denominator)
@@ -213,10 +255,9 @@
         1.0,
         0.0,
     ).astype(jnp.float32)
-    out_w = out_w_ref[...]
-    channels = current_ref.shape[0]
+    out_w = transposed(out_w_ref[...]).astype(jnp.bfloat16)
     for a in range(band_rows // 4):
-        spread = jnp.dot(
+        spread_mixed = jnp.dot(
             mixed[:, a * tokens_per_row : (a + 1) * tokens_per_row],
             expand,
             precision=lax.Precision.HIGHEST,
@@ -225,13 +266,14 @@
         for u in range(4):
             r = 4 * a + u
             start = r * width
-            combined = hidden_ref[:, start : start + width] + spread
+            combined = hidden_ref[:, start : start + width] + spread_mixed
             act = silu(normalize_features(combined)).astype(jnp.bfloat16)
-            field = jnp.dot(out_w, act, preferred_element_type=jnp.float32)[0:channels]
-            state = current_ref[:, r, :]
+            field = jnp.dot(out_w, act, preferred_element_type=jnp.float32)
+            state = jnp.where(first_step, start_ref[:, r, :], previous_ref[0, :, r, :])
             denoised = scale_skip * state + scale_out * field
             denoised_ref[:, r, :] = denoised
-            drift_ref[:, r, :] = sigma_gap * (state - denoised) / sigma_low
+            drift = sigma_gap * (state - denoised) / sigma_low
+            seed_ref[:, r, :] = drift + jnp.where(first_step, state, 0.0)
 
 
 def vmem():
@@ -247,14 +289,6 @@
     last = lax.slice_in_dim(x, length - width, length, axis=dim)
     leading = lax.slice_in_dim(x, 0, width, axis=dim)
     return jnp.where(lax.axis_index(axis) == 0, last, leading)
-
-
-def place_halo(x, incoming, axis, dim):
-    me = lax.axis_index(axis)
-    zero = jnp.zeros_like(incoming)
-    before = jnp.where(me == 0, zero, incoming)
-    after = jnp.where(me == 0, incoming, zero)
-    return jnp.concatenate([before, x, after], axis=dim)
 
 
 def local(
@@ -273,79 +307,66 @@
     level_count = 2 * lax.axis_size("step") + 1
     bands = lax.axis_size("rows")
     steps = lax.axis_size("step")
-    first_step = lax.axis_index("step") == 0
+    assert bands == 2
+    swap = [(0, 1), (1, 0)]
     previous = from_behind(iterates, "step", 1)
-    if bands == 2:
-        pairs = [(j * 2 + b, (j + 1) * 2 + (1 - b)) for j in range(steps - 1) for b in range(2)]
-        iterate_halo = lax.ppermute(edge_rows(iterates[0], "rows", 1, HALO), ("step", "rows"), pairs)
-        start_halo = lax.ppermute(edge_rows(window_start, "rows", 1, HALO), "rows", [(0, 1), (1, 0)])
-        coarse_halo = lax.ppermute(edge_rows(coarse, "rows", 1, HALO), "rows", [(0, 1), (1, 0)])
-    current = jnp.where(first_step, window_start, previous[0])
-    if bands == 2:
-        current_halo = place_halo(current, jnp.where(first_step, start_halo, iterate_halo), "rows", 1)
-        coarse_halo = place_halo(coarse, coarse_halo, "rows", 1)
-    else:
-        current_halo = with_halo(current, "rows", 1, HALO)
-        coarse_halo = with_halo(coarse, "rows", 1, HALO)
-    levels = step_levels[0]
-    sigmas = noise_level(levels, level_count)
-    sigma_low = sigmas[0]
-    sigma_high = sigmas[1]
-    spread = sigma_low * sigma_low + 0.25
-    scale_in = lax.rsqrt(spread)
-    scale_skip = 0.25 / spread
-    scale_out = 0.5 * sigma_low * lax.rsqrt(spread)
-
-    channels, band_rows, width = current.shape
+    pairs = [(j * 2 + b, (j + 1) * 2 + (1 - b)) for j in range(steps - 1) for b in range(2)]
+    iterate_halo = lax.ppermute(edge_rows(iterates[0], "rows", 1, HALO), ("step", "rows"), pairs)
+    start_other = lax.ppermute(window_start, "rows", swap)
+    coarse_other = lax.ppermute(coarse, "rows", swap)
+
+    channels, band_rows, width = window_start.shape
     feat = lift_weight.shape[1]
-    inputs = jnp.concatenate([(scale_in * current_halo).astype(jnp.bfloat16), coarse_halo], axis=0)
-    inputs = inputs.reshape(inputs.shape[0], -1)
-    picker = (jnp.arange(level_count) == levels[0]).astype(jnp.bfloat16)[None]
-    embed_row = jnp.dot(picker, level_embed, preferred_element_type=jnp.float32)[0]
-    band_index = lax.axis_index("rows").astype(jnp.int32).reshape(1)
-
     pixels = band_rows * width
     tokens = (band_rows // 4) * (width // 4)
     trunk = pl.pallas_call(
-        lambda *refs: trunk_kernel(*refs, width=width, band_rows=band_rows, bands=bands),
+        lambda *refs: trunk_kernel(
+            *refs, width=width, band_rows=band_rows, bands=bands, level_count=level_count
+        ),
         out_shape=(
             jax.ShapeDtypeStruct((feat, pixels), jnp.float32),
             jax.ShapeDtypeStruct((feat, tokens), jnp.float32),
             jax.ShapeDtypeStruct((feat, 2 * HEAD_DIM), jnp.float32),
         ),
-        in_specs=[smem()] + [vmem()] * 6,
+        in_specs=[smem()] + [vmem()] * 11,
         out_specs=(vmem(), vmem(), vmem()),
         scratch_shapes=[
+            pltpu.VMEM((channels + coarse.shape[0], (band_rows + 2 * HALO) * width), jnp.float32),
             pltpu.VMEM((feat, (band_rows + 2 * HALO) * width), jnp.bfloat16),
             pltpu.VMEM((feat, pixels), jnp.bfloat16),
             pltpu.VMEM((feat, (band_rows + 2) * width), jnp.bfloat16),
         ],
     )
     hidden, queries, stats_own = trunk(
-        band_index,
-        inputs,
-        lift_weight.T,
-        embed_row.reshape(feat, 1),
+        step_levels,
+        previous,
+        window_start,
+        start_other,
+        iterate_halo,
+        coarse,
+        coarse_other,
+        lift_weight,
+        level_embed,
         conv_first,
         conv_second,
         project_weight,
     )
-    stats = band_sum(stats_own, "rows")
-
-    out_w = jnp.pad(output_weight.T, ((0, 16 - channels), (0, 0)))
-    scalars = jnp.stack([scale_skip, scale_out, sigma_high - sigma_low, sigma_low]).astype(jnp.float32)
+    stats_other = lax.ppermute(stats_own, "rows", swap)
+
     head = pl.pallas_call(
-        lambda *refs: head_kernel(*refs, width=width, band_rows=band_rows),
+        lambda *refs: head_kernel(*refs, width=width, band_rows=band_rows, level_count=level_count),
         out_shape=(
-            jax.ShapeDtypeStruct(current.shape, jnp.float32),
-            jax.ShapeDtypeStruct(current.shape, jnp.float32),
+            jax.ShapeDtypeStruct(window_start.shape, jnp.float32),
+            jax.ShapeDtypeStruct(window_start.shape, jnp.float32),
         ),
-        in_specs=[smem()] + [vmem()] * 6,
+        in_specs=[smem()] + [vmem()] * 8,
         out_specs=(vmem(), vmem()),
     )
-    denoised, drift_step = head(scalars, hidden, queries, stats, mix_weight, out_w, current)
-    summed = prefix_sum(drift_step, "step")
-    trajectory = window_start + summed
+    denoised, seed = head(
+        step_levels, hidden, queries, stats_own, stats_other, mix_weight, output_weight,
+        previous, window_start,
+    )
+    trajectory = prefix_sum(seed, "step")
     return (trajectory[None], denoised[None])
 
 

time: 70.3 us -> 62.3 us (0.89)
  the two profiles are of different devices: /device:TPU:0 before, /device:TPU:24 now
where the time goes in v5:
time: 62.3 us; the launch traced here: 62 us
  waiting for transfers between devices  24.9 us (40%)
  Pallas kernels  20 us (32%)
  starting transfers between devices  10.5 us (17%)
  local copies, waits for them, and re-layouts  3.39 us (5%)
  other arithmetic  2.5 us (4%)
  between operations  0.71 us (1%)
    ppermute x3, waiting for transfers between devices, prefix_sum(): x = x + lax.ppermute(x, axis, pairs)  20.9 us
    pallas_call x1, Pallas kernels, local(): trunk(step_levels, previous, window_start, start_other, iterate_halo, coa...  13.2 us
    pallas_call x1, Pallas kernels, local(): head(step_levels, hidden, queries, stats_own, stats_other, mix_weight, ou...  6.85 us
    ppermute x3, starting transfers between devices, prefix_sum(): x = x + lax.ppermute(x, axis, pairs)  4.49 us
    ppermute x1, waiting for transfers between devices, local(): lax.ppermute(edge_rows(iterates[0], 'rows', 1, HALO), ('step', 'rows'), p...  4.03 us
    ppermute x1, starting transfers between devices, from_behind(): return lax.ppermute(x, axis, pairs)  3.4 us
    unnamed x11, local copies, waits for them, and re-layouts  3.39 us
    ppermute x1, starting transfers between devices, local(): lax.ppermute(edge_rows(iterates[0], 'rows', 1, HALO), ('step', 'rows'), p...  1.92 us
  transfers between devices with their start and end apart: 8, of which 4 were waited for; matrix products, arithmetic and copies ran while one was open for 4% of the time, Pallas kernels for 0%

profile of v5, /device:TPU:24, one launch (start us, length us, event | category | flops | bytes accessed | tf_op | source)
XLA Modules:
  0.0 62.0 jit_solution(2488338125498733136)
XLA Ops:
  0.6 3.4 %collective-permute-start = (f32[1,4,16,512]{3,2,1,0:T(8,128)}, f32[1,4,16,512]{3,2,1,0:T(8,128)S(1)}, u32[]{:S(2)}, u32[]{:S(2)}) collective-permute-start(f32[1,4,16,512]{3,2,1,0:T(8,128)} %param.11), channel_id=1, source_target_pairs={{0,2},{2,4},{4,6},{6,8},{8,10},{10,12},{12,14},{1,3},{3,5},{5,7},{... | collective-permute-start | bytes 393224 | tf_op jit(solution)/shard_map/ppermute | solution.py:21
  4.0 0.1 collective-permute-start.3
  4.1 0.5 collective-permute-start.1
  4.6 0.9 %slice_select_fusion = f32[4,2,512]{2,1,0:T(2,128)S(1)} fusion(f32[4,16,512]{2,1,0:T(8,128)} %bitcast.4, pred[]{:T(512)S(6)} %eq.3), kind=kLoop, calls=%fused_computation.1 | loop fusion | flops 4096 | bytes 49153 | tf_op jit(solution)/shard_map/jit(_where)/select_n | solution.py:291
  5.5 1.9 %collective-permute-start.2 = (f32[4,2,512]{2,1,0:T(2,128)S(1)}, f32[4,2,512]{2,1,0:T(2,128)S(1)}, u32[]{:S(2)}, u32[]{:S(2)}) collective-permute-start(f32[4,2,512]{2,1,0:T(2,128)S(1)} %slice_select_fusion), channel_id=1, source_target_pairs={{0,3},{1,2},{2,5},{3,4},{4,7},{5,6},{6,9},{7,8},{8,11},{9,10},{10,... | collective-permute-start | bytes 49160 | tf_op jit(solution)/shard_map/ppermute | solution.py:314
  7.4 4.0 %collective-permute-done.2.refs_4_ = f32[4,2,512]{2,1,0:T(2,128)S(1)} collective-permute-done((f32[4,2,512]{2,1,0:T(2,128)S(1)}, f32[4,2,512]{2,1,0:T(2,128)S(1)}, u32[]{:S(2)}, u32[]{:S(2)}) %collective-permute-start.2) | collective-permute-done | bytes 16416 | tf_op jit(solution)/shard_map/ppermute | solution.py:314
  11.5 0.0 copy-start.4
  11.5 0.0 collective-permute-done.refs_1_.refs_7_
  11.5 0.0 copy-start
  11.5 0.0 collective-permute-done.1.refs_3_
  11.5 0.0 copy-start.2
  11.5 0.0 collective-permute-done.3.refs_6_
  11.5 0.6 copy-done.4
  12.1 0.1 copy-done
  12.1 0.0 copy-done.2
  12.2 0.0 copy-start.1
  12.2 0.7 %copy-done.1 = bf16[12,16,512]{2,1,0:T(8,128)(2,1)} copy-done((bf16[12,16,512]{2,1,0:T(8,128)(2,1)}, bf16[12,16,512]{2,1,0:T(8,128)(2,1)S(1)}, u32[]{:S(2)}) %copy-start.1) | copy-done | bytes 196632
  12.8 13.2 %shard_map.122 = (f32[128,8192]{1,0:T(8,128)}, f32[128,512]{1,0:T(8,128)}, f32[128,128]{1,0:T(8,128)}) custom-call(s32[1,2]{1,0:T(1,128)} %refs_0_.3, f32[1,4,16,512]{3,2,1,0:T(8,128)} %copy-done, f32[4,16,512]{2,1,0:T(8,128)} %refs_8_.3, f32[4,16,512]{2,1,0:T(8,128)} %copy-done.2, f32[4,2,512]{2,1,0:T(2,128)} %copy-done.4, bf16[12,16,512]{2,1,0:T(8,128)(2,1)} %refs_5_.2, ...), custom_call_target="tpu_custom_call" | custom-call | tf_op jit(solution)/shard_map/pallas_call | solution.py:340
  26.0 0.1 collective-permute-start.4
  26.1 1.4 %copy.13.refs_6_ = bf16[128,4]{1,0:T(8,128)(2,1)} copy(bf16[128,4]{0,1:T(4,128)(2,1)} %param.21) | data formatting | bytes 2048 | tf_op args[10]
  27.5 0.0 collective-permute-done.4.refs_4_
  27.5 0.0 copy-start.3
  27.5 0.6 %copy-done.3 = f32[128,128]{1,0:T(8,128)} copy-done((f32[128,128]{1,0:T(8,128)}, f32[128,128]{1,0:T(8,128)S(1)}, u32[]{:S(2)}) %copy-start.3) | copy-done | bytes 65560
  28.2 6.8 %shard_map.123 = (f32[4,16,512]{2,1,0:T(8,128)}, f32[4,16,512]{2,1,0:T(8,128)}) custom-call(s32[1,2]{1,0:T(1,128)} %refs_0_.3, f32[128,8192]{1,0:T(8,128)} %get-tuple-element.7.refs_1_, f32[128,512]{1,0:T(8,128)} %get-tuple-element.8.refs_2_, f32[128,128]{1,0:T(8,128)} %get-tuple-element.9.refs_3_, f32[128,128]{1,0:T(8,128)} %copy-done.3, ...), custom_call_target="tpu_custom_call" | custom-call | tf_op jit(solution)/shard_map/pallas_call | solution.py:365
  35.0 1.9 %collective-permute-start.5 = (f32[4,16,512]{2,1,0:T(8,128)}, f32[4,16,512]{2,1,0:T(8,128)S(1)}, u32[]{:S(2)}, u32[]{:S(2)}) collective-permute-start(f32[4,16,512]{2,1,0:T(8,128)} %get-tuple-element.10), channel_id=1, source_target_pairs={{0,2},{2,4},{4,6},{6,8},{8,10},{10,12},{12,14},{1,3},{3,5},{5,7},{... | collective-permute-start | bytes 393224 | tf_op jit(solution)/shard_map/ppermute | solution.py:55
  36.9 6.9 %collective-permute-done.5 = f32[4,16,512]{2,1,0:T(8,128)S(1)} collective-permute-done((f32[4,16,512]{2,1,0:T(8,128)}, f32[4,16,512]{2,1,0:T(8,128)S(1)}, u32[]{:S(2)}, u32[]{:S(2)}) %collective-permute-start.5) | collective-permute-done | bytes 131104 | tf_op jit(solution)/shard_map/ppermute | solution.py:55
  43.8 0.9 %add.9 = f32[4,16,512]{2,1,0:T(8,128)S(1)} add(f32[4,16,512]{2,1,0:T(8,128)} %get-tuple-element.10, f32[4,16,512]{2,1,0:T(8,128)S(1)} %collective-permute-done.5) | non-fusion elementwise | flops 32768 | bytes 393216 | tf_op jit(solution)/shard_map/add | solution.py:55
  44.8 1.3 %collective-permute-start.6 = (f32[4,16,512]{2,1,0:T(8,128)S(1)}, f32[4,16,512]{2,1,0:T(8,128)S(1)}, u32[]{:S(2)}, u32[]{:S(2)}) collective-permute-start(f32[4,16,512]{2,1,0:T(8,128)S(1)} %add.9), channel_id=1, source_target_pairs={{0,4},{2,6},{4,8},{6,10},{8,12},{10,14},{1,5},{3,7},{5,9},{7,11},{... | collective-permute-start | bytes 393224 | tf_op jit(solution)/shard_map/ppermute | solution.py:55
  46.1 5.6 %collective-permute-done.6 = f32[4,16,512]{2,1,0:T(8,128)S(1)} collective-permute-done((f32[4,16,512]{2,1,0:T(8,128)S(1)}, f32[4,16,512]{2,1,0:T(8,128)S(1)}, u32[]{:S(2)}, u32[]{:S(2)}) %collective-permute-start.6) | collective-permute-done | bytes 131104 | tf_op jit(solution)/shard_map/ppermute | solution.py:55
  51.7 1.3 %collective-permute-start.7 = (f32[4,16,512]{2,1,0:T(8,128)S(1)}, f32[4,16,512]{2,1,0:T(8,128)S(1)}, u32[]{:S(2)}, u32[]{:S(2)}) collective-permute-start(f32[4,16,512]{2,1,0:T(8,128)S(1)} %add.10), channel_id=1, source_target_pairs={{0,8},{2,10},{4,12},{6,14},{1,9},{3,11},{5,13},{7,15},{16,24},{18,... | collective-permute-start | bytes 393224 | tf_op jit(solution)/shard_map/ppermute | solution.py:55
  53.0 8.3 %collective-permute-done.7 = f32[4,16,512]{2,1,0:T(8,128)S(1)} collective-permute-done((f32[4,16,512]{2,1,0:T(8,128)S(1)}, f32[4,16,512]{2,1,0:T(8,128)S(1)}, u32[]{:S(2)}, u32[]{:S(2)}) %collective-permute-start.7) | collective-permute-done | bytes 131104 | tf_op jit(solution)/shard_map/ppermute | solution.py:55
  61.3 0.7 %add_bitcast_fusion = f32[1,4,16,512]{3,2,1,0:T(8,128)} fusion(f32[4,16,512]{2,1,0:T(8,128)S(1)} %add.10, f32[4,16,512]{2,1,0:T(8,128)S(1)} %collective-permute-done.7), kind=kLoop, calls=%fused_computation | loop fusion | flops 32768 | bytes 393216 | tf_op jit(solution)/shard_map/broadcast_in_dim | solution.py:370
  (1 shorter events, 0.0 us)
Async XLA Ops:
  0.6 10.8 %collective-permute-start = (f32[1,4,16,512]{3,2,1,0:T(8,128)}, f32[1,4,16,512]{3,2,1,0:T(8,128)S(1)}, u32[]{:S(2)}, u32[]{:S(2)}) collective-permute-start(f32[1,4,16,512]{3,2,1,0:T(8,128)} %param.11), channel_id=1, source_target_pairs={{0,2},{2,4},{4,6},{6,8},{8,10},{10,12},{12,14},{1,3},{3,5},{5,7},{... | collective-permute-start | bytes 393224 | tf_op jit(solution)/shard_map/ppermute | solution.py:21
  4.0 7.4 %collective-permute-start.3 = (bf16[12,16,512]{2,1,0:T(8,128)(2,1)}, bf16[12,16,512]{2,1,0:T(8,128)(2,1)S(1)}, u32[]{:S(2)}, u32[]{:S(2)}) collective-permute-start(bf16[12,16,512]{2,1,0:T(8,128)(2,1)} %refs_5_.2), channel_id=1, source_target_pairs={{0,1},{1,0},{2,3},{3,2},{4,5},{5,4},{6,7},{7,6},{8,9},{9,8},{10,11... | collective-permute-start | bytes 589832 | tf_op jit(solution)/shard_map/ppermute | solution.py:316
  4.1 7.3 %collective-permute-start.1 = (f32[4,16,512]{2,1,0:T(8,128)}, f32[4,16,512]{2,1,0:T(8,128)S(1)}, u32[]{:S(2)}, u32[]{:S(2)}) collective-permute-start(f32[4,16,512]{2,1,0:T(8,128)} %refs_8_.3), channel_id=1, source_target_pairs={{0,1},{1,0},{2,3},{3,2},{4,5},{5,4},{6,7},{7,6},{8,9},{9,8},{10,11... | collective-permute-start | bytes 393224 | tf_op jit(solution)/shard_map/ppermute | solution.py:315
  5.5 6.0 %collective-permute-start.2 = (f32[4,2,512]{2,1,0:T(2,128)S(1)}, f32[4,2,512]{2,1,0:T(2,128)S(1)}, u32[]{:S(2)}, u32[]{:S(2)}) collective-permute-start(f32[4,2,512]{2,1,0:T(2,128)S(1)} %slice_select_fusion), channel_id=1, source_target_pairs={{0,3},{1,2},{2,5},{3,4},{4,7},{5,6},{6,9},{7,8},{8,11},{9,10},{10,... | collective-permute-start | bytes 49160 | tf_op jit(solution)/shard_map/ppermute | solution.py:314
  11.5 0.6 copy-start.4
  11.5 0.7 %copy-start = (f32[1,4,16,512]{3,2,1,0:T(8,128)}, f32[1,4,16,512]{3,2,1,0:T(8,128)S(1)}, u32[]{:S(2)}) copy-start(f32[1,4,16,512]{3,2,1,0:T(8,128)S(1)} %collective-permute-done.refs_1_.refs_7_) | copy-start | bytes 393220
  11.5 0.7 %copy-start.2 = (f32[4,16,512]{2,1,0:T(8,128)}, f32[4,16,512]{2,1,0:T(8,128)S(1)}, u32[]{:S(2)}) copy-start(f32[4,16,512]{2,1,0:T(8,128)S(1)} %collective-permute-done.1.refs_3_) | copy-start | bytes 393220
  12.2 0.7 %copy-start.1 = (bf16[12,16,512]{2,1,0:T(8,128)(2,1)}, bf16[12,16,512]{2,1,0:T(8,128)(2,1)S(1)}, u32[]{:S(2)}) copy-start(bf16[12,16,512]{2,1,0:T(8,128)(2,1)S(1)} %collective-permute-done.3.refs_6_) | copy-start | bytes 589828
  26.0 1.5 %collective-permute-start.4 = (f32[128,128]{1,0:T(8,128)}, f32[128,128]{1,0:T(8,128)S(1)}, u32[]{:S(2)}, u32[]{:S(2)}) collective-permute-start(f32[128,128]{1,0:T(8,128)} %get-tuple-element.9.refs_3_), channel_id=1, source_target_pairs={{0,1},{1,0},{2,3},{3,2},{4,5},{5,4},{6,7},{7,6},{8,9},{9,8},{10,11... | collective-permute-start | bytes 196616 | tf_op jit(solution)/shard_map/ppermute | solution.py:354
  27.5 0.6 %copy-start.3 = (f32[128,128]{1,0:T(8,128)}, f32[128,128]{1,0:T(8,128)S(1)}, u32[]{:S(2)}) copy-start(f32[128,128]{1,0:T(8,128)S(1)} %collective-permute-done.4.refs_4_) | copy-start | bytes 196612
  35.0 8.8 %collective-permute-start.5 = (f32[4,16,512]{2,1,0:T(8,128)}, f32[4,16,512]{2,1,0:T(8,128)S(1)}, u32[]{:S(2)}, u32[]{:S(2)}) collective-permute-start(f32[4,16,512]{2,1,0:T(8,128)} %get-tuple-element.10), channel_id=1, source_target_pairs={{0,2},{2,4},{4,6},{6,8},{8,10},{10,12},{12,14},{1,3},{3,5},{5,7},{... | collective-permute-start | bytes 393224 | tf_op jit(solution)/shard_map/ppermute | solution.py:55
  44.8 6.9 %collective-permute-start.6 = (f32[4,16,512]{2,1,0:T(8,128)S(1)}, f32[4,16,512]{2,1,0:T(8,128)S(1)}, u32[]{:S(2)}, u32[]{:S(2)}) collective-permute-start(f32[4,16,512]{2,1,0:T(8,128)S(1)} %add.9), channel_id=1, source_target_pairs={{0,4},{2,6},{4,8},{6,10},{8,12},{10,14},{1,5},{3,7},{5,9},{7,11},{... | collective-permute-start | bytes 393224 | tf_op jit(solution)/shard_map/ppermute | solution.py:55
  51.7 9.6 %collective-permute-start.7 = (f32[4,16,512]{2,1,0:T(8,128)S(1)}, f32[4,16,512]{2,1,0:T(8,128)S(1)}, u32[]{:S(2)}, u32[]{:S(2)}) collective-permute-start(f32[4,16,512]{2,1,0:T(8,128)S(1)} %add.10), channel_id=1, source_target_pairs={{0,8},{2,10},{4,12},{6,14},{1,9},{3,11},{5,13},{7,15},{16,24},{18,... | collective-permute-start | bytes 393224 | tf_op jit(solution)/shard_map/ppermute | solution.py:55

commit v6 on v5

--- a/solution.py
+++ b/solution.py
@@ -9,6 +9,7 @@
 HEAD_DIM = 64
 HALO = 2
 CHUNK_ROWS = 2
+CONV_ROWS = 4
 
 SIGMA_TOP = 8.0
 SIGMA_END = 0.002
@@ -91,6 +92,15 @@
     return result
 
 
+def row_chunks(rows):
+    chunks, first = [], 0
+    while first < rows:
+        size = min(CONV_ROWS, rows - first)
+        chunks.append((first, size))
+        first += size
+    return chunks
+
+
 def transposed(block):
     return block.astype(jnp.float32).T
 
@@ -118,7 +128,7 @@
 
 
 def trunk_kernel(
-    levels_ref, previous_ref, start_ref, start_other_ref, iterate_halo_ref, coarse_ref,
+    levels_ref, previous_ref, start_ref, start_other_ref, previous_other_ref, coarse_ref,
     coarse_other_ref, lift_ref, embed_ref, first_ref, second_ref, project_ref,
     hidden_ref, query_ref, stats_ref, inputs, act_first, lifted_keep, act_next,
     *, width, band_rows, bands, level_count,
@@ -136,10 +146,10 @@
             state = jnp.where(first_step, start_ref[:, v, :], previous_ref[0, :, v, :])
             cond = coarse_ref[:, v, :]
         elif v < 0:
-            state = jnp.where(first_step, start_other_ref[:, band_rows + v, :], iterate_halo_ref[:, v + HALO, :])
+            state = jnp.where(first_step, start_other_ref[:, band_rows + v, :], previous_other_ref[0, :, band_rows + v, :])
             cond = coarse_other_ref[:, band_rows + v, :]
         else:
-            state = jnp.where(first_step, start_other_ref[:, v - band_rows, :], iterate_halo_ref[:, v - band_rows, :])
+            state = jnp.where(first_step, start_other_ref[:, v - band_rows, :], previous_other_ref[0, :, v - band_rows, :])
             cond = coarse_other_ref[:, v - band_rows, :]
         scaled = (scale_in * state).astype(jnp.bfloat16).astype(jnp.float32)
         inputs[0:channels, u * width : (u + 1) * width] = scaled
@@ -153,8 +163,6 @@
     lift_w = transposed(lift_ref[...]).astype(jnp.bfloat16)
 
     span = CHUNK_ROWS * width
-    column = lax.broadcasted_iota(jnp.int32, (1, span), 1) % width
-    upper_row = lax.broadcasted_iota(jnp.int32, (1, span), 1) < width
     in_rows = band_rows + 2 * HALO
     for q in range(in_rows // CHUNK_ROWS):
         start = q * span
@@ -173,19 +181,23 @@
         act_first[:, start : start + span] = act.astype(jnp.bfloat16)
     first_w = stack_taps(first_ref)
     mid_rows = band_rows + 2
-    for q in range(mid_rows // CHUNK_ROWS):
-        start = q * span
-        middle = conv_chunk(act_first, first_w, q * CHUNK_ROWS, CHUNK_ROWS, width, column)
+    chunks = row_chunks(mid_rows)
+    for q, (first, rows) in enumerate(chunks):
+        span = rows * width
+        lanes = lax.broadcasted_iota(jnp.int32, (1, span), 1)
+        middle = conv_chunk(act_first, first_w, first, rows, width, lanes % width)
         act = silu(normalize_features(middle))
         if q == 0:
-            act = jnp.where(jnp.logical_and(top_outside, upper_row), 0.0, act)
-        if q == mid_rows // CHUNK_ROWS - 1:
-            act = jnp.where(jnp.logical_and(bottom_outside, jnp.logical_not(upper_row)), 0.0, act)
-        act_next[:, start : start + span] = act.astype(jnp.bfloat16)
+            act = jnp.where(jnp.logical_and(top_outside, lanes < width), 0.0, act)
+        if q == len(chunks) - 1:
+            act = jnp.where(jnp.logical_and(bottom_outside, lanes >= span - width), 0.0, act)
+        act_next[:, first * width : first * width + span] = act.astype(jnp.bfloat16)
     second_w = stack_taps(second_ref)
-    for q in range(band_rows // CHUNK_ROWS):
-        start = q * span
-        conv = conv_chunk(act_next, second_w, q * CHUNK_ROWS, CHUNK_ROWS, width, column)
+    for first, rows in row_chunks(band_rows):
+        span = rows * width
+        lanes = lax.broadcasted_iota(jnp.int32, (1, span), 1)
+        conv = conv_chunk(act_next, second_w, first, rows, width, lanes % width)
+        start = first * width
         hidden_ref[:, start : start + span] = lifted_keep[:, start : start + span].astype(jnp.float32) + conv
     tokens_per_row = width // 4
     pool_w = jnp.where(
@@ -255,7 +267,7 @@
         1.0,
         0.0,
     ).astype(jnp.float32)
-    out_w = transposed(out_w_ref[...]).astype(jnp.bfloat16)
+    out_w = out_w_ref[...]
     for a in range(band_rows // 4):
         spread_mixed = jnp.dot(
             mixed[:, a * tokens_per_row : (a + 1) * tokens_per_row],
@@ -310,8 +322,7 @@
     assert bands == 2
     swap = [(0, 1), (1, 0)]
     previous = from_behind(iterates, "step", 1)
-    pairs = [(j * 2 + b, (j + 1) * 2 + (1 - b)) for j in range(steps - 1) for b in range(2)]
-    iterate_halo = lax.ppermute(edge_rows(iterates[0], "rows", 1, HALO), ("step", "rows"), pairs)
+    previous_other = lax.ppermute(previous, "rows", swap)
     start_other = lax.ppermute(window_start, "rows", swap)
     coarse_other = lax.ppermute(coarse, "rows", swap)
 
@@ -342,7 +353,7 @@
         previous,
         window_start,
         start_other,
-        iterate_halo,
+        previous_other,
         coarse,
         coarse_other,
         lift_weight,
@@ -363,7 +374,7 @@
         out_specs=(vmem(), vmem()),
     )
     denoised, seed = head(
-        step_levels, hidden, queries, stats_own, stats_other, mix_weight, output_weight,
+        step_levels, hidden, queries, stats_own, stats_other, mix_weight, output_weight.T,
         previous, window_start,
     )
     trajectory = prefix_sum(seed, "step")

time: 62.3 us -> 59.5 us (0.955)
  the two profiles are of different devices: /device:TPU:24 before, /device:TPU:0 now
where the time goes in v6:
time: 59.5 us; the launch traced here: 58.6 us
  starting transfers between devices  21.4 us (36%)
  Pallas kernels  20.2 us (34%)
  waiting for transfers between devices  13.5 us (23%)
  other arithmetic  1.62 us (3%)
  local copies, waits for them, and re-layouts  1.28 us (2%)
  between operations  0.72 us (1%)
    ppermute x3, starting transfers between devices, prefix_sum(): x = x + lax.ppermute(x, axis, pairs)  15.8 us
    pallas_call x1, Pallas kernels, local(): trunk(step_levels, previous, window_start, start_other, previous_other, c...  13.1 us
    ppermute x3, waiting for transfers between devices, prefix_sum(): x = x + lax.ppermute(x, axis, pairs)  8.36 us
    pallas_call x1, Pallas kernels, local(): head(step_levels, hidden, queries, stats_own, stats_other, mix_weight, ou...  7.02 us
    ppermute x1, starting transfers between devices, from_behind(): return lax.ppermute(x, axis, pairs)  4.85 us
    ppermute x1, waiting for transfers between devices, from_behind(): return lax.ppermute(x, axis, pairs)  2.47 us
    ppermute x1, waiting for transfers between devices, local(): stats_other = lax.ppermute(stats_own, 'rows', swap)  1.32 us
    ppermute x1, waiting for transfers between devices, local(): previous_other = lax.ppermute(previous, 'rows', swap)  1.31 us
  transfers between devices with their start and end apart: 8, of which 6 were waited for; matrix products, arithmetic and copies ran while one was open for 0% of the time, Pallas kernels for 0%

profile of v6, /device:TPU:0, one launch (start us, length us, event | category | flops | bytes accessed | tf_op | source)
XLA Modules:
  0.0 58.6 jit_solution(3994649181187507480)
XLA Ops:
  0.6 4.8 %collective-permute-start = (f32[1,4,16,512]{3,2,1,0:T(8,128)}, f32[1,4,16,512]{3,2,1,0:T(8,128)S(1)}, u32[]{:S(2)}, u32[]{:S(2)}) collective-permute-start(f32[1,4,16,512]{3,2,1,0:T(8,128)} %param.11), channel_id=1, source_target_pairs={{0,2},{2,4},{4,6},{6,8},{8,10},{10,12},{12,14},{1,3},{3,5},{5,7},{... | collective-permute-start | bytes 393224 | tf_op jit(solution)/shard_map/ppermute | solution.py:22
  5.5 0.1 collective-permute-start.3
  5.6 0.5 collective-permute-start.1
  6.1 2.5 %collective-permute-done.refs_1_.refs_7_ = f32[1,4,16,512]{3,2,1,0:T(8,128)S(1)} collective-permute-done((f32[1,4,16,512]{3,2,1,0:T(8,128)}, f32[1,4,16,512]{3,2,1,0:T(8,128)S(1)}, u32[]{:S(2)}, u32[]{:S(2)}) %collective-permute-start) | collective-permute-done | bytes 131104 | tf_op jit(solution)/shard_map/ppermute | solution.py:22
  8.5 0.0 copy-start
  8.5 0.0 collective-permute-start.2
  8.5 0.0 collective-permute-done.1.refs_3_
  8.5 0.0 copy-start.2
  8.6 0.0 collective-permute-done.3.refs_6_
  8.6 0.0 copy-start.1
  8.6 1.3 %collective-permute-done.2.refs_4_ = f32[1,4,16,512]{3,2,1,0:T(8,128)S(1)} collective-permute-done((f32[1,4,16,512]{3,2,1,0:T(8,128)S(1)}, f32[1,4,16,512]{3,2,1,0:T(8,128)S(1)}, u32[]{:S(2)}, u32[]{:S(2)}) %collective-permute-start.2) | collective-permute-done | bytes 131104 | tf_op jit(solution)/shard_map/ppermute | solution.py:325
  9.9 0.0 copy-done
  9.9 0.0 copy-done.2
  9.9 0.0 copy-done.1
  9.9 0.0 copy-start.3
  9.9 0.6 %copy-done.3 = f32[1,4,16,512]{3,2,1,0:T(8,128)} copy-done((f32[1,4,16,512]{3,2,1,0:T(8,128)}, f32[1,4,16,512]{3,2,1,0:T(8,128)S(1)}, u32[]{:S(2)}) %copy-start.3) | copy-done | bytes 131096
  10.5 13.1 %shard_map.122 = (f32[128,8192]{1,0:T(8,128)}, f32[128,512]{1,0:T(8,128)}, f32[128,128]{1,0:T(8,128)}) custom-call(s32[1,2]{1,0:T(1,128)} %refs_0_.3, f32[1,4,16,512]{3,2,1,0:T(8,128)} %copy-done, f32[4,16,512]{2,1,0:T(8,128)} %refs_8_.3, f32[4,16,512]{2,1,0:T(8,128)} %copy-done.2, f32[1,4,16,512]{3,2,1,0:T(8,128)} %copy-done.3, ...), custom_call_target="tpu_custom_call" | custom-call | tf_op jit(solution)/shard_map/pallas_call | solution.py:351
  23.7 0.1 collective-permute-start.4
  23.8 1.3 %collective-permute-done.4.refs_4_ = f32[128,128]{1,0:T(8,128)S(1)} collective-permute-done((f32[128,128]{1,0:T(8,128)}, f32[128,128]{1,0:T(8,128)S(1)}, u32[]{:S(2)}, u32[]{:S(2)}) %collective-permute-start.4) | collective-permute-done | bytes 65568 | tf_op jit(solution)/shard_map/ppermute | solution.py:365
  25.2 0.0 copy-start.4
  25.2 0.6 %copy-done.4 = f32[128,128]{1,0:T(8,128)} copy-done((f32[128,128]{1,0:T(8,128)}, f32[128,128]{1,0:T(8,128)S(1)}, u32[]{:S(2)}) %copy-start.4) | copy-done | bytes 65560
  25.8 7.0 %shard_map.123 = (f32[4,16,512]{2,1,0:T(8,128)}, f32[4,16,512]{2,1,0:T(8,128)}) custom-call(s32[1,2]{1,0:T(1,128)} %refs_0_.3, f32[128,8192]{1,0:T(8,128)} %get-tuple-element.7.refs_1_, f32[128,512]{1,0:T(8,128)} %get-tuple-element.8.refs_2_, f32[128,128]{1,0:T(8,128)} %get-tuple-element.9.refs_3_, f32[128,128]{1,0:T(8,128)} %copy-done.4, ...), custom_call_target="tpu_custom_call" | custom-call | tf_op jit(solution)/shard_map/pallas_call | solution.py:376
  32.8 4.3 %collective-permute-start.5 = (f32[4,16,512]{2,1,0:T(8,128)}, f32[4,16,512]{2,1,0:T(8,128)S(1)}, u32[]{:S(2)}, u32[]{:S(2)}) collective-permute-start(f32[4,16,512]{2,1,0:T(8,128)} %get-tuple-element.10), channel_id=1, source_target_pairs={{0,2},{2,4},{4,6},{6,8},{8,10},{10,12},{12,14},{1,3},{3,5},{5,7},{... | collective-permute-start | bytes 393224 | tf_op jit(solution)/shard_map/ppermute | solution.py:56
  37.1 3.4 %collective-permute-done.5 = f32[4,16,512]{2,1,0:T(8,128)S(1)} collective-permute-done((f32[4,16,512]{2,1,0:T(8,128)}, f32[4,16,512]{2,1,0:T(8,128)S(1)}, u32[]{:S(2)}, u32[]{:S(2)}) %collective-permute-start.5) | collective-permute-done | bytes 131104 | tf_op jit(solution)/shard_map/ppermute | solution.py:56
  40.5 0.9 %add.9 = f32[4,16,512]{2,1,0:T(8,128)S(1)} add(f32[4,16,512]{2,1,0:T(8,128)} %get-tuple-element.10, f32[4,16,512]{2,1,0:T(8,128)S(1)} %collective-permute-done.5) | non-fusion elementwise | flops 32768 | bytes 393216 | tf_op jit(solution)/shard_map/add | solution.py:56
  41.4 6.2 %collective-permute-start.6 = (f32[4,16,512]{2,1,0:T(8,128)S(1)}, f32[4,16,512]{2,1,0:T(8,128)S(1)}, u32[]{:S(2)}, u32[]{:S(2)}) collective-permute-start(f32[4,16,512]{2,1,0:T(8,128)S(1)} %add.9), channel_id=1, source_target_pairs={{0,4},{2,6},{4,8},{6,10},{8,12},{10,14},{1,5},{3,7},{5,9},{7,11},{... | collective-permute-start | bytes 393224 | tf_op jit(solution)/shard_map/ppermute | solution.py:56
  47.6 2.5 %collective-permute-done.6 = f32[4,16,512]{2,1,0:T(8,128)S(1)} collective-permute-done((f32[4,16,512]{2,1,0:T(8,128)S(1)}, f32[4,16,512]{2,1,0:T(8,128)S(1)}, u32[]{:S(2)}, u32[]{:S(2)}) %collective-permute-start.6) | collective-permute-done | bytes 131104 | tf_op jit(solution)/shard_map/ppermute | solution.py:56
  50.1 5.4 %collective-permute-start.7 = (f32[4,16,512]{2,1,0:T(8,128)S(1)}, f32[4,16,512]{2,1,0:T(8,128)S(1)}, u32[]{:S(2)}, u32[]{:S(2)}) collective-permute-start(f32[4,16,512]{2,1,0:T(8,128)S(1)} %add.10), channel_id=1, source_target_pairs={{0,8},{2,10},{4,12},{6,14},{1,9},{3,11},{5,13},{7,15},{16,24},{18,... | collective-permute-start | bytes 393224 | tf_op jit(solution)/shard_map/ppermute | solution.py:56
  55.5 2.5 %collective-permute-done.7 = f32[4,16,512]{2,1,0:T(8,128)S(1)} collective-permute-done((f32[4,16,512]{2,1,0:T(8,128)S(1)}, f32[4,16,512]{2,1,0:T(8,128)S(1)}, u32[]{:S(2)}, u32[]{:S(2)}) %collective-permute-start.7) | collective-permute-done | bytes 131104 | tf_op jit(solution)/shard_map/ppermute | solution.py:56
  58.0 0.7 %add_bitcast_fusion = f32[1,4,16,512]{3,2,1,0:T(8,128)} fusion(f32[4,16,512]{2,1,0:T(8,128)S(1)} %add.10, f32[4,16,512]{2,1,0:T(8,128)S(1)} %collective-permute-done.7), kind=kLoop, calls=%fused_computation | loop fusion | flops 32768 | bytes 393216 | tf_op jit(solution)/shard_map/broadcast_in_dim | solution.py:381
  (1 shorter events, 0.0 us)
Async XLA Ops:
  0.6 7.9 %collective-permute-start = (f32[1,4,16,512]{3,2,1,0:T(8,128)}, f32[1,4,16,512]{3,2,1,0:T(8,128)S(1)}, u32[]{:S(2)}, u32[]{:S(2)}) collective-permute-start(f32[1,4,16,512]{3,2,1,0:T(8,128)} %param.11), channel_id=1, source_target_pairs={{0,2},{2,4},{4,6},{6,8},{8,10},{10,12},{12,14},{1,3},{3,5},{5,7},{... | collective-permute-start | bytes 393224 | tf_op jit(solution)/shard_map/ppermute | solution.py:22
  5.5 3.1 %collective-permute-start.3 = (bf16[12,16,512]{2,1,0:T(8,128)(2,1)}, bf16[12,16,512]{2,1,0:T(8,128)(2,1)S(1)}, u32[]{:S(2)}, u32[]{:S(2)}) collective-permute-start(bf16[12,16,512]{2,1,0:T(8,128)(2,1)} %refs_5_.2), channel_id=1, source_target_pairs={{0,1},{1,0},{2,3},{3,2},{4,5},{5,4},{6,7},{7,6},{8,9},{9,8},{10,11... | collective-permute-start | bytes 589832 | tf_op jit(solution)/shard_map/ppermute | solution.py:327
  5.6 3.0 %collective-permute-start.1 = (f32[4,16,512]{2,1,0:T(8,128)}, f32[4,16,512]{2,1,0:T(8,128)S(1)}, u32[]{:S(2)}, u32[]{:S(2)}) collective-permute-start(f32[4,16,512]{2,1,0:T(8,128)} %refs_8_.3), channel_id=1, source_target_pairs={{0,1},{1,0},{2,3},{3,2},{4,5},{5,4},{6,7},{7,6},{8,9},{9,8},{10,11... | collective-permute-start | bytes 393224 | tf_op jit(solution)/shard_map/ppermute | solution.py:326
  8.5 1.4 %copy-start = (f32[1,4,16,512]{3,2,1,0:T(8,128)}, f32[1,4,16,512]{3,2,1,0:T(8,128)S(1)}, u32[]{:S(2)}) copy-start(f32[1,4,16,512]{3,2,1,0:T(8,128)S(1)} %collective-permute-done.refs_1_.refs_7_) | copy-start | bytes 393220
  8.5 1.3 %collective-permute-start.2 = (f32[1,4,16,512]{3,2,1,0:T(8,128)S(1)}, f32[1,4,16,512]{3,2,1,0:T(8,128)S(1)}, u32[]{:S(2)}, u32[]{:S(2)}) collective-permute-start(f32[1,4,16,512]{3,2,1,0:T(8,128)S(1)} %collective-permute-done.refs_1_.refs_7_), channel_id=1, source_target_pairs={{0,1},{1,0},{2,3},{3,2},{4,5},{5,4},{6,7},{7,6},{8,9},{9,8},{10,11... | collective-permute-start | bytes 393224 | tf_op jit(solution)/shard_map/ppermute | solution.py:325
  8.5 1.3 %copy-start.2 = (f32[4,16,512]{2,1,0:T(8,128)}, f32[4,16,512]{2,1,0:T(8,128)S(1)}, u32[]{:S(2)}) copy-start(f32[4,16,512]{2,1,0:T(8,128)S(1)} %collective-permute-done.1.refs_3_) | copy-start | bytes 393220
  8.6 1.3 %copy-start.1 = (bf16[12,16,512]{2,1,0:T(8,128)(2,1)}, bf16[12,16,512]{2,1,0:T(8,128)(2,1)S(1)}, u32[]{:S(2)}) copy-start(bf16[12,16,512]{2,1,0:T(8,128)(2,1)S(1)} %collective-permute-done.3.refs_6_) | copy-start | bytes 589828
  9.9 0.7 %copy-start.3 = (f32[1,4,16,512]{3,2,1,0:T(8,128)}, f32[1,4,16,512]{3,2,1,0:T(8,128)S(1)}, u32[]{:S(2)}) copy-start(f32[1,4,16,512]{3,2,1,0:T(8,128)S(1)} %collective-permute-done.2.refs_4_) | copy-start | bytes 393220
  23.7 1.5 %collective-permute-start.4 = (f32[128,128]{1,0:T(8,128)}, f32[128,128]{1,0:T(8,128)S(1)}, u32[]{:S(2)}, u32[]{:S(2)}) collective-permute-start(f32[128,128]{1,0:T(8,128)} %get-tuple-element.9.refs_3_), channel_id=1, source_target_pairs={{0,1},{1,0},{2,3},{3,2},{4,5},{5,4},{6,7},{7,6},{8,9},{9,8},{10,11... | collective-permute-start | bytes 196616 | tf_op jit(solution)/shard_map/ppermute | solution.py:365
  25.2 0.6 %copy-start.4 = (f32[128,128]{1,0:T(8,128)}, f32[128,128]{1,0:T(8,128)S(1)}, u32[]{:S(2)}) copy-start(f32[128,128]{1,0:T(8,128)S(1)} %collective-permute-done.4.refs_4_) | copy-start | bytes 196612
  32.8 7.6 %collective-permute-start.5 = (f32[4,16,512]{2,1,0:T(8,128)}, f32[4,16,512]{2,1,0:T(8,128)S(1)}, u32[]{:S(2)}, u32[]{:S(2)}) collective-permute-start(f32[4,16,512]{2,1,0:T(8,128)} %get-tuple-element.10), channel_id=1, source_target_pairs={{0,2},{2,4},{4,6},{6,8},{8,10},{10,12},{12,14},{1,3},{3,5},{5,7},{... | collective-permute-start | bytes 393224 | tf_op jit(solution)/shard_map/ppermute | solution.py:56
  41.4 8.7 %collective-permute-start.6 = (f32[4,16,512]{2,1,0:T(8,128)S(1)}, f32[4,16,512]{2,1,0:T(8,128)S(1)}, u32[]{:S(2)}, u32[]{:S(2)}) collective-permute-start(f32[4,16,512]{2,1,0:T(8,128)S(1)} %add.9), channel_id=1, source_target_pairs={{0,4},{2,6},{4,8},{6,10},{8,12},{10,14},{1,5},{3,7},{5,9},{7,11},{... | collective-permute-start | bytes 393224 | tf_op jit(solution)/shard_map/ppermute | solution.py:56
  50.1 7.9 %collective-permute-start.7 = (f32[4,16,512]{2,1,0:T(8,128)S(1)}, f32[4,16,512]{2,1,0:T(8,128)S(1)}, u32[]{:S(2)}, u32[]{:S(2)}) collective-permute-start(f32[4,16,512]{2,1,0:T(8,128)S(1)} %add.10), channel_id=1, source_target_pairs={{0,8},{2,10},{4,12},{6,14},{1,9},{3,11},{5,13},{7,15},{16,24},{18,... | collective-permute-start | bytes 393224 | tf_op jit(solution)/shard_map/ppermute | solution.py:56

commit v7 on v6

--- a/solution.py
+++ b/solution.py
@@ -69,7 +69,8 @@
 
 
 def silu(values):
-    return values / (1.0 + jnp.exp(-values))
+    half = 0.5 * values
+    return half + half * jnp.tanh(half)
 
 
 def feature_map(values):

time: 59.5 us -> 59.5 us (level)
  no operation moved by 1% of the time
where the time goes in v7:
time: 59.5 us; the launch traced here: 58.7 us
  starting transfers between devices  21.4 us (36%)
  Pallas kernels  20.2 us (34%)
  waiting for transfers between devices  13.5 us (23%)
  other arithmetic  1.62 us (3%)
  local copies, waits for them, and re-layouts  1.28 us (2%)
  between operations  0.72 us (1%)
    ppermute x3, starting transfers between devices, prefix_sum(): x = x + lax.ppermute(x, axis, pairs)  15.8 us
    pallas_call x1, Pallas kernels, local(): trunk(step_levels, previous, window_start, start_other, previous_other, c...  13.5 us
    ppermute x3, waiting for transfers between devices, prefix_sum(): x = x + lax.ppermute(x, axis, pairs)  8.35 us
    pallas_call x1, Pallas kernels, local(): head(step_levels, hidden, queries, stats_own, stats_other, mix_weight, ou...  6.72 us
    ppermute x1, starting transfers between devices, from_behind(): return lax.ppermute(x, axis, pairs)  4.85 us
    ppermute x1, waiting for transfers between devices, from_behind(): return lax.ppermute(x, axis, pairs)  2.47 us
    ppermute x1, waiting for transfers between devices, local(): stats_other = lax.ppermute(stats_own, 'rows', swap)  1.33 us
    ppermute x1, waiting for transfers between devices, local(): previous_other = lax.ppermute(previous, 'rows', swap)  1.31 us
  transfers between devices with their start and end apart: 8, of which 6 were waited for; matrix products, arithmetic and copies ran while one was open for 0% of the time, Pallas kernels for 0%

profile of v7, /device:TPU:0, one launch (start us, length us, event | category | flops | bytes accessed | tf_op | source)
XLA Modules:
  0.0 58.7 jit_solution(17927287670934690430)
XLA Ops:
  0.6 4.8 %collective-permute-start = (f32[1,4,16,512]{3,2,1,0:T(8,128)}, f32[1,4,16,512]{3,2,1,0:T(8,128)S(1)}, u32[]{:S(2)}, u32[]{:S(2)}) collective-permute-start(f32[1,4,16,512]{3,2,1,0:T(8,128)} %param.11), channel_id=1, source_target_pairs={{0,2},{2,4},{4,6},{6,8},{8,10},{10,12},{12,14},{1,3},{3,5},{5,7},{... | collective-permute-start | bytes 393224 | tf_op jit(solution)/shard_map/ppermute | solution.py:22
  5.5 0.1 collective-permute-start.3
  5.6 0.5 collective-permute-start.1
  6.1 2.5 %collective-permute-done.refs_1_.refs_7_ = f32[1,4,16,512]{3,2,1,0:T(8,128)S(1)} collective-permute-done((f32[1,4,16,512]{3,2,1,0:T(8,128)}, f32[1,4,16,512]{3,2,1,0:T(8,128)S(1)}, u32[]{:S(2)}, u32[]{:S(2)}) %collective-permute-start) | collective-permute-done | bytes 131104 | tf_op jit(solution)/shard_map/ppermute | solution.py:22
  8.5 0.0 copy-start
  8.5 0.0 collective-permute-start.2
  8.5 0.0 collective-permute-done.1.refs_3_
  8.5 0.0 copy-start.2
  8.6 0.0 collective-permute-done.3.refs_6_
  8.6 0.0 copy-start.1
  8.6 1.3 %collective-permute-done.2.refs_4_ = f32[1,4,16,512]{3,2,1,0:T(8,128)S(1)} collective-permute-done((f32[1,4,16,512]{3,2,1,0:T(8,128)S(1)}, f32[1,4,16,512]{3,2,1,0:T(8,128)S(1)}, u32[]{:S(2)}, u32[]{:S(2)}) %collective-permute-start.2) | collective-permute-done | bytes 131104 | tf_op jit(solution)/shard_map/ppermute | solution.py:326
  9.9 0.0 copy-done
  9.9 0.0 copy-done.2
  9.9 0.0 copy-done.1
  9.9 0.0 copy-start.3
  9.9 0.6 %copy-done.3 = f32[1,4,16,512]{3,2,1,0:T(8,128)} copy-done((f32[1,4,16,512]{3,2,1,0:T(8,128)}, f32[1,4,16,512]{3,2,1,0:T(8,128)S(1)}, u32[]{:S(2)}) %copy-start.3) | copy-done | bytes 131096
  10.5 13.5 %shard_map.122 = (f32[128,8192]{1,0:T(8,128)}, f32[128,512]{1,0:T(8,128)}, f32[128,128]{1,0:T(8,128)}) custom-call(s32[1,2]{1,0:T(1,128)} %refs_0_.3, f32[1,4,16,512]{3,2,1,0:T(8,128)} %copy-done, f32[4,16,512]{2,1,0:T(8,128)} %refs_8_.3, f32[4,16,512]{2,1,0:T(8,128)} %copy-done.2, f32[1,4,16,512]{3,2,1,0:T(8,128)} %copy-done.3, ...), custom_call_target="tpu_custom_call" | custom-call | tf_op jit(solution)/shard_map/pallas_call | solution.py:352
  24.1 0.1 collective-permute-start.4
  24.2 1.3 %collective-permute-done.4.refs_4_ = f32[128,128]{1,0:T(8,128)S(1)} collective-permute-done((f32[128,128]{1,0:T(8,128)}, f32[128,128]{1,0:T(8,128)S(1)}, u32[]{:S(2)}, u32[]{:S(2)}) %collective-permute-start.4) | collective-permute-done | bytes 65568 | tf_op jit(solution)/shard_map/ppermute | solution.py:366
  25.5 0.0 copy-start.4
  25.5 0.6 %copy-done.4 = f32[128,128]{1,0:T(8,128)} copy-done((f32[128,128]{1,0:T(8,128)}, f32[128,128]{1,0:T(8,128)S(1)}, u32[]{:S(2)}) %copy-start.4) | copy-done | bytes 65560
  26.2 6.7 %shard_map.123 = (f32[4,16,512]{2,1,0:T(8,128)}, f32[4,16,512]{2,1,0:T(8,128)}) custom-call(s32[1,2]{1,0:T(1,128)} %refs_0_.3, f32[128,8192]{1,0:T(8,128)} %get-tuple-element.7.refs_1_, f32[128,512]{1,0:T(8,128)} %get-tuple-element.8.refs_2_, f32[128,128]{1,0:T(8,128)} %get-tuple-element.9.refs_3_, f32[128,128]{1,0:T(8,128)} %copy-done.4, ...), custom_call_target="tpu_custom_call" | custom-call | tf_op jit(solution)/shard_map/pallas_call | solution.py:377
  32.9 4.3 %collective-permute-start.5 = (f32[4,16,512]{2,1,0:T(8,128)}, f32[4,16,512]{2,1,0:T(8,128)S(1)}, u32[]{:S(2)}, u32[]{:S(2)}) collective-permute-start(f32[4,16,512]{2,1,0:T(8,128)} %get-tuple-element.10), channel_id=1, source_target_pairs={{0,2},{2,4},{4,6},{6,8},{8,10},{10,12},{12,14},{1,3},{3,5},{5,7},{... | collective-permute-start | bytes 393224 | tf_op jit(solution)/shard_map/ppermute | solution.py:56
  37.2 3.4 %collective-permute-done.5 = f32[4,16,512]{2,1,0:T(8,128)S(1)} collective-permute-done((f32[4,16,512]{2,1,0:T(8,128)}, f32[4,16,512]{2,1,0:T(8,128)S(1)}, u32[]{:S(2)}, u32[]{:S(2)}) %collective-permute-start.5) | collective-permute-done | bytes 131104 | tf_op jit(solution)/shard_map/ppermute | solution.py:56
  40.5 0.9 %add.9 = f32[4,16,512]{2,1,0:T(8,128)S(1)} add(f32[4,16,512]{2,1,0:T(8,128)} %get-tuple-element.10, f32[4,16,512]{2,1,0:T(8,128)S(1)} %collective-permute-done.5) | non-fusion elementwise | flops 32768 | bytes 393216 | tf_op jit(solution)/shard_map/add | solution.py:56
  41.4 6.2 %collective-permute-start.6 = (f32[4,16,512]{2,1,0:T(8,128)S(1)}, f32[4,16,512]{2,1,0:T(8,128)S(1)}, u32[]{:S(2)}, u32[]{:S(2)}) collective-permute-start(f32[4,16,512]{2,1,0:T(8,128)S(1)} %add.9), channel_id=1, source_target_pairs={{0,4},{2,6},{4,8},{6,10},{8,12},{10,14},{1,5},{3,7},{5,9},{7,11},{... | collective-permute-start | bytes 393224 | tf_op jit(solution)/shard_map/ppermute | solution.py:56
  47.6 2.5 %collective-permute-done.6 = f32[4,16,512]{2,1,0:T(8,128)S(1)} collective-permute-done((f32[4,16,512]{2,1,0:T(8,128)S(1)}, f32[4,16,512]{2,1,0:T(8,128)S(1)}, u32[]{:S(2)}, u32[]{:S(2)}) %collective-permute-start.6) | collective-permute-done | bytes 131104 | tf_op jit(solution)/shard_map/ppermute | solution.py:56
  50.1 5.4 %collective-permute-start.7 = (f32[4,16,512]{2,1,0:T(8,128)S(1)}, f32[4,16,512]{2,1,0:T(8,128)S(1)}, u32[]{:S(2)}, u32[]{:S(2)}) collective-permute-start(f32[4,16,512]{2,1,0:T(8,128)S(1)} %add.10), channel_id=1, source_target_pairs={{0,8},{2,10},{4,12},{6,14},{1,9},{3,11},{5,13},{7,15},{16,24},{18,... | collective-permute-start | bytes 393224 | tf_op jit(solution)/shard_map/ppermute | solution.py:56
  55.5 2.5 %collective-permute-done.7 = f32[4,16,512]{2,1,0:T(8,128)S(1)} collective-permute-done((f32[4,16,512]{2,1,0:T(8,128)S(1)}, f32[4,16,512]{2,1,0:T(8,128)S(1)}, u32[]{:S(2)}, u32[]{:S(2)}) %collective-permute-start.7) | collective-permute-done | bytes 131104 | tf_op jit(solution)/shard_map/ppermute | solution.py:56
  58.0 0.7 %add_bitcast_fusion = f32[1,4,16,512]{3,2,1,0:T(8,128)} fusion(f32[4,16,512]{2,1,0:T(8,128)S(1)} %add.10, f32[4,16,512]{2,1,0:T(8,128)S(1)} %collective-permute-done.7), kind=kLoop, calls=%fused_computation | loop fusion | flops 32768 | bytes 393216 | tf_op jit(solution)/shard_map/broadcast_in_dim | solution.py:382
  (1 shorter events, 0.0 us)
Async XLA Ops:
  0.6 7.9 %collective-permute-start = (f32[1,4,16,512]{3,2,1,0:T(8,128)}, f32[1,4,16,512]{3,2,1,0:T(8,128)S(1)}, u32[]{:S(2)}, u32[]{:S(2)}) collective-permute-start(f32[1,4,16,512]{3,2,1,0:T(8,128)} %param.11), channel_id=1, source_target_pairs={{0,2},{2,4},{4,6},{6,8},{8,10},{10,12},{12,14},{1,3},{3,5},{5,7},{... | collective-permute-start | bytes 393224 | tf_op jit(solution)/shard_map/ppermute | solution.py:22
  5.5 3.1 %collective-permute-start.3 = (bf16[12,16,512]{2,1,0:T(8,128)(2,1)}, bf16[12,16,512]{2,1,0:T(8,128)(2,1)S(1)}, u32[]{:S(2)}, u32[]{:S(2)}) collective-permute-start(bf16[12,16,512]{2,1,0:T(8,128)(2,1)} %refs_5_.2), channel_id=1, source_target_pairs={{0,1},{1,0},{2,3},{3,2},{4,5},{5,4},{6,7},{7,6},{8,9},{9,8},{10,11... | collective-permute-start | bytes 589832 | tf_op jit(solution)/shard_map/ppermute | solution.py:328
  5.6 3.0 %collective-permute-start.1 = (f32[4,16,512]{2,1,0:T(8,128)}, f32[4,16,512]{2,1,0:T(8,128)S(1)}, u32[]{:S(2)}, u32[]{:S(2)}) collective-permute-start(f32[4,16,512]{2,1,0:T(8,128)} %refs_8_.3), channel_id=1, source_target_pairs={{0,1},{1,0},{2,3},{3,2},{4,5},{5,4},{6,7},{7,6},{8,9},{9,8},{10,11... | collective-permute-start | bytes 393224 | tf_op jit(solution)/shard_map/ppermute | solution.py:327
  8.5 1.4 %copy-start = (f32[1,4,16,512]{3,2,1,0:T(8,128)}, f32[1,4,16,512]{3,2,1,0:T(8,128)S(1)}, u32[]{:S(2)}) copy-start(f32[1,4,16,512]{3,2,1,0:T(8,128)S(1)} %collective-permute-done.refs_1_.refs_7_) | copy-start | bytes 393220
  8.5 1.3 %collective-permute-start.2 = (f32[1,4,16,512]{3,2,1,0:T(8,128)S(1)}, f32[1,4,16,512]{3,2,1,0:T(8,128)S(1)}, u32[]{:S(2)}, u32[]{:S(2)}) collective-permute-start(f32[1,4,16,512]{3,2,1,0:T(8,128)S(1)} %collective-permute-done.refs_1_.refs_7_), channel_id=1, source_target_pairs={{0,1},{1,0},{2,3},{3,2},{4,5},{5,4},{6,7},{7,6},{8,9},{9,8},{10,11... | collective-permute-start | bytes 393224 | tf_op jit(solution)/shard_map/ppermute | solution.py:326
  8.5 1.3 %copy-start.2 = (f32[4,16,512]{2,1,0:T(8,128)}, f32[4,16,512]{2,1,0:T(8,128)S(1)}, u32[]{:S(2)}) copy-start(f32[4,16,512]{2,1,0:T(8,128)S(1)} %collective-permute-done.1.refs_3_) | copy-start | bytes 393220
  8.6 1.3 %copy-start.1 = (bf16[12,16,512]{2,1,0:T(8,128)(2,1)}, bf16[12,16,512]{2,1,0:T(8,128)(2,1)S(1)}, u32[]{:S(2)}) copy-start(bf16[12,16,512]{2,1,0:T(8,128)(2,1)S(1)} %collective-permute-done.3.refs_6_) | copy-start | bytes 589828
  9.9 0.7 %copy-start.3 = (f32[1,4,16,512]{3,2,1,0:T(8,128)}, f32[1,4,16,512]{3,2,1,0:T(8,128)S(1)}, u32[]{:S(2)}) copy-start(f32[1,4,16,512]{3,2,1,0:T(8,128)S(1)} %collective-permute-done.2.refs_4_) | copy-start | bytes 393220
  24.1 1.5 %collective-permute-start.4 = (f32[128,128]{1,0:T(8,128)}, f32[128,128]{1,0:T(8,128)S(1)}, u32[]{:S(2)}, u32[]{:S(2)}) collective-permute-start(f32[128,128]{1,0:T(8,128)} %get-tuple-element.9.refs_3_), channel_id=1, source_target_pairs={{0,1},{1,0},{2,3},{3,2},{4,5},{5,4},{6,7},{7,6},{8,9},{9,8},{10,11... | collective-permute-start | bytes 196616 | tf_op jit(solution)/shard_map/ppermute | solution.py:366
  25.5 0.6 %copy-start.4 = (f32[128,128]{1,0:T(8,128)}, f32[128,128]{1,0:T(8,128)S(1)}, u32[]{:S(2)}) copy-start(f32[128,128]{1,0:T(8,128)S(1)} %collective-permute-done.4.refs_4_) | copy-start | bytes 196612
  32.9 7.6 %collective-permute-start.5 = (f32[4,16,512]{2,1,0:T(8,128)}, f32[4,16,512]{2,1,0:T(8,128)S(1)}, u32[]{:S(2)}, u32[]{:S(2)}) collective-permute-start(f32[4,16,512]{2,1,0:T(8,128)} %get-tuple-element.10), channel_id=1, source_target_pairs={{0,2},{2,4},{4,6},{6,8},{8,10},{10,12},{12,14},{1,3},{3,5},{5,7},{... | collective-permute-start | bytes 393224 | tf_op jit(solution)/shard_map/ppermute | solution.py:56
  41.4 8.7 %collective-permute-start.6 = (f32[4,16,512]{2,1,0:T(8,128)S(1)}, f32[4,16,512]{2,1,0:T(8,128)S(1)}, u32[]{:S(2)}, u32[]{:S(2)}) collective-permute-start(f32[4,16,512]{2,1,0:T(8,128)S(1)} %add.9), channel_id=1, source_target_pairs={{0,4},{2,6},{4,8},{6,10},{8,12},{10,14},{1,5},{3,7},{5,9},{7,11},{... | collective-permute-start | bytes 393224 | tf_op jit(solution)/shard_map/ppermute | solution.py:56
  50.1 7.9 %collective-permute-start.7 = (f32[4,16,512]{2,1,0:T(8,128)S(1)}, f32[4,16,512]{2,1,0:T(8,128)S(1)}, u32[]{:S(2)}, u32[]{:S(2)}) collective-permute-start(f32[4,16,512]{2,1,0:T(8,128)S(1)} %add.10), channel_id=1, source_target_pairs={{0,8},{2,10},{4,12},{6,14},{1,9},{3,11},{5,13},{7,15},{16,24},{18,... | collective-permute-start | bytes 393224 | tf_op jit(solution)/shard_map/ppermute | solution.py:56

commit v8 on v6

--- a/solution.py
+++ b/solution.py
@@ -130,8 +130,8 @@
 def trunk_kernel(
     levels_ref, previous_ref, start_ref, start_other_ref, previous_other_ref, coarse_ref,
     coarse_other_ref, lift_ref, embed_ref, first_ref, second_ref, project_ref,
-    hidden_ref, query_ref, stats_ref, inputs, act_first, lifted_keep, act_next,
-    *, width, band_rows, bands, level_count,
+    hidden_ref, query_ref, stats_ref, inputs, act_first, lifted_keep, act_next, hidden_local,
+    hidden_sems, *, width, band_rows, bands, level_count,
 ):
     band = lax.axis_index("rows")
     first_step = lax.axis_index("step") == 0
@@ -193,12 +193,18 @@
             act = jnp.where(jnp.logical_and(bottom_outside, lanes >= span - width), 0.0, act)
         act_next[:, first * width : first * width + span] = act.astype(jnp.bfloat16)
     second_w = stack_taps(second_ref)
-    for first, rows in row_chunks(band_rows):
+    outgoing = []
+    for q, (first, rows) in enumerate(row_chunks(band_rows)):
         span = rows * width
         lanes = lax.broadcasted_iota(jnp.int32, (1, span), 1)
         conv = conv_chunk(act_next, second_w, first, rows, width, lanes % width)
         start = first * width
-        hidden_ref[:, start : start + span] = lifted_keep[:, start : start + span].astype(jnp.float32) + conv
+        hidden_local[:, start : start + span] = lifted_keep[:, start : start + span].astype(jnp.float32) + conv
+        copy = pltpu.make_async_copy(
+            hidden_local.at[:, pl.ds(start, span)], hidden_ref.at[:, pl.ds(start, span)], hidden_sems.at[q]
+        )
+        copy.start()
+        outgoing.append(copy)
     tokens_per_row = width // 4
     pool_w = jnp.where(
         lax.broadcasted_iota(jnp.int32, (width, tokens_per_row), 0) // 4
@@ -208,9 +214,9 @@
     ).astype(jnp.float32)
     pooled = []
     for a in range(band_rows // 4):
-        row_sum = hidden_ref[:, (4 * a) * width : (4 * a + 1) * width]
+        row_sum = hidden_local[:, (4 * a) * width : (4 * a + 1) * width]
         for u in range(1, 4):
-            row_sum = row_sum + hidden_ref[:, (4 * a + u) * width : (4 * a + u + 1) * width]
+            row_sum = row_sum + hidden_local[:, (4 * a + u) * width : (4 * a + u + 1) * width]
         pooled.append(
             jnp.dot(row_sum, pool_w, precision=lax.Precision.HIGHEST, preferred_element_type=jnp.float32)
         )
@@ -231,12 +237,23 @@
         summary_t = lax.dot_general(values_h, keys_h, contract_tokens, preferred_element_type=jnp.float32)
         totals = lax.dot_general(ones, keys_h, contract_tokens, preferred_element_type=jnp.float32)
         stats_ref[h * HEAD_DIM : (h + 1) * HEAD_DIM, :] = jnp.concatenate([summary_t, totals], axis=1)
+    for copy in outgoing:
+        copy.wait()
 
 
 def head_kernel(
     levels_ref, hidden_ref, query_ref, stats_own_ref, stats_other_ref, mix_ref, out_w_ref,
-    previous_ref, start_ref, denoised_ref, seed_ref, *, width, band_rows, level_count,
+    previous_ref, start_ref, denoised_ref, seed_ref, hidden_local, hidden_sems,
+    *, width, band_rows, level_count,
 ):
+    group = 4 * width
+    incoming = []
+    for a in range(band_rows // 4):
+        copy = pltpu.make_async_copy(
+            hidden_ref.at[:, pl.ds(a * group, group)], hidden_local.at[:, pl.ds(a * group, group)], hidden_sems.at[a]
+        )
+        copy.start()
+        incoming.append(copy)
     first_step = lax.axis_index("step") == 0
     sigma_low, sigma_high, spread = step_scalars(levels_ref, level_count, (1, width))
     scale_skip = 0.25 / spread
@@ -269,6 +286,7 @@
     ).astype(jnp.float32)
     out_w = out_w_ref[...]
     for a in range(band_rows // 4):
+        incoming[a].wait()
         spread_mixed = jnp.dot(
             mixed[:, a * tokens_per_row : (a + 1) * tokens_per_row],
             expand,
@@ -278,7 +296,7 @@
         for u in range(4):
             r = 4 * a + u
             start = r * width
-            combined = hidden_ref[:, start : start + width] + spread_mixed
+            combined = hidden_local[:, start : start + width] + spread_mixed
             act = silu(normalize_features(combined)).astype(jnp.bfloat16)
             field = jnp.dot(out_w, act, preferred_element_type=jnp.float32)
             state = jnp.where(first_step, start_ref[:, r, :], previous_ref[0, :, r, :])
@@ -340,12 +358,14 @@
             jax.ShapeDtypeStruct((feat, 2 * HEAD_DIM), jnp.float32),
         ),
         in_specs=[smem()] + [vmem()] * 11,
-        out_specs=(vmem(), vmem(), vmem()),
+        out_specs=(pl.BlockSpec(memory_space=pl.ANY), vmem(), vmem()),
         scratch_shapes=[
             pltpu.VMEM((channels + coarse.shape[0], (band_rows + 2 * HALO) * width), jnp.float32),
             pltpu.VMEM((feat, (band_rows + 2 * HALO) * width), jnp.bfloat16),
             pltpu.VMEM((feat, pixels), jnp.bfloat16),
             pltpu.VMEM((feat, (band_rows + 2) * width), jnp.bfloat16),
+            pltpu.VMEM((feat, pixels), jnp.float32),
+            pltpu.SemaphoreType.DMA((len(row_chunks(band_rows)),)),
         ],
     )
     hidden, queries, stats_own = trunk(
@@ -370,8 +390,12 @@
             jax.ShapeDtypeStruct(window_start.shape, jnp.float32),
             jax.ShapeDtypeStruct(window_start.shape, jnp.float32),
         ),
-        in_specs=[smem()] + [vmem()] * 8,
+        in_specs=[smem(), pl.BlockSpec(memory_space=pl.ANY)] + [vmem()] * 7,
         out_specs=(vmem(), vmem()),
+        scratch_shapes=[
+            pltpu.VMEM((feat, pixels), jnp.float32),
+            pltpu.SemaphoreType.DMA((band_rows // 4,)),
+        ],
     )
     denoised, seed = head(
         step_levels, hidden, queries, stats_own, stats_other, mix_weight, output_weight.T,

time: 59.5 us -> 59.4 us (level)
  no operation moved by 1% of the time
where the time goes in v8:
time: 59.4 us; the launch traced here: 58.5 us
  starting transfers between devices  21.4 us (36%)
  Pallas kernels  19.9 us (34%)
  waiting for transfers between devices  13.5 us (23%)
  other arithmetic  1.62 us (3%)
  local copies, waits for them, and re-layouts  1.28 us (2%)
  between operations  0.73 us (1%)
    ppermute x3, starting transfers between devices, prefix_sum(): x = x + lax.ppermute(x, axis, pairs)  15.8 us
    pallas_call x1, Pallas kernels, local(): trunk(step_levels, previous, window_start, start_other, previous_other, c...  13 us
    ppermute x3, waiting for transfers between devices, prefix_sum(): x = x + lax.ppermute(x, axis, pairs)  8.37 us
    pallas_call x1, Pallas kernels, local(): head(step_levels, hidden, queries, stats_own, stats_other, mix_weight, ou...  6.95 us
    ppermute x1, starting transfers between devices, from_behind(): return lax.ppermute(x, axis, pairs)  4.85 us
    ppermute x1, waiting for transfers between devices, from_behind(): return lax.ppermute(x, axis, pairs)  2.47 us
    ppermute x1, waiting for transfers between devices, local(): stats_other = lax.ppermute(stats_own, 'rows', swap)  1.33 us
    ppermute x1, waiting for transfers between devices, local(): previous_other = lax.ppermute(previous, 'rows', swap)  1.31 us
  transfers between devices with their start and end apart: 8, of which 6 were waited for; matrix products, arithmetic and copies ran while one was open for 0% of the time, Pallas kernels for 0%

profile of v8, /device:TPU:0, one launch (start us, length us, event | category | flops | bytes accessed | tf_op | source)
XLA Modules:
  0.0 58.5 jit_solution(3652740956690157808)
XLA Ops:
  0.6 4.8 %collective-permute-start = (f32[1,4,16,512]{3,2,1,0:T(8,128)}, f32[1,4,16,512]{3,2,1,0:T(8,128)S(1)}, u32[]{:S(2)}, u32[]{:S(2)}) collective-permute-start(f32[1,4,16,512]{3,2,1,0:T(8,128)} %param.11), channel_id=1, source_target_pairs={{0,2},{2,4},{4,6},{6,8},{8,10},{10,12},{12,14},{1,3},{3,5},{5,7},{... | collective-permute-start | bytes 393224 | tf_op jit(solution)/shard_map/ppermute | solution.py:22
  5.5 0.1 collective-permute-start.3
  5.6 0.5 collective-permute-start.1
  6.1 2.5 %collective-permute-done.refs_1_.refs_7_ = f32[1,4,16,512]{3,2,1,0:T(8,128)S(1)} collective-permute-done((f32[1,4,16,512]{3,2,1,0:T(8,128)}, f32[1,4,16,512]{3,2,1,0:T(8,128)S(1)}, u32[]{:S(2)}, u32[]{:S(2)}) %collective-permute-start) | collective-permute-done | bytes 131104 | tf_op jit(solution)/shard_map/ppermute | solution.py:22
  8.5 0.0 copy-start
  8.5 0.0 collective-permute-start.2
  8.5 0.0 collective-permute-done.1.refs_3_
  8.5 0.0 copy-start.2
  8.6 0.0 collective-permute-done.3.refs_6_
  8.6 0.0 copy-start.1
  8.6 1.3 %collective-permute-done.2.refs_4_ = f32[1,4,16,512]{3,2,1,0:T(8,128)S(1)} collective-permute-done((f32[1,4,16,512]{3,2,1,0:T(8,128)S(1)}, f32[1,4,16,512]{3,2,1,0:T(8,128)S(1)}, u32[]{:S(2)}, u32[]{:S(2)}) %collective-permute-start.2) | collective-permute-done | bytes 131104 | tf_op jit(solution)/shard_map/ppermute | solution.py:343
  9.9 0.0 copy-done
  9.9 0.0 copy-done.2
  9.9 0.0 copy-done.1
  9.9 0.0 copy-start.3
  9.9 0.6 %copy-done.3 = f32[1,4,16,512]{3,2,1,0:T(8,128)} copy-done((f32[1,4,16,512]{3,2,1,0:T(8,128)}, f32[1,4,16,512]{3,2,1,0:T(8,128)S(1)}, u32[]{:S(2)}) %copy-start.3) | copy-done | bytes 131096
  10.5 13.0 %shard_map.122 = (f32[128,8192]{1,0:T(8,128)}, f32[128,512]{1,0:T(8,128)}, f32[128,128]{1,0:T(8,128)}) custom-call(s32[1,2]{1,0:T(1,128)} %refs_0_.3, f32[1,4,16,512]{3,2,1,0:T(8,128)} %copy-done, f32[4,16,512]{2,1,0:T(8,128)} %refs_8_.3, f32[4,16,512]{2,1,0:T(8,128)} %copy-done.2, f32[1,4,16,512]{3,2,1,0:T(8,128)} %copy-done.3, ...), custom_call_target="tpu_custom_call" | custom-call | tf_op jit(solution)/shard_map/pallas_call | solution.py:371
  23.6 0.2 collective-permute-start.4
  23.8 1.3 %collective-permute-done.4.refs_4_ = f32[128,128]{1,0:T(8,128)S(1)} collective-permute-done((f32[128,128]{1,0:T(8,128)}, f32[128,128]{1,0:T(8,128)S(1)}, u32[]{:S(2)}, u32[]{:S(2)}) %collective-permute-start.4) | collective-permute-done | bytes 65568 | tf_op jit(solution)/shard_map/ppermute | solution.py:385
  25.1 0.0 copy-start.4
  25.1 0.6 %copy-done.4 = f32[128,128]{1,0:T(8,128)} copy-done((f32[128,128]{1,0:T(8,128)}, f32[128,128]{1,0:T(8,128)S(1)}, u32[]{:S(2)}) %copy-start.4) | copy-done | bytes 65560
  25.7 6.9 %shard_map.123 = (f32[4,16,512]{2,1,0:T(8,128)}, f32[4,16,512]{2,1,0:T(8,128)}) custom-call(s32[1,2]{1,0:T(1,128)} %refs_0_.3, f32[128,8192]{1,0:T(8,128)} %get-tuple-element.7.refs_1_, f32[128,512]{1,0:T(8,128)} %get-tuple-element.8.refs_2_, f32[128,128]{1,0:T(8,128)} %get-tuple-element.9.refs_3_, f32[128,128]{1,0:T(8,128)} %copy-done.4, ...), custom_call_target="tpu_custom_call" | custom-call | tf_op jit(solution)/shard_map/pallas_call | solution.py:400
  32.7 4.3 %collective-permute-start.5 = (f32[4,16,512]{2,1,0:T(8,128)}, f32[4,16,512]{2,1,0:T(8,128)S(1)}, u32[]{:S(2)}, u32[]{:S(2)}) collective-permute-start(f32[4,16,512]{2,1,0:T(8,128)} %get-tuple-element.10), channel_id=1, source_target_pairs={{0,2},{2,4},{4,6},{6,8},{8,10},{10,12},{12,14},{1,3},{3,5},{5,7},{... | collective-permute-start | bytes 393224 | tf_op jit(solution)/shard_map/ppermute | solution.py:56
  37.0 3.4 %collective-permute-done.5 = f32[4,16,512]{2,1,0:T(8,128)S(1)} collective-permute-done((f32[4,16,512]{2,1,0:T(8,128)}, f32[4,16,512]{2,1,0:T(8,128)S(1)}, u32[]{:S(2)}, u32[]{:S(2)}) %collective-permute-start.5) | collective-permute-done | bytes 131104 | tf_op jit(solution)/shard_map/ppermute | solution.py:56
  40.3 0.9 %add.9 = f32[4,16,512]{2,1,0:T(8,128)S(1)} add(f32[4,16,512]{2,1,0:T(8,128)} %get-tuple-element.10, f32[4,16,512]{2,1,0:T(8,128)S(1)} %collective-permute-done.5) | non-fusion elementwise | flops 32768 | bytes 393216 | tf_op jit(solution)/shard_map/add | solution.py:56
  41.3 6.2 %collective-permute-start.6 = (f32[4,16,512]{2,1,0:T(8,128)S(1)}, f32[4,16,512]{2,1,0:T(8,128)S(1)}, u32[]{:S(2)}, u32[]{:S(2)}) collective-permute-start(f32[4,16,512]{2,1,0:T(8,128)S(1)} %add.9), channel_id=1, source_target_pairs={{0,4},{2,6},{4,8},{6,10},{8,12},{10,14},{1,5},{3,7},{5,9},{7,11},{... | collective-permute-start | bytes 393224 | tf_op jit(solution)/shard_map/ppermute | solution.py:56
  47.5 2.5 %collective-permute-done.6 = f32[4,16,512]{2,1,0:T(8,128)S(1)} collective-permute-done((f32[4,16,512]{2,1,0:T(8,128)S(1)}, f32[4,16,512]{2,1,0:T(8,128)S(1)}, u32[]{:S(2)}, u32[]{:S(2)}) %collective-permute-start.6) | collective-permute-done | bytes 131104 | tf_op jit(solution)/shard_map/ppermute | solution.py:56
  50.0 5.4 %collective-permute-start.7 = (f32[4,16,512]{2,1,0:T(8,128)S(1)}, f32[4,16,512]{2,1,0:T(8,128)S(1)}, u32[]{:S(2)}, u32[]{:S(2)}) collective-permute-start(f32[4,16,512]{2,1,0:T(8,128)S(1)} %add.10), channel_id=1, source_target_pairs={{0,8},{2,10},{4,12},{6,14},{1,9},{3,11},{5,13},{7,15},{16,24},{18,... | collective-permute-start | bytes 393224 | tf_op jit(solution)/shard_map/ppermute | solution.py:56
  55.3 2.5 %collective-permute-done.7 = f32[4,16,512]{2,1,0:T(8,128)S(1)} collective-permute-done((f32[4,16,512]{2,1,0:T(8,128)S(1)}, f32[4,16,512]{2,1,0:T(8,128)S(1)}, u32[]{:S(2)}, u32[]{:S(2)}) %collective-permute-start.7) | collective-permute-done | bytes 131104 | tf_op jit(solution)/shard_map/ppermute | solution.py:56
  57.8 0.7 %add_bitcast_fusion = f32[1,4,16,512]{3,2,1,0:T(8,128)} fusion(f32[4,16,512]{2,1,0:T(8,128)S(1)} %add.10, f32[4,16,512]{2,1,0:T(8,128)S(1)} %collective-permute-done.7), kind=kLoop, calls=%fused_computation | loop fusion | flops 32768 | bytes 393216 | tf_op jit(solution)/shard_map/broadcast_in_dim | solution.py:405
  (1 shorter events, 0.0 us)
Async XLA Ops:
  0.6 7.9 %collective-permute-start = (f32[1,4,16,512]{3,2,1,0:T(8,128)}, f32[1,4,16,512]{3,2,1,0:T(8,128)S(1)}, u32[]{:S(2)}, u32[]{:S(2)}) collective-permute-start(f32[1,4,16,512]{3,2,1,0:T(8,128)} %param.11), channel_id=1, source_target_pairs={{0,2},{2,4},{4,6},{6,8},{8,10},{10,12},{12,14},{1,3},{3,5},{5,7},{... | collective-permute-start | bytes 393224 | tf_op jit(solution)/shard_map/ppermute | solution.py:22
  5.5 3.1 %collective-permute-start.3 = (bf16[12,16,512]{2,1,0:T(8,128)(2,1)}, bf16[12,16,512]{2,1,0:T(8,128)(2,1)S(1)}, u32[]{:S(2)}, u32[]{:S(2)}) collective-permute-start(bf16[12,16,512]{2,1,0:T(8,128)(2,1)} %refs_5_.2), channel_id=1, source_target_pairs={{0,1},{1,0},{2,3},{3,2},{4,5},{5,4},{6,7},{7,6},{8,9},{9,8},{10,11... | collective-permute-start | bytes 589832 | tf_op jit(solution)/shard_map/ppermute | solution.py:345
  5.6 3.0 %collective-permute-start.1 = (f32[4,16,512]{2,1,0:T(8,128)}, f32[4,16,512]{2,1,0:T(8,128)S(1)}, u32[]{:S(2)}, u32[]{:S(2)}) collective-permute-start(f32[4,16,512]{2,1,0:T(8,128)} %refs_8_.3), channel_id=1, source_target_pairs={{0,1},{1,0},{2,3},{3,2},{4,5},{5,4},{6,7},{7,6},{8,9},{9,8},{10,11... | collective-permute-start | bytes 393224 | tf_op jit(solution)/shard_map/ppermute | solution.py:344
  8.5 1.4 %copy-start = (f32[1,4,16,512]{3,2,1,0:T(8,128)}, f32[1,4,16,512]{3,2,1,0:T(8,128)S(1)}, u32[]{:S(2)}) copy-start(f32[1,4,16,512]{3,2,1,0:T(8,128)S(1)} %collective-permute-done.refs_1_.refs_7_) | copy-start | bytes 393220
  8.5 1.3 %collective-permute-start.2 = (f32[1,4,16,512]{3,2,1,0:T(8,128)S(1)}, f32[1,4,16,512]{3,2,1,0:T(8,128)S(1)}, u32[]{:S(2)}, u32[]{:S(2)}) collective-permute-start(f32[1,4,16,512]{3,2,1,0:T(8,128)S(1)} %collective-permute-done.refs_1_.refs_7_), channel_id=1, source_target_pairs={{0,1},{1,0},{2,3},{3,2},{4,5},{5,4},{6,7},{7,6},{8,9},{9,8},{10,11... | collective-permute-start | bytes 393224 | tf_op jit(solution)/shard_map/ppermute | solution.py:343
  8.5 1.3 %copy-start.2 = (f32[4,16,512]{2,1,0:T(8,128)}, f32[4,16,512]{2,1,0:T(8,128)S(1)}, u32[]{:S(2)}) copy-start(f32[4,16,512]{2,1,0:T(8,128)S(1)} %collective-permute-done.1.refs_3_) | copy-start | bytes 393220
  8.6 1.3 %copy-start.1 = (bf16[12,16,512]{2,1,0:T(8,128)(2,1)}, bf16[12,16,512]{2,1,0:T(8,128)(2,1)S(1)}, u32[]{:S(2)}) copy-start(bf16[12,16,512]{2,1,0:T(8,128)(2,1)S(1)} %collective-permute-done.3.refs_6_) | copy-start | bytes 589828
  9.9 0.7 %copy-start.3 = (f32[1,4,16,512]{3,2,1,0:T(8,128)}, f32[1,4,16,512]{3,2,1,0:T(8,128)S(1)}, u32[]{:S(2)}) copy-start(f32[1,4,16,512]{3,2,1,0:T(8,128)S(1)} %collective-permute-done.2.refs_4_) | copy-start | bytes 393220
  23.6 1.5 %collective-permute-start.4 = (f32[128,128]{1,0:T(8,128)}, f32[128,128]{1,0:T(8,128)S(1)}, u32[]{:S(2)}, u32[]{:S(2)}) collective-permute-start(f32[128,128]{1,0:T(8,128)} %get-tuple-element.9.refs_3_), channel_id=1, source_target_pairs={{0,1},{1,0},{2,3},{3,2},{4,5},{5,4},{6,7},{7,6},{8,9},{9,8},{10,11... | collective-permute-start | bytes 196616 | tf_op jit(solution)/shard_map/ppermute | solution.py:385
  25.1 0.6 %copy-start.4 = (f32[128,128]{1,0:T(8,128)}, f32[128,128]{1,0:T(8,128)S(1)}, u32[]{:S(2)}) copy-start(f32[128,128]{1,0:T(8,128)S(1)} %collective-permute-done.4.refs_4_) | copy-start | bytes 196612
  32.7 7.7 %collective-permute-start.5 = (f32[4,16,512]{2,1,0:T(8,128)}, f32[4,16,512]{2,1,0:T(8,128)S(1)}, u32[]{:S(2)}, u32[]{:S(2)}) collective-permute-start(f32[4,16,512]{2,1,0:T(8,128)} %get-tuple-element.10), channel_id=1, source_target_pairs={{0,2},{2,4},{4,6},{6,8},{8,10},{10,12},{12,14},{1,3},{3,5},{5,7},{... | collective-permute-start | bytes 393224 | tf_op jit(solution)/shard_map/ppermute | solution.py:56
  41.3 8.7 %collective-permute-start.6 = (f32[4,16,512]{2,1,0:T(8,128)S(1)}, f32[4,16,512]{2,1,0:T(8,128)S(1)}, u32[]{:S(2)}, u32[]{:S(2)}) collective-permute-start(f32[4,16,512]{2,1,0:T(8,128)S(1)} %add.9), channel_id=1, source_target_pairs={{0,4},{2,6},{4,8},{6,10},{8,12},{10,14},{1,5},{3,7},{5,9},{7,11},{... | collective-permute-start | bytes 393224 | tf_op jit(solution)/shard_map/ppermute | solution.py:56
  50.0 7.9 %collective-permute-start.7 = (f32[4,16,512]{2,1,0:T(8,128)S(1)}, f32[4,16,512]{2,1,0:T(8,128)S(1)}, u32[]{:S(2)}, u32[]{:S(2)}) collective-permute-start(f32[4,16,512]{2,1,0:T(8,128)S(1)} %add.10), channel_id=1, source_target_pairs={{0,8},{2,10},{4,12},{6,14},{1,9},{3,11},{5,13},{7,15},{16,24},{18,... | collective-permute-start | bytes 393224 | tf_op jit(solution)/shard_map/ppermute | solution.py:56

commit v9 on v8

--- a/solution.py
+++ b/solution.py
@@ -99,6 +99,14 @@
         chunks.append((first, size))
         first += size
     return chunks
+
+
+def exact_weight_dot(values, weight):
+    high = values.astype(jnp.bfloat16)
+    low = (values - high.astype(jnp.float32)).astype(jnp.bfloat16)
+    return jnp.dot(high, weight, preferred_element_type=jnp.float32) + jnp.dot(
+        low, weight, preferred_element_type=jnp.float32
+    )
 
 
 def transposed(block):
@@ -211,15 +219,13 @@
         == lax.broadcasted_iota(jnp.int32, (width, tokens_per_row), 1),
         1.0 / 16.0,
         0.0,
-    ).astype(jnp.float32)
+    ).astype(jnp.bfloat16)
     pooled = []
     for a in range(band_rows // 4):
         row_sum = hidden_local[:, (4 * a) * width : (4 * a + 1) * width]
         for u in range(1, 4):
             row_sum = row_sum + hidden_local[:, (4 * a + u) * width : (4 * a + u + 1) * width]
-        pooled.append(
-            jnp.dot(row_sum, pool_w, precision=lax.Precision.HIGHEST, preferred_element_type=jnp.float32)
-        )
+        pooled.append(exact_weight_dot(row_sum, pool_w))
     pooled = jnp.concatenate(pooled, axis=1)
     tokens = normalize_features(pooled).astype(jnp.bfloat16)
     project_t = jnp.concatenate(
@@ -243,9 +249,11 @@
 
 def head_kernel(
     levels_ref, hidden_ref, query_ref, stats_own_ref, stats_other_ref, mix_ref, out_w_ref,
-    previous_ref, start_ref, denoised_ref, seed_ref, hidden_local, hidden_sems,
-    *, width, band_rows, level_count,
+    previous_ref, start_ref, denoised_ref, seed_ref, hidden_local, hidden_sems, stats_local,
+    stats_sem, *, width, band_rows, level_count,
 ):
+    stats_copy = pltpu.make_async_copy(stats_other_ref, stats_local, stats_sem.at[0])
+    stats_copy.start()
     group = 4 * width
     incoming = []
     for a in range(band_rows // 4):
@@ -260,11 +268,12 @@
     scale_out = 0.5 * sigma_low * lax.rsqrt(spread)
     sigma_gap = sigma_high - sigma_low
     feat = query_ref.shape[0]
+    stats_copy.wait()
     contexts = []
     for h in range(feat // HEAD_DIM):
         rows = slice(h * HEAD_DIM, (h + 1) * HEAD_DIM)
         queries_h = query_ref[rows, :]
-        stats_h = stats_own_ref[rows, :] + stats_other_ref[rows, :]
+        stats_h = stats_own_ref[rows, :] + stats_local[rows, :]
         numerator = jnp.dot(
             stats_h[:, 0:HEAD_DIM], queries_h,
             precision=lax.Precision.HIGHEST, preferred_element_type=jnp.float32,
@@ -283,16 +292,11 @@
         == lax.broadcasted_iota(jnp.int32, (tokens_per_row, width), 1) // 4,
         1.0,
         0.0,
-    ).astype(jnp.float32)
+    ).astype(jnp.bfloat16)
     out_w = out_w_ref[...]
     for a in range(band_rows // 4):
         incoming[a].wait()
-        spread_mixed = jnp.dot(
-            mixed[:, a * tokens_per_row : (a + 1) * tokens_per_row],
-            expand,
-            precision=lax.Precision.HIGHEST,
-            preferred_element_type=jnp.float32,
-        )
+        spread_mixed = exact_weight_dot(mixed[:, a * tokens_per_row : (a + 1) * tokens_per_row], expand)
         for u in range(4):
             r = 4 * a + u
             start = r * width
@@ -390,11 +394,14 @@
             jax.ShapeDtypeStruct(window_start.shape, jnp.float32),
             jax.ShapeDtypeStruct(window_start.shape, jnp.float32),
         ),
-        in_specs=[smem(), pl.BlockSpec(memory_space=pl.ANY)] + [vmem()] * 7,
+        in_specs=[smem(), pl.BlockSpec(memory_space=pl.ANY), vmem(), vmem(),
+                  pl.BlockSpec(memory_space=pl.ANY)] + [vmem()] * 4,
         out_specs=(vmem(), vmem()),
         scratch_shapes=[
             pltpu.VMEM((feat, pixels), jnp.float32),
             pltpu.SemaphoreType.DMA((band_rows // 4,)),
+            pltpu.VMEM((feat, 2 * HEAD_DIM), jnp.float32),
+            pltpu.SemaphoreType.DMA((1,)),
         ],
     )
     denoised, seed = head(

time: 59.4 us -> 59.6 us (level)
  no operation moved by 1% of the time
where the time goes in v9:
time: 59.6 us; the launch traced here: 58.7 us
  starting transfers between devices  21.4 us (36%)
  Pallas kernels  20.2 us (34%)
  waiting for transfers between devices  13.5 us (23%)
  other arithmetic  1.62 us (3%)
  local copies, waits for them, and re-layouts  1.28 us (2%)
  between operations  0.73 us (1%)
    ppermute x3, starting transfers between devices, prefix_sum(): x = x + lax.ppermute(x, axis, pairs)  15.8 us
    pallas_call x1, Pallas kernels, local(): trunk(step_levels, previous, window_start, start_other, previous_other, c...  12.9 us
    ppermute x3, waiting for transfers between devices, prefix_sum(): x = x + lax.ppermute(x, axis, pairs)  8.36 us
    pallas_call x1, Pallas kernels, local(): head(step_levels, hidden, queries, stats_own, stats_other, mix_weight, ou...  7.28 us
    ppermute x1, starting transfers between devices, from_behind(): return lax.ppermute(x, axis, pairs)  4.85 us
    ppermute x1, waiting for transfers between devices, from_behind(): return lax.ppermute(x, axis, pairs)  2.47 us
    ppermute x1, waiting for transfers between devices, local(): stats_other = lax.ppermute(stats_own, 'rows', swap)  1.34 us
    ppermute x1, waiting for transfers between devices, local(): previous_other = lax.ppermute(previous, 'rows', swap)  1.31 us
  transfers between devices with their start and end apart: 8, of which 6 were waited for; matrix products, arithmetic and copies ran while one was open for 0% of the time, Pallas kernels for 0%

profile of v9, /device:TPU:0, one launch (start us, length us, event | category | flops | bytes accessed | tf_op | source)
XLA Modules:
  0.0 58.7 jit_solution(11510805804012782501)
XLA Ops:
  0.6 4.8 %collective-permute-start = (f32[1,4,16,512]{3,2,1,0:T(8,128)}, f32[1,4,16,512]{3,2,1,0:T(8,128)S(1)}, u32[]{:S(2)}, u32[]{:S(2)}) collective-permute-start(f32[1,4,16,512]{3,2,1,0:T(8,128)} %param.11), channel_id=1, source_target_pairs={{0,2},{2,4},{4,6},{6,8},{8,10},{10,12},{12,14},{1,3},{3,5},{5,7},{... | collective-permute-start | bytes 393224 | tf_op jit(solution)/shard_map/ppermute | solution.py:22
  5.5 0.1 collective-permute-start.3
  5.6 0.5 collective-permute-start.1
  6.1 2.5 %collective-permute-done.refs_1_.refs_7_ = f32[1,4,16,512]{3,2,1,0:T(8,128)S(1)} collective-permute-done((f32[1,4,16,512]{3,2,1,0:T(8,128)}, f32[1,4,16,512]{3,2,1,0:T(8,128)S(1)}, u32[]{:S(2)}, u32[]{:S(2)}) %collective-permute-start) | collective-permute-done | bytes 131104 | tf_op jit(solution)/shard_map/ppermute | solution.py:22
  8.5 0.0 copy-start
  8.5 0.0 collective-permute-start.2
  8.5 0.0 collective-permute-done.1.refs_3_
  8.5 0.0 copy-start.2
  8.6 0.0 collective-permute-done.3.refs_6_
  8.6 0.0 copy-start.1
  8.6 1.3 %collective-permute-done.2.refs_4_ = f32[1,4,16,512]{3,2,1,0:T(8,128)S(1)} collective-permute-done((f32[1,4,16,512]{3,2,1,0:T(8,128)S(1)}, f32[1,4,16,512]{3,2,1,0:T(8,128)S(1)}, u32[]{:S(2)}, u32[]{:S(2)}) %collective-permute-start.2) | collective-permute-done | bytes 131104 | tf_op jit(solution)/shard_map/ppermute | solution.py:347
  9.9 0.0 copy-done
  9.9 0.0 copy-done.2
  9.9 0.0 copy-done.1
  9.9 0.0 copy-start.3
  9.9 0.6 %copy-done.3 = f32[1,4,16,512]{3,2,1,0:T(8,128)} copy-done((f32[1,4,16,512]{3,2,1,0:T(8,128)}, f32[1,4,16,512]{3,2,1,0:T(8,128)S(1)}, u32[]{:S(2)}) %copy-start.3) | copy-done | bytes 131096
  10.5 12.9 %shard_map.122 = (f32[128,8192]{1,0:T(8,128)}, f32[128,512]{1,0:T(8,128)}, f32[128,128]{1,0:T(8,128)}) custom-call(s32[1,2]{1,0:T(1,128)} %refs_0_.3, f32[1,4,16,512]{3,2,1,0:T(8,128)} %copy-done, f32[4,16,512]{2,1,0:T(8,128)} %refs_8_.3, f32[4,16,512]{2,1,0:T(8,128)} %copy-done.2, f32[1,4,16,512]{3,2,1,0:T(8,128)} %copy-done.3, ...), custom_call_target="tpu_custom_call" | custom-call | tf_op jit(solution)/shard_map/pallas_call | solution.py:375
  23.5 0.2 collective-permute-start.4
  23.6 1.3 %collective-permute-done.4.refs_4_ = f32[128,128]{1,0:T(8,128)S(1)} collective-permute-done((f32[128,128]{1,0:T(8,128)}, f32[128,128]{1,0:T(8,128)S(1)}, u32[]{:S(2)}, u32[]{:S(2)}) %collective-permute-start.4) | collective-permute-done | bytes 65568 | tf_op jit(solution)/shard_map/ppermute | solution.py:389
  25.0 0.0 copy-start.4
  25.0 0.6 %copy-done.4 = f32[128,128]{1,0:T(8,128)} copy-done((f32[128,128]{1,0:T(8,128)}, f32[128,128]{1,0:T(8,128)S(1)}, u32[]{:S(2)}) %copy-start.4) | copy-done | bytes 65560
  25.6 7.3 %shard_map.123 = (f32[4,16,512]{2,1,0:T(8,128)}, f32[4,16,512]{2,1,0:T(8,128)}) custom-call(s32[1,2]{1,0:T(1,128)} %refs_0_.3, f32[128,8192]{1,0:T(8,128)} %get-tuple-element.7.refs_1_, f32[128,512]{1,0:T(8,128)} %get-tuple-element.8.refs_2_, f32[128,128]{1,0:T(8,128)} %get-tuple-element.9.refs_3_, f32[128,128]{1,0:T(8,128)} %copy-done.4, ...), custom_call_target="tpu_custom_call" | custom-call | tf_op jit(solution)/shard_map/pallas_call | solution.py:407
  32.9 4.3 %collective-permute-start.5 = (f32[4,16,512]{2,1,0:T(8,128)}, f32[4,16,512]{2,1,0:T(8,128)S(1)}, u32[]{:S(2)}, u32[]{:S(2)}) collective-permute-start(f32[4,16,512]{2,1,0:T(8,128)} %get-tuple-element.10), channel_id=1, source_target_pairs={{0,2},{2,4},{4,6},{6,8},{8,10},{10,12},{12,14},{1,3},{3,5},{5,7},{... | collective-permute-start | bytes 393224 | tf_op jit(solution)/shard_map/ppermute | solution.py:56
  37.2 3.4 %collective-permute-done.5 = f32[4,16,512]{2,1,0:T(8,128)S(1)} collective-permute-done((f32[4,16,512]{2,1,0:T(8,128)}, f32[4,16,512]{2,1,0:T(8,128)S(1)}, u32[]{:S(2)}, u32[]{:S(2)}) %collective-permute-start.5) | collective-permute-done | bytes 131104 | tf_op jit(solution)/shard_map/ppermute | solution.py:56
  40.6 0.9 %add.9 = f32[4,16,512]{2,1,0:T(8,128)S(1)} add(f32[4,16,512]{2,1,0:T(8,128)} %get-tuple-element.10, f32[4,16,512]{2,1,0:T(8,128)S(1)} %collective-permute-done.5) | non-fusion elementwise | flops 32768 | bytes 393216 | tf_op jit(solution)/shard_map/add | solution.py:56
  41.5 6.2 %collective-permute-start.6 = (f32[4,16,512]{2,1,0:T(8,128)S(1)}, f32[4,16,512]{2,1,0:T(8,128)S(1)}, u32[]{:S(2)}, u32[]{:S(2)}) collective-permute-start(f32[4,16,512]{2,1,0:T(8,128)S(1)} %add.9), channel_id=1, source_target_pairs={{0,4},{2,6},{4,8},{6,10},{8,12},{10,14},{1,5},{3,7},{5,9},{7,11},{... | collective-permute-start | bytes 393224 | tf_op jit(solution)/shard_map/ppermute | solution.py:56
  47.7 2.5 %collective-permute-done.6 = f32[4,16,512]{2,1,0:T(8,128)S(1)} collective-permute-done((f32[4,16,512]{2,1,0:T(8,128)S(1)}, f32[4,16,512]{2,1,0:T(8,128)S(1)}, u32[]{:S(2)}, u32[]{:S(2)}) %collective-permute-start.6) | collective-permute-done | bytes 131104 | tf_op jit(solution)/shard_map/ppermute | solution.py:56
  50.2 5.4 %collective-permute-start.7 = (f32[4,16,512]{2,1,0:T(8,128)S(1)}, f32[4,16,512]{2,1,0:T(8,128)S(1)}, u32[]{:S(2)}, u32[]{:S(2)}) collective-permute-start(f32[4,16,512]{2,1,0:T(8,128)S(1)} %add.10), channel_id=1, source_target_pairs={{0,8},{2,10},{4,12},{6,14},{1,9},{3,11},{5,13},{7,15},{16,24},{18,... | collective-permute-start | bytes 393224 | tf_op jit(solution)/shard_map/ppermute | solution.py:56
  55.5 2.5 %collective-permute-done.7 = f32[4,16,512]{2,1,0:T(8,128)S(1)} collective-permute-done((f32[4,16,512]{2,1,0:T(8,128)S(1)}, f32[4,16,512]{2,1,0:T(8,128)S(1)}, u32[]{:S(2)}, u32[]{:S(2)}) %collective-permute-start.7) | collective-permute-done | bytes 131104 | tf_op jit(solution)/shard_map/ppermute | solution.py:56
  58.0 0.7 %add_bitcast_fusion = f32[1,4,16,512]{3,2,1,0:T(8,128)} fusion(f32[4,16,512]{2,1,0:T(8,128)S(1)} %add.10, f32[4,16,512]{2,1,0:T(8,128)S(1)} %collective-permute-done.7), kind=kLoop, calls=%fused_computation | loop fusion | flops 32768 | bytes 393216 | tf_op jit(solution)/shard_map/broadcast_in_dim | solution.py:412
  (1 shorter events, 0.0 us)
Async XLA Ops:
  0.6 7.9 %collective-permute-start = (f32[1,4,16,512]{3,2,1,0:T(8,128)}, f32[1,4,16,512]{3,2,1,0:T(8,128)S(1)}, u32[]{:S(2)}, u32[]{:S(2)}) collective-permute-start(f32[1,4,16,512]{3,2,1,0:T(8,128)} %param.11), channel_id=1, source_target_pairs={{0,2},{2,4},{4,6},{6,8},{8,10},{10,12},{12,14},{1,3},{3,5},{5,7},{... | collective-permute-start | bytes 393224 | tf_op jit(solution)/shard_map/ppermute | solution.py:22
  5.5 3.1 %collective-permute-start.3 = (bf16[12,16,512]{2,1,0:T(8,128)(2,1)}, bf16[12,16,512]{2,1,0:T(8,128)(2,1)S(1)}, u32[]{:S(2)}, u32[]{:S(2)}) collective-permute-start(bf16[12,16,512]{2,1,0:T(8,128)(2,1)} %refs_5_.2), channel_id=1, source_target_pairs={{0,1},{1,0},{2,3},{3,2},{4,5},{5,4},{6,7},{7,6},{8,9},{9,8},{10,11... | collective-permute-start | bytes 589832 | tf_op jit(solution)/shard_map/ppermute | solution.py:349
  5.6 3.0 %collective-permute-start.1 = (f32[4,16,512]{2,1,0:T(8,128)}, f32[4,16,512]{2,1,0:T(8,128)S(1)}, u32[]{:S(2)}, u32[]{:S(2)}) collective-permute-start(f32[4,16,512]{2,1,0:T(8,128)} %refs_8_.3), channel_id=1, source_target_pairs={{0,1},{1,0},{2,3},{3,2},{4,5},{5,4},{6,7},{7,6},{8,9},{9,8},{10,11... | collective-permute-start | bytes 393224 | tf_op jit(solution)/shard_map/ppermute | solution.py:348
  8.5 1.4 %copy-start = (f32[1,4,16,512]{3,2,1,0:T(8,128)}, f32[1,4,16,512]{3,2,1,0:T(8,128)S(1)}, u32[]{:S(2)}) copy-start(f32[1,4,16,512]{3,2,1,0:T(8,128)S(1)} %collective-permute-done.refs_1_.refs_7_) | copy-start | bytes 393220
  8.5 1.3 %collective-permute-start.2 = (f32[1,4,16,512]{3,2,1,0:T(8,128)S(1)}, f32[1,4,16,512]{3,2,1,0:T(8,128)S(1)}, u32[]{:S(2)}, u32[]{:S(2)}) collective-permute-start(f32[1,4,16,512]{3,2,1,0:T(8,128)S(1)} %collective-permute-done.refs_1_.refs_7_), channel_id=1, source_target_pairs={{0,1},{1,0},{2,3},{3,2},{4,5},{5,4},{6,7},{7,6},{8,9},{9,8},{10,11... | collective-permute-start | bytes 393224 | tf_op jit(solution)/shard_map/ppermute | solution.py:347
  8.5 1.3 %copy-start.2 = (f32[4,16,512]{2,1,0:T(8,128)}, f32[4,16,512]{2,1,0:T(8,128)S(1)}, u32[]{:S(2)}) copy-start(f32[4,16,512]{2,1,0:T(8,128)S(1)} %collective-permute-done.1.refs_3_) | copy-start | bytes 393220
  8.6 1.3 %copy-start.1 = (bf16[12,16,512]{2,1,0:T(8,128)(2,1)}, bf16[12,16,512]{2,1,0:T(8,128)(2,1)S(1)}, u32[]{:S(2)}) copy-start(bf16[12,16,512]{2,1,0:T(8,128)(2,1)S(1)} %collective-permute-done.3.refs_6_) | copy-start | bytes 589828
  9.9 0.7 %copy-start.3 = (f32[1,4,16,512]{3,2,1,0:T(8,128)}, f32[1,4,16,512]{3,2,1,0:T(8,128)S(1)}, u32[]{:S(2)}) copy-start(f32[1,4,16,512]{3,2,1,0:T(8,128)S(1)} %collective-permute-done.2.refs_4_) | copy-start | bytes 393220
  23.5 1.5 %collective-permute-start.4 = (f32[128,128]{1,0:T(8,128)}, f32[128,128]{1,0:T(8,128)S(1)}, u32[]{:S(2)}, u32[]{:S(2)}) collective-permute-start(f32[128,128]{1,0:T(8,128)} %get-tuple-element.9.refs_3_), channel_id=1, source_target_pairs={{0,1},{1,0},{2,3},{3,2},{4,5},{5,4},{6,7},{7,6},{8,9},{9,8},{10,11... | collective-permute-start | bytes 196616 | tf_op jit(solution)/shard_map/ppermute | solution.py:389
  25.0 0.6 %copy-start.4 = (f32[128,128]{1,0:T(8,128)}, f32[128,128]{1,0:T(8,128)S(1)}, u32[]{:S(2)}) copy-start(f32[128,128]{1,0:T(8,128)S(1)} %collective-permute-done.4.refs_4_) | copy-start | bytes 196612
  32.9 7.7 %collective-permute-start.5 = (f32[4,16,512]{2,1,0:T(8,128)}, f32[4,16,512]{2,1,0:T(8,128)S(1)}, u32[]{:S(2)}, u32[]{:S(2)}) collective-permute-start(f32[4,16,512]{2,1,0:T(8,128)} %get-tuple-element.10), channel_id=1, source_target_pairs={{0,2},{2,4},{4,6},{6,8},{8,10},{10,12},{12,14},{1,3},{3,5},{5,7},{... | collective-permute-start | bytes 393224 | tf_op jit(solution)/shard_map/ppermute | solution.py:56
  41.5 8.7 %collective-permute-start.6 = (f32[4,16,512]{2,1,0:T(8,128)S(1)}, f32[4,16,512]{2,1,0:T(8,128)S(1)}, u32[]{:S(2)}, u32[]{:S(2)}) collective-permute-start(f32[4,16,512]{2,1,0:T(8,128)S(1)} %add.9), channel_id=1, source_target_pairs={{0,4},{2,6},{4,8},{6,10},{8,12},{10,14},{1,5},{3,7},{5,9},{7,11},{... | collective-permute-start | bytes 393224 | tf_op jit(solution)/shard_map/ppermute | solution.py:56
  50.2 7.9 %collective-permute-start.7 = (f32[4,16,512]{2,1,0:T(8,128)S(1)}, f32[4,16,512]{2,1,0:T(8,128)S(1)}, u32[]{:S(2)}, u32[]{:S(2)}) collective-permute-start(f32[4,16,512]{2,1,0:T(8,128)S(1)} %add.10), channel_id=1, source_target_pairs={{0,8},{2,10},{4,12},{6,14},{1,9},{3,11},{5,13},{7,15},{16,24},{18,... | collective-permute-start | bytes 393224 | tf_op jit(solution)/shard_map/ppermute | solution.py:56

commit v10 on v8

--- a/solution.py
+++ b/solution.py
@@ -115,16 +115,13 @@
     ).astype(jnp.bfloat16)
 
 
-def step_scalars(levels_ref, level_count, shape):
-    def sigma(k):
-        level = jnp.full(shape, levels_ref[0, k].astype(jnp.float32))
-        fraction = level / jnp.float32(level_count - 1)
-        return SIGMA_TOP * jnp.exp(fraction * LOG_RATIO)
-
-    sigma_low = sigma(0)
-    sigma_high = sigma(1)
-    spread = sigma_low * sigma_low + 0.25
-    return sigma_low, sigma_high, spread
+def level_sigma(level, level_count, shape):
+    fraction = jnp.full(shape, level.astype(jnp.float32)) / jnp.float32(level_count - 1)
+    return SIGMA_TOP * jnp.exp(fraction * LOG_RATIO)
+
+
+def start_level(levels_ref, first_step):
+    return jnp.where(first_step, 0, levels_ref[0, 1])
 
 
 def trunk_kernel(
@@ -134,11 +131,13 @@
     hidden_sems, *, width, band_rows, bands, level_count,
 ):
     band = lax.axis_index("rows")
-    first_step = lax.axis_index("step") == 0
+    first_step = lax.axis_index("step") == lax.axis_size("step") - 1
     top_outside = band == 0
     bottom_outside = band == bands - 1
     channels = start_ref.shape[0]
-    sigma_low, _, spread = step_scalars(levels_ref, level_count, (1, width))
+    level = start_level(levels_ref, first_step)
+    sigma_low = level_sigma(level, level_count, (1, width))
+    spread = sigma_low * sigma_low + 0.25
     scale_in = lax.rsqrt(spread)
     for u in range(band_rows + 2 * HALO):
         v = u - HALO
@@ -154,7 +153,6 @@
         scaled = (scale_in * state).astype(jnp.bfloat16).astype(jnp.float32)
         inputs[0:channels, u * width : (u + 1) * width] = scaled
         inputs[channels:, u * width : (u + 1) * width] = cond.astype(jnp.float32)
-    level = levels_ref[0, 0]
     table = embed_ref[...].astype(jnp.float32)
     picked = jnp.where(lax.broadcasted_iota(jnp.int32, table.shape, 0) == level, table, 0.0)
     embed_row = jnp.sum(picked, axis=0, keepdims=True)
@@ -242,7 +240,7 @@
 
 
 def head_kernel(
-    levels_ref, hidden_ref, query_ref, stats_own_ref, stats_other_ref, mix_ref, out_w_ref,
+    levels_ref, next_levels_ref, hidden_ref, query_ref, stats_own_ref, stats_other_ref, mix_ref, out_w_ref,
     previous_ref, start_ref, denoised_ref, seed_ref, hidden_local, hidden_sems,
     *, width, band_rows, level_count,
 ):
@@ -254,8 +252,10 @@
         )
         copy.start()
         incoming.append(copy)
-    first_step = lax.axis_index("step") == 0
-    sigma_low, sigma_high, spread = step_scalars(levels_ref, level_count, (1, width))
+    first_step = lax.axis_index("step") == lax.axis_size("step") - 1
+    sigma_low = level_sigma(start_level(levels_ref, first_step), level_count, (1, width))
+    sigma_high = level_sigma(next_levels_ref[0, 1], level_count, (1, width))
+    spread = sigma_low * sigma_low + 0.25
     scale_skip = 0.25 / spread
     scale_out = 0.5 * sigma_low * lax.rsqrt(spread)
     sigma_gap = sigma_high - sigma_low
@@ -339,7 +339,8 @@
     steps = lax.axis_size("step")
     assert bands == 2
     swap = [(0, 1), (1, 0)]
-    previous = from_behind(iterates, "step", 1)
+    next_levels = lax.ppermute(step_levels, "step", [((h + 1) % steps, h) for h in range(steps)])
+    previous = iterates
     previous_other = lax.ppermute(previous, "rows", swap)
     start_other = lax.ppermute(window_start, "rows", swap)
     coarse_other = lax.ppermute(coarse, "rows", swap)
@@ -390,7 +391,7 @@
             jax.ShapeDtypeStruct(window_start.shape, jnp.float32),
             jax.ShapeDtypeStruct(window_start.shape, jnp.float32),
         ),
-        in_specs=[smem(), pl.BlockSpec(memory_space=pl.ANY)] + [vmem()] * 7,
+        in_specs=[smem(), smem(), pl.BlockSpec(memory_space=pl.ANY)] + [vmem()] * 7,
         out_specs=(vmem(), vmem()),
         scratch_shapes=[
             pltpu.VMEM((feat, pixels), jnp.float32),
@@ -398,11 +399,29 @@
         ],
     )
     denoised, seed = head(
-        step_levels, hidden, queries, stats_own, stats_other, mix_weight, output_weight.T,
+        step_levels, next_levels, hidden, queries, stats_own, stats_other, mix_weight, output_weight.T,
         previous, window_start,
     )
-    trajectory = prefix_sum(seed, "step")
+    trajectory, denoised = rotated_prefix(seed, denoised, "step")
     return (trajectory[None], denoised[None])
+
+
+def rotated_prefix(seed, denoised, axis):
+    steps = lax.axis_size(axis)
+    holder = lambda position: (position - 1) % steps
+    shift = 1
+    while 2 * shift < steps:
+        pairs = [(holder(p), holder(p + shift)) for p in range(steps - shift)]
+        seed = seed + lax.ppermute(seed, axis, pairs)
+        shift *= 2
+    moved = lax.ppermute(
+        jnp.concatenate([seed, denoised], axis=0), axis, [(h, (h + 1) % steps) for h in range(steps)]
+    )
+    channels = seed.shape[0]
+    if steps == 1:
+        return moved[:channels], moved[channels:]
+    far = lax.ppermute(seed, axis, [(holder(q), q + shift) for q in range(steps - shift)])
+    return moved[:channels] + far, moved[channels:]
 
 
 def solution(mesh):

time: 59.4 us -> 58.7 us (0.988); the launches traced: 58.5 us -> 58.5 us
  starting transfers between devices: 21.4 us -> 16.5 us
  waiting for transfers between devices: 13.5 us -> 17 us
  other arithmetic: 1.62 us -> 2.6 us
  local copies, waits for them, and re-layouts: 1.28 us -> 1.97 us
    ppermute x4 -> x5, starting transfers between devices: 20.7 us -> 15.1 us  [the longest x1 5.76 us: local(): lax.ppermute(step_levels, 'step', [((h + 1) % steps, h) for h in range(st...]
    ppermute x4 -> x5, waiting for transfers between devices: 10.8 us -> 15.7 us  [the longest x2 10.2 us: rotated_prefix(): seed = seed + lax.ppermute(seed, axis, pairs)]
    ppermute x1, waiting for transfers between devices: 1.33 us -> 0.01 us  [local(): stats_other = lax.ppermute(stats_own, 'rows', swap)]
    ppermute x1, waiting for transfers between devices: 1.31 us -> 0.18 us  [local(): previous_other = lax.ppermute(previous, 'rows', swap)]
    ppermute x1, waiting for transfers between devices: 0.01 us -> 1.05 us  [local(): start_other = lax.ppermute(window_start, 'rows', swap)]
    concatenate x0 -> x1, other arithmetic: none -> 0.93 us  [rotated_prefix(): jnp.concatenate([seed, denoised], axis=0)]
    unnamed x10, local copies, waits for them, and re-layouts: 1.28 us -> 1.97 us
  transfers between devices with their start and end apart: 8 -> 9, of which waited for: 6 -> 7; matrix products, arithmetic and copies ran while one was open for 0% -> 0% of each run, Pallas kernels for 0% -> 0%
where the time goes in v10:
time: 58.7 us; the launch traced here: 58.5 us
  Pallas kernels  19.8 us (34%)
  waiting for transfers between devices  17 us (29%)
  starting transfers between devices  16.5 us (28%)
  other arithmetic  2.6 us (4%)
  local copies, waits for them, and re-layouts  1.97 us (3%)
  between operations  0.69 us (1%)
    pallas_call x1, Pallas kernels, local(): trunk(step_levels, previous, window_start, start_other, previous_other, c...  13 us
    ppermute x2, waiting for transfers between devices, rotated_prefix(): seed = seed + lax.ppermute(seed, axis, pairs)  10.2 us
    pallas_call x1, Pallas kernels, local(): head(step_levels, next_levels, hidden, queries, stats_own, stats_other, m...  6.77 us
    ppermute x1, starting transfers between devices, local(): lax.ppermute(step_levels, 'step', [((h + 1) % steps, h) for h in range(st...  5.76 us
    ppermute x1, starting transfers between devices, rotated_prefix(): lax.ppermute(seed, axis, [(holder(q), q + shift) for q in range(steps - s...  3.64 us
    ppermute x2, starting transfers between devices, rotated_prefix(): seed = seed + lax.ppermute(seed, axis, pairs)  3.31 us
    ppermute x1, waiting for transfers between devices, rotated_prefix(): lax.ppermute(seed, axis, [(holder(q), q + shift) for q in range(steps - s...  2.5 us
    ppermute x1, starting transfers between devices, rotated_prefix(): lax.ppermute(jnp.concatenate([seed, denoised], axis=0), axis, [(h, (h + 1...  2.36 us
  transfers between devices with their start and end apart: 9, of which 7 were waited for; matrix products, arithmetic and copies ran while one was open for 0% of the time, Pallas kernels for 0%

profile of v10, /device:TPU:0, one launch (start us, length us, event | category | flops | bytes accessed | tf_op | source)
XLA Modules:
  0.0 58.5 jit_solution(7463850755441101124)
XLA Ops:
  0.6 0.5 collective-permute-start.3
  1.1 0.1 collective-permute-start.1
  1.2 0.4 collective-permute-start.2
  1.7 1.0 %collective-permute-done.1.refs_3_ = f32[4,16,512]{2,1,0:T(8,128)S(1)} collective-permute-done((f32[4,16,512]{2,1,0:T(8,128)}, f32[4,16,512]{2,1,0:T(8,128)S(1)}, u32[]{:S(2)}, u32[]{:S(2)}) %collective-permute-start.1) | collective-permute-done | bytes 131104 | tf_op jit(solution)/shard_map/ppermute | solution.py:345
  2.7 0.0 copy-start.1
  2.7 0.2 collective-permute-done.2.refs_4_
  2.9 0.0 copy-start.2
  2.9 0.0 collective-permute-done.3.refs_6_
  2.9 0.5 copy-done.1
  3.4 0.2 copy-done.2
  3.6 0.0 copy-start
  3.6 0.7 %copy-done = bf16[12,16,512]{2,1,0:T(8,128)(2,1)} copy-done((bf16[12,16,512]{2,1,0:T(8,128)(2,1)}, bf16[12,16,512]{2,1,0:T(8,128)(2,1)S(1)}, u32[]{:S(2)}) %copy-start) | copy-done | bytes 196632
  4.2 13.0 %shard_map.122 = (f32[128,8192]{1,0:T(8,128)}, f32[128,512]{1,0:T(8,128)}, f32[128,128]{1,0:T(8,128)}) custom-call(s32[1,2]{1,0:T(1,128)} %refs_0_.3, f32[1,4,16,512]{3,2,1,0:T(8,128)} %refs_8_.3, f32[4,16,512]{2,1,0:T(8,128)} %refs_9_.3, f32[4,16,512]{2,1,0:T(8,128)} %copy-done.1, f32[1,4,16,512]{3,2,1,0:T(8,128)} %copy-done.2, ...), custom_call_target="tpu_custom_call" | custom-call | tf_op jit(solution)/shard_map/pallas_call | solution.py:372
  17.2 0.4 collective-permute-start.4
  17.6 5.8 %collective-permute-start = (s32[1,2]{1,0:T(1,128)}, s32[1,2]{1,0:T(1,128)S(1)}, u32[]{:S(2)}, u32[]{:S(2)}) collective-permute-start(s32[1,2]{1,0:T(1,128)} %refs_0_.3), channel_id=1, source_target_pairs={{2,0},{4,2},{6,4},{8,6},{10,8},{12,10},{14,12},{0,14},{3,1},{5,3},... | collective-permute-start | bytes 32 | tf_op jit(solution)/shard_map/ppermute | solution.py:342
  23.4 1.4 %collective-permute-done.refs_1_ = s32[1,2]{1,0:T(1,128)S(1)} collective-permute-done((s32[1,2]{1,0:T(1,128)}, s32[1,2]{1,0:T(1,128)S(1)}, u32[]{:S(2)}, u32[]{:S(2)}) %collective-permute-start) | collective-permute-done | bytes 40 | tf_op jit(solution)/shard_map/ppermute | solution.py:342
  24.8 0.0 copy-start.4
  24.8 0.0 collective-permute-done.4.refs_5_
  24.8 0.0 copy-start.3
  24.8 0.5 copy-done.4
  25.3 0.1 copy-done.3
  25.5 6.8 %shard_map.123 = (f32[4,16,512]{2,1,0:T(8,128)}, f32[4,16,512]{2,1,0:T(8,128)}) custom-call(s32[1,2]{1,0:T(1,128)} %refs_0_.3, s32[1,2]{1,0:T(1,128)} %copy-done.4, f32[128,8192]{1,0:T(8,128)} %get-tuple-element.7.refs_2_, f32[128,512]{1,0:T(8,128)} %get-tuple-element.8.refs_3_, f32[128,128]{1,0:T(8,128)} %get-tuple-element.9.refs_4_, f32[128,128]{1,0:T(8,128)} %copy-done.3, ...), custom_call_target="tpu_custom_call" | custom-call | tf_op jit(solution)/shard_map/pallas_call | solution.py:401
  32.2 2.0 %collective-permute-start.5 = (f32[4,16,512]{2,1,0:T(8,128)}, f32[4,16,512]{2,1,0:T(8,128)S(1)}, u32[]{:S(2)}, u32[]{:S(2)}) collective-permute-start(f32[4,16,512]{2,1,0:T(8,128)} %get-tuple-element.10), channel_id=1, source_target_pairs={{14,0},{0,2},{2,4},{4,6},{6,8},{8,10},{10,12},{15,1},{1,3},{3,5},{... | collective-permute-start | bytes 393224 | tf_op jit(solution)/shard_map/ppermute | solution.py:415
  34.3 7.7 %collective-permute-done.5 = f32[4,16,512]{2,1,0:T(8,128)S(1)} collective-permute-done((f32[4,16,512]{2,1,0:T(8,128)}, f32[4,16,512]{2,1,0:T(8,128)S(1)}, u32[]{:S(2)}, u32[]{:S(2)}) %collective-permute-start.5) | collective-permute-done | bytes 131104 | tf_op jit(solution)/shard_map/ppermute | solution.py:415
  42.0 0.9 %add.9 = f32[4,16,512]{2,1,0:T(8,128)S(1)} add(f32[4,16,512]{2,1,0:T(8,128)} %get-tuple-element.10, f32[4,16,512]{2,1,0:T(8,128)S(1)} %collective-permute-done.5) | non-fusion elementwise | flops 32768 | bytes 393216 | tf_op jit(solution)/shard_map/add | solution.py:415
  42.9 1.3 %collective-permute-start.6 = (f32[4,16,512]{2,1,0:T(8,128)S(1)}, f32[4,16,512]{2,1,0:T(8,128)S(1)}, u32[]{:S(2)}, u32[]{:S(2)}) collective-permute-start(f32[4,16,512]{2,1,0:T(8,128)S(1)} %add.9), channel_id=1, source_target_pairs={{14,2},{0,4},{2,6},{4,8},{6,10},{8,12},{15,3},{1,5},{3,7},{5,9},{7... | collective-permute-start | bytes 393224 | tf_op jit(solution)/shard_map/ppermute | solution.py:415
  44.2 2.5 %collective-permute-done.6 = f32[4,16,512]{2,1,0:T(8,128)S(1)} collective-permute-done((f32[4,16,512]{2,1,0:T(8,128)S(1)}, f32[4,16,512]{2,1,0:T(8,128)S(1)}, u32[]{:S(2)}, u32[]{:S(2)}) %collective-permute-start.6) | collective-permute-done | bytes 131104 | tf_op jit(solution)/shard_map/ppermute | solution.py:415
  46.8 0.9 %pad_maximum_fusion = f32[8,16,512]{2,1,0:T(8,128)S(1)} fusion(f32[4,16,512]{2,1,0:T(8,128)} %get-tuple-element.11, f32[4,16,512]{2,1,0:T(8,128)S(1)} %add.10), kind=kLoop, calls=%fused_computation | loop fusion | flops 65536 | bytes 524288 | tf_op jit(solution)/shard_map/concatenate | solution.py:418
  47.7 2.4 %collective-permute-start.7 = (f32[8,16,512]{2,1,0:T(8,128)S(1)}, f32[8,16,512]{2,1,0:T(8,128)S(1)}, u32[]{:S(2)}, u32[]{:S(2)}) collective-permute-start(f32[8,16,512]{2,1,0:T(8,128)S(1)} %pad_maximum_fusion), channel_id=1, source_target_pairs={{0,2},{2,4},{4,6},{6,8},{8,10},{10,12},{12,14},{14,0},{1,3},{3,5},... | collective-permute-start | bytes 786440 | tf_op jit(solution)/shard_map/ppermute | solution.py:417
  50.0 3.6 %collective-permute-start.8 = (f32[4,16,512]{2,1,0:T(8,128)S(1)}, f32[4,16,512]{2,1,0:T(8,128)S(1)}, u32[]{:S(2)}, u32[]{:S(2)}) collective-permute-start(f32[4,16,512]{2,1,0:T(8,128)S(1)} %add.10), channel_id=1, source_target_pairs={{14,8},{0,10},{2,12},{4,14},{15,9},{1,11},{3,13},{5,15},{30,24},{1... | collective-permute-start | bytes 393224 | tf_op jit(solution)/shard_map/ppermute | solution.py:423
  53.7 2.5 %collective-permute-done.8 = f32[4,16,512]{2,1,0:T(8,128)S(1)} collective-permute-done((f32[4,16,512]{2,1,0:T(8,128)S(1)}, f32[4,16,512]{2,1,0:T(8,128)S(1)}, u32[]{:S(2)}, u32[]{:S(2)}) %collective-permute-start.8) | collective-permute-done | bytes 131104 | tf_op jit(solution)/shard_map/ppermute | solution.py:423
  56.2 1.5 %collective-permute-done.7 = f32[8,16,512]{2,1,0:T(8,128)S(1)} collective-permute-done((f32[8,16,512]{2,1,0:T(8,128)S(1)}, f32[8,16,512]{2,1,0:T(8,128)S(1)}, u32[]{:S(2)}, u32[]{:S(2)}) %collective-permute-start.7) | collective-permute-done | bytes 262176 | tf_op jit(solution)/shard_map/ppermute | solution.py:417
  57.8 0.7 %slice_bitcast_fusion = (f32[1,4,16,512]{3,2,1,0:T(8,128)}, f32[1,4,16,512]{3,2,1,0:T(8,128)}) fusion(f32[8,16,512]{2,1,0:T(8,128)S(1)} %collective-permute-done.7, f32[4,16,512]{2,1,0:T(8,128)S(1)} %collective-permute-done.8), kind=kLoop, calls=%fused_computation.1 | loop fusion | flops 32768 | bytes 655360 | tf_op jit(solution)/shard_map/broadcast_in_dim | solution.py:406
  (1 shorter events, 0.0 us)
Async XLA Ops:
  0.6 2.3 %collective-permute-start.3 = (bf16[12,16,512]{2,1,0:T(8,128)(2,1)}, bf16[12,16,512]{2,1,0:T(8,128)(2,1)S(1)}, u32[]{:S(2)}, u32[]{:S(2)}) collective-permute-start(bf16[12,16,512]{2,1,0:T(8,128)(2,1)} %refs_5_.1), channel_id=1, source_target_pairs={{0,1},{1,0},{2,3},{3,2},{4,5},{5,4},{6,7},{7,6},{8,9},{9,8},{10,11... | collective-permute-start | bytes 589832 | tf_op jit(solution)/shard_map/ppermute | solution.py:346
  1.1 1.6 %collective-permute-start.1 = (f32[4,16,512]{2,1,0:T(8,128)}, f32[4,16,512]{2,1,0:T(8,128)S(1)}, u32[]{:S(2)}, u32[]{:S(2)}) collective-permute-start(f32[4,16,512]{2,1,0:T(8,128)} %refs_9_.3), channel_id=1, source_target_pairs={{0,1},{1,0},{2,3},{3,2},{4,5},{5,4},{6,7},{7,6},{8,9},{9,8},{10,11... | collective-permute-start | bytes 393224 | tf_op jit(solution)/shard_map/ppermute | solution.py:345
  1.2 1.7 %collective-permute-start.2 = (f32[1,4,16,512]{3,2,1,0:T(8,128)}, f32[1,4,16,512]{3,2,1,0:T(8,128)S(1)}, u32[]{:S(2)}, u32[]{:S(2)}) collective-permute-start(f32[1,4,16,512]{3,2,1,0:T(8,128)} %refs_8_.3), channel_id=1, source_target_pairs={{0,1},{1,0},{2,3},{3,2},{4,5},{5,4},{6,7},{7,6},{8,9},{9,8},{10,11... | collective-permute-start | bytes 393224 | tf_op jit(solution)/shard_map/ppermute | solution.py:344
  2.7 0.7 %copy-start.1 = (f32[4,16,512]{2,1,0:T(8,128)}, f32[4,16,512]{2,1,0:T(8,128)S(1)}, u32[]{:S(2)}) copy-start(f32[4,16,512]{2,1,0:T(8,128)S(1)} %collective-permute-done.1.refs_3_) | copy-start | bytes 393220
  2.9 0.7 %copy-start.2 = (f32[1,4,16,512]{3,2,1,0:T(8,128)}, f32[1,4,16,512]{3,2,1,0:T(8,128)S(1)}, u32[]{:S(2)}) copy-start(f32[1,4,16,512]{3,2,1,0:T(8,128)S(1)} %collective-permute-done.2.refs_4_) | copy-start | bytes 393220
  3.6 0.7 %copy-start = (bf16[12,16,512]{2,1,0:T(8,128)(2,1)}, bf16[12,16,512]{2,1,0:T(8,128)(2,1)S(1)}, u32[]{:S(2)}) copy-start(bf16[12,16,512]{2,1,0:T(8,128)(2,1)S(1)} %collective-permute-done.3.refs_6_) | copy-start | bytes 589828
  17.2 7.6 %collective-permute-start.4 = (f32[128,128]{1,0:T(8,128)}, f32[128,128]{1,0:T(8,128)S(1)}, u32[]{:S(2)}, u32[]{:S(2)}) collective-permute-start(f32[128,128]{1,0:T(8,128)} %get-tuple-element.9.refs_4_), channel_id=1, source_target_pairs={{0,1},{1,0},{2,3},{3,2},{4,5},{5,4},{6,7},{7,6},{8,9},{9,8},{10,11... | collective-permute-start | bytes 196616 | tf_op jit(solution)/shard_map/ppermute | solution.py:386
  17.6 7.2 %collective-permute-start = (s32[1,2]{1,0:T(1,128)}, s32[1,2]{1,0:T(1,128)S(1)}, u32[]{:S(2)}, u32[]{:S(2)}) collective-permute-start(s32[1,2]{1,0:T(1,128)} %refs_0_.3), channel_id=1, source_target_pairs={{2,0},{4,2},{6,4},{8,6},{10,8},{12,10},{14,12},{0,14},{3,1},{5,3},... | collective-permute-start | bytes 32 | tf_op jit(solution)/shard_map/ppermute | solution.py:342
  24.8 0.5 copy-start.4
  24.8 0.6 %copy-start.3 = (f32[128,128]{1,0:T(8,128)}, f32[128,128]{1,0:T(8,128)S(1)}, u32[]{:S(2)}) copy-start(f32[128,128]{1,0:T(8,128)S(1)} %collective-permute-done.4.refs_5_) | copy-start | bytes 196612
  32.2 9.8 %collective-permute-start.5 = (f32[4,16,512]{2,1,0:T(8,128)}, f32[4,16,512]{2,1,0:T(8,128)S(1)}, u32[]{:S(2)}, u32[]{:S(2)}) collective-permute-start(f32[4,16,512]{2,1,0:T(8,128)} %get-tuple-element.10), channel_id=1, source_target_pairs={{14,0},{0,2},{2,4},{4,6},{6,8},{8,10},{10,12},{15,1},{1,3},{3,5},{... | collective-permute-start | bytes 393224 | tf_op jit(solution)/shard_map/ppermute | solution.py:415
  42.9 3.8 %collective-permute-start.6 = (f32[4,16,512]{2,1,0:T(8,128)S(1)}, f32[4,16,512]{2,1,0:T(8,128)S(1)}, u32[]{:S(2)}, u32[]{:S(2)}) collective-permute-start(f32[4,16,512]{2,1,0:T(8,128)S(1)} %add.9), channel_id=1, source_target_pairs={{14,2},{0,4},{2,6},{4,8},{6,10},{8,12},{15,3},{1,5},{3,7},{5,9},{7... | collective-permute-start | bytes 393224 | tf_op jit(solution)/shard_map/ppermute | solution.py:415
  47.7 10.1 %collective-permute-start.7 = (f32[8,16,512]{2,1,0:T(8,128)S(1)}, f32[8,16,512]{2,1,0:T(8,128)S(1)}, u32[]{:S(2)}, u32[]{:S(2)}) collective-permute-start(f32[8,16,512]{2,1,0:T(8,128)S(1)} %pad_maximum_fusion), channel_id=1, source_target_pairs={{0,2},{2,4},{4,6},{6,8},{8,10},{10,12},{12,14},{14,0},{1,3},{3,5},... | collective-permute-start | bytes 786440 | tf_op jit(solution)/shard_map/ppermute | solution.py:417
  50.0 6.2 %collective-permute-start.8 = (f32[4,16,512]{2,1,0:T(8,128)S(1)}, f32[4,16,512]{2,1,0:T(8,128)S(1)}, u32[]{:S(2)}, u32[]{:S(2)}) collective-permute-start(f32[4,16,512]{2,1,0:T(8,128)S(1)} %add.10), channel_id=1, source_target_pairs={{14,8},{0,10},{2,12},{4,14},{15,9},{1,11},{3,13},{5,15},{30,24},{1... | collective-permute-start | bytes 393224 | tf_op jit(solution)/shard_map/ppermute | solution.py:423

commit v11 on v10

--- a/solution.py
+++ b/solution.py
@@ -125,7 +125,7 @@
 
 
 def trunk_kernel(
-    levels_ref, previous_ref, start_ref, start_other_ref, previous_other_ref, coarse_ref,
+    levels_ref, next_levels_ref, previous_ref, start_ref, start_other_ref, previous_other_ref, coarse_ref,
     coarse_other_ref, lift_ref, embed_ref, first_ref, second_ref, project_ref,
     hidden_ref, query_ref, stats_ref, inputs, act_first, lifted_keep, act_next, hidden_local,
     hidden_sems, *, width, band_rows, bands, level_count,
@@ -358,8 +358,13 @@
             jax.ShapeDtypeStruct((feat, tokens), jnp.float32),
             jax.ShapeDtypeStruct((feat, 2 * HEAD_DIM), jnp.float32),
         ),
-        in_specs=[smem()] + [vmem()] * 11,
+        in_specs=[smem(), smem()] + [vmem()] * 11,
         out_specs=(pl.BlockSpec(memory_space=pl.ANY), vmem(), vmem()),
+        cost_estimate=pl.CostEstimate(
+            flops=2 * (3 * feat) ** 2 * (2 * band_rows + 2) * width,
+            transcendentals=3 * feat * (band_rows + 2 * HALO) * width,
+            bytes_accessed=6 * feat * pixels,
+        ),
         scratch_shapes=[
             pltpu.VMEM((channels + coarse.shape[0], (band_rows + 2 * HALO) * width), jnp.float32),
             pltpu.VMEM((feat, (band_rows + 2 * HALO) * width), jnp.bfloat16),
@@ -371,6 +376,7 @@
     )
     hidden, queries, stats_own = trunk(
         step_levels,
+        next_levels,
         previous,
         window_start,
         start_other,
@@ -393,6 +399,11 @@
         ),
         in_specs=[smem(), smem(), pl.BlockSpec(memory_space=pl.ANY)] + [vmem()] * 7,
         out_specs=(vmem(), vmem()),
+        cost_estimate=pl.CostEstimate(
+            flops=8 * feat * feat * pixels,
+            transcendentals=2 * feat * pixels,
+            bytes_accessed=5 * feat * pixels,
+        ),
         scratch_shapes=[
             pltpu.VMEM((feat, pixels), jnp.float32),
             pltpu.SemaphoreType.DMA((band_rows // 4,)),

time: 58.7 us -> 60.4 us (1.029)
  waiting for transfers between devices: 17 us -> 18.8 us
    ppermute x1, waiting for transfers between devices: 0.01 us -> 1.45 us  [local(): stats_other = lax.ppermute(stats_own, 'rows', swap)]
    ppermute x1, waiting for transfers between devices: 1.54 us -> 2.61 us  [rotated_prefix(): lax.ppermute(jnp.concatenate([seed, denoised], axis=0), axis, [(h, (h + 1...]
    ppermute x1, waiting for transfers between devices: 1.05 us -> 0.01 us  [local(): start_other = lax.ppermute(window_start, 'rows', swap)]
  transfers between devices with their start and end apart: 9 -> 9, of which waited for: 7 -> 6; matrix products, arithmetic and copies ran while one was open for 0% -> 0% of each run, Pallas kernels for 0% -> 0%
where the time goes in v11:
time: 60.4 us; the launch traced here: 60.1 us
  Pallas kernels  19.9 us (33%)
  waiting for transfers between devices  18.8 us (31%)
  starting transfers between devices  16 us (26%)
  other arithmetic  2.6 us (4%)
  local copies, waits for them, and re-layouts  1.99 us (3%)
  between operations  0.72 us (1%)
    pallas_call x1, Pallas kernels, local(): trunk(step_levels, next_levels, previous, window_start, start_other, prev...  13 us
    ppermute x2, waiting for transfers between devices, rotated_prefix(): seed = seed + lax.ppermute(seed, axis, pairs)  10.8 us
    pallas_call x1, Pallas kernels, local(): head(step_levels, next_levels, hidden, queries, stats_own, stats_other, m...  6.95 us
    ppermute x1, starting transfers between devices, local(): lax.ppermute(step_levels, 'step', [((h + 1) % steps, h) for h in range(st...  5.6 us
    ppermute x1, starting transfers between devices, rotated_prefix(): lax.ppermute(seed, axis, [(holder(q), q + shift) for q in range(steps - s...  3.49 us
    ppermute x2, starting transfers between devices, rotated_prefix(): seed = seed + lax.ppermute(seed, axis, pairs)  3.31 us
    ppermute x1, waiting for transfers between devices, rotated_prefix(): lax.ppermute(jnp.concatenate([seed, denoised], axis=0), axis, [(h, (h + 1...  2.61 us
    ppermute x1, waiting for transfers between devices, rotated_prefix(): lax.ppermute(seed, axis, [(holder(q), q + shift) for q in range(steps - s...  2.51 us
  transfers between devices with their start and end apart: 9, of which 6 were waited for; matrix products, arithmetic and copies ran while one was open for 0% of the time, Pallas kernels for 0%

profile of v11, /device:TPU:0, one launch (start us, length us, event | category | flops | bytes accessed | tf_op | source)
XLA Modules:
  0.0 60.1 jit_solution(6612148727331851781)
XLA Ops:
  0.6 0.5 collective-permute-start.3
  1.1 0.1 collective-permute-start.2
  1.2 0.4 collective-permute-start.1
  1.7 5.6 %collective-permute-start = (s32[1,2]{1,0:T(1,128)}, s32[1,2]{1,0:T(1,128)S(1)}, u32[]{:S(2)}, u32[]{:S(2)}) collective-permute-start(s32[1,2]{1,0:T(1,128)} %refs_0_.3), channel_id=1, source_target_pairs={{2,0},{4,2},{6,4},{8,6},{10,8},{12,10},{14,12},{0,14},{3,1},{5,3},... | collective-permute-start | bytes 32 | tf_op jit(solution)/shard_map/ppermute | solution.py:342
  7.3 1.4 %collective-permute-done.refs_1_ = s32[1,2]{1,0:T(1,128)S(1)} collective-permute-done((s32[1,2]{1,0:T(1,128)}, s32[1,2]{1,0:T(1,128)S(1)}, u32[]{:S(2)}, u32[]{:S(2)}) %collective-permute-start) | collective-permute-done | bytes 40 | tf_op jit(solution)/shard_map/ppermute | solution.py:342
  8.7 0.0 copy-start.1
  8.7 0.0 collective-permute-done.2.refs_5_
  8.7 0.0 copy-start.3
  8.7 0.0 collective-permute-done.1.refs_4_
  8.7 0.0 copy-start.4
  8.7 0.0 collective-permute-done.3.refs_7_
  8.7 0.5 copy-done.1
  9.3 0.1 copy-done.3
  9.4 0.0 copy-done.4
  9.4 0.0 copy-start.2
  9.4 0.7 %copy-done.2 = bf16[12,16,512]{2,1,0:T(8,128)(2,1)} copy-done((bf16[12,16,512]{2,1,0:T(8,128)(2,1)}, bf16[12,16,512]{2,1,0:T(8,128)(2,1)S(1)}, u32[]{:S(2)}) %copy-start.2) | copy-done | bytes 196632
  10.1 13.0 %shard_map.122 = (f32[128,8192]{1,0:T(8,128)}, f32[128,512]{1,0:T(8,128)}, f32[128,128]{1,0:T(8,128)}) custom-call(s32[1,2]{1,0:T(1,128)} %refs_0_.3, s32[1,2]{1,0:T(1,128)} %copy-done.1, f32[1,4,16,512]{3,2,1,0:T(8,128)} %refs_8_.3, f32[4,16,512]{2,1,0:T(8,128)} %refs_9_.3, f32[4,16,512]{2,1,0:T(8,128)} %copy-done.4, f32[1,4,16,512]{3,2,1,0:T(8,128)} %copy-done.3, ...), custom_call_target="tpu_custom_call" | custom-call | flops 5133828096 | bytes 6291456 | tf_op jit(solution)/shard_map/pallas_call | solution.py:377
  23.1 0.1 collective-permute-start.4
  23.2 1.5 %collective-permute-done.4.refs_5_ = f32[128,128]{1,0:T(8,128)S(1)} collective-permute-done((f32[128,128]{1,0:T(8,128)}, f32[128,128]{1,0:T(8,128)S(1)}, u32[]{:S(2)}, u32[]{:S(2)}) %collective-permute-start.4) | collective-permute-done | bytes 65568 | tf_op jit(solution)/shard_map/ppermute | solution.py:392
  24.6 0.0 copy-start
  24.6 0.6 %copy-done = f32[128,128]{1,0:T(8,128)} copy-done((f32[128,128]{1,0:T(8,128)}, f32[128,128]{1,0:T(8,128)S(1)}, u32[]{:S(2)}) %copy-start) | copy-done | bytes 65560
  25.2 7.0 %shard_map.123 = (f32[4,16,512]{2,1,0:T(8,128)}, f32[4,16,512]{2,1,0:T(8,128)}) custom-call(s32[1,2]{1,0:T(1,128)} %refs_0_.3, s32[1,2]{1,0:T(1,128)} %copy-done.1, f32[128,8192]{1,0:T(8,128)} %get-tuple-element.7.refs_2_, f32[128,512]{1,0:T(8,128)} %get-tuple-element.8.refs_3_, f32[128,128]{1,0:T(8,128)} %get-tuple-element.9.refs_4_, f32[128,128]{1,0:T(8,128)} %copy-done, ...), custom_call_target="tpu_custom_call" | custom-call | flops 1073741824 | bytes 5242880 | tf_op jit(solution)/shard_map/pallas_call | solution.py:412
  32.2 2.0 %collective-permute-start.5 = (f32[4,16,512]{2,1,0:T(8,128)}, f32[4,16,512]{2,1,0:T(8,128)S(1)}, u32[]{:S(2)}, u32[]{:S(2)}) collective-permute-start(f32[4,16,512]{2,1,0:T(8,128)} %get-tuple-element.10), channel_id=1, source_target_pairs={{14,0},{0,2},{2,4},{4,6},{6,8},{8,10},{10,12},{15,1},{1,3},{3,5},{... | collective-permute-start | bytes 393224 | tf_op jit(solution)/shard_map/ppermute | solution.py:426
  34.2 8.3 %collective-permute-done.5 = f32[4,16,512]{2,1,0:T(8,128)S(1)} collective-permute-done((f32[4,16,512]{2,1,0:T(8,128)}, f32[4,16,512]{2,1,0:T(8,128)S(1)}, u32[]{:S(2)}, u32[]{:S(2)}) %collective-permute-start.5) | collective-permute-done | bytes 131104 | tf_op jit(solution)/shard_map/ppermute | solution.py:426
  42.6 0.9 %add.9 = f32[4,16,512]{2,1,0:T(8,128)S(1)} add(f32[4,16,512]{2,1,0:T(8,128)} %get-tuple-element.10, f32[4,16,512]{2,1,0:T(8,128)S(1)} %collective-permute-done.5) | non-fusion elementwise | flops 32768 | bytes 393216 | tf_op jit(solution)/shard_map/add | solution.py:426
  43.5 1.3 %collective-permute-start.6 = (f32[4,16,512]{2,1,0:T(8,128)S(1)}, f32[4,16,512]{2,1,0:T(8,128)S(1)}, u32[]{:S(2)}, u32[]{:S(2)}) collective-permute-start(f32[4,16,512]{2,1,0:T(8,128)S(1)} %add.9), channel_id=1, source_target_pairs={{14,2},{0,4},{2,6},{4,8},{6,10},{8,12},{15,3},{1,5},{3,7},{5,9},{7... | collective-permute-start | bytes 393224 | tf_op jit(solution)/shard_map/ppermute | solution.py:426
  44.8 2.5 %collective-permute-done.6 = f32[4,16,512]{2,1,0:T(8,128)S(1)} collective-permute-done((f32[4,16,512]{2,1,0:T(8,128)S(1)}, f32[4,16,512]{2,1,0:T(8,128)S(1)}, u32[]{:S(2)}, u32[]{:S(2)}) %collective-permute-start.6) | collective-permute-done | bytes 131104 | tf_op jit(solution)/shard_map/ppermute | solution.py:426
  47.3 0.9 %pad_maximum_fusion = f32[8,16,512]{2,1,0:T(8,128)S(1)} fusion(f32[4,16,512]{2,1,0:T(8,128)} %get-tuple-element.11, f32[4,16,512]{2,1,0:T(8,128)S(1)} %add.10), kind=kLoop, calls=%fused_computation | loop fusion | flops 65536 | bytes 524288 | tf_op jit(solution)/shard_map/concatenate | solution.py:429
  48.3 2.5 %collective-permute-start.7 = (f32[8,16,512]{2,1,0:T(8,128)S(1)}, f32[8,16,512]{2,1,0:T(8,128)S(1)}, u32[]{:S(2)}, u32[]{:S(2)}) collective-permute-start(f32[8,16,512]{2,1,0:T(8,128)S(1)} %pad_maximum_fusion), channel_id=1, source_target_pairs={{0,2},{2,4},{4,6},{6,8},{8,10},{10,12},{12,14},{14,0},{1,3},{3,5},... | collective-permute-start | bytes 786440 | tf_op jit(solution)/shard_map/ppermute | solution.py:428
  50.8 3.5 %collective-permute-start.8 = (f32[4,16,512]{2,1,0:T(8,128)S(1)}, f32[4,16,512]{2,1,0:T(8,128)S(1)}, u32[]{:S(2)}, u32[]{:S(2)}) collective-permute-start(f32[4,16,512]{2,1,0:T(8,128)S(1)} %add.10), channel_id=1, source_target_pairs={{14,8},{0,10},{2,12},{4,14},{15,9},{1,11},{3,13},{5,15},{30,24},{1... | collective-permute-start | bytes 393224 | tf_op jit(solution)/shard_map/ppermute | solution.py:434
  54.3 2.5 %collective-permute-done.8 = f32[4,16,512]{2,1,0:T(8,128)S(1)} collective-permute-done((f32[4,16,512]{2,1,0:T(8,128)S(1)}, f32[4,16,512]{2,1,0:T(8,128)S(1)}, u32[]{:S(2)}, u32[]{:S(2)}) %collective-permute-start.8) | collective-permute-done | bytes 131104 | tf_op jit(solution)/shard_map/ppermute | solution.py:434
  56.8 2.6 %collective-permute-done.7 = f32[8,16,512]{2,1,0:T(8,128)S(1)} collective-permute-done((f32[8,16,512]{2,1,0:T(8,128)S(1)}, f32[8,16,512]{2,1,0:T(8,128)S(1)}, u32[]{:S(2)}, u32[]{:S(2)}) %collective-permute-start.7) | collective-permute-done | bytes 262176 | tf_op jit(solution)/shard_map/ppermute | solution.py:428
  59.4 0.7 %slice_bitcast_fusion = (f32[1,4,16,512]{3,2,1,0:T(8,128)}, f32[1,4,16,512]{3,2,1,0:T(8,128)}) fusion(f32[8,16,512]{2,1,0:T(8,128)S(1)} %collective-permute-done.7, f32[4,16,512]{2,1,0:T(8,128)S(1)} %collective-permute-done.8), kind=kLoop, calls=%fused_computation.1 | loop fusion | flops 32768 | bytes 655360 | tf_op jit(solution)/shard_map/broadcast_in_dim | solution.py:417
  (1 shorter events, 0.0 us)
Async XLA Ops:
  0.6 8.1 %collective-permute-start.3 = (bf16[12,16,512]{2,1,0:T(8,128)(2,1)}, bf16[12,16,512]{2,1,0:T(8,128)(2,1)S(1)}, u32[]{:S(2)}, u32[]{:S(2)}) collective-permute-start(bf16[12,16,512]{2,1,0:T(8,128)(2,1)} %refs_6_.2), channel_id=1, source_target_pairs={{0,1},{1,0},{2,3},{3,2},{4,5},{5,4},{6,7},{7,6},{8,9},{9,8},{10,11... | collective-permute-start | bytes 589832 | tf_op jit(solution)/shard_map/ppermute | solution.py:346
  1.1 7.5 %collective-permute-start.2 = (f32[1,4,16,512]{3,2,1,0:T(8,128)}, f32[1,4,16,512]{3,2,1,0:T(8,128)S(1)}, u32[]{:S(2)}, u32[]{:S(2)}) collective-permute-start(f32[1,4,16,512]{3,2,1,0:T(8,128)} %refs_8_.3), channel_id=1, source_target_pairs={{0,1},{1,0},{2,3},{3,2},{4,5},{5,4},{6,7},{7,6},{8,9},{9,8},{10,11... | collective-permute-start | bytes 393224 | tf_op jit(solution)/shard_map/ppermute | solution.py:344
  1.2 7.5 %collective-permute-start.1 = (f32[4,16,512]{2,1,0:T(8,128)}, f32[4,16,512]{2,1,0:T(8,128)S(1)}, u32[]{:S(2)}, u32[]{:S(2)}) collective-permute-start(f32[4,16,512]{2,1,0:T(8,128)} %refs_9_.3), channel_id=1, source_target_pairs={{0,1},{1,0},{2,3},{3,2},{4,5},{5,4},{6,7},{7,6},{8,9},{9,8},{10,11... | collective-permute-start | bytes 393224 | tf_op jit(solution)/shard_map/ppermute | solution.py:345
  1.7 7.0 %collective-permute-start = (s32[1,2]{1,0:T(1,128)}, s32[1,2]{1,0:T(1,128)S(1)}, u32[]{:S(2)}, u32[]{:S(2)}) collective-permute-start(s32[1,2]{1,0:T(1,128)} %refs_0_.3), channel_id=1, source_target_pairs={{2,0},{4,2},{6,4},{8,6},{10,8},{12,10},{14,12},{0,14},{3,1},{5,3},... | collective-permute-start | bytes 32 | tf_op jit(solution)/shard_map/ppermute | solution.py:342
  8.7 0.6 copy-start.1
  8.7 0.7 %copy-start.3 = (f32[1,4,16,512]{3,2,1,0:T(8,128)}, f32[1,4,16,512]{3,2,1,0:T(8,128)S(1)}, u32[]{:S(2)}) copy-start(f32[1,4,16,512]{3,2,1,0:T(8,128)S(1)} %collective-permute-done.2.refs_5_) | copy-start | bytes 393220
  8.7 0.7 %copy-start.4 = (f32[4,16,512]{2,1,0:T(8,128)}, f32[4,16,512]{2,1,0:T(8,128)S(1)}, u32[]{:S(2)}) copy-start(f32[4,16,512]{2,1,0:T(8,128)S(1)} %collective-permute-done.1.refs_4_) | copy-start | bytes 393220
  9.4 0.7 %copy-start.2 = (bf16[12,16,512]{2,1,0:T(8,128)(2,1)}, bf16[12,16,512]{2,1,0:T(8,128)(2,1)S(1)}, u32[]{:S(2)}) copy-start(bf16[12,16,512]{2,1,0:T(8,128)(2,1)S(1)} %collective-permute-done.3.refs_7_) | copy-start | bytes 589828
  23.1 1.5 %collective-permute-start.4 = (f32[128,128]{1,0:T(8,128)}, f32[128,128]{1,0:T(8,128)S(1)}, u32[]{:S(2)}, u32[]{:S(2)}) collective-permute-start(f32[128,128]{1,0:T(8,128)} %get-tuple-element.9.refs_4_), channel_id=1, source_target_pairs={{0,1},{1,0},{2,3},{3,2},{4,5},{5,4},{6,7},{7,6},{8,9},{9,8},{10,11... | collective-permute-start | bytes 196616 | tf_op jit(solution)/shard_map/ppermute | solution.py:392
  24.6 0.6 %copy-start = (f32[128,128]{1,0:T(8,128)}, f32[128,128]{1,0:T(8,128)S(1)}, u32[]{:S(2)}) copy-start(f32[128,128]{1,0:T(8,128)S(1)} %collective-permute-done.4.refs_5_) | copy-start | bytes 196612
  32.2 10.4 %collective-permute-start.5 = (f32[4,16,512]{2,1,0:T(8,128)}, f32[4,16,512]{2,1,0:T(8,128)S(1)}, u32[]{:S(2)}, u32[]{:S(2)}) collective-permute-start(f32[4,16,512]{2,1,0:T(8,128)} %get-tuple-element.10), channel_id=1, source_target_pairs={{14,0},{0,2},{2,4},{4,6},{6,8},{8,10},{10,12},{15,1},{1,3},{3,5},{... | collective-permute-start | bytes 393224 | tf_op jit(solution)/shard_map/ppermute | solution.py:426
  43.5 3.8 %collective-permute-start.6 = (f32[4,16,512]{2,1,0:T(8,128)S(1)}, f32[4,16,512]{2,1,0:T(8,128)S(1)}, u32[]{:S(2)}, u32[]{:S(2)}) collective-permute-start(f32[4,16,512]{2,1,0:T(8,128)S(1)} %add.9), channel_id=1, source_target_pairs={{14,2},{0,4},{2,6},{4,8},{6,10},{8,12},{15,3},{1,5},{3,7},{5,9},{7... | collective-permute-start | bytes 393224 | tf_op jit(solution)/shard_map/ppermute | solution.py:426
  48.3 11.1 %collective-permute-start.7 = (f32[8,16,512]{2,1,0:T(8,128)S(1)}, f32[8,16,512]{2,1,0:T(8,128)S(1)}, u32[]{:S(2)}, u32[]{:S(2)}) collective-permute-start(f32[8,16,512]{2,1,0:T(8,128)S(1)} %pad_maximum_fusion), channel_id=1, source_target_pairs={{0,2},{2,4},{4,6},{6,8},{8,10},{10,12},{12,14},{14,0},{1,3},{3,5},... | collective-permute-start | bytes 786440 | tf_op jit(solution)/shard_map/ppermute | solution.py:428
  50.8 6.0 %collective-permute-start.8 = (f32[4,16,512]{2,1,0:T(8,128)S(1)}, f32[4,16,512]{2,1,0:T(8,128)S(1)}, u32[]{:S(2)}, u32[]{:S(2)}) collective-permute-start(f32[4,16,512]{2,1,0:T(8,128)S(1)} %add.10), channel_id=1, source_target_pairs={{14,8},{0,10},{2,12},{4,14},{15,9},{1,11},{3,13},{5,15},{30,24},{1... | collective-permute-start | bytes 393224 | tf_op jit(solution)/shard_map/ppermute | solution.py:434

commit v12 on v10

--- a/solution.py
+++ b/solution.py
@@ -128,7 +128,7 @@
     levels_ref, previous_ref, start_ref, start_other_ref, previous_other_ref, coarse_ref,
     coarse_other_ref, lift_ref, embed_ref, first_ref, second_ref, project_ref,
     hidden_ref, query_ref, stats_ref, inputs, act_first, lifted_keep, act_next, hidden_local,
-    hidden_sems, *, width, band_rows, bands, level_count,
+    hidden_staged, hidden_sems, *, width, band_rows, bands, level_count,
 ):
     band = lax.axis_index("rows")
     first_step = lax.axis_index("step") == lax.axis_size("step") - 1
@@ -197,9 +197,11 @@
         lanes = lax.broadcasted_iota(jnp.int32, (1, span), 1)
         conv = conv_chunk(act_next, second_w, first, rows, width, lanes % width)
         start = first * width
-        hidden_local[:, start : start + span] = lifted_keep[:, start : start + span].astype(jnp.float32) + conv
+        hidden = lifted_keep[:, start : start + span].astype(jnp.float32) + conv
+        hidden_local[:, start : start + span] = hidden
+        hidden_staged[:, start : start + span] = hidden.astype(jnp.bfloat16)
         copy = pltpu.make_async_copy(
-            hidden_local.at[:, pl.ds(start, span)], hidden_ref.at[:, pl.ds(start, span)], hidden_sems.at[q]
+            hidden_staged.at[:, pl.ds(start, span)], hidden_ref.at[:, pl.ds(start, span)], hidden_sems.at[q]
         )
         copy.start()
         outgoing.append(copy)
@@ -296,7 +298,7 @@
         for u in range(4):
             r = 4 * a + u
             start = r * width
-            combined = hidden_local[:, start : start + width] + spread_mixed
+            combined = hidden_local[:, start : start + width].astype(jnp.float32) + spread_mixed
             act = silu(normalize_features(combined)).astype(jnp.bfloat16)
             field = jnp.dot(out_w, act, preferred_element_type=jnp.float32)
             state = jnp.where(first_step, start_ref[:, r, :], previous_ref[0, :, r, :])
@@ -354,7 +356,7 @@
             *refs, width=width, band_rows=band_rows, bands=bands, level_count=level_count
         ),
         out_shape=(
-            jax.ShapeDtypeStruct((feat, pixels), jnp.float32),
+            jax.ShapeDtypeStruct((feat, pixels), jnp.bfloat16),
             jax.ShapeDtypeStruct((feat, tokens), jnp.float32),
             jax.ShapeDtypeStruct((feat, 2 * HEAD_DIM), jnp.float32),
         ),
@@ -366,6 +368,7 @@
             pltpu.VMEM((feat, pixels), jnp.bfloat16),
             pltpu.VMEM((feat, (band_rows + 2) * width), jnp.bfloat16),
             pltpu.VMEM((feat, pixels), jnp.float32),
+            pltpu.VMEM((feat, pixels), jnp.bfloat16),
             pltpu.SemaphoreType.DMA((len(row_chunks(band_rows)),)),
         ],
     )
@@ -394,7 +397,7 @@
         in_specs=[smem(), smem(), pl.BlockSpec(memory_space=pl.ANY)] + [vmem()] * 7,
         out_specs=(vmem(), vmem()),
         scratch_shapes=[
-            pltpu.VMEM((feat, pixels), jnp.float32),
+            pltpu.VMEM((feat, pixels), jnp.bfloat16),
             pltpu.SemaphoreType.DMA((band_rows // 4,)),
         ],
     )

time: 58.7 us -> 58.5 us (level)
  no operation moved by 1% of the time
where the time goes in v12:
time: 58.5 us; the launch traced here: 58.2 us
  Pallas kernels  19.5 us (33%)
  waiting for transfers between devices  17 us (29%)
  starting transfers between devices  16.5 us (28%)
  other arithmetic  2.6 us (4%)
  local copies, waits for them, and re-layouts  1.96 us (3%)
  between operations  0.69 us (1%)
    pallas_call x1, Pallas kernels, local(): trunk(step_levels, previous, window_start, start_other, previous_other, c...  13.1 us
    ppermute x2, waiting for transfers between devices, rotated_prefix(): seed = seed + lax.ppermute(seed, axis, pairs)  10.2 us
    pallas_call x1, Pallas kernels, local(): head(step_levels, next_levels, hidden, queries, stats_own, stats_other, m...  6.44 us
    ppermute x1, starting transfers between devices, local(): lax.ppermute(step_levels, 'step', [((h + 1) % steps, h) for h in range(st...  5.77 us
    ppermute x1, starting transfers between devices, rotated_prefix(): lax.ppermute(seed, axis, [(holder(q), q + shift) for q in range(steps - s...  3.64 us
    ppermute x2, starting transfers between devices, rotated_prefix(): seed = seed + lax.ppermute(seed, axis, pairs)  3.31 us
    ppermute x1, waiting for transfers between devices, rotated_prefix(): lax.ppermute(seed, axis, [(holder(q), q + shift) for q in range(steps - s...  2.51 us
    ppermute x1, starting transfers between devices, rotated_prefix(): lax.ppermute(jnp.concatenate([seed, denoised], axis=0), axis, [(h, (h + 1...  2.36 us
  transfers between devices with their start and end apart: 9, of which 7 were waited for; matrix products, arithmetic and copies ran while one was open for 0% of the time, Pallas kernels for 0%

profile of v12, /device:TPU:0, one launch (start us, length us, event | category | flops | bytes accessed | tf_op | source)
XLA Modules:
  0.0 58.2 jit_solution(251589360704176350)
XLA Ops:
  0.6 0.5 collective-permute-start.3
  1.1 0.1 collective-permute-start.1
  1.2 0.4 collective-permute-start.2
  1.7 1.0 %collective-permute-done.1.refs_3_ = f32[4,16,512]{2,1,0:T(8,128)S(1)} collective-permute-done((f32[4,16,512]{2,1,0:T(8,128)}, f32[4,16,512]{2,1,0:T(8,128)S(1)}, u32[]{:S(2)}, u32[]{:S(2)}) %collective-permute-start.1) | collective-permute-done | bytes 131104 | tf_op jit(solution)/shard_map/ppermute | solution.py:347
  2.7 0.0 copy-start.1
  2.7 0.2 collective-permute-done.2.refs_4_
  2.9 0.0 copy-start.2
  2.9 0.0 collective-permute-done.3.refs_6_
  2.9 0.5 copy-done.1
  3.4 0.2 copy-done.2
  3.6 0.0 copy-start
  3.6 0.7 %copy-done = bf16[12,16,512]{2,1,0:T(8,128)(2,1)} copy-done((bf16[12,16,512]{2,1,0:T(8,128)(2,1)}, bf16[12,16,512]{2,1,0:T(8,128)(2,1)S(1)}, u32[]{:S(2)}) %copy-start) | copy-done | bytes 196632
  4.2 13.1 %shard_map.122 = (bf16[128,8192]{1,0:T(8,128)(2,1)}, f32[128,512]{1,0:T(8,128)}, f32[128,128]{1,0:T(8,128)}) custom-call(s32[1,2]{1,0:T(1,128)} %refs_0_.3, f32[1,4,16,512]{3,2,1,0:T(8,128)} %refs_8_.3, f32[4,16,512]{2,1,0:T(8,128)} %refs_9_.3, f32[4,16,512]{2,1,0:T(8,128)} %copy-done.1, f32[1,4,16,512]{3,2,1,0:T(8,128)} %copy-done.2, ...), custom_call_target="tpu_custom_call" | custom-call | tf_op jit(solution)/shard_map/pallas_call | solution.py:375
  17.3 0.4 collective-permute-start.4
  17.7 5.8 %collective-permute-start = (s32[1,2]{1,0:T(1,128)}, s32[1,2]{1,0:T(1,128)S(1)}, u32[]{:S(2)}, u32[]{:S(2)}) collective-permute-start(s32[1,2]{1,0:T(1,128)} %refs_0_.3), channel_id=1, source_target_pairs={{2,0},{4,2},{6,4},{8,6},{10,8},{12,10},{14,12},{0,14},{3,1},{5,3},... | collective-permute-start | bytes 32 | tf_op jit(solution)/shard_map/ppermute | solution.py:344
  23.5 1.4 %collective-permute-done.refs_1_ = s32[1,2]{1,0:T(1,128)S(1)} collective-permute-done((s32[1,2]{1,0:T(1,128)}, s32[1,2]{1,0:T(1,128)S(1)}, u32[]{:S(2)}, u32[]{:S(2)}) %collective-permute-start) | collective-permute-done | bytes 40 | tf_op jit(solution)/shard_map/ppermute | solution.py:344
  24.9 0.0 copy-start.4
  24.9 0.0 collective-permute-done.4.refs_5_
  24.9 0.0 copy-start.3
  24.9 0.6 %copy-done.4 = s32[1,2]{1,0:T(1,128)} copy-done((s32[1,2]{1,0:T(1,128)}, s32[1,2]{1,0:T(1,128)S(1)}, u32[]{:S(2)}) %copy-start.4) | copy-done | bytes 32
  25.5 0.0 copy-done.3
  25.5 6.4 %shard_map.123 = (f32[4,16,512]{2,1,0:T(8,128)}, f32[4,16,512]{2,1,0:T(8,128)}) custom-call(s32[1,2]{1,0:T(1,128)} %refs_0_.3, s32[1,2]{1,0:T(1,128)} %copy-done.4, bf16[128,8192]{1,0:T(8,128)(2,1)} %get-tuple-element.7.refs_2_, f32[128,512]{1,0:T(8,128)} %get-tuple-element.8.refs_3_, f32[128,128]{1,0:T(8,128)} %get-tuple-element.9.refs_4_, ...), custom_call_target="tpu_custom_call" | custom-call | tf_op jit(solution)/shard_map/pallas_call | solution.py:404
  32.0 2.0 %collective-permute-start.5 = (f32[4,16,512]{2,1,0:T(8,128)}, f32[4,16,512]{2,1,0:T(8,128)S(1)}, u32[]{:S(2)}, u32[]{:S(2)}) collective-permute-start(f32[4,16,512]{2,1,0:T(8,128)} %get-tuple-element.10), channel_id=1, source_target_pairs={{14,0},{0,2},{2,4},{4,6},{6,8},{8,10},{10,12},{15,1},{1,3},{3,5},{... | collective-permute-start | bytes 393224 | tf_op jit(solution)/shard_map/ppermute | solution.py:418
  34.0 7.7 %collective-permute-done.5 = f32[4,16,512]{2,1,0:T(8,128)S(1)} collective-permute-done((f32[4,16,512]{2,1,0:T(8,128)}, f32[4,16,512]{2,1,0:T(8,128)S(1)}, u32[]{:S(2)}, u32[]{:S(2)}) %collective-permute-start.5) | collective-permute-done | bytes 131104 | tf_op jit(solution)/shard_map/ppermute | solution.py:418
  41.8 0.9 %add.9 = f32[4,16,512]{2,1,0:T(8,128)S(1)} add(f32[4,16,512]{2,1,0:T(8,128)} %get-tuple-element.10, f32[4,16,512]{2,1,0:T(8,128)S(1)} %collective-permute-done.5) | non-fusion elementwise | flops 32768 | bytes 393216 | tf_op jit(solution)/shard_map/add | solution.py:418
  42.7 1.3 %collective-permute-start.6 = (f32[4,16,512]{2,1,0:T(8,128)S(1)}, f32[4,16,512]{2,1,0:T(8,128)S(1)}, u32[]{:S(2)}, u32[]{:S(2)}) collective-permute-start(f32[4,16,512]{2,1,0:T(8,128)S(1)} %add.9), channel_id=1, source_target_pairs={{14,2},{0,4},{2,6},{4,8},{6,10},{8,12},{15,3},{1,5},{3,7},{5,9},{7... | collective-permute-start | bytes 393224 | tf_op jit(solution)/shard_map/ppermute | solution.py:418
  44.0 2.5 %collective-permute-done.6 = f32[4,16,512]{2,1,0:T(8,128)S(1)} collective-permute-done((f32[4,16,512]{2,1,0:T(8,128)S(1)}, f32[4,16,512]{2,1,0:T(8,128)S(1)}, u32[]{:S(2)}, u32[]{:S(2)}) %collective-permute-start.6) | collective-permute-done | bytes 131104 | tf_op jit(solution)/shard_map/ppermute | solution.py:418
  46.5 0.9 %pad_maximum_fusion = f32[8,16,512]{2,1,0:T(8,128)S(1)} fusion(f32[4,16,512]{2,1,0:T(8,128)} %get-tuple-element.11, f32[4,16,512]{2,1,0:T(8,128)S(1)} %add.10), kind=kLoop, calls=%fused_computation | loop fusion | flops 65536 | bytes 524288 | tf_op jit(solution)/shard_map/concatenate | solution.py:421
  47.4 2.4 %collective-permute-start.7 = (f32[8,16,512]{2,1,0:T(8,128)S(1)}, f32[8,16,512]{2,1,0:T(8,128)S(1)}, u32[]{:S(2)}, u32[]{:S(2)}) collective-permute-start(f32[8,16,512]{2,1,0:T(8,128)S(1)} %pad_maximum_fusion), channel_id=1, source_target_pairs={{0,2},{2,4},{4,6},{6,8},{8,10},{10,12},{12,14},{14,0},{1,3},{3,5},... | collective-permute-start | bytes 786440 | tf_op jit(solution)/shard_map/ppermute | solution.py:420
  49.8 3.6 %collective-permute-start.8 = (f32[4,16,512]{2,1,0:T(8,128)S(1)}, f32[4,16,512]{2,1,0:T(8,128)S(1)}, u32[]{:S(2)}, u32[]{:S(2)}) collective-permute-start(f32[4,16,512]{2,1,0:T(8,128)S(1)} %add.10), channel_id=1, source_target_pairs={{14,8},{0,10},{2,12},{4,14},{15,9},{1,11},{3,13},{5,15},{30,24},{1... | collective-permute-start | bytes 393224 | tf_op jit(solution)/shard_map/ppermute | solution.py:426
  53.4 2.5 %collective-permute-done.8 = f32[4,16,512]{2,1,0:T(8,128)S(1)} collective-permute-done((f32[4,16,512]{2,1,0:T(8,128)S(1)}, f32[4,16,512]{2,1,0:T(8,128)S(1)}, u32[]{:S(2)}, u32[]{:S(2)}) %collective-permute-start.8) | collective-permute-done | bytes 131104 | tf_op jit(solution)/shard_map/ppermute | solution.py:426
  56.0 1.5 %collective-permute-done.7 = f32[8,16,512]{2,1,0:T(8,128)S(1)} collective-permute-done((f32[8,16,512]{2,1,0:T(8,128)S(1)}, f32[8,16,512]{2,1,0:T(8,128)S(1)}, u32[]{:S(2)}, u32[]{:S(2)}) %collective-permute-start.7) | collective-permute-done | bytes 262176 | tf_op jit(solution)/shard_map/ppermute | solution.py:420
  57.5 0.7 %slice_bitcast_fusion = (f32[1,4,16,512]{3,2,1,0:T(8,128)}, f32[1,4,16,512]{3,2,1,0:T(8,128)}) fusion(f32[8,16,512]{2,1,0:T(8,128)S(1)} %collective-permute-done.7, f32[4,16,512]{2,1,0:T(8,128)S(1)} %collective-permute-done.8), kind=kLoop, calls=%fused_computation.1 | loop fusion | flops 32768 | bytes 655360 | tf_op jit(solution)/shard_map/broadcast_in_dim | solution.py:409
  (1 shorter events, 0.0 us)
Async XLA Ops:
  0.6 2.3 %collective-permute-start.3 = (bf16[12,16,512]{2,1,0:T(8,128)(2,1)}, bf16[12,16,512]{2,1,0:T(8,128)(2,1)S(1)}, u32[]{:S(2)}, u32[]{:S(2)}) collective-permute-start(bf16[12,16,512]{2,1,0:T(8,128)(2,1)} %refs_5_.1), channel_id=1, source_target_pairs={{0,1},{1,0},{2,3},{3,2},{4,5},{5,4},{6,7},{7,6},{8,9},{9,8},{10,11... | collective-permute-start | bytes 589832 | tf_op jit(solution)/shard_map/ppermute | solution.py:348
  1.1 1.6 %collective-permute-start.1 = (f32[4,16,512]{2,1,0:T(8,128)}, f32[4,16,512]{2,1,0:T(8,128)S(1)}, u32[]{:S(2)}, u32[]{:S(2)}) collective-permute-start(f32[4,16,512]{2,1,0:T(8,128)} %refs_9_.3), channel_id=1, source_target_pairs={{0,1},{1,0},{2,3},{3,2},{4,5},{5,4},{6,7},{7,6},{8,9},{9,8},{10,11... | collective-permute-start | bytes 393224 | tf_op jit(solution)/shard_map/ppermute | solution.py:347
  1.2 1.7 %collective-permute-start.2 = (f32[1,4,16,512]{3,2,1,0:T(8,128)}, f32[1,4,16,512]{3,2,1,0:T(8,128)S(1)}, u32[]{:S(2)}, u32[]{:S(2)}) collective-permute-start(f32[1,4,16,512]{3,2,1,0:T(8,128)} %refs_8_.3), channel_id=1, source_target_pairs={{0,1},{1,0},{2,3},{3,2},{4,5},{5,4},{6,7},{7,6},{8,9},{9,8},{10,11... | collective-permute-start | bytes 393224 | tf_op jit(solution)/shard_map/ppermute | solution.py:346
  2.7 0.7 %copy-start.1 = (f32[4,16,512]{2,1,0:T(8,128)}, f32[4,16,512]{2,1,0:T(8,128)S(1)}, u32[]{:S(2)}) copy-start(f32[4,16,512]{2,1,0:T(8,128)S(1)} %collective-permute-done.1.refs_3_) | copy-start | bytes 393220
  2.9 0.7 %copy-start.2 = (f32[1,4,16,512]{3,2,1,0:T(8,128)}, f32[1,4,16,512]{3,2,1,0:T(8,128)S(1)}, u32[]{:S(2)}) copy-start(f32[1,4,16,512]{3,2,1,0:T(8,128)S(1)} %collective-permute-done.2.refs_4_) | copy-start | bytes 393220
  3.6 0.7 %copy-start = (bf16[12,16,512]{2,1,0:T(8,128)(2,1)}, bf16[12,16,512]{2,1,0:T(8,128)(2,1)S(1)}, u32[]{:S(2)}) copy-start(bf16[12,16,512]{2,1,0:T(8,128)(2,1)S(1)} %collective-permute-done.3.refs_6_) | copy-start | bytes 589828
  17.3 7.6 %collective-permute-start.4 = (f32[128,128]{1,0:T(8,128)}, f32[128,128]{1,0:T(8,128)S(1)}, u32[]{:S(2)}, u32[]{:S(2)}) collective-permute-start(f32[128,128]{1,0:T(8,128)} %get-tuple-element.9.refs_4_), channel_id=1, source_target_pairs={{0,1},{1,0},{2,3},{3,2},{4,5},{5,4},{6,7},{7,6},{8,9},{9,8},{10,11... | collective-permute-start | bytes 196616 | tf_op jit(solution)/shard_map/ppermute | solution.py:389
  17.7 7.2 %collective-permute-start = (s32[1,2]{1,0:T(1,128)}, s32[1,2]{1,0:T(1,128)S(1)}, u32[]{:S(2)}, u32[]{:S(2)}) collective-permute-start(s32[1,2]{1,0:T(1,128)} %refs_0_.3), channel_id=1, source_target_pairs={{2,0},{4,2},{6,4},{8,6},{10,8},{12,10},{14,12},{0,14},{3,1},{5,3},... | collective-permute-start | bytes 32 | tf_op jit(solution)/shard_map/ppermute | solution.py:344
  24.9 0.6 %copy-start.4 = (s32[1,2]{1,0:T(1,128)}, s32[1,2]{1,0:T(1,128)S(1)}, u32[]{:S(2)}) copy-start(s32[1,2]{1,0:T(1,128)S(1)} %collective-permute-done.refs_1_) | copy-start | bytes 28
  24.9 0.6 %copy-start.3 = (f32[128,128]{1,0:T(8,128)}, f32[128,128]{1,0:T(8,128)S(1)}, u32[]{:S(2)}) copy-start(f32[128,128]{1,0:T(8,128)S(1)} %collective-permute-done.4.refs_5_) | copy-start | bytes 196612
  32.0 9.8 %collective-permute-start.5 = (f32[4,16,512]{2,1,0:T(8,128)}, f32[4,16,512]{2,1,0:T(8,128)S(1)}, u32[]{:S(2)}, u32[]{:S(2)}) collective-permute-start(f32[4,16,512]{2,1,0:T(8,128)} %get-tuple-element.10), channel_id=1, source_target_pairs={{14,0},{0,2},{2,4},{4,6},{6,8},{8,10},{10,12},{15,1},{1,3},{3,5},{... | collective-permute-start | bytes 393224 | tf_op jit(solution)/shard_map/ppermute | solution.py:418
  42.7 3.8 %collective-permute-start.6 = (f32[4,16,512]{2,1,0:T(8,128)S(1)}, f32[4,16,512]{2,1,0:T(8,128)S(1)}, u32[]{:S(2)}, u32[]{:S(2)}) collective-permute-start(f32[4,16,512]{2,1,0:T(8,128)S(1)} %add.9), channel_id=1, source_target_pairs={{14,2},{0,4},{2,6},{4,8},{6,10},{8,12},{15,3},{1,5},{3,7},{5,9},{7... | collective-permute-start | bytes 393224 | tf_op jit(solution)/shard_map/ppermute | solution.py:418
  47.4 10.1 %collective-permute-start.7 = (f32[8,16,512]{2,1,0:T(8,128)S(1)}, f32[8,16,512]{2,1,0:T(8,128)S(1)}, u32[]{:S(2)}, u32[]{:S(2)}) collective-permute-start(f32[8,16,512]{2,1,0:T(8,128)S(1)} %pad_maximum_fusion), channel_id=1, source_target_pairs={{0,2},{2,4},{4,6},{6,8},{8,10},{10,12},{12,14},{14,0},{1,3},{3,5},... | collective-permute-start | bytes 786440 | tf_op jit(solution)/shard_map/ppermute | solution.py:420
  49.8 6.2 %collective-permute-start.8 = (f32[4,16,512]{2,1,0:T(8,128)S(1)}, f32[4,16,512]{2,1,0:T(8,128)S(1)}, u32[]{:S(2)}, u32[]{:S(2)}) collective-permute-start(f32[4,16,512]{2,1,0:T(8,128)S(1)} %add.10), channel_id=1, source_target_pairs={{14,8},{0,10},{2,12},{4,14},{15,9},{1,11},{3,13},{5,15},{30,24},{1... | collective-permute-start | bytes 393224 | tf_op jit(solution)/shard_map/ppermute | solution.py:426

commit v13 on v10

--- a/solution.py
+++ b/solution.py
@@ -9,7 +9,7 @@
 HEAD_DIM = 64
 HALO = 2
 CHUNK_ROWS = 2
-CONV_ROWS = 4
+CONV_ROWS = 8
 
 SIGMA_TOP = 8.0
 SIGMA_END = 0.002

time: 58.7 us -> 59.2 us (level)
  no operation moved by 1% of the time
where the time goes in v13:
time: 59.2 us; the launch traced here: 58.9 us
  Pallas kernels  20.2 us (34%)
  waiting for transfers between devices  17 us (29%)
  starting transfers between devices  16.5 us (28%)
  other arithmetic  2.6 us (4%)
  local copies, waits for them, and re-layouts  1.97 us (3%)
  between operations  0.69 us (1%)
    pallas_call x1, Pallas kernels, local(): trunk(step_levels, previous, window_start, start_other, previous_other, c...  13.4 us
    ppermute x2, waiting for transfers between devices, rotated_prefix(): seed = seed + lax.ppermute(seed, axis, pairs)  10.2 us
    pallas_call x1, Pallas kernels, local(): head(step_levels, next_levels, hidden, queries, stats_own, stats_other, m...  6.77 us
    ppermute x1, starting transfers between devices, local(): lax.ppermute(step_levels, 'step', [((h + 1) % steps, h) for h in range(st...  5.77 us
    ppermute x1, starting transfers between devices, rotated_prefix(): lax.ppermute(seed, axis, [(holder(q), q + shift) for q in range(steps - s...  3.64 us
    ppermute x2, starting transfers between devices, rotated_prefix(): seed = seed + lax.ppermute(seed, axis, pairs)  3.31 us
    ppermute x1, waiting for transfers between devices, rotated_prefix(): lax.ppermute(seed, axis, [(holder(q), q + shift) for q in range(steps - s...  2.51 us
    ppermute x1, starting transfers between devices, rotated_prefix(): lax.ppermute(jnp.concatenate([seed, denoised], axis=0), axis, [(h, (h + 1...  2.36 us
  transfers between devices with their start and end apart: 9, of which 7 were waited for; matrix products, arithmetic and copies ran while one was open for 0% of the time, Pallas kernels for 0%

profile of v13, /device:TPU:0, one launch (start us, length us, event | category | flops | bytes accessed | tf_op | source)
XLA Modules:
  0.0 58.9 jit_solution(7283422924828542903)
XLA Ops:
  0.6 0.5 collective-permute-start.3
  1.1 0.1 collective-permute-start.1
  1.2 0.4 collective-permute-start.2
  1.7 1.0 %collective-permute-done.1.refs_3_ = f32[4,16,512]{2,1,0:T(8,128)S(1)} collective-permute-done((f32[4,16,512]{2,1,0:T(8,128)}, f32[4,16,512]{2,1,0:T(8,128)S(1)}, u32[]{:S(2)}, u32[]{:S(2)}) %collective-permute-start.1) | collective-permute-done | bytes 131104 | tf_op jit(solution)/shard_map/ppermute | solution.py:345
  2.7 0.0 copy-start.1
  2.7 0.2 collective-permute-done.2.refs_4_
  2.9 0.0 copy-start.2
  2.9 0.0 collective-permute-done.3.refs_6_
  2.9 0.5 copy-done.1
  3.4 0.2 copy-done.2
  3.6 0.0 copy-start
  3.6 0.7 %copy-done = bf16[12,16,512]{2,1,0:T(8,128)(2,1)} copy-done((bf16[12,16,512]{2,1,0:T(8,128)(2,1)}, bf16[12,16,512]{2,1,0:T(8,128)(2,1)S(1)}, u32[]{:S(2)}) %copy-start) | copy-done | bytes 196632
  4.2 13.4 %shard_map.122 = (f32[128,8192]{1,0:T(8,128)}, f32[128,512]{1,0:T(8,128)}, f32[128,128]{1,0:T(8,128)}) custom-call(s32[1,2]{1,0:T(1,128)} %refs_0_.3, f32[1,4,16,512]{3,2,1,0:T(8,128)} %refs_8_.3, f32[4,16,512]{2,1,0:T(8,128)} %refs_9_.3, f32[4,16,512]{2,1,0:T(8,128)} %copy-done.1, f32[1,4,16,512]{3,2,1,0:T(8,128)} %copy-done.2, ...), custom_call_target="tpu_custom_call" | custom-call | tf_op jit(solution)/shard_map/pallas_call | solution.py:372
  17.7 0.4 collective-permute-start.4
  18.1 5.8 %collective-permute-start = (s32[1,2]{1,0:T(1,128)}, s32[1,2]{1,0:T(1,128)S(1)}, u32[]{:S(2)}, u32[]{:S(2)}) collective-permute-start(s32[1,2]{1,0:T(1,128)} %refs_0_.3), channel_id=1, source_target_pairs={{2,0},{4,2},{6,4},{8,6},{10,8},{12,10},{14,12},{0,14},{3,1},{5,3},... | collective-permute-start | bytes 32 | tf_op jit(solution)/shard_map/ppermute | solution.py:342
  23.9 1.4 %collective-permute-done.refs_1_ = s32[1,2]{1,0:T(1,128)S(1)} collective-permute-done((s32[1,2]{1,0:T(1,128)}, s32[1,2]{1,0:T(1,128)S(1)}, u32[]{:S(2)}, u32[]{:S(2)}) %collective-permute-start) | collective-permute-done | bytes 40 | tf_op jit(solution)/shard_map/ppermute | solution.py:342
  25.3 0.0 copy-start.4
  25.3 0.0 collective-permute-done.4.refs_5_
  25.3 0.0 copy-start.3
  25.3 0.5 copy-done.4
  25.8 0.1 copy-done.3
  25.9 6.8 %shard_map.123 = (f32[4,16,512]{2,1,0:T(8,128)}, f32[4,16,512]{2,1,0:T(8,128)}) custom-call(s32[1,2]{1,0:T(1,128)} %refs_0_.3, s32[1,2]{1,0:T(1,128)} %copy-done.4, f32[128,8192]{1,0:T(8,128)} %get-tuple-element.7.refs_2_, f32[128,512]{1,0:T(8,128)} %get-tuple-element.8.refs_3_, f32[128,128]{1,0:T(8,128)} %get-tuple-element.9.refs_4_, f32[128,128]{1,0:T(8,128)} %copy-done.3, ...), custom_call_target="tpu_custom_call" | custom-call | tf_op jit(solution)/shard_map/pallas_call | solution.py:401
  32.7 2.0 %collective-permute-start.5 = (f32[4,16,512]{2,1,0:T(8,128)}, f32[4,16,512]{2,1,0:T(8,128)S(1)}, u32[]{:S(2)}, u32[]{:S(2)}) collective-permute-start(f32[4,16,512]{2,1,0:T(8,128)} %get-tuple-element.10), channel_id=1, source_target_pairs={{14,0},{0,2},{2,4},{4,6},{6,8},{8,10},{10,12},{15,1},{1,3},{3,5},{... | collective-permute-start | bytes 393224 | tf_op jit(solution)/shard_map/ppermute | solution.py:415
  34.7 7.7 %collective-permute-done.5 = f32[4,16,512]{2,1,0:T(8,128)S(1)} collective-permute-done((f32[4,16,512]{2,1,0:T(8,128)}, f32[4,16,512]{2,1,0:T(8,128)S(1)}, u32[]{:S(2)}, u32[]{:S(2)}) %collective-permute-start.5) | collective-permute-done | bytes 131104 | tf_op jit(solution)/shard_map/ppermute | solution.py:415
  42.5 0.9 %add.9 = f32[4,16,512]{2,1,0:T(8,128)S(1)} add(f32[4,16,512]{2,1,0:T(8,128)} %get-tuple-element.10, f32[4,16,512]{2,1,0:T(8,128)S(1)} %collective-permute-done.5) | non-fusion elementwise | flops 32768 | bytes 393216 | tf_op jit(solution)/shard_map/add | solution.py:415
  43.4 1.3 %collective-permute-start.6 = (f32[4,16,512]{2,1,0:T(8,128)S(1)}, f32[4,16,512]{2,1,0:T(8,128)S(1)}, u32[]{:S(2)}, u32[]{:S(2)}) collective-permute-start(f32[4,16,512]{2,1,0:T(8,128)S(1)} %add.9), channel_id=1, source_target_pairs={{14,2},{0,4},{2,6},{4,8},{6,10},{8,12},{15,3},{1,5},{3,7},{5,9},{7... | collective-permute-start | bytes 393224 | tf_op jit(solution)/shard_map/ppermute | solution.py:415
  44.7 2.5 %collective-permute-done.6 = f32[4,16,512]{2,1,0:T(8,128)S(1)} collective-permute-done((f32[4,16,512]{2,1,0:T(8,128)S(1)}, f32[4,16,512]{2,1,0:T(8,128)S(1)}, u32[]{:S(2)}, u32[]{:S(2)}) %collective-permute-start.6) | collective-permute-done | bytes 131104 | tf_op jit(solution)/shard_map/ppermute | solution.py:415
  47.2 0.9 %pad_maximum_fusion = f32[8,16,512]{2,1,0:T(8,128)S(1)} fusion(f32[4,16,512]{2,1,0:T(8,128)} %get-tuple-element.11, f32[4,16,512]{2,1,0:T(8,128)S(1)} %add.10), kind=kLoop, calls=%fused_computation | loop fusion | flops 65536 | bytes 524288 | tf_op jit(solution)/shard_map/concatenate | solution.py:418
  48.2 2.4 %collective-permute-start.7 = (f32[8,16,512]{2,1,0:T(8,128)S(1)}, f32[8,16,512]{2,1,0:T(8,128)S(1)}, u32[]{:S(2)}, u32[]{:S(2)}) collective-permute-start(f32[8,16,512]{2,1,0:T(8,128)S(1)} %pad_maximum_fusion), channel_id=1, source_target_pairs={{0,2},{2,4},{4,6},{6,8},{8,10},{10,12},{12,14},{14,0},{1,3},{3,5},... | collective-permute-start | bytes 786440 | tf_op jit(solution)/shard_map/ppermute | solution.py:417
  50.5 3.6 %collective-permute-start.8 = (f32[4,16,512]{2,1,0:T(8,128)S(1)}, f32[4,16,512]{2,1,0:T(8,128)S(1)}, u32[]{:S(2)}, u32[]{:S(2)}) collective-permute-start(f32[4,16,512]{2,1,0:T(8,128)S(1)} %add.10), channel_id=1, source_target_pairs={{14,8},{0,10},{2,12},{4,14},{15,9},{1,11},{3,13},{5,15},{30,24},{1... | collective-permute-start | bytes 393224 | tf_op jit(solution)/shard_map/ppermute | solution.py:423
  54.2 2.5 %collective-permute-done.8 = f32[4,16,512]{2,1,0:T(8,128)S(1)} collective-permute-done((f32[4,16,512]{2,1,0:T(8,128)S(1)}, f32[4,16,512]{2,1,0:T(8,128)S(1)}, u32[]{:S(2)}, u32[]{:S(2)}) %collective-permute-start.8) | collective-permute-done | bytes 131104 | tf_op jit(solution)/shard_map/ppermute | solution.py:423
  56.7 1.5 %collective-permute-done.7 = f32[8,16,512]{2,1,0:T(8,128)S(1)} collective-permute-done((f32[8,16,512]{2,1,0:T(8,128)S(1)}, f32[8,16,512]{2,1,0:T(8,128)S(1)}, u32[]{:S(2)}, u32[]{:S(2)}) %collective-permute-start.7) | collective-permute-done | bytes 262176 | tf_op jit(solution)/shard_map/ppermute | solution.py:417
  58.2 0.7 %slice_bitcast_fusion = (f32[1,4,16,512]{3,2,1,0:T(8,128)}, f32[1,4,16,512]{3,2,1,0:T(8,128)}) fusion(f32[8,16,512]{2,1,0:T(8,128)S(1)} %collective-permute-done.7, f32[4,16,512]{2,1,0:T(8,128)S(1)} %collective-permute-done.8), kind=kLoop, calls=%fused_computation.1 | loop fusion | flops 32768 | bytes 655360 | tf_op jit(solution)/shard_map/broadcast_in_dim | solution.py:406
  (1 shorter events, 0.0 us)
Async XLA Ops:
  0.6 2.3 %collective-permute-start.3 = (bf16[12,16,512]{2,1,0:T(8,128)(2,1)}, bf16[12,16,512]{2,1,0:T(8,128)(2,1)S(1)}, u32[]{:S(2)}, u32[]{:S(2)}) collective-permute-start(bf16[12,16,512]{2,1,0:T(8,128)(2,1)} %refs_5_.1), channel_id=1, source_target_pairs={{0,1},{1,0},{2,3},{3,2},{4,5},{5,4},{6,7},{7,6},{8,9},{9,8},{10,11... | collective-permute-start | bytes 589832 | tf_op jit(solution)/shard_map/ppermute | solution.py:346
  1.1 1.6 %collective-permute-start.1 = (f32[4,16,512]{2,1,0:T(8,128)}, f32[4,16,512]{2,1,0:T(8,128)S(1)}, u32[]{:S(2)}, u32[]{:S(2)}) collective-permute-start(f32[4,16,512]{2,1,0:T(8,128)} %refs_9_.3), channel_id=1, source_target_pairs={{0,1},{1,0},{2,3},{3,2},{4,5},{5,4},{6,7},{7,6},{8,9},{9,8},{10,11... | collective-permute-start | bytes 393224 | tf_op jit(solution)/shard_map/ppermute | solution.py:345
  1.2 1.7 %collective-permute-start.2 = (f32[1,4,16,512]{3,2,1,0:T(8,128)}, f32[1,4,16,512]{3,2,1,0:T(8,128)S(1)}, u32[]{:S(2)}, u32[]{:S(2)}) collective-permute-start(f32[1,4,16,512]{3,2,1,0:T(8,128)} %refs_8_.3), channel_id=1, source_target_pairs={{0,1},{1,0},{2,3},{3,2},{4,5},{5,4},{6,7},{7,6},{8,9},{9,8},{10,11... | collective-permute-start | bytes 393224 | tf_op jit(solution)/shard_map/ppermute | solution.py:344
  2.7 0.7 %copy-start.1 = (f32[4,16,512]{2,1,0:T(8,128)}, f32[4,16,512]{2,1,0:T(8,128)S(1)}, u32[]{:S(2)}) copy-start(f32[4,16,512]{2,1,0:T(8,128)S(1)} %collective-permute-done.1.refs_3_) | copy-start | bytes 393220
  2.9 0.7 %copy-start.2 = (f32[1,4,16,512]{3,2,1,0:T(8,128)}, f32[1,4,16,512]{3,2,1,0:T(8,128)S(1)}, u32[]{:S(2)}) copy-start(f32[1,4,16,512]{3,2,1,0:T(8,128)S(1)} %collective-permute-done.2.refs_4_) | copy-start | bytes 393220
  3.6 0.7 %copy-start = (bf16[12,16,512]{2,1,0:T(8,128)(2,1)}, bf16[12,16,512]{2,1,0:T(8,128)(2,1)S(1)}, u32[]{:S(2)}) copy-start(bf16[12,16,512]{2,1,0:T(8,128)(2,1)S(1)} %collective-permute-done.3.refs_6_) | copy-start | bytes 589828
  17.7 7.6 %collective-permute-start.4 = (f32[128,128]{1,0:T(8,128)}, f32[128,128]{1,0:T(8,128)S(1)}, u32[]{:S(2)}, u32[]{:S(2)}) collective-permute-start(f32[128,128]{1,0:T(8,128)} %get-tuple-element.9.refs_4_), channel_id=1, source_target_pairs={{0,1},{1,0},{2,3},{3,2},{4,5},{5,4},{6,7},{7,6},{8,9},{9,8},{10,11... | collective-permute-start | bytes 196616 | tf_op jit(solution)/shard_map/ppermute | solution.py:386
  18.1 7.2 %collective-permute-start = (s32[1,2]{1,0:T(1,128)}, s32[1,2]{1,0:T(1,128)S(1)}, u32[]{:S(2)}, u32[]{:S(2)}) collective-permute-start(s32[1,2]{1,0:T(1,128)} %refs_0_.3), channel_id=1, source_target_pairs={{2,0},{4,2},{6,4},{8,6},{10,8},{12,10},{14,12},{0,14},{3,1},{5,3},... | collective-permute-start | bytes 32 | tf_op jit(solution)/shard_map/ppermute | solution.py:342
  25.3 0.5 copy-start.4
  25.3 0.6 %copy-start.3 = (f32[128,128]{1,0:T(8,128)}, f32[128,128]{1,0:T(8,128)S(1)}, u32[]{:S(2)}) copy-start(f32[128,128]{1,0:T(8,128)S(1)} %collective-permute-done.4.refs_5_) | copy-start | bytes 196612
  32.7 9.8 %collective-permute-start.5 = (f32[4,16,512]{2,1,0:T(8,128)}, f32[4,16,512]{2,1,0:T(8,128)S(1)}, u32[]{:S(2)}, u32[]{:S(2)}) collective-permute-start(f32[4,16,512]{2,1,0:T(8,128)} %get-tuple-element.10), channel_id=1, source_target_pairs={{14,0},{0,2},{2,4},{4,6},{6,8},{8,10},{10,12},{15,1},{1,3},{3,5},{... | collective-permute-start | bytes 393224 | tf_op jit(solution)/shard_map/ppermute | solution.py:415
  43.4 3.8 %collective-permute-start.6 = (f32[4,16,512]{2,1,0:T(8,128)S(1)}, f32[4,16,512]{2,1,0:T(8,128)S(1)}, u32[]{:S(2)}, u32[]{:S(2)}) collective-permute-start(f32[4,16,512]{2,1,0:T(8,128)S(1)} %add.9), channel_id=1, source_target_pairs={{14,2},{0,4},{2,6},{4,8},{6,10},{8,12},{15,3},{1,5},{3,7},{5,9},{7... | collective-permute-start | bytes 393224 | tf_op jit(solution)/shard_map/ppermute | solution.py:415
  48.2 10.1 %collective-permute-start.7 = (f32[8,16,512]{2,1,0:T(8,128)S(1)}, f32[8,16,512]{2,1,0:T(8,128)S(1)}, u32[]{:S(2)}, u32[]{:S(2)}) collective-permute-start(f32[8,16,512]{2,1,0:T(8,128)S(1)} %pad_maximum_fusion), channel_id=1, source_target_pairs={{0,2},{2,4},{4,6},{6,8},{8,10},{10,12},{12,14},{14,0},{1,3},{3,5},... | collective-permute-start | bytes 786440 | tf_op jit(solution)/shard_map/ppermute | solution.py:417
  50.5 6.2 %collective-permute-start.8 = (f32[4,16,512]{2,1,0:T(8,128)S(1)}, f32[4,16,512]{2,1,0:T(8,128)S(1)}, u32[]{:S(2)}, u32[]{:S(2)}) collective-permute-start(f32[4,16,512]{2,1,0:T(8,128)S(1)} %add.10), channel_id=1, source_target_pairs={{14,8},{0,10},{2,12},{4,14},{15,9},{1,11},{3,13},{5,15},{30,24},{1... | collective-permute-start | bytes 393224 | tf_op jit(solution)/shard_map/ppermute | solution.py:423

commit v14 on v12

--- a/solution.py
+++ b/solution.py
@@ -70,6 +70,11 @@
 
 def silu(values):
     return values / (1.0 + jnp.exp(-values))
+
+
+def silu_tanh(values):
+    half = 0.5 * values
+    return half + half * jnp.tanh(half)
 
 
 def feature_map(values):
@@ -299,7 +304,7 @@
             r = 4 * a + u
             start = r * width
             combined = hidden_local[:, start : start + width].astype(jnp.float32) + spread_mixed
-            act = silu(normalize_features(combined)).astype(jnp.bfloat16)
+            act = silu_tanh(normalize_features(combined)).astype(jnp.bfloat16)
             field = jnp.dot(out_w, act, preferred_element_type=jnp.float32)
             state = jnp.where(first_step, start_ref[:, r, :], previous_ref[0, :, r, :])
             denoised = scale_skip * state + scale_out * field

time: 58.5 us -> 58.2 us (level)
  no operation moved by 1% of the time
where the time goes in v14:
time: 58.2 us; the launch traced here: 57.9 us
  Pallas kernels  19.2 us (33%)
  waiting for transfers between devices  17 us (29%)
  starting transfers between devices  16.5 us (28%)
  other arithmetic  2.6 us (4%)
  local copies, waits for them, and re-layouts  1.96 us (3%)
  between operations  0.69 us (1%)
    pallas_call x1, Pallas kernels, local(): trunk(step_levels, previous, window_start, start_other, previous_other, c...  13.1 us
    ppermute x2, waiting for transfers between devices, rotated_prefix(): seed = seed + lax.ppermute(seed, axis, pairs)  10.2 us
    pallas_call x1, Pallas kernels, local(): head(step_levels, next_levels, hidden, queries, stats_own, stats_other, m...  6.13 us
    ppermute x1, starting transfers between devices, local(): lax.ppermute(step_levels, 'step', [((h + 1) % steps, h) for h in range(st...  5.77 us
    ppermute x1, starting transfers between devices, rotated_prefix(): lax.ppermute(seed, axis, [(holder(q), q + shift) for q in range(steps - s...  3.65 us
    ppermute x2, starting transfers between devices, rotated_prefix(): seed = seed + lax.ppermute(seed, axis, pairs)  3.32 us
    ppermute x1, waiting for transfers between devices, rotated_prefix(): lax.ppermute(seed, axis, [(holder(q), q + shift) for q in range(steps - s...  2.51 us
    ppermute x1, starting transfers between devices, rotated_prefix(): lax.ppermute(jnp.concatenate([seed, denoised], axis=0), axis, [(h, (h + 1...  2.36 us
  transfers between devices with their start and end apart: 9, of which 7 were waited for; matrix products, arithmetic and copies ran while one was open for 0% of the time, Pallas kernels for 0%

profile of v14, /device:TPU:0, one launch (start us, length us, event | category | flops | bytes accessed | tf_op | source)
XLA Modules:
  0.0 57.9 jit_solution(17342245512767881648)
XLA Ops:
  0.6 0.5 collective-permute-start.3
  1.1 0.1 collective-permute-start.1
  1.2 0.4 collective-permute-start.2
  1.7 1.0 %collective-permute-done.1.refs_3_ = f32[4,16,512]{2,1,0:T(8,128)S(1)} collective-permute-done((f32[4,16,512]{2,1,0:T(8,128)}, f32[4,16,512]{2,1,0:T(8,128)S(1)}, u32[]{:S(2)}, u32[]{:S(2)}) %collective-permute-start.1) | collective-permute-done | bytes 131104 | tf_op jit(solution)/shard_map/ppermute | solution.py:352
  2.7 0.0 copy-start.1
  2.7 0.2 collective-permute-done.2.refs_4_
  2.9 0.0 copy-start.2
  2.9 0.0 collective-permute-done.3.refs_6_
  2.9 0.5 copy-done.1
  3.4 0.2 copy-done.2
  3.6 0.0 copy-start
  3.6 0.7 %copy-done = bf16[12,16,512]{2,1,0:T(8,128)(2,1)} copy-done((bf16[12,16,512]{2,1,0:T(8,128)(2,1)}, bf16[12,16,512]{2,1,0:T(8,128)(2,1)S(1)}, u32[]{:S(2)}) %copy-start) | copy-done | bytes 196632
  4.2 13.1 %shard_map.122 = (bf16[128,8192]{1,0:T(8,128)(2,1)}, f32[128,512]{1,0:T(8,128)}, f32[128,128]{1,0:T(8,128)}) custom-call(s32[1,2]{1,0:T(1,128)} %refs_0_.3, f32[1,4,16,512]{3,2,1,0:T(8,128)} %refs_8_.3, f32[4,16,512]{2,1,0:T(8,128)} %refs_9_.3, f32[4,16,512]{2,1,0:T(8,128)} %copy-done.1, f32[1,4,16,512]{3,2,1,0:T(8,128)} %copy-done.2, ...), custom_call_target="tpu_custom_call" | custom-call | tf_op jit(solution)/shard_map/pallas_call | solution.py:380
  17.3 0.4 collective-permute-start.4
  17.7 5.8 %collective-permute-start = (s32[1,2]{1,0:T(1,128)}, s32[1,2]{1,0:T(1,128)S(1)}, u32[]{:S(2)}, u32[]{:S(2)}) collective-permute-start(s32[1,2]{1,0:T(1,128)} %refs_0_.3), channel_id=1, source_target_pairs={{2,0},{4,2},{6,4},{8,6},{10,8},{12,10},{14,12},{0,14},{3,1},{5,3},... | collective-permute-start | bytes 32 | tf_op jit(solution)/shard_map/ppermute | solution.py:349
  23.5 1.4 %collective-permute-done.refs_1_ = s32[1,2]{1,0:T(1,128)S(1)} collective-permute-done((s32[1,2]{1,0:T(1,128)}, s32[1,2]{1,0:T(1,128)S(1)}, u32[]{:S(2)}, u32[]{:S(2)}) %collective-permute-start) | collective-permute-done | bytes 40 | tf_op jit(solution)/shard_map/ppermute | solution.py:349
  24.9 0.0 copy-start.4
  24.9 0.0 collective-permute-done.4.refs_5_
  24.9 0.0 copy-start.3
  24.9 0.6 %copy-done.4 = s32[1,2]{1,0:T(1,128)} copy-done((s32[1,2]{1,0:T(1,128)}, s32[1,2]{1,0:T(1,128)S(1)}, u32[]{:S(2)}) %copy-start.4) | copy-done | bytes 32
  25.5 0.0 copy-done.3
  25.5 6.1 %shard_map.123 = (f32[4,16,512]{2,1,0:T(8,128)}, f32[4,16,512]{2,1,0:T(8,128)}) custom-call(s32[1,2]{1,0:T(1,128)} %refs_0_.3, s32[1,2]{1,0:T(1,128)} %copy-done.4, bf16[128,8192]{1,0:T(8,128)(2,1)} %get-tuple-element.7.refs_2_, f32[128,512]{1,0:T(8,128)} %get-tuple-element.8.refs_3_, f32[128,128]{1,0:T(8,128)} %get-tuple-element.9.refs_4_, ...), custom_call_target="tpu_custom_call" | custom-call | tf_op jit(solution)/shard_map/pallas_call | solution.py:409
  31.7 2.0 %collective-permute-start.5 = (f32[4,16,512]{2,1,0:T(8,128)}, f32[4,16,512]{2,1,0:T(8,128)S(1)}, u32[]{:S(2)}, u32[]{:S(2)}) collective-permute-start(f32[4,16,512]{2,1,0:T(8,128)} %get-tuple-element.10), channel_id=1, source_target_pairs={{14,0},{0,2},{2,4},{4,6},{6,8},{8,10},{10,12},{15,1},{1,3},{3,5},{... | collective-permute-start | bytes 393224 | tf_op jit(solution)/shard_map/ppermute | solution.py:423
  33.7 7.7 %collective-permute-done.5 = f32[4,16,512]{2,1,0:T(8,128)S(1)} collective-permute-done((f32[4,16,512]{2,1,0:T(8,128)}, f32[4,16,512]{2,1,0:T(8,128)S(1)}, u32[]{:S(2)}, u32[]{:S(2)}) %collective-permute-start.5) | collective-permute-done | bytes 131104 | tf_op jit(solution)/shard_map/ppermute | solution.py:423
  41.5 0.9 %add.9 = f32[4,16,512]{2,1,0:T(8,128)S(1)} add(f32[4,16,512]{2,1,0:T(8,128)} %get-tuple-element.10, f32[4,16,512]{2,1,0:T(8,128)S(1)} %collective-permute-done.5) | non-fusion elementwise | flops 32768 | bytes 393216 | tf_op jit(solution)/shard_map/add | solution.py:423
  42.4 1.3 %collective-permute-start.6 = (f32[4,16,512]{2,1,0:T(8,128)S(1)}, f32[4,16,512]{2,1,0:T(8,128)S(1)}, u32[]{:S(2)}, u32[]{:S(2)}) collective-permute-start(f32[4,16,512]{2,1,0:T(8,128)S(1)} %add.9), channel_id=1, source_target_pairs={{14,2},{0,4},{2,6},{4,8},{6,10},{8,12},{15,3},{1,5},{3,7},{5,9},{7... | collective-permute-start | bytes 393224 | tf_op jit(solution)/shard_map/ppermute | solution.py:423
  43.7 2.5 %collective-permute-done.6 = f32[4,16,512]{2,1,0:T(8,128)S(1)} collective-permute-done((f32[4,16,512]{2,1,0:T(8,128)S(1)}, f32[4,16,512]{2,1,0:T(8,128)S(1)}, u32[]{:S(2)}, u32[]{:S(2)}) %collective-permute-start.6) | collective-permute-done | bytes 131104 | tf_op jit(solution)/shard_map/ppermute | solution.py:423
  46.2 0.9 %pad_maximum_fusion = f32[8,16,512]{2,1,0:T(8,128)S(1)} fusion(f32[4,16,512]{2,1,0:T(8,128)} %get-tuple-element.11, f32[4,16,512]{2,1,0:T(8,128)S(1)} %add.10), kind=kLoop, calls=%fused_computation | loop fusion | flops 65536 | bytes 524288 | tf_op jit(solution)/shard_map/concatenate | solution.py:426
  47.1 2.4 %collective-permute-start.7 = (f32[8,16,512]{2,1,0:T(8,128)S(1)}, f32[8,16,512]{2,1,0:T(8,128)S(1)}, u32[]{:S(2)}, u32[]{:S(2)}) collective-permute-start(f32[8,16,512]{2,1,0:T(8,128)S(1)} %pad_maximum_fusion), channel_id=1, source_target_pairs={{0,2},{2,4},{4,6},{6,8},{8,10},{10,12},{12,14},{14,0},{1,3},{3,5},... | collective-permute-start | bytes 786440 | tf_op jit(solution)/shard_map/ppermute | solution.py:425
  49.5 3.6 %collective-permute-start.8 = (f32[4,16,512]{2,1,0:T(8,128)S(1)}, f32[4,16,512]{2,1,0:T(8,128)S(1)}, u32[]{:S(2)}, u32[]{:S(2)}) collective-permute-start(f32[4,16,512]{2,1,0:T(8,128)S(1)} %add.10), channel_id=1, source_target_pairs={{14,8},{0,10},{2,12},{4,14},{15,9},{1,11},{3,13},{5,15},{30,24},{1... | collective-permute-start | bytes 393224 | tf_op jit(solution)/shard_map/ppermute | solution.py:431
  53.1 2.5 %collective-permute-done.8 = f32[4,16,512]{2,1,0:T(8,128)S(1)} collective-permute-done((f32[4,16,512]{2,1,0:T(8,128)S(1)}, f32[4,16,512]{2,1,0:T(8,128)S(1)}, u32[]{:S(2)}, u32[]{:S(2)}) %collective-permute-start.8) | collective-permute-done | bytes 131104 | tf_op jit(solution)/shard_map/ppermute | solution.py:431
  55.6 1.5 %collective-permute-done.7 = f32[8,16,512]{2,1,0:T(8,128)S(1)} collective-permute-done((f32[8,16,512]{2,1,0:T(8,128)S(1)}, f32[8,16,512]{2,1,0:T(8,128)S(1)}, u32[]{:S(2)}, u32[]{:S(2)}) %collective-permute-start.7) | collective-permute-done | bytes 262176 | tf_op jit(solution)/shard_map/ppermute | solution.py:425
  57.2 0.7 %slice_bitcast_fusion = (f32[1,4,16,512]{3,2,1,0:T(8,128)}, f32[1,4,16,512]{3,2,1,0:T(8,128)}) fusion(f32[8,16,512]{2,1,0:T(8,128)S(1)} %collective-permute-done.7, f32[4,16,512]{2,1,0:T(8,128)S(1)} %collective-permute-done.8), kind=kLoop, calls=%fused_computation.1 | loop fusion | flops 32768 | bytes 655360 | tf_op jit(solution)/shard_map/broadcast_in_dim | solution.py:414
  (1 shorter events, 0.0 us)
Async XLA Ops:
  0.6 2.3 %collective-permute-start.3 = (bf16[12,16,512]{2,1,0:T(8,128)(2,1)}, bf16[12,16,512]{2,1,0:T(8,128)(2,1)S(1)}, u32[]{:S(2)}, u32[]{:S(2)}) collective-permute-start(bf16[12,16,512]{2,1,0:T(8,128)(2,1)} %refs_5_.1), channel_id=1, source_target_pairs={{0,1},{1,0},{2,3},{3,2},{4,5},{5,4},{6,7},{7,6},{8,9},{9,8},{10,11... | collective-permute-start | bytes 589832 | tf_op jit(solution)/shard_map/ppermute | solution.py:353
  1.1 1.6 %collective-permute-start.1 = (f32[4,16,512]{2,1,0:T(8,128)}, f32[4,16,512]{2,1,0:T(8,128)S(1)}, u32[]{:S(2)}, u32[]{:S(2)}) collective-permute-start(f32[4,16,512]{2,1,0:T(8,128)} %refs_9_.3), channel_id=1, source_target_pairs={{0,1},{1,0},{2,3},{3,2},{4,5},{5,4},{6,7},{7,6},{8,9},{9,8},{10,11... | collective-permute-start | bytes 393224 | tf_op jit(solution)/shard_map/ppermute | solution.py:352
  1.2 1.7 %collective-permute-start.2 = (f32[1,4,16,512]{3,2,1,0:T(8,128)}, f32[1,4,16,512]{3,2,1,0:T(8,128)S(1)}, u32[]{:S(2)}, u32[]{:S(2)}) collective-permute-start(f32[1,4,16,512]{3,2,1,0:T(8,128)} %refs_8_.3), channel_id=1, source_target_pairs={{0,1},{1,0},{2,3},{3,2},{4,5},{5,4},{6,7},{7,6},{8,9},{9,8},{10,11... | collective-permute-start | bytes 393224 | tf_op jit(solution)/shard_map/ppermute | solution.py:351
  2.7 0.7 %copy-start.1 = (f32[4,16,512]{2,1,0:T(8,128)}, f32[4,16,512]{2,1,0:T(8,128)S(1)}, u32[]{:S(2)}) copy-start(f32[4,16,512]{2,1,0:T(8,128)S(1)} %collective-permute-done.1.refs_3_) | copy-start | bytes 393220
  2.9 0.7 %copy-start.2 = (f32[1,4,16,512]{3,2,1,0:T(8,128)}, f32[1,4,16,512]{3,2,1,0:T(8,128)S(1)}, u32[]{:S(2)}) copy-start(f32[1,4,16,512]{3,2,1,0:T(8,128)S(1)} %collective-permute-done.2.refs_4_) | copy-start | bytes 393220
  3.6 0.7 %copy-start = (bf16[12,16,512]{2,1,0:T(8,128)(2,1)}, bf16[12,16,512]{2,1,0:T(8,128)(2,1)S(1)}, u32[]{:S(2)}) copy-start(bf16[12,16,512]{2,1,0:T(8,128)(2,1)S(1)} %collective-permute-done.3.refs_6_) | copy-start | bytes 589828
  17.3 7.6 %collective-permute-start.4 = (f32[128,128]{1,0:T(8,128)}, f32[128,128]{1,0:T(8,128)S(1)}, u32[]{:S(2)}, u32[]{:S(2)}) collective-permute-start(f32[128,128]{1,0:T(8,128)} %get-tuple-element.9.refs_4_), channel_id=1, source_target_pairs={{0,1},{1,0},{2,3},{3,2},{4,5},{5,4},{6,7},{7,6},{8,9},{9,8},{10,11... | collective-permute-start | bytes 196616 | tf_op jit(solution)/shard_map/ppermute | solution.py:394
  17.7 7.2 %collective-permute-start = (s32[1,2]{1,0:T(1,128)}, s32[1,2]{1,0:T(1,128)S(1)}, u32[]{:S(2)}, u32[]{:S(2)}) collective-permute-start(s32[1,2]{1,0:T(1,128)} %refs_0_.3), channel_id=1, source_target_pairs={{2,0},{4,2},{6,4},{8,6},{10,8},{12,10},{14,12},{0,14},{3,1},{5,3},... | collective-permute-start | bytes 32 | tf_op jit(solution)/shard_map/ppermute | solution.py:349
  24.9 0.6 %copy-start.4 = (s32[1,2]{1,0:T(1,128)}, s32[1,2]{1,0:T(1,128)S(1)}, u32[]{:S(2)}) copy-start(s32[1,2]{1,0:T(1,128)S(1)} %collective-permute-done.refs_1_) | copy-start | bytes 28
  24.9 0.6 %copy-start.3 = (f32[128,128]{1,0:T(8,128)}, f32[128,128]{1,0:T(8,128)S(1)}, u32[]{:S(2)}) copy-start(f32[128,128]{1,0:T(8,128)S(1)} %collective-permute-done.4.refs_5_) | copy-start | bytes 196612
  31.7 9.8 %collective-permute-start.5 = (f32[4,16,512]{2,1,0:T(8,128)}, f32[4,16,512]{2,1,0:T(8,128)S(1)}, u32[]{:S(2)}, u32[]{:S(2)}) collective-permute-start(f32[4,16,512]{2,1,0:T(8,128)} %get-tuple-element.10), channel_id=1, source_target_pairs={{14,0},{0,2},{2,4},{4,6},{6,8},{8,10},{10,12},{15,1},{1,3},{3,5},{... | collective-permute-start | bytes 393224 | tf_op jit(solution)/shard_map/ppermute | solution.py:423
  42.4 3.8 %collective-permute-start.6 = (f32[4,16,512]{2,1,0:T(8,128)S(1)}, f32[4,16,512]{2,1,0:T(8,128)S(1)}, u32[]{:S(2)}, u32[]{:S(2)}) collective-permute-start(f32[4,16,512]{2,1,0:T(8,128)S(1)} %add.9), channel_id=1, source_target_pairs={{14,2},{0,4},{2,6},{4,8},{6,10},{8,12},{15,3},{1,5},{3,7},{5,9},{7... | collective-permute-start | bytes 393224 | tf_op jit(solution)/shard_map/ppermute | solution.py:423
  47.1 10.1 %collective-permute-start.7 = (f32[8,16,512]{2,1,0:T(8,128)S(1)}, f32[8,16,512]{2,1,0:T(8,128)S(1)}, u32[]{:S(2)}, u32[]{:S(2)}) collective-permute-start(f32[8,16,512]{2,1,0:T(8,128)S(1)} %pad_maximum_fusion), channel_id=1, source_target_pairs={{0,2},{2,4},{4,6},{6,8},{8,10},{10,12},{12,14},{14,0},{1,3},{3,5},... | collective-permute-start | bytes 786440 | tf_op jit(solution)/shard_map/ppermute | solution.py:425
  49.5 6.2 %collective-permute-start.8 = (f32[4,16,512]{2,1,0:T(8,128)S(1)}, f32[4,16,512]{2,1,0:T(8,128)S(1)}, u32[]{:S(2)}, u32[]{:S(2)}) collective-permute-start(f32[4,16,512]{2,1,0:T(8,128)S(1)} %add.10), channel_id=1, source_target_pairs={{14,8},{0,10},{2,12},{4,14},{15,9},{1,11},{3,13},{5,15},{30,24},{1... | collective-permute-start | bytes 393224 | tf_op jit(solution)/shard_map/ppermute | solution.py:431

commit v15 on v14

--- a/solution.py
+++ b/solution.py
@@ -167,21 +167,30 @@
 
     span = CHUNK_ROWS * width
     in_rows = band_rows + 2 * HALO
-    for q in range(in_rows // CHUNK_ROWS):
-        start = q * span
+    def lift_chunk(start, keep):
         chunk = inputs[:, start : start + span].astype(jnp.bfloat16)
         lifted = jnp.dot(lift_w, chunk, preferred_element_type=jnp.float32)
         lifted = (lifted + embed).astype(jnp.bfloat16)
+        if keep is not None:
+            lifted_keep[:, keep : keep + span] = lifted
+        act = silu(normalize_features(lifted.astype(jnp.float32)))
+        act_first[:, start : start + span] = act.astype(jnp.bfloat16)
+
+    for q in range(in_rows // CHUNK_ROWS):
+        start = q * span
         row0 = q * CHUNK_ROWS
         if HALO <= row0 < HALO + band_rows:
-            keep = (row0 - HALO) * width
-            lifted_keep[:, keep : keep + span] = lifted
-        act = silu(normalize_features(lifted.astype(jnp.float32)))
-        if row0 < HALO:
-            act = jnp.where(top_outside, 0.0, act)
-        if row0 >= HALO + band_rows:
-            act = jnp.where(bottom_outside, 0.0, act)
-        act_first[:, start : start + span] = act.astype(jnp.bfloat16)
+            lift_chunk(start, (row0 - HALO) * width)
+            continue
+        outside = top_outside if row0 < HALO else bottom_outside
+
+        @pl.when(outside)
+        def _():
+            act_first[:, start : start + span] = jnp.zeros((act_first.shape[0], span), jnp.bfloat16)
+
+        @pl.when(jnp.logical_not(outside))
+        def _():
+            lift_chunk(start, None)
     first_w = stack_taps(first_ref)
     mid_rows = band_rows + 2
     chunks = row_chunks(mid_rows)

time: 58.2 us -> 59.7 us (1.026)
  Pallas kernels: 19.2 us -> 20.7 us
    pallas_call x1, Pallas kernels: 13.1 us -> 14.5 us  [local(): trunk(step_levels, previous, window_start, start_other, previous_other, c...]
where the time goes in v15:
time: 59.7 us; the launch traced here: 59.4 us
  Pallas kernels  20.7 us (35%)
  waiting for transfers between devices  16.9 us (28%)
  starting transfers between devices  16.5 us (28%)
  other arithmetic  2.6 us (4%)
  local copies, waits for them, and re-layouts  1.96 us (3%)
  between operations  0.69 us (1%)
    pallas_call x1, Pallas kernels, local(): trunk(step_levels, previous, window_start, start_other, previous_other, c...  14.5 us
    ppermute x2, waiting for transfers between devices, rotated_prefix(): seed = seed + lax.ppermute(seed, axis, pairs)  10.2 us
    pallas_call x1, Pallas kernels, local(): head(step_levels, next_levels, hidden, queries, stats_own, stats_other, m...  6.13 us
    ppermute x1, starting transfers between devices, local(): lax.ppermute(step_levels, 'step', [((h + 1) % steps, h) for h in range(st...  5.8 us
    ppermute x1, starting transfers between devices, rotated_prefix(): lax.ppermute(seed, axis, [(holder(q), q + shift) for q in range(steps - s...  3.68 us
    ppermute x2, starting transfers between devices, rotated_prefix(): seed = seed + lax.ppermute(seed, axis, pairs)  3.31 us
    ppermute x1, waiting for transfers between devices, rotated_prefix(): lax.ppermute(seed, axis, [(holder(q), q + shift) for q in range(steps - s...  2.51 us
    ppermute x1, starting transfers between devices, rotated_prefix(): lax.ppermute(jnp.concatenate([seed, denoised], axis=0), axis, [(h, (h + 1...  2.32 us
  transfers between devices with their start and end apart: 9, of which 7 were waited for; matrix products, arithmetic and copies ran while one was open for 0% of the time, Pallas kernels for 0%

profile of v15, /device:TPU:0, one launch (start us, length us, event | category | flops | bytes accessed | tf_op | source)
XLA Modules:
  0.0 59.4 jit_solution(18237875370501253826)
XLA Ops:
  0.6 0.5 collective-permute-start.3
  1.1 0.1 collective-permute-start.1
  1.2 0.4 collective-permute-start.2
  1.7 1.0 %collective-permute-done.1.refs_3_ = f32[4,16,512]{2,1,0:T(8,128)S(1)} collective-permute-done((f32[4,16,512]{2,1,0:T(8,128)}, f32[4,16,512]{2,1,0:T(8,128)S(1)}, u32[]{:S(2)}, u32[]{:S(2)}) %collective-permute-start.1) | collective-permute-done | bytes 131104 | tf_op jit(solution)/shard_map/ppermute | solution.py:361
  2.7 0.0 copy-start.1
  2.7 0.2 collective-permute-done.2.refs_4_
  2.9 0.0 copy-start.2
  2.9 0.0 collective-permute-done.3.refs_6_
  2.9 0.5 copy-done.1
  3.4 0.2 copy-done.2
  3.6 0.0 copy-start
  3.6 0.7 %copy-done = bf16[12,16,512]{2,1,0:T(8,128)(2,1)} copy-done((bf16[12,16,512]{2,1,0:T(8,128)(2,1)}, bf16[12,16,512]{2,1,0:T(8,128)(2,1)S(1)}, u32[]{:S(2)}) %copy-start) | copy-done | bytes 196632
  4.2 14.5 %shard_map.122 = (bf16[128,8192]{1,0:T(8,128)(2,1)}, f32[128,512]{1,0:T(8,128)}, f32[128,128]{1,0:T(8,128)}) custom-call(s32[1,2]{1,0:T(1,128)} %refs_0_.3, f32[1,4,16,512]{3,2,1,0:T(8,128)} %refs_8_.3, f32[4,16,512]{2,1,0:T(8,128)} %refs_9_.3, f32[4,16,512]{2,1,0:T(8,128)} %copy-done.1, f32[1,4,16,512]{3,2,1,0:T(8,128)} %copy-done.2, ...), custom_call_target="tpu_custom_call" | custom-call | tf_op jit(solution)/shard_map/pallas_call | solution.py:389
  18.8 0.4 collective-permute-start.4
  19.2 5.8 %collective-permute-start = (s32[1,2]{1,0:T(1,128)}, s32[1,2]{1,0:T(1,128)S(1)}, u32[]{:S(2)}, u32[]{:S(2)}) collective-permute-start(s32[1,2]{1,0:T(1,128)} %refs_0_.3), channel_id=1, source_target_pairs={{2,0},{4,2},{6,4},{8,6},{10,8},{12,10},{14,12},{0,14},{3,1},{5,3},... | collective-permute-start | bytes 32 | tf_op jit(solution)/shard_map/ppermute | solution.py:358
  25.0 1.4 %collective-permute-done.refs_1_ = s32[1,2]{1,0:T(1,128)S(1)} collective-permute-done((s32[1,2]{1,0:T(1,128)}, s32[1,2]{1,0:T(1,128)S(1)}, u32[]{:S(2)}, u32[]{:S(2)}) %collective-permute-start) | collective-permute-done | bytes 40 | tf_op jit(solution)/shard_map/ppermute | solution.py:358
  26.4 0.0 copy-start.4
  26.4 0.0 collective-permute-done.4.refs_5_
  26.4 0.0 copy-start.3
  26.4 0.6 copy-done.4
  27.0 0.0 copy-done.3
  27.0 6.1 %shard_map.123 = (f32[4,16,512]{2,1,0:T(8,128)}, f32[4,16,512]{2,1,0:T(8,128)}) custom-call(s32[1,2]{1,0:T(1,128)} %refs_0_.3, s32[1,2]{1,0:T(1,128)} %copy-done.4, bf16[128,8192]{1,0:T(8,128)(2,1)} %get-tuple-element.7.refs_2_, f32[128,512]{1,0:T(8,128)} %get-tuple-element.8.refs_3_, f32[128,128]{1,0:T(8,128)} %get-tuple-element.9.refs_4_, ...), custom_call_target="tpu_custom_call" | custom-call | tf_op jit(solution)/shard_map/pallas_call | solution.py:418
  33.2 2.0 %collective-permute-start.5 = (f32[4,16,512]{2,1,0:T(8,128)}, f32[4,16,512]{2,1,0:T(8,128)S(1)}, u32[]{:S(2)}, u32[]{:S(2)}) collective-permute-start(f32[4,16,512]{2,1,0:T(8,128)} %get-tuple-element.10), channel_id=1, source_target_pairs={{14,0},{0,2},{2,4},{4,6},{6,8},{8,10},{10,12},{15,1},{1,3},{3,5},{... | collective-permute-start | bytes 393224 | tf_op jit(solution)/shard_map/ppermute | solution.py:432
  35.2 7.7 %collective-permute-done.5 = f32[4,16,512]{2,1,0:T(8,128)S(1)} collective-permute-done((f32[4,16,512]{2,1,0:T(8,128)}, f32[4,16,512]{2,1,0:T(8,128)S(1)}, u32[]{:S(2)}, u32[]{:S(2)}) %collective-permute-start.5) | collective-permute-done | bytes 131104 | tf_op jit(solution)/shard_map/ppermute | solution.py:432
  42.9 0.9 %add.9 = f32[4,16,512]{2,1,0:T(8,128)S(1)} add(f32[4,16,512]{2,1,0:T(8,128)} %get-tuple-element.10, f32[4,16,512]{2,1,0:T(8,128)S(1)} %collective-permute-done.5) | non-fusion elementwise | flops 32768 | bytes 393216 | tf_op jit(solution)/shard_map/add | solution.py:432
  43.9 1.3 %collective-permute-start.6 = (f32[4,16,512]{2,1,0:T(8,128)S(1)}, f32[4,16,512]{2,1,0:T(8,128)S(1)}, u32[]{:S(2)}, u32[]{:S(2)}) collective-permute-start(f32[4,16,512]{2,1,0:T(8,128)S(1)} %add.9), channel_id=1, source_target_pairs={{14,2},{0,4},{2,6},{4,8},{6,10},{8,12},{15,3},{1,5},{3,7},{5,9},{7... | collective-permute-start | bytes 393224 | tf_op jit(solution)/shard_map/ppermute | solution.py:432
  45.2 2.5 %collective-permute-done.6 = f32[4,16,512]{2,1,0:T(8,128)S(1)} collective-permute-done((f32[4,16,512]{2,1,0:T(8,128)S(1)}, f32[4,16,512]{2,1,0:T(8,128)S(1)}, u32[]{:S(2)}, u32[]{:S(2)}) %collective-permute-start.6) | collective-permute-done | bytes 131104 | tf_op jit(solution)/shard_map/ppermute | solution.py:432
  47.7 0.9 %pad_maximum_fusion = f32[8,16,512]{2,1,0:T(8,128)S(1)} fusion(f32[4,16,512]{2,1,0:T(8,128)} %get-tuple-element.11, f32[4,16,512]{2,1,0:T(8,128)S(1)} %add.10), kind=kLoop, calls=%fused_computation | loop fusion | flops 65536 | bytes 524288 | tf_op jit(solution)/shard_map/concatenate | solution.py:435
  48.6 2.3 %collective-permute-start.7 = (f32[8,16,512]{2,1,0:T(8,128)S(1)}, f32[8,16,512]{2,1,0:T(8,128)S(1)}, u32[]{:S(2)}, u32[]{:S(2)}) collective-permute-start(f32[8,16,512]{2,1,0:T(8,128)S(1)} %pad_maximum_fusion), channel_id=1, source_target_pairs={{0,2},{2,4},{4,6},{6,8},{8,10},{10,12},{12,14},{14,0},{1,3},{3,5},... | collective-permute-start | bytes 786440 | tf_op jit(solution)/shard_map/ppermute | solution.py:434
  50.9 3.7 %collective-permute-start.8 = (f32[4,16,512]{2,1,0:T(8,128)S(1)}, f32[4,16,512]{2,1,0:T(8,128)S(1)}, u32[]{:S(2)}, u32[]{:S(2)}) collective-permute-start(f32[4,16,512]{2,1,0:T(8,128)S(1)} %add.10), channel_id=1, source_target_pairs={{14,8},{0,10},{2,12},{4,14},{15,9},{1,11},{3,13},{5,15},{30,24},{1... | collective-permute-start | bytes 393224 | tf_op jit(solution)/shard_map/ppermute | solution.py:440
  54.6 2.5 %collective-permute-done.8 = f32[4,16,512]{2,1,0:T(8,128)S(1)} collective-permute-done((f32[4,16,512]{2,1,0:T(8,128)S(1)}, f32[4,16,512]{2,1,0:T(8,128)S(1)}, u32[]{:S(2)}, u32[]{:S(2)}) %collective-permute-start.8) | collective-permute-done | bytes 131104 | tf_op jit(solution)/shard_map/ppermute | solution.py:440
  57.1 1.5 %collective-permute-done.7 = f32[8,16,512]{2,1,0:T(8,128)S(1)} collective-permute-done((f32[8,16,512]{2,1,0:T(8,128)S(1)}, f32[8,16,512]{2,1,0:T(8,128)S(1)}, u32[]{:S(2)}, u32[]{:S(2)}) %collective-permute-start.7) | collective-permute-done | bytes 262176 | tf_op jit(solution)/shard_map/ppermute | solution.py:434
  58.6 0.7 %slice_bitcast_fusion = (f32[1,4,16,512]{3,2,1,0:T(8,128)}, f32[1,4,16,512]{3,2,1,0:T(8,128)}) fusion(f32[8,16,512]{2,1,0:T(8,128)S(1)} %collective-permute-done.7, f32[4,16,512]{2,1,0:T(8,128)S(1)} %collective-permute-done.8), kind=kLoop, calls=%fused_computation.1 | loop fusion | flops 32768 | bytes 655360 | tf_op jit(solution)/shard_map/broadcast_in_dim | solution.py:423
  (1 shorter events, 0.0 us)
Async XLA Ops:
  0.6 2.3 %collective-permute-start.3 = (bf16[12,16,512]{2,1,0:T(8,128)(2,1)}, bf16[12,16,512]{2,1,0:T(8,128)(2,1)S(1)}, u32[]{:S(2)}, u32[]{:S(2)}) collective-permute-start(bf16[12,16,512]{2,1,0:T(8,128)(2,1)} %refs_5_.1), channel_id=1, source_target_pairs={{0,1},{1,0},{2,3},{3,2},{4,5},{5,4},{6,7},{7,6},{8,9},{9,8},{10,11... | collective-permute-start | bytes 589832 | tf_op jit(solution)/shard_map/ppermute | solution.py:362
  1.1 1.6 %collective-permute-start.1 = (f32[4,16,512]{2,1,0:T(8,128)}, f32[4,16,512]{2,1,0:T(8,128)S(1)}, u32[]{:S(2)}, u32[]{:S(2)}) collective-permute-start(f32[4,16,512]{2,1,0:T(8,128)} %refs_9_.3), channel_id=1, source_target_pairs={{0,1},{1,0},{2,3},{3,2},{4,5},{5,4},{6,7},{7,6},{8,9},{9,8},{10,11... | collective-permute-start | bytes 393224 | tf_op jit(solution)/shard_map/ppermute | solution.py:361
  1.2 1.7 %collective-permute-start.2 = (f32[1,4,16,512]{3,2,1,0:T(8,128)}, f32[1,4,16,512]{3,2,1,0:T(8,128)S(1)}, u32[]{:S(2)}, u32[]{:S(2)}) collective-permute-start(f32[1,4,16,512]{3,2,1,0:T(8,128)} %refs_8_.3), channel_id=1, source_target_pairs={{0,1},{1,0},{2,3},{3,2},{4,5},{5,4},{6,7},{7,6},{8,9},{9,8},{10,11... | collective-permute-start | bytes 393224 | tf_op jit(solution)/shard_map/ppermute | solution.py:360
  2.7 0.7 %copy-start.1 = (f32[4,16,512]{2,1,0:T(8,128)}, f32[4,16,512]{2,1,0:T(8,128)S(1)}, u32[]{:S(2)}) copy-start(f32[4,16,512]{2,1,0:T(8,128)S(1)} %collective-permute-done.1.refs_3_) | copy-start | bytes 393220
  2.9 0.7 %copy-start.2 = (f32[1,4,16,512]{3,2,1,0:T(8,128)}, f32[1,4,16,512]{3,2,1,0:T(8,128)S(1)}, u32[]{:S(2)}) copy-start(f32[1,4,16,512]{3,2,1,0:T(8,128)S(1)} %collective-permute-done.2.refs_4_) | copy-start | bytes 393220
  3.6 0.7 %copy-start = (bf16[12,16,512]{2,1,0:T(8,128)(2,1)}, bf16[12,16,512]{2,1,0:T(8,128)(2,1)S(1)}, u32[]{:S(2)}) copy-start(bf16[12,16,512]{2,1,0:T(8,128)(2,1)S(1)} %collective-permute-done.3.refs_6_) | copy-start | bytes 589828
  18.8 7.6 %collective-permute-start.4 = (f32[128,128]{1,0:T(8,128)}, f32[128,128]{1,0:T(8,128)S(1)}, u32[]{:S(2)}, u32[]{:S(2)}) collective-permute-start(f32[128,128]{1,0:T(8,128)} %get-tuple-element.9.refs_4_), channel_id=1, source_target_pairs={{0,1},{1,0},{2,3},{3,2},{4,5},{5,4},{6,7},{7,6},{8,9},{9,8},{10,11... | collective-permute-start | bytes 196616 | tf_op jit(solution)/shard_map/ppermute | solution.py:403
  19.2 7.2 %collective-permute-start = (s32[1,2]{1,0:T(1,128)}, s32[1,2]{1,0:T(1,128)S(1)}, u32[]{:S(2)}, u32[]{:S(2)}) collective-permute-start(s32[1,2]{1,0:T(1,128)} %refs_0_.3), channel_id=1, source_target_pairs={{2,0},{4,2},{6,4},{8,6},{10,8},{12,10},{14,12},{0,14},{3,1},{5,3},... | collective-permute-start | bytes 32 | tf_op jit(solution)/shard_map/ppermute | solution.py:358
  26.4 0.6 copy-start.4
  26.4 0.6 %copy-start.3 = (f32[128,128]{1,0:T(8,128)}, f32[128,128]{1,0:T(8,128)S(1)}, u32[]{:S(2)}) copy-start(f32[128,128]{1,0:T(8,128)S(1)} %collective-permute-done.4.refs_5_) | copy-start | bytes 196612
  33.2 9.8 %collective-permute-start.5 = (f32[4,16,512]{2,1,0:T(8,128)}, f32[4,16,512]{2,1,0:T(8,128)S(1)}, u32[]{:S(2)}, u32[]{:S(2)}) collective-permute-start(f32[4,16,512]{2,1,0:T(8,128)} %get-tuple-element.10), channel_id=1, source_target_pairs={{14,0},{0,2},{2,4},{4,6},{6,8},{8,10},{10,12},{15,1},{1,3},{3,5},{... | collective-permute-start | bytes 393224 | tf_op jit(solution)/shard_map/ppermute | solution.py:432
  43.9 3.8 %collective-permute-start.6 = (f32[4,16,512]{2,1,0:T(8,128)S(1)}, f32[4,16,512]{2,1,0:T(8,128)S(1)}, u32[]{:S(2)}, u32[]{:S(2)}) collective-permute-start(f32[4,16,512]{2,1,0:T(8,128)S(1)} %add.9), channel_id=1, source_target_pairs={{14,2},{0,4},{2,6},{4,8},{6,10},{8,12},{15,3},{1,5},{3,7},{5,9},{7... | collective-permute-start | bytes 393224 | tf_op jit(solution)/shard_map/ppermute | solution.py:432
  48.6 10.0 %collective-permute-start.7 = (f32[8,16,512]{2,1,0:T(8,128)S(1)}, f32[8,16,512]{2,1,0:T(8,128)S(1)}, u32[]{:S(2)}, u32[]{:S(2)}) collective-permute-start(f32[8,16,512]{2,1,0:T(8,128)S(1)} %pad_maximum_fusion), channel_id=1, source_target_pairs={{0,2},{2,4},{4,6},{6,8},{8,10},{10,12},{12,14},{14,0},{1,3},{3,5},... | collective-permute-start | bytes 786440 | tf_op jit(solution)/shard_map/ppermute | solution.py:434
  50.9 6.2 %collective-permute-start.8 = (f32[4,16,512]{2,1,0:T(8,128)S(1)}, f32[4,16,512]{2,1,0:T(8,128)S(1)}, u32[]{:S(2)}, u32[]{:S(2)}) collective-permute-start(f32[4,16,512]{2,1,0:T(8,128)S(1)} %add.10), channel_id=1, source_target_pairs={{14,8},{0,10},{2,12},{4,14},{15,9},{1,11},{3,13},{5,15},{30,24},{1... | collective-permute-start | bytes 393224 | tf_op jit(solution)/shard_map/ppermute | solution.py:440

commit v16 on v14

--- a/solution.py
+++ b/solution.py
@@ -189,7 +189,7 @@
         span = rows * width
         lanes = lax.broadcasted_iota(jnp.int32, (1, span), 1)
         middle = conv_chunk(act_first, first_w, first, rows, width, lanes % width)
-        act = silu(normalize_features(middle))
+        act = silu_tanh(normalize_features(middle))
         if q == 0:
             act = jnp.where(jnp.logical_and(top_outside, lanes < width), 0.0, act)
         if q == len(chunks) - 1:

time: 58.2 us -> 58.3 us (level)
  no operation moved by 1% of the time
where the time goes in v16:
time: 58.3 us; the launch traced here: 58 us
  Pallas kernels  19.4 us (33%)
  waiting for transfers between devices  17 us (29%)
  starting transfers between devices  16.5 us (28%)
  other arithmetic  2.6 us (4%)
  local copies, waits for them, and re-layouts  1.96 us (3%)
  between operations  0.69 us (1%)
    pallas_call x1, Pallas kernels, local(): trunk(step_levels, previous, window_start, start_other, previous_other, c...  13.2 us
    ppermute x2, waiting for transfers between devices, rotated_prefix(): seed = seed + lax.ppermute(seed, axis, pairs)  10.2 us
    pallas_call x1, Pallas kernels, local(): head(step_levels, next_levels, hidden, queries, stats_own, stats_other, m...  6.13 us
    ppermute x1, starting transfers between devices, local(): lax.ppermute(step_levels, 'step', [((h + 1) % steps, h) for h in range(st...  5.77 us
    ppermute x1, starting transfers between devices, rotated_prefix(): lax.ppermute(seed, axis, [(holder(q), q + shift) for q in range(steps - s...  3.63 us
    ppermute x2, starting transfers between devices, rotated_prefix(): seed = seed + lax.ppermute(seed, axis, pairs)  3.3 us
    ppermute x1, waiting for transfers between devices, rotated_prefix(): lax.ppermute(seed, axis, [(holder(q), q + shift) for q in range(steps - s...  2.51 us
    ppermute x1, starting transfers between devices, rotated_prefix(): lax.ppermute(jnp.concatenate([seed, denoised], axis=0), axis, [(h, (h + 1...  2.35 us
  transfers between devices with their start and end apart: 9, of which 7 were waited for; matrix products, arithmetic and copies ran while one was open for 0% of the time, Pallas kernels for 0%

profile of v16, /device:TPU:0, one launch (start us, length us, event | category | flops | bytes accessed | tf_op | source)
XLA Modules:
  0.0 58.0 jit_solution(2097291307522666612)
XLA Ops:
  0.6 0.5 collective-permute-start.3
  1.1 0.1 collective-permute-start.1
  1.2 0.4 collective-permute-start.2
  1.7 1.0 %collective-permute-done.1.refs_3_ = f32[4,16,512]{2,1,0:T(8,128)S(1)} collective-permute-done((f32[4,16,512]{2,1,0:T(8,128)}, f32[4,16,512]{2,1,0:T(8,128)S(1)}, u32[]{:S(2)}, u32[]{:S(2)}) %collective-permute-start.1) | collective-permute-done | bytes 131104 | tf_op jit(solution)/shard_map/ppermute | solution.py:352
  2.7 0.0 copy-start.1
  2.7 0.2 collective-permute-done.2.refs_4_
  2.9 0.0 copy-start.2
  2.9 0.0 collective-permute-done.3.refs_6_
  2.9 0.5 copy-done.1
  3.4 0.2 copy-done.2
  3.6 0.0 copy-start
  3.6 0.7 %copy-done = bf16[12,16,512]{2,1,0:T(8,128)(2,1)} copy-done((bf16[12,16,512]{2,1,0:T(8,128)(2,1)}, bf16[12,16,512]{2,1,0:T(8,128)(2,1)S(1)}, u32[]{:S(2)}) %copy-start) | copy-done | bytes 196632
  4.2 13.2 %shard_map.122 = (bf16[128,8192]{1,0:T(8,128)(2,1)}, f32[128,512]{1,0:T(8,128)}, f32[128,128]{1,0:T(8,128)}) custom-call(s32[1,2]{1,0:T(1,128)} %refs_0_.3, f32[1,4,16,512]{3,2,1,0:T(8,128)} %refs_8_.3, f32[4,16,512]{2,1,0:T(8,128)} %refs_9_.3, f32[4,16,512]{2,1,0:T(8,128)} %copy-done.1, f32[1,4,16,512]{3,2,1,0:T(8,128)} %copy-done.2, ...), custom_call_target="tpu_custom_call" | custom-call | tf_op jit(solution)/shard_map/pallas_call | solution.py:380
  17.5 0.4 collective-permute-start.4
  17.8 5.8 %collective-permute-start = (s32[1,2]{1,0:T(1,128)}, s32[1,2]{1,0:T(1,128)S(1)}, u32[]{:S(2)}, u32[]{:S(2)}) collective-permute-start(s32[1,2]{1,0:T(1,128)} %refs_0_.3), channel_id=1, source_target_pairs={{2,0},{4,2},{6,4},{8,6},{10,8},{12,10},{14,12},{0,14},{3,1},{5,3},... | collective-permute-start | bytes 32 | tf_op jit(solution)/shard_map/ppermute | solution.py:349
  23.6 1.4 %collective-permute-done.refs_1_ = s32[1,2]{1,0:T(1,128)S(1)} collective-permute-done((s32[1,2]{1,0:T(1,128)}, s32[1,2]{1,0:T(1,128)S(1)}, u32[]{:S(2)}, u32[]{:S(2)}) %collective-permute-start) | collective-permute-done | bytes 40 | tf_op jit(solution)/shard_map/ppermute | solution.py:349
  25.1 0.0 copy-start.4
  25.1 0.0 collective-permute-done.4.refs_5_
  25.1 0.0 copy-start.3
  25.1 0.6 %copy-done.4 = s32[1,2]{1,0:T(1,128)} copy-done((s32[1,2]{1,0:T(1,128)}, s32[1,2]{1,0:T(1,128)S(1)}, u32[]{:S(2)}) %copy-start.4) | copy-done | bytes 32
  25.6 0.0 copy-done.3
  25.7 6.1 %shard_map.123 = (f32[4,16,512]{2,1,0:T(8,128)}, f32[4,16,512]{2,1,0:T(8,128)}) custom-call(s32[1,2]{1,0:T(1,128)} %refs_0_.3, s32[1,2]{1,0:T(1,128)} %copy-done.4, bf16[128,8192]{1,0:T(8,128)(2,1)} %get-tuple-element.7.refs_2_, f32[128,512]{1,0:T(8,128)} %get-tuple-element.8.refs_3_, f32[128,128]{1,0:T(8,128)} %get-tuple-element.9.refs_4_, ...), custom_call_target="tpu_custom_call" | custom-call | tf_op jit(solution)/shard_map/pallas_call | solution.py:409
  31.8 2.0 %collective-permute-start.5 = (f32[4,16,512]{2,1,0:T(8,128)}, f32[4,16,512]{2,1,0:T(8,128)S(1)}, u32[]{:S(2)}, u32[]{:S(2)}) collective-permute-start(f32[4,16,512]{2,1,0:T(8,128)} %get-tuple-element.10), channel_id=1, source_target_pairs={{14,0},{0,2},{2,4},{4,6},{6,8},{8,10},{10,12},{15,1},{1,3},{3,5},{... | collective-permute-start | bytes 393224 | tf_op jit(solution)/shard_map/ppermute | solution.py:423
  33.8 7.8 %collective-permute-done.5 = f32[4,16,512]{2,1,0:T(8,128)S(1)} collective-permute-done((f32[4,16,512]{2,1,0:T(8,128)}, f32[4,16,512]{2,1,0:T(8,128)S(1)}, u32[]{:S(2)}, u32[]{:S(2)}) %collective-permute-start.5) | collective-permute-done | bytes 131104 | tf_op jit(solution)/shard_map/ppermute | solution.py:423
  41.6 0.9 %add.9 = f32[4,16,512]{2,1,0:T(8,128)S(1)} add(f32[4,16,512]{2,1,0:T(8,128)} %get-tuple-element.10, f32[4,16,512]{2,1,0:T(8,128)S(1)} %collective-permute-done.5) | non-fusion elementwise | flops 32768 | bytes 393216 | tf_op jit(solution)/shard_map/add | solution.py:423
  42.5 1.3 %collective-permute-start.6 = (f32[4,16,512]{2,1,0:T(8,128)S(1)}, f32[4,16,512]{2,1,0:T(8,128)S(1)}, u32[]{:S(2)}, u32[]{:S(2)}) collective-permute-start(f32[4,16,512]{2,1,0:T(8,128)S(1)} %add.9), channel_id=1, source_target_pairs={{14,2},{0,4},{2,6},{4,8},{6,10},{8,12},{15,3},{1,5},{3,7},{5,9},{7... | collective-permute-start | bytes 393224 | tf_op jit(solution)/shard_map/ppermute | solution.py:423
  43.8 2.5 %collective-permute-done.6 = f32[4,16,512]{2,1,0:T(8,128)S(1)} collective-permute-done((f32[4,16,512]{2,1,0:T(8,128)S(1)}, f32[4,16,512]{2,1,0:T(8,128)S(1)}, u32[]{:S(2)}, u32[]{:S(2)}) %collective-permute-start.6) | collective-permute-done | bytes 131104 | tf_op jit(solution)/shard_map/ppermute | solution.py:423
  46.3 0.9 %pad_maximum_fusion = f32[8,16,512]{2,1,0:T(8,128)S(1)} fusion(f32[4,16,512]{2,1,0:T(8,128)} %get-tuple-element.11, f32[4,16,512]{2,1,0:T(8,128)S(1)} %add.10), kind=kLoop, calls=%fused_computation | loop fusion | flops 65536 | bytes 524288 | tf_op jit(solution)/shard_map/concatenate | solution.py:426
  47.3 2.3 %collective-permute-start.7 = (f32[8,16,512]{2,1,0:T(8,128)S(1)}, f32[8,16,512]{2,1,0:T(8,128)S(1)}, u32[]{:S(2)}, u32[]{:S(2)}) collective-permute-start(f32[8,16,512]{2,1,0:T(8,128)S(1)} %pad_maximum_fusion), channel_id=1, source_target_pairs={{0,2},{2,4},{4,6},{6,8},{8,10},{10,12},{12,14},{14,0},{1,3},{3,5},... | collective-permute-start | bytes 786440 | tf_op jit(solution)/shard_map/ppermute | solution.py:425
  49.6 3.6 %collective-permute-start.8 = (f32[4,16,512]{2,1,0:T(8,128)S(1)}, f32[4,16,512]{2,1,0:T(8,128)S(1)}, u32[]{:S(2)}, u32[]{:S(2)}) collective-permute-start(f32[4,16,512]{2,1,0:T(8,128)S(1)} %add.10), channel_id=1, source_target_pairs={{14,8},{0,10},{2,12},{4,14},{15,9},{1,11},{3,13},{5,15},{30,24},{1... | collective-permute-start | bytes 393224 | tf_op jit(solution)/shard_map/ppermute | solution.py:431
  53.3 2.5 %collective-permute-done.8 = f32[4,16,512]{2,1,0:T(8,128)S(1)} collective-permute-done((f32[4,16,512]{2,1,0:T(8,128)S(1)}, f32[4,16,512]{2,1,0:T(8,128)S(1)}, u32[]{:S(2)}, u32[]{:S(2)}) %collective-permute-start.8) | collective-permute-done | bytes 131104 | tf_op jit(solution)/shard_map/ppermute | solution.py:431
  55.8 1.6 %collective-permute-done.7 = f32[8,16,512]{2,1,0:T(8,128)S(1)} collective-permute-done((f32[8,16,512]{2,1,0:T(8,128)S(1)}, f32[8,16,512]{2,1,0:T(8,128)S(1)}, u32[]{:S(2)}, u32[]{:S(2)}) %collective-permute-start.7) | collective-permute-done | bytes 262176 | tf_op jit(solution)/shard_map/ppermute | solution.py:425
  57.3 0.7 %slice_bitcast_fusion = (f32[1,4,16,512]{3,2,1,0:T(8,128)}, f32[1,4,16,512]{3,2,1,0:T(8,128)}) fusion(f32[8,16,512]{2,1,0:T(8,128)S(1)} %collective-permute-done.7, f32[4,16,512]{2,1,0:T(8,128)S(1)} %collective-permute-done.8), kind=kLoop, calls=%fused_computation.1 | loop fusion | flops 32768 | bytes 655360 | tf_op jit(solution)/shard_map/broadcast_in_dim | solution.py:414
  (1 shorter events, 0.0 us)
Async XLA Ops:
  0.6 2.3 %collective-permute-start.3 = (bf16[12,16,512]{2,1,0:T(8,128)(2,1)}, bf16[12,16,512]{2,1,0:T(8,128)(2,1)S(1)}, u32[]{:S(2)}, u32[]{:S(2)}) collective-permute-start(bf16[12,16,512]{2,1,0:T(8,128)(2,1)} %refs_5_.1), channel_id=1, source_target_pairs={{0,1},{1,0},{2,3},{3,2},{4,5},{5,4},{6,7},{7,6},{8,9},{9,8},{10,11... | collective-permute-start | bytes 589832 | tf_op jit(solution)/shard_map/ppermute | solution.py:353
  1.1 1.6 %collective-permute-start.1 = (f32[4,16,512]{2,1,0:T(8,128)}, f32[4,16,512]{2,1,0:T(8,128)S(1)}, u32[]{:S(2)}, u32[]{:S(2)}) collective-permute-start(f32[4,16,512]{2,1,0:T(8,128)} %refs_9_.3), channel_id=1, source_target_pairs={{0,1},{1,0},{2,3},{3,2},{4,5},{5,4},{6,7},{7,6},{8,9},{9,8},{10,11... | collective-permute-start | bytes 393224 | tf_op jit(solution)/shard_map/ppermute | solution.py:352
  1.2 1.7 %collective-permute-start.2 = (f32[1,4,16,512]{3,2,1,0:T(8,128)}, f32[1,4,16,512]{3,2,1,0:T(8,128)S(1)}, u32[]{:S(2)}, u32[]{:S(2)}) collective-permute-start(f32[1,4,16,512]{3,2,1,0:T(8,128)} %refs_8_.3), channel_id=1, source_target_pairs={{0,1},{1,0},{2,3},{3,2},{4,5},{5,4},{6,7},{7,6},{8,9},{9,8},{10,11... | collective-permute-start | bytes 393224 | tf_op jit(solution)/shard_map/ppermute | solution.py:351
  2.7 0.7 %copy-start.1 = (f32[4,16,512]{2,1,0:T(8,128)}, f32[4,16,512]{2,1,0:T(8,128)S(1)}, u32[]{:S(2)}) copy-start(f32[4,16,512]{2,1,0:T(8,128)S(1)} %collective-permute-done.1.refs_3_) | copy-start | bytes 393220
  2.9 0.7 %copy-start.2 = (f32[1,4,16,512]{3,2,1,0:T(8,128)}, f32[1,4,16,512]{3,2,1,0:T(8,128)S(1)}, u32[]{:S(2)}) copy-start(f32[1,4,16,512]{3,2,1,0:T(8,128)S(1)} %collective-permute-done.2.refs_4_) | copy-start | bytes 393220
  3.6 0.7 %copy-start = (bf16[12,16,512]{2,1,0:T(8,128)(2,1)}, bf16[12,16,512]{2,1,0:T(8,128)(2,1)S(1)}, u32[]{:S(2)}) copy-start(bf16[12,16,512]{2,1,0:T(8,128)(2,1)S(1)} %collective-permute-done.3.refs_6_) | copy-start | bytes 589828
  17.5 7.6 %collective-permute-start.4 = (f32[128,128]{1,0:T(8,128)}, f32[128,128]{1,0:T(8,128)S(1)}, u32[]{:S(2)}, u32[]{:S(2)}) collective-permute-start(f32[128,128]{1,0:T(8,128)} %get-tuple-element.9.refs_4_), channel_id=1, source_target_pairs={{0,1},{1,0},{2,3},{3,2},{4,5},{5,4},{6,7},{7,6},{8,9},{9,8},{10,11... | collective-permute-start | bytes 196616 | tf_op jit(solution)/shard_map/ppermute | solution.py:394
  17.8 7.2 %collective-permute-start = (s32[1,2]{1,0:T(1,128)}, s32[1,2]{1,0:T(1,128)S(1)}, u32[]{:S(2)}, u32[]{:S(2)}) collective-permute-start(s32[1,2]{1,0:T(1,128)} %refs_0_.3), channel_id=1, source_target_pairs={{2,0},{4,2},{6,4},{8,6},{10,8},{12,10},{14,12},{0,14},{3,1},{5,3},... | collective-permute-start | bytes 32 | tf_op jit(solution)/shard_map/ppermute | solution.py:349
  25.1 0.6 %copy-start.4 = (s32[1,2]{1,0:T(1,128)}, s32[1,2]{1,0:T(1,128)S(1)}, u32[]{:S(2)}) copy-start(s32[1,2]{1,0:T(1,128)S(1)} %collective-permute-done.refs_1_) | copy-start | bytes 28
  25.1 0.6 %copy-start.3 = (f32[128,128]{1,0:T(8,128)}, f32[128,128]{1,0:T(8,128)S(1)}, u32[]{:S(2)}) copy-start(f32[128,128]{1,0:T(8,128)S(1)} %collective-permute-done.4.refs_5_) | copy-start | bytes 196612
  31.8 9.8 %collective-permute-start.5 = (f32[4,16,512]{2,1,0:T(8,128)}, f32[4,16,512]{2,1,0:T(8,128)S(1)}, u32[]{:S(2)}, u32[]{:S(2)}) collective-permute-start(f32[4,16,512]{2,1,0:T(8,128)} %get-tuple-element.10), channel_id=1, source_target_pairs={{14,0},{0,2},{2,4},{4,6},{6,8},{8,10},{10,12},{15,1},{1,3},{3,5},{... | collective-permute-start | bytes 393224 | tf_op jit(solution)/shard_map/ppermute | solution.py:423
  42.5 3.8 %collective-permute-start.6 = (f32[4,16,512]{2,1,0:T(8,128)S(1)}, f32[4,16,512]{2,1,0:T(8,128)S(1)}, u32[]{:S(2)}, u32[]{:S(2)}) collective-permute-start(f32[4,16,512]{2,1,0:T(8,128)S(1)} %add.9), channel_id=1, source_target_pairs={{14,2},{0,4},{2,6},{4,8},{6,10},{8,12},{15,3},{1,5},{3,7},{5,9},{7... | collective-permute-start | bytes 393224 | tf_op jit(solution)/shard_map/ppermute | solution.py:423
  47.3 10.1 %collective-permute-start.7 = (f32[8,16,512]{2,1,0:T(8,128)S(1)}, f32[8,16,512]{2,1,0:T(8,128)S(1)}, u32[]{:S(2)}, u32[]{:S(2)}) collective-permute-start(f32[8,16,512]{2,1,0:T(8,128)S(1)} %pad_maximum_fusion), channel_id=1, source_target_pairs={{0,2},{2,4},{4,6},{6,8},{8,10},{10,12},{12,14},{14,0},{1,3},{3,5},... | collective-permute-start | bytes 786440 | tf_op jit(solution)/shard_map/ppermute | solution.py:425
  49.6 6.1 %collective-permute-start.8 = (f32[4,16,512]{2,1,0:T(8,128)S(1)}, f32[4,16,512]{2,1,0:T(8,128)S(1)}, u32[]{:S(2)}, u32[]{:S(2)}) collective-permute-start(f32[4,16,512]{2,1,0:T(8,128)S(1)} %add.10), channel_id=1, source_target_pairs={{14,8},{0,10},{2,12},{4,14},{15,9},{1,11},{3,13},{5,15},{30,24},{1... | collective-permute-start | bytes 393224 | tf_op jit(solution)/shard_map/ppermute | solution.py:431
